TPU v7x, 256 devices: a whole 4x4x8 slice. The times are simulated.
256 devices in a mesh: ctx: 64 (over x, y_hi, z), pipe: 4 (over y_lo, core).
Axes of the slice: x: 4, y: 4 (y_hi: 2, y_lo: 2; y = y_hi * 2 + y_lo), z: 8, core: 2. Of those that a mesh axis runs over, the one named last changes fastest.
Arguments:
- inputs: bfloat16 [4, 8192, 4096], P('pipe', 'ctx'), may hold values from -16 to 16
- q_raw: bfloat16 [4, 8192, 2048], P('pipe', 'ctx'), may hold values from -6 to 6
- grad_out: bfloat16 [4, 8192, 2048], P('pipe', 'ctx'), may hold values from -6 to 6
- segments: int32 [4, 8192], P('pipe'), may hold values from 0 to 4, never falling along the last dimension, each value on 1 to 3072 neighbouring positions
- w_key: bfloat16 [4, 4096, 512], P('pipe', 'ctx'), may hold values from -0.09375 to 0.09375
- w_value: bfloat16 [4, 4096, 512], P('pipe', 'ctx'), may hold values from -0.09375 to 0.09375
- q_gain: float32 [4, 128], P('pipe'), may hold values from 0.1 to 1.9
- k_gain: float32 [4, 128], P('pipe'), may hold values from 0.1 to 1.9
Outputs:
- query_grad: bfloat16 [4, 8192, 2048], P('pipe', 'ctx')
- key_weight_grad: float32 [4, 4096, 512], P('pipe', 'ctx')
- value_weight_grad: float32 [4, 4096, 512], P('pipe', 'ctx')
- section_grad: bfloat16 [4, 8192, 4096], P('pipe', 'ctx')
Inputs may be any that keep to these rules, and one draw needn't show every extreme that they name: `segments`: along each section's sequence the document numbers never fall; every document has 1 to 3072 tokens and one has exactly 3072.
All inputs are finite; a program needn't handle non-finite values.
Results may differ from a plain program's by a relative error of at most 0.019.
Values may be sent and summed in bfloat16 or wider, within the bound.
No kernel may reach another device: no remote copies, remote signals or barrier semaphores. Data moves between devices by JAX's collectives and lax.ppermute only.
A program may use at most 128 MiB of HBM per device.

v0:
```python
import jax
import jax.numpy as jnp
from jax import lax
from jax.sharding import PartitionSpec as P

HEAD = 128
WINDOW = 768


epsilon = 1e-06
theta_base = 1000000.0


def passed_along(block, axis, distance):
    devices = range(lax.axis_size(axis))
    route = [(i - distance, i) for i in devices if i - distance in devices]
    return lax.ppermute(block, axis, route)


def shifted(shard, axis, by):
    devices = lax.axis_size(axis)
    return lax.ppermute(shard, axis, [(i, (i + by) % devices) for i in range(devices)])


def rope_tables(positions):
    half_width = HEAD // 2
    frequency = jnp.exp(
        jnp.arange(half_width, dtype=jnp.float32) * (-2.0 * jnp.log(jnp.float32(theta_base)) / HEAD)
    )
    angles = positions.astype(jnp.float32)[:, None] * frequency[None, :]
    return (jnp.cos(angles), jnp.sin(angles))


def rotate(values, cosine, sine_table):
    half_width = values.shape[-1] // 2
    front_half = values[..., :half_width]
    back_half = values[..., half_width:]
    cos_b = cosine[:, None, :]
    sin_b = sine_table[:, None, :]
    return jnp.concatenate(
        [front_half * cos_b - back_half * sin_b, back_half * cos_b + front_half * sin_b], -1
    )


def unrotate(upstream, cosine, sine_table):
    half_width = upstream.shape[-1] // 2
    front_half = upstream[..., :half_width]
    back_half = upstream[..., half_width:]
    cos_b = cosine[:, None, :]
    sin_b = sine_table[:, None, :]
    return jnp.concatenate(
        [front_half * cos_b + back_half * sin_b, back_half * cos_b - front_half * sin_b], -1
    )


def normalize(values, gain_row):
    inverse = lax.rsqrt(jnp.mean(values * values, -1, keepdims=True) + epsilon)
    return (values * inverse * gain_row, inverse)


def normalize_back(values, inverse, gain_row, upstream):
    scaled = upstream * gain_row
    cubed = inverse * inverse * inverse
    return inverse * scaled - values * cubed * jnp.mean(values * scaled, -1, keepdims=True)


def guarded(tile_work, operands):
    return tile_work(*operands)


def local(inputs, q_raw, grad_out, segments, w_key, w_value, q_gain, k_gain):
    tokens_here = inputs[0]
    tok_rows = tokens_here.shape[0]
    kv_width = w_key.shape[2]
    kv_heads = kv_width // HEAD
    q_heads = q_raw.shape[2] // HEAD
    group = q_heads // kv_heads
    score_scale = HEAD ** (-0.5)
    reach_blocks = WINDOW // tok_rows
    ctx_index = lax.axis_index("ctx")
    key_full, value_full = (
        lax.all_gather(w_key[0], "ctx", axis=0, tiled=True),
        lax.all_gather(w_value[0], "ctx", axis=0, tiled=True),
    )
    key_raw = jnp.dot(tokens_here, key_full, preferred_element_type=jnp.float32).astype(
        jnp.bfloat16
    )
    value_own = (
        jnp.dot(tokens_here, value_full, preferred_element_type=jnp.float32)
        .astype(jnp.bfloat16)
        .reshape(tok_rows, kv_heads, HEAD)
    )
    local_pos = jnp.arange(tok_rows, dtype=jnp.int32)
    positions = ctx_index * tok_rows + local_pos
    cosine, sine_table = rope_tables(positions)
    query_in = q_raw[0].astype(jnp.float32).reshape(tok_rows, q_heads, HEAD)
    query_norm, query_inv = normalize(query_in, q_gain[0])
    query_rot = rotate(query_norm, cosine, sine_table).astype(jnp.bfloat16)
    key_in = key_raw.astype(jnp.float32).reshape(tok_rows, kv_heads, HEAD)
    key_norm, key_inv = normalize(key_in, k_gain[0])
    key_rot = rotate(key_norm, cosine, sine_table).astype(jnp.bfloat16)
    own_pair = jnp.stack([key_rot, value_own])
    key_blocks = [own_pair]
    for distance in range(1, reach_blocks + 1):
        key_blocks.append(passed_along(own_pair, "ctx", distance))
    seg_all = segments[0]
    seg_query = lax.dynamic_slice_in_dim(seg_all, ctx_index * tok_rows, tok_rows)
    allowed_list = []
    for distance in range(reach_blocks + 1):
        key_pos = (ctx_index - distance) * tok_rows + local_pos
        seg_key = lax.dynamic_slice_in_dim(
            seg_all, jnp.maximum(ctx_index - distance, 0) * tok_rows, tok_rows
        )
        offset = positions[:, None] - key_pos[None, :]
        allowed = (
            (offset >= 0)
            & (offset < WINDOW)
            & (key_pos >= 0)[None, :]
            & (seg_query[:, None] == seg_key[None, :])
        )
        allowed_list.append(allowed)
    q_group = query_rot.reshape(tok_rows, kv_heads, group, HEAD)
    out_grad = grad_out[0].reshape(tok_rows, kv_heads, group, HEAD)

    def exp_block(key_pair, allowed):
        scores = (
            jnp.einsum("qgrd,kgd->grqk", q_group, key_pair[0], preferred_element_type=jnp.float32)
            * score_scale
        )
        return jnp.where(allowed, jnp.exp(scores), 0.0)

    def total_block(key_pair, allowed):
        return jnp.sum(exp_block(key_pair, allowed), -1)

    zero_total = jnp.zeros((kv_heads, group, tok_rows), jnp.float32)
    row_total = zero_total
    for distance in range(reach_blocks + 1):
        row_total = row_total + guarded(total_block, (key_blocks[distance], allowed_list[distance]))

    def prob_block(key_pair, allowed):
        prob_tile = (exp_block(key_pair, allowed) / row_total[..., None]).astype(jnp.bfloat16)
        out_tile = jnp.einsum(
            "grqk,kgd->qgrd", prob_tile, key_pair[1], preferred_element_type=jnp.float32
        )
        return (prob_tile, out_tile)

    zero_query = jnp.zeros((tok_rows, kv_heads, group, HEAD), jnp.float32)
    prob_list = []
    attn_out = zero_query
    for distance in range(reach_blocks + 1):
        prob_tile, out_tile = guarded(prob_block, (key_blocks[distance], allowed_list[distance]))
        prob_list.append(prob_tile)
        attn_out = attn_out + out_tile
    row_delta = jnp.sum(out_grad.astype(jnp.float32) * attn_out, -1).transpose(1, 2, 0)[..., None]

    def grad_block(key_pair, prob_tile):
        prob_grad = jnp.einsum(
            "qgrd,kgd->grqk", out_grad, key_pair[1], preferred_element_type=jnp.float32
        )
        score_grad = (prob_tile.astype(jnp.float32) * (prob_grad - row_delta)).astype(jnp.bfloat16)
        value_grad = jnp.einsum(
            "grqk,qgrd->kgd", prob_tile, out_grad, preferred_element_type=jnp.float32
        )
        key_grad = (
            jnp.einsum("grqk,qgrd->kgd", score_grad, q_group, preferred_element_type=jnp.float32)
            * score_scale
        )
        query_part = (
            jnp.einsum(
                "grqk,kgd->qgrd", score_grad, key_pair[0], preferred_element_type=jnp.float32
            )
            * score_scale
        )
        return (query_part, jnp.stack([key_grad, value_grad]))

    zero_pair = jnp.zeros((2, tok_rows, kv_heads, HEAD), jnp.float32)
    query_rot_grad = zero_query
    kv_total = zero_pair
    for distance in range(reach_blocks + 1):
        query_part, kv_part = guarded(grad_block, (key_blocks[distance], prob_list[distance]))
        query_rot_grad = query_rot_grad + query_part
        if distance == 0:
            kv_total = kv_part
        else:
            returned = passed_along(kv_part.astype(jnp.bfloat16), "ctx", -distance)
            kv_total = kv_total + returned.astype(jnp.float32)
    query_grad = normalize_back(
        query_in,
        query_inv,
        q_gain[0],
        unrotate(query_rot_grad.reshape(tok_rows, q_heads, HEAD), cosine, sine_table),
    )
    query_grad = query_grad.reshape(tok_rows, q_heads * HEAD).astype(jnp.bfloat16)
    key_back = normalize_back(key_in, key_inv, k_gain[0], unrotate(kv_total[0], cosine, sine_table))
    key_back = key_back.reshape(tok_rows, kv_width).astype(jnp.bfloat16)
    value_back = kv_total[1].reshape(tok_rows, kv_width).astype(jnp.bfloat16)
    both_back = jnp.concatenate([key_back, value_back], 1)
    grad_rows = lax.psum_scatter(
        lax.dot_general(
            tokens_here, both_back, (((0,), (0,)), ((), ())), preferred_element_type=jnp.float32
        ),
        "ctx",
        scatter_dimension=0,
        tiled=True,
    )
    input_grad = lax.dot_general(
        key_back, key_full, (((1,), (1,)), ((), ())), preferred_element_type=jnp.float32
    )
    input_grad = input_grad + lax.dot_general(
        value_back, value_full, (((1,), (1,)), ((), ())), preferred_element_type=jnp.float32
    )
    passed = shifted(input_grad.astype(jnp.bfloat16), "pipe", -1)
    return (
        query_grad[None],
        grad_rows[:, :kv_width][None],
        grad_rows[:, kv_width:][None],
        passed[None],
    )


def solution(mesh):
    return jax.shard_map(
        local,
        mesh=mesh,
        in_specs=(
            P("pipe", "ctx", None),
            P("pipe", "ctx", None),
            P("pipe", "ctx", None),
            P("pipe", None),
            P("pipe", "ctx", None),
            P("pipe", "ctx", None),
            P("pipe", None),
            P("pipe", None),
        ),
        out_specs=(
            P("pipe", "ctx", None),
            P("pipe", "ctx", None),
            P("pipe", "ctx", None),
            P("pipe", "ctx", None),
        ),
        check_vma=False,
    )
```

profile of v0, /device:TPU:0, one launch (start us, length us, event | category | flops | bytes accessed | tf_op | source)
XLA Modules:
  0.0 868.9 jit_solution(1845894031588987251)
XLA Ops:
  8.8 1.3 copy.348
  16.9 1.5 pad_maximum_fusion.1
  20.3 120.0 %all-gather.7.cloned.1.call-done = bf16[1,4096,512]{2,1,0:T(8,128)(2,1)} async-done(((bf16[1,64,512]{2,1,0:T(8,128)(2,1)}), bf16[1,4096,512]{2,1,0:T(8,128)(2,1)}) %all-gather.7.cloned.1.call-update) | async-done | bytes 4194320 | tf_op jit(solution)/shard_map/all_gather | solution.py:83
  140.3 2.9 fusion.76
  144.0 124.1 %all-gather.5.cloned.1.call-done = bf16[1,4096,512]{2,1,0:T(8,128)(2,1)} async-done(((bf16[1,64,512]{2,1,0:T(8,128)(2,1)}), bf16[1,4096,512]{2,1,0:T(8,128)(2,1)}) %all-gather.5.cloned.1.call-update) | async-done | bytes 4194320 | tf_op jit(solution)/shard_map/all_gather | solution.py:82
  268.1 2.9 fusion.73
  271.8 1.8 multiply_reduce_fusion.2
  273.6 1.5 copy.342
  276.4 1.4 copy.554
  277.8 1.5 fusion.116
  282.0 1.7 pad_maximum_fusion.2
  283.7 4.4 collective-permute-start.5
  288.1 6.4 collective-permute-start.4
  294.4 4.0 collective-permute-start.3
  298.4 6.3 collective-permute-start.2
  304.7 4.3 collective-permute-start.1
  309.0 1.7 copy.433
  310.6 1.4 copy.418
  312.1 1.4 fusion.171
  313.4 2.7 collective-permute-start
  320.0 1.3 collective-permute-done.2
  322.7 13.7 %collective-permute-done.1 = bf16[2,128,4,128]{3,1,2,0:T(8,128)(2,1)} collective-permute-done((bf16[2,128,4,128]{3,1,2,0:T(8,128)(2,1)}, bf16[2,128,4,128]{3,1,2,0:T(8,128)(2,1)}, u32[]{:S(2)}, u32[]{:S(2)}) %collective-permute-start.1) | collective-permute-done | bytes 262176 | tf_op jit(solution)/shard_map/ppermute | solution.py:17
  337.6 2.2 collective-permute-done
  348.8 1.5 fusion.61
  359.3 1.3 collective-permute-start.6
  366.4 2.5 collective-permute-done.6
  368.9 1.5 collective-permute-start.11
  371.0 10.9 %collective-permute-done.7 = bf16[2,128,4,128]{3,1,2,0:T(8,128)(2,1)S(1)} collective-permute-done((bf16[2,128,4,128]{3,1,2,0:T(8,128)(2,1)S(1)}, bf16[2,128,4,128]{3,1,2,0:T(8,128)(2,1)S(1)}, u32[]{:S(2)}, u32[]{:S(2)}) %collective-permute-start.7) | collective-permute-done | bytes 262176 | tf_op jit(solution)/shard_map/ppermute | solution.py:17
  382.0 9.7 %collective-permute-done.8 = bf16[2,128,4,128]{3,1,2,0:T(8,128)(2,1)S(1)} collective-permute-done((bf16[2,128,4,128]{3,1,2,0:T(8,128)(2,1)S(1)}, bf16[2,128,4,128]{3,1,2,0:T(8,128)(2,1)S(1)}, u32[]{:S(2)}, u32[]{:S(2)}) %collective-permute-start.8) | collective-permute-done | bytes 262176 | tf_op jit(solution)/shard_map/ppermute | solution.py:17
  391.7 9.5 %collective-permute-done.11 = bf16[2,128,4,128]{3,1,2,0:T(8,128)(2,1)S(1)} collective-permute-done((bf16[2,128,4,128]{3,1,2,0:T(8,128)(2,1)S(1)}, bf16[2,128,4,128]{3,1,2,0:T(8,128)(2,1)S(1)}, u32[]{:S(2)}, u32[]{:S(2)}) %collective-permute-start.11) | collective-permute-done | bytes 262176 | tf_op jit(solution)/shard_map/ppermute | solution.py:17
  405.3 9.1 %convolution_bitcast_fusion = f32[4096,1024]{0,1:T(8,128)} fusion(bf16[1,128,4096]{2,1,0:T(8,128)(2,1)S(1)} %copy-done, bf16[128,512]{1,0:T(8,128)(2,1)} %bitcast.613, bf16[128,512]{1,0:T(8,128)(2,1)S(1)} %fusion.115), kind=kOutput, calls=%fused_computation | convolution fusion | flops 1074266112 | bytes 18087936 | tf_op jit(solution)/shard_map/dot_general | solution.py:199
  414.4 17.5 %copy.546 = f32[4096,1024]{1,0:T(8,128)} copy(f32[4096,1024]{0,1:T(8,128)} %convolution_bitcast_fusion) | data formatting | bytes 33554432
  434.2 1.3 mul.514
  435.5 2.4 mul.515
  438.4 1.5 fusion.121
  439.9 1.3 fusion.122
  444.1 1.4 fusion.20
  445.7 1.4 copy.549
  447.1 1.4 copy.548
  448.5 1.9 multiply_add_fusion
  451.3 1.5 fusion.4
  453.5 2.5 fusion
  456.9 1.3 multiply_reduce_fusion
  459.7 2.4 concatenate.48
  462.2 3.1 fusion.105
  465.3 10.3 %collective-permute-done.12 = bf16[128,4096]{1,0:T(8,128)(2,1)} collective-permute-done((bf16[128,4096]{1,0:T(8,128)(2,1)}, bf16[128,4096]{1,0:T(8,128)(2,1)}, u32[]{:S(2)}, u32[]{:S(2)}) %collective-permute-start.12) | collective-permute-done | bytes 1048608 | tf_op jit(solution)/shard_map/ppermute | solution.py:22
  475.6 381.7 %reduce-scatter.4.cloned.1.call-done = f32[64,1024]{1,0:T(8,128)} async-done(((f32[4096,1024]{1,0:T(8,128)}), f32[64,1024]{1,0:T(8,128)}) %reduce-scatter.4.cloned.1.call-update) | async-done | bytes 262160
  860.1 2.3 copy.572
  (207 shorter events, 62.5 us)
Async XLA Ops:
  7.2 133.2 %copy-start = (bf16[1,128,4096]{2,1,0:T(8,128)(2,1)S(1)}, bf16[1,128,4096]{2,1,0:T(8,128)(2,1)}, u32[]{:S(2)}) copy-start(bf16[1,128,4096]{2,1,0:T(8,128)(2,1)} %param.8) | copy-start | bytes 3145732
  7.2 5.6 copy-start.44
  7.2 133.1 %all-gather.7.cloned.1.call-start = ((), (), s32[]{:S(2)}) async-start(), calls=%async_computation.2 | async-start | bytes 4259840 | tf_op jit(solution)/shard_map/all_gather | solution.py:83
  7.9 260.2 %all-gather.5.cloned.1.call-start = ((), (), s32[]{:S(2)}) async-start(), calls=%async_computation.1 | async-start | bytes 4259840 | tf_op jit(solution)/shard_map/all_gather | solution.py:82
  8.7 848.6 %reduce-scatter.4.cloned.1.call-start = ((), (), s32[]{:S(2)}) async-start(), calls=%async_computation.3 | async-start | bytes 17039360
  12.8 5.6 copy-start.42
  283.7 29.8 %collective-permute-start.5 = (bf16[2,128,4,128]{3,1,2,0:T(8,128)(2,1)}, bf16[2,128,4,128]{3,1,2,0:T(8,128)(2,1)}, u32[]{:S(2)}, u32[]{:S(2)}) collective-permute-start(bf16[2,128,4,128]{3,1,2,0:T(8,128)(2,1)} %pad_maximum_fusion.2), channel_id=1, source_target_pairs={{0,24},{4,28},{8,32},{12,36},{16,40},{20,44},{24,48},{28,52},{32,5... | collective-permute-start | bytes 786440 | tf_op jit(solution)/shard_map/ppermute | solution.py:17
  288.1 29.4 %collective-permute-start.4 = (bf16[2,128,4,128]{3,1,2,0:T(8,128)(2,1)}, bf16[2,128,4,128]{3,1,2,0:T(8,128)(2,1)}, u32[]{:S(2)}, u32[]{:S(2)}) collective-permute-start(bf16[2,128,4,128]{3,1,2,0:T(8,128)(2,1)} %pad_maximum_fusion.2), channel_id=1, source_target_pairs={{0,20},{4,24},{8,28},{12,32},{16,36},{20,40},{24,44},{28,48},{32,5... | collective-permute-start | bytes 786440 | tf_op jit(solution)/shard_map/ppermute | solution.py:17
  294.4 24.3 %collective-permute-start.3 = (bf16[2,128,4,128]{3,1,2,0:T(8,128)(2,1)}, bf16[2,128,4,128]{3,1,2,0:T(8,128)(2,1)}, u32[]{:S(2)}, u32[]{:S(2)}) collective-permute-start(bf16[2,128,4,128]{3,1,2,0:T(8,128)(2,1)} %pad_maximum_fusion.2), channel_id=1, source_target_pairs={{0,16},{4,20},{8,24},{12,28},{16,32},{20,36},{24,40},{28,44},{32,4... | collective-permute-start | bytes 786440 | tf_op jit(solution)/shard_map/ppermute | solution.py:17
  298.4 22.9 %collective-permute-start.2 = (bf16[2,128,4,128]{3,1,2,0:T(8,128)(2,1)}, bf16[2,128,4,128]{3,1,2,0:T(8,128)(2,1)}, u32[]{:S(2)}, u32[]{:S(2)}) collective-permute-start(bf16[2,128,4,128]{3,1,2,0:T(8,128)(2,1)} %pad_maximum_fusion.2), channel_id=1, source_target_pairs={{0,12},{4,16},{8,20},{12,24},{16,28},{20,32},{24,36},{28,40},{32,4... | collective-permute-start | bytes 786440 | tf_op jit(solution)/shard_map/ppermute | solution.py:17
  304.7 31.7 %collective-permute-start.1 = (bf16[2,128,4,128]{3,1,2,0:T(8,128)(2,1)}, bf16[2,128,4,128]{3,1,2,0:T(8,128)(2,1)}, u32[]{:S(2)}, u32[]{:S(2)}) collective-permute-start(bf16[2,128,4,128]{3,1,2,0:T(8,128)(2,1)} %pad_maximum_fusion.2), channel_id=1, source_target_pairs={{0,8},{4,12},{8,16},{12,20},{16,24},{20,28},{24,32},{28,36},{32,40... | collective-permute-start | bytes 786440 | tf_op jit(solution)/shard_map/ppermute | solution.py:17
  312.1 6.7 copy-start.40
  312.1 9.3 %copy-start.39 = (pred[128,128]{0,1:T(8,128)(4,1)S(1)}, pred[128,128]{0,1:T(8,128)(4,1)}, u32[]{:S(2)}) copy-start(pred[128,128]{0,1:T(8,128)(4,1)} %get-tuple-element.61) | copy-start | bytes 49156
  312.1 24.3 %copy-start.38 = (pred[128,128]{0,1:T(8,128)(4,1)S(1)}, pred[128,128]{0,1:T(8,128)(4,1)}, u32[]{:S(2)}) copy-start(pred[128,128]{0,1:T(8,128)(4,1)} %get-tuple-element.60) | copy-start | bytes 49156
  313.4 26.4 %copy-start.37 = (pred[128,128]{0,1:T(8,128)(4,1)S(1)}, pred[128,128]{0,1:T(8,128)(4,1)}, u32[]{:S(2)}) copy-start(pred[128,128]{0,1:T(8,128)(4,1)} %get-tuple-element.59) | copy-start | bytes 49156
  313.4 26.4 %collective-permute-start = (bf16[2,128,4,128]{3,1,2,0:T(8,128)(2,1)}, bf16[2,128,4,128]{3,1,2,0:T(8,128)(2,1)S(1)}, u32[]{:S(2)}, u32[]{:S(2)}) collective-permute-start(bf16[2,128,4,128]{3,1,2,0:T(8,128)(2,1)} %pad_maximum_fusion.2), channel_id=1, source_target_pairs={{0,4},{4,8},{8,12},{12,16},{16,20},{20,24},{24,28},{28,32},{32,36}... | collective-permute-start | bytes 786440 | tf_op jit(solution)/shard_map/ppermute | solution.py:17
  339.8 18.8 %copy-start.32 = (bf16[2,128,4,128]{3,1,2,0:T(8,128)(2,1)}, bf16[2,128,4,128]{3,1,2,0:T(8,128)(2,1)S(1)}, u32[]{:S(2)}) copy-start(bf16[2,128,4,128]{3,1,2,0:T(8,128)(2,1)S(1)} %collective-permute-done) | copy-start | bytes 786436
  351.5 4.5 copy-start.6
  353.0 4.5 copy-start.8
  354.5 4.4 copy-start.10
  356.0 5.9 copy-start.12
  359.0 7.0 copy-start.13
  359.3 9.6 %collective-permute-start.6 = (bf16[2,128,4,128]{3,1,2,0:T(8,128)(2,1)S(1)}, bf16[2,128,4,128]{3,1,2,0:T(8,128)(2,1)S(1)}, u32[]{:S(2)}, u32[]{:S(2)}) collective-permute-start(bf16[2,128,4,128]{3,1,2,0:T(8,128)(2,1)S(1)} %pad_maximum_fusion.3), channel_id=1, source_target_pairs={{4,0},{8,4},{12,8},{16,12},{20,16},{24,20},{28,24},{32,28},{36,32}... | collective-permute-start | bytes 786440 | tf_op jit(solution)/shard_map/ppermute | solution.py:17
  360.6 21.3 %collective-permute-start.7 = (bf16[2,128,4,128]{3,1,2,0:T(8,128)(2,1)S(1)}, bf16[2,128,4,128]{3,1,2,0:T(8,128)(2,1)S(1)}, u32[]{:S(2)}, u32[]{:S(2)}) collective-permute-start(bf16[2,128,4,128]{3,1,2,0:T(8,128)(2,1)S(1)} %pad_maximum_fusion.4), channel_id=1, source_target_pairs={{8,0},{12,4},{16,8},{20,12},{24,16},{28,20},{32,24},{36,28},{40,32... | collective-permute-start | bytes 786440 | tf_op jit(solution)/shard_map/ppermute | solution.py:17
  362.0 29.7 %collective-permute-start.8 = (bf16[2,128,4,128]{3,1,2,0:T(8,128)(2,1)S(1)}, bf16[2,128,4,128]{3,1,2,0:T(8,128)(2,1)S(1)}, u32[]{:S(2)}, u32[]{:S(2)}) collective-permute-start(bf16[2,128,4,128]{3,1,2,0:T(8,128)(2,1)S(1)} %pad_maximum_fusion.5), channel_id=1, source_target_pairs={{12,0},{16,4},{20,8},{24,12},{28,16},{32,20},{36,24},{40,28},{44,3... | collective-permute-start | bytes 786440 | tf_op jit(solution)/shard_map/ppermute | solution.py:17
  363.3 28.4 %collective-permute-start.9 = (bf16[2,128,4,128]{3,1,2,0:T(8,128)(2,1)S(1)}, bf16[2,128,4,128]{3,1,2,0:T(8,128)(2,1)S(1)}, u32[]{:S(2)}, u32[]{:S(2)}) collective-permute-start(bf16[2,128,4,128]{3,1,2,0:T(8,128)(2,1)S(1)} %pad_maximum_fusion.6), channel_id=1, source_target_pairs={{16,0},{20,4},{24,8},{28,12},{32,16},{36,20},{40,24},{44,28},{48,3... | collective-permute-start | bytes 786440 | tf_op jit(solution)/shard_map/ppermute | solution.py:17
  364.7 27.1 %collective-permute-start.10 = (bf16[2,128,4,128]{3,1,2,0:T(8,128)(2,1)S(1)}, bf16[2,128,4,128]{3,1,2,0:T(8,128)(2,1)S(1)}, u32[]{:S(2)}, u32[]{:S(2)}) collective-permute-start(bf16[2,128,4,128]{3,1,2,0:T(8,128)(2,1)S(1)} %pad_maximum_fusion.7), channel_id=1, source_target_pairs={{20,0},{24,4},{28,8},{32,12},{36,16},{40,20},{44,24},{48,28},{52,3... | collective-permute-start | bytes 786440 | tf_op jit(solution)/shard_map/ppermute | solution.py:17
  366.0 36.4 %copy-start.22 = (f32[128,64]{1,0:T(8,128)S(1)}, f32[128,64]{1,0:T(8,128)}, u32[]{:S(2)}) copy-start(f32[128,64]{1,0:T(8,128)} %copy-done.21) | copy-start | bytes 98308
  366.0 36.4 %copy-start.25 = (f32[128,64]{1,0:T(8,128)S(1)}, f32[128,64]{1,0:T(8,128)}, u32[]{:S(2)}) copy-start(f32[128,64]{1,0:T(8,128)} %copy-done.24) | copy-start | bytes 98308
  366.4 4.7 copy-start.4
  366.4 36.1 %copy-start.43 = (f32[1,128]{1,0:T(1,128)S(1)}, f32[1,128]{1,0:T(1,128)}, u32[]{:S(2)}) copy-start(f32[1,128]{1,0:T(1,128)} %param.15) | copy-start | bytes 1540
  368.9 32.3 %collective-permute-start.11 = (bf16[2,128,4,128]{3,1,2,0:T(8,128)(2,1)S(1)}, bf16[2,128,4,128]{3,1,2,0:T(8,128)(2,1)S(1)}, u32[]{:S(2)}, u32[]{:S(2)}) collective-permute-start(bf16[2,128,4,128]{3,1,2,0:T(8,128)(2,1)S(1)} %pad_maximum_fusion.8), channel_id=1, source_target_pairs={{24,0},{28,4},{32,8},{36,12},{40,16},{44,20},{48,24},{52,28},{56,3... | collective-permute-start | bytes 786440 | tf_op jit(solution)/shard_map/ppermute | solution.py:17
  370.7 34.5 %copy-start.41 = (f32[512]{0:T(512)S(1)}, f32[512]{0:T(512)}, u32[]{:S(2)}) copy-start(f32[512]{0:T(512)} %broadcast_bitcast_fusion.1) | copy-start | bytes 6148
  401.7 12.8 %copy-start.27 = (bf16[1,128,4,128]{3,2,1,0:T(4,128)(2,1)}, bf16[1,128,4,128]{3,2,1,0:T(4,128)(2,1)S(1)}, u32[]{:S(2)}) copy-start(bf16[1,128,4,128]{3,2,1,0:T(4,128)(2,1)S(1)} %copy.421) | copy-start | bytes 393220
  405.3 9.1 %copy-start.29 = (bf16[128,512]{1,0:T(8,128)(2,1)}, bf16[128,512]{1,0:T(8,128)(2,1)S(1)}, u32[]{:S(2)}) copy-start(bf16[128,512]{1,0:T(8,128)(2,1)S(1)} %fusion.115) | copy-start | bytes 393220
  431.9 6.0 copy-start.45
  431.9 6.0 copy-start.5
  431.9 6.0 copy-start.19
  433.1 6.8 copy-start.11
  434.2 7.0 copy-start.9
  435.5 6.9 copy-start.7
  438.0 5.8 copy-start.14
  438.0 5.8 copy-start.33
  439.9 4.2 copy-start.16
  445.7 4.7 copy-start.30
  455.9 19.6 %collective-permute-start.12 = (bf16[128,4096]{1,0:T(8,128)(2,1)}, bf16[128,4096]{1,0:T(8,128)(2,1)}, u32[]{:S(2)}, u32[]{:S(2)}) collective-permute-start(bf16[128,4096]{1,0:T(8,128)(2,1)} %fusion), channel_id=1, source_target_pairs={{0,3},{1,0},{2,1},{3,2},{4,7},{5,4},{6,5},{7,6},{8,11},{9,8},{10,9... | collective-permute-start | bytes 3145736 | tf_op jit(solution)/shard_map/ppermute | solution.py:22
  456.9 5.3 copy-start.20
  459.7 402.6 %copy-start.1 = (bf16[1,128,4096]{2,1,0:T(8,128)(2,1)S(1)}, bf16[1,128,4096]{2,1,0:T(8,128)(2,1)}, u32[]{:S(2)}) copy-start(bf16[1,128,4096]{2,1,0:T(8,128)(2,1)} %param.8) | copy-start | bytes 3145732
  (14 other events, 29.6 us)
Sparse Core Ops, SparseCore 0:
  11.6 128.6 all-gather.6
  143.9 124.1 all-gather.4
  432.0 425.1 reduce-scatter.3
where the time goes:
time: 871 us; the launch traced here: 869 us
  waiting for transfers between devices  687 us (79%)
  local copies, waits for them, and re-layouts  55.3 us (6%)
  matrix products  52.3 us (6%)
  starting transfers between devices  37.1 us (4%)
  other arithmetic  22 us (3%)
  between operations  14.8 us (2%)
    unnamed x4, waiting for transfers between devices  383 us
    all_gather x1, waiting for transfers between devices, local(): lax.all_gather(w_key[0], 'ctx', axis=0, tiled=True)  124 us
    all_gather x1, waiting for transfers between devices, local(): lax.all_gather(w_value[0], 'ctx', axis=0, tiled=True)  120 us
    ppermute x12, waiting for transfers between devices, passed_along(): return lax.ppermute(block, axis, route)  50 us
    ppermute x12, starting transfers between devices, passed_along(): return lax.ppermute(block, axis, route)  36 us
    unnamed x104, local copies, waits for them, and re-layouts  32.2 us
  transfers between devices with their start and end apart: 16, of which 11 were waited for; matrix products, arithmetic and copies ran while one was open for 6% of the time, Pallas kernels for 0%

commit v1 on v0

--- a/solution.py
+++ b/solution.py
@@ -1,7 +1,9 @@
 import jax
 import jax.numpy as jnp
 from jax import lax
-from jax.sharding import PartitionSpec as P
+import functools
+
+from jax.sharding import Mesh, NamedSharding, PartitionSpec as P
 
 HEAD = 128
 WINDOW = 768
@@ -11,14 +13,22 @@
 theta_base = 1000000.0
 
 
+def axis_count(axis):
+    names = axis if isinstance(axis, tuple) else (axis,)
+    count = 1
+    for name in names:
+        count *= lax.axis_size(name)
+    return count
+
+
 def passed_along(block, axis, distance):
-    devices = range(lax.axis_size(axis))
+    devices = range(axis_count(axis))
     route = [(i - distance, i) for i in devices if i - distance in devices]
     return lax.ppermute(block, axis, route)
 
 
 def shifted(shard, axis, by):
-    devices = lax.axis_size(axis)
+    devices = axis_count(axis)
     return lax.ppermute(shard, axis, [(i, (i + by) % devices) for i in range(devices)])
 
 
@@ -68,7 +78,7 @@
     return tile_work(*operands)
 
 
-def local(inputs, q_raw, grad_out, segments, w_key, w_value, q_gain, k_gain):
+def local(inputs, q_raw, grad_out, segments, w_key, w_value, q_gain, k_gain, row_parts, col_parts):
     tokens_here = inputs[0]
     tok_rows = tokens_here.shape[0]
     kv_width = w_key.shape[2]
@@ -77,19 +87,19 @@
     group = q_heads // kv_heads
     score_scale = HEAD ** (-0.5)
     reach_blocks = WINDOW // tok_rows
-    ctx_index = lax.axis_index("ctx")
-    key_full, value_full = (
-        lax.all_gather(w_key[0], "ctx", axis=0, tiled=True),
-        lax.all_gather(w_value[0], "ctx", axis=0, tiled=True),
-    )
-    key_raw = jnp.dot(tokens_here, key_full, preferred_element_type=jnp.float32).astype(
-        jnp.bfloat16
-    )
-    value_own = (
-        jnp.dot(tokens_here, value_full, preferred_element_type=jnp.float32)
-        .astype(jnp.bfloat16)
-        .reshape(tok_rows, kv_heads, HEAD)
-    )
+    col_index = lax.axis_index("cz")
+    ctx_index = lax.axis_index("cb") * col_parts + col_index
+    both_rows = jnp.concatenate([w_key[0], w_value[0]], 1)
+    weight_slice = lax.all_gather(both_rows, "cz", axis=0, tiled=True)
+    inputs_slice = lax.all_to_all(tokens_here, "cb", 1, 0, tiled=True)
+    projected = lax.psum_scatter(
+        jnp.dot(inputs_slice, weight_slice, preferred_element_type=jnp.float32),
+        "cb",
+        scatter_dimension=0,
+        tiled=True,
+    )
+    key_raw = projected[:, :kv_width].astype(jnp.bfloat16)
+    value_own = projected[:, kv_width:].astype(jnp.bfloat16).reshape(tok_rows, kv_heads, HEAD)
     local_pos = jnp.arange(tok_rows, dtype=jnp.int32)
     positions = ctx_index * tok_rows + local_pos
     cosine, sine_table = rope_tables(positions)
@@ -102,7 +112,7 @@
     own_pair = jnp.stack([key_rot, value_own])
     key_blocks = [own_pair]
     for distance in range(1, reach_blocks + 1):
-        key_blocks.append(passed_along(own_pair, "ctx", distance))
+        key_blocks.append(passed_along(own_pair, CTX, distance))
     seg_all = segments[0]
     seg_query = lax.dynamic_slice_in_dim(seg_all, ctx_index * tok_rows, tok_rows)
     allowed_list = []
@@ -182,7 +192,7 @@
         if distance == 0:
             kv_total = kv_part
         else:
-            returned = passed_along(kv_part.astype(jnp.bfloat16), "ctx", -distance)
+            returned = passed_along(kv_part.astype(jnp.bfloat16), CTX, -distance)
             kv_total = kv_total + returned.astype(jnp.float32)
     query_grad = normalize_back(
         query_in,
@@ -195,21 +205,20 @@
     key_back = key_back.reshape(tok_rows, kv_width).astype(jnp.bfloat16)
     value_back = kv_total[1].reshape(tok_rows, kv_width).astype(jnp.bfloat16)
     both_back = jnp.concatenate([key_back, value_back], 1)
+    group_back = lax.all_gather(both_back, "cb", axis=0, tiled=True)
     grad_rows = lax.psum_scatter(
         lax.dot_general(
-            tokens_here, both_back, (((0,), (0,)), ((), ())), preferred_element_type=jnp.float32
+            inputs_slice, group_back, (((0,), (0,)), ((), ())), preferred_element_type=jnp.float32
         ),
-        "ctx",
+        "cz",
         scatter_dimension=0,
         tiled=True,
     )
-    input_grad = lax.dot_general(
-        key_back, key_full, (((1,), (1,)), ((), ())), preferred_element_type=jnp.float32
-    )
-    input_grad = input_grad + lax.dot_general(
-        value_back, value_full, (((1,), (1,)), ((), ())), preferred_element_type=jnp.float32
-    )
-    passed = shifted(input_grad.astype(jnp.bfloat16), "pipe", -1)
+    slice_grad = lax.dot_general(
+        group_back, weight_slice, (((1,), (1,)), ((), ())), preferred_element_type=jnp.float32
+    ).astype(jnp.bfloat16)
+    input_grad = lax.all_to_all(slice_grad, "cb", 0, 1, tiled=True)
+    passed = shifted(input_grad, "pipe", -1)
     return (
         query_grad[None],
         grad_rows[:, :kv_width][None],
@@ -218,25 +227,25 @@
     )
 
 
+CTX = ("cb", "cz")
+
+
 def solution(mesh):
-    return jax.shard_map(
-        local,
-        mesh=mesh,
-        in_specs=(
-            P("pipe", "ctx", None),
-            P("pipe", "ctx", None),
-            P("pipe", "ctx", None),
-            P("pipe", None),
-            P("pipe", "ctx", None),
-            P("pipe", "ctx", None),
-            P("pipe", None),
-            P("pipe", None),
-        ),
-        out_specs=(
-            P("pipe", "ctx", None),
-            P("pipe", "ctx", None),
-            P("pipe", "ctx", None),
-            P("pipe", "ctx", None),
-        ),
+    col_parts = 8
+    row_parts = mesh.shape["ctx"] // col_parts
+    grid = mesh.devices.reshape(row_parts, col_parts, mesh.shape["pipe"])
+    split_mesh = Mesh(grid, ("cb", "cz", "pipe"))
+    rows = P("pipe", CTX, None)
+    inner = jax.shard_map(
+        functools.partial(local, row_parts=row_parts, col_parts=col_parts),
+        mesh=split_mesh,
+        in_specs=(rows, rows, rows, P("pipe", None), rows, rows, P("pipe", None), P("pipe", None)),
+        out_specs=(rows, rows, rows, rows),
         check_vma=False,
     )
+    placed = NamedSharding(mesh, P("pipe", "ctx", None))
+
+    def run(*args):
+        return tuple(lax.with_sharding_constraint(out, placed) for out in inner(*args))
+
+    return run

time: 871 us -> 401 us (0.46)
  the two profiles are of different devices: /device:TPU:0 before, /device:TPU:33 now
where the time goes in v1:
time: 401 us; the launch traced here: 399 us
  waiting for transfers between devices  230 us (57%)
  starting transfers between devices  46.3 us (12%)
  matrix products  34.7 us (9%)
  local copies, waits for them, and re-layouts  34.5 us (9%)
  blocking collectives  21.8 us (5%)
  other arithmetic  16.6 us (4%)
  between operations  15 us (4%)
    reduce_scatter x1, waiting for transfers between devices, local(): lax.psum_scatter(jnp.dot(inputs_slice, weight_slice, preferred_element_ty...  84.1 us
    all_gather x1, waiting for transfers between devices, local(): group_back = lax.all_gather(both_back, 'cb', axis=0, tiled=True)  63.2 us
    ppermute x12, waiting for transfers between devices, passed_along(): return lax.ppermute(block, axis, route)  60.6 us
    ppermute x12, starting transfers between devices, passed_along(): return lax.ppermute(block, axis, route)  39.5 us
    all_to_all x1, blocking collectives, local(): inputs_slice = lax.all_to_all(tokens_here, 'cb', 1, 0, tiled=True)  21.8 us
    unnamed x125, local copies, waits for them, and re-layouts  17.4 us
    all_gather x1, waiting for transfers between devices, local(): weight_slice = lax.all_gather(both_rows, 'cz', axis=0, tiled=True)  13.4 us
    dot_general x7, matrix products, grad_block(): jnp.einsum('grqk,kgd->qgrd', score_grad, key_pair[0], preferred_element_t...  11.1 us
  transfers between devices with their start and end apart: 18, of which 12 were waited for; matrix products, arithmetic and copies ran while one was open for 13% of the time, Pallas kernels for 0%

profile of v1, /device:TPU:33, one launch (start us, length us, event | category | flops | bytes accessed | tf_op | source)
XLA Modules:
  0.0 398.8 jit_solution(7884223318868163470)
XLA Ops:
  7.2 1.5 pad_maximum_fusion.11
  8.8 1.6 copy.260
  10.4 21.8 %all_to_all.38 = bf16[128,8,512]{0,2,1:T(8,128)(2,1)S(1)} all-to-all(bf16[128,8,512]{0,2,1:T(8,128)(2,1)S(1)} %bitcast.575), channel_id=1, replica_groups=mesh['cb'=8,'cz'=8,'pipe'=4] {'cb'}, dimensions={1} | all-to-all | bytes 2097152 | tf_op jit(solution)/shard_map/all_to_all | solution.py:94
  32.8 13.4 %all-gather.3.cloned.1.call-done = bf16[512,1024]{1,0:T(8,128)(2,1)} async-done(((bf16[64,1024]{1,0:T(8,128)(2,1)}), bf16[512,1024]{1,0:T(8,128)(2,1)}) %all-gather.3.cloned.1.call-update) | async-done | bytes 1048592 | tf_op jit(solution)/shard_map/all_gather | solution.py:93
  46.2 4.5 %convolution_bitcast_fusion = f32[1024,1024]{0,1:T(8,128)} fusion(bf16[512,1024]{1,0:T(8,128)(2,1)} %all-gather.3.cloned.1.call-done, bf16[1024,512]{1,0:T(8,128)(2,1)S(1)} %bitcast.586), kind=kOutput, calls=%fused_computation | convolution fusion | flops 1073741824 | bytes 6291456 | tf_op jit(solution)/shard_map/dot_general | solution.py:96
  54.9 1.3 copy.266
  59.4 84.1 %reduce-scatter.5.cloned.1.call-done = f32[128,1024]{0,1:T(8,128)} async-done(((f32[1024,1024]{0,1:T(8,128)}), f32[128,1024]{0,1:T(8,128)}) %reduce-scatter.5.cloned.1.call-update) | async-done | bytes 524304 | tf_op jit(solution)/shard_map/reduce_scatter | solution.py:95
  146.4 3.2 collective-permute-start
  149.6 5.5 %collective-permute-start.2 = (bf16[2,128,4,128]{3,1,2,0:T(8,128)(2,1)S(1)}, bf16[2,128,4,128]{3,1,2,0:T(8,128)(2,1)S(1)}, u32[]{:S(2)}, u32[]{:S(2)}) collective-permute-start(bf16[2,128,4,128]{3,1,2,0:T(8,128)(2,1)S(1)} %pad_maximum_fusion.2), channel_id=1, source_target_pairs={{0,12},{4,16},{8,20},{12,24},{16,28},{20,32},{24,36},{28,40},{32,4... | collective-permute-start | bytes 786440 | tf_op jit(solution)/shard_map/ppermute | solution.py:27
  155.1 2.7 collective-permute-start.3
  157.8 5.6 %collective-permute-start.4 = (bf16[2,128,4,128]{3,1,2,0:T(8,128)(2,1)S(1)}, bf16[2,128,4,128]{3,1,2,0:T(8,128)(2,1)S(1)}, u32[]{:S(2)}, u32[]{:S(2)}) collective-permute-start(bf16[2,128,4,128]{3,1,2,0:T(8,128)(2,1)S(1)} %pad_maximum_fusion.2), channel_id=1, source_target_pairs={{0,20},{4,24},{8,28},{12,32},{16,36},{20,40},{24,44},{28,48},{32,5... | collective-permute-start | bytes 786440 | tf_op jit(solution)/shard_map/ppermute | solution.py:27
  163.5 7.0 %collective-permute-start.5 = (bf16[2,128,4,128]{3,1,2,0:T(8,128)(2,1)S(1)}, bf16[2,128,4,128]{3,1,2,0:T(8,128)(2,1)S(1)}, u32[]{:S(2)}, u32[]{:S(2)}) collective-permute-start(bf16[2,128,4,128]{3,1,2,0:T(8,128)(2,1)S(1)} %pad_maximum_fusion.2), channel_id=1, source_target_pairs={{0,24},{4,28},{8,32},{12,36},{16,40},{20,44},{24,48},{28,52},{32,5... | collective-permute-start | bytes 786440 | tf_op jit(solution)/shard_map/ppermute | solution.py:27
  170.9 2.6 collective-permute-start.1
  175.5 2.8 collective-permute-done.4
  178.7 8.8 %collective-permute-done.5 = bf16[2,128,4,128]{3,1,2,0:T(8,128)(2,1)S(1)} collective-permute-done((bf16[2,128,4,128]{3,1,2,0:T(8,128)(2,1)S(1)}, bf16[2,128,4,128]{3,1,2,0:T(8,128)(2,1)S(1)}, u32[]{:S(2)}, u32[]{:S(2)}) %collective-permute-start.5) | collective-permute-done | bytes 262176 | tf_op jit(solution)/shard_map/ppermute | solution.py:27
  187.9 6.1 %collective-permute-done.1 = bf16[2,128,4,128]{3,1,2,0:T(8,128)(2,1)S(1)} collective-permute-done((bf16[2,128,4,128]{3,1,2,0:T(8,128)(2,1)S(1)}, bf16[2,128,4,128]{3,1,2,0:T(8,128)(2,1)S(1)}, u32[]{:S(2)}, u32[]{:S(2)}) %collective-permute-start.1) | collective-permute-done | bytes 262176 | tf_op jit(solution)/shard_map/ppermute | solution.py:27
  200.6 6.3 %collective-permute-start.6 = (bf16[2,128,4,128]{3,1,2,0:T(8,128)(2,1)S(1)}, bf16[2,128,4,128]{3,1,2,0:T(8,128)(2,1)S(1)}, u32[]{:S(2)}, u32[]{:S(2)}) collective-permute-start(bf16[2,128,4,128]{3,1,2,0:T(8,128)(2,1)S(1)} %pad_maximum_fusion.3), channel_id=1, source_target_pairs={{4,0},{8,4},{12,8},{16,12},{20,16},{24,20},{28,24},{32,28},{36,32}... | collective-permute-start | bytes 786440 | tf_op jit(solution)/shard_map/ppermute | solution.py:27
  207.6 1.3 collective-permute-start.7
  209.5 1.3 collective-permute-start.8
  211.5 1.3 collective-permute-start.9
  213.5 1.4 collective-permute-start.10
  216.4 1.3 collective-permute-start.11
  218.3 5.6 %collective-permute-done.7 = bf16[2,128,4,128]{3,1,2,0:T(8,128)(2,1)S(1)} collective-permute-done((bf16[2,128,4,128]{3,1,2,0:T(8,128)(2,1)S(1)}, bf16[2,128,4,128]{3,1,2,0:T(8,128)(2,1)S(1)}, u32[]{:S(2)}, u32[]{:S(2)}) %collective-permute-start.7) | collective-permute-done | bytes 262176 | tf_op jit(solution)/shard_map/ppermute | solution.py:27
  223.9 15.6 %collective-permute-done.8 = bf16[2,128,4,128]{3,1,2,0:T(8,128)(2,1)S(1)} collective-permute-done((bf16[2,128,4,128]{3,1,2,0:T(8,128)(2,1)S(1)}, bf16[2,128,4,128]{3,1,2,0:T(8,128)(2,1)S(1)}, u32[]{:S(2)}, u32[]{:S(2)}) %collective-permute-start.8) | collective-permute-done | bytes 262176 | tf_op jit(solution)/shard_map/ppermute | solution.py:27
  239.5 17.9 %collective-permute-done.9 = bf16[2,128,4,128]{3,1,2,0:T(8,128)(2,1)S(1)} collective-permute-done((bf16[2,128,4,128]{3,1,2,0:T(8,128)(2,1)S(1)}, bf16[2,128,4,128]{3,1,2,0:T(8,128)(2,1)S(1)}, u32[]{:S(2)}, u32[]{:S(2)}) %collective-permute-start.9) | collective-permute-done | bytes 262176 | tf_op jit(solution)/shard_map/ppermute | solution.py:27
  257.4 3.7 collective-permute-done.11
  266.1 1.2 mul.518
  269.6 63.2 %all-gather.5.cloned.1.call-done = bf16[1024,1024]{0,1:T(8,128)(2,1)} async-done(((bf16[128,1024]{0,1:T(8,128)(2,1)}), bf16[1024,1024]{0,1:T(8,128)(2,1)}) %all-gather.5.cloned.1.call-update) | async-done | bytes 2097168 | tf_op jit(solution)/shard_map/all_gather | solution.py:208
  332.7 4.5 %convolution_bitcast_fusion.1 = f32[512,1024]{0,1:T(8,128)} fusion(bf16[1024,1024]{0,1:T(8,128)(2,1)} %all-gather.5.cloned.1.call-done, bf16[1024,512]{1,0:T(8,128)(2,1)} %bitcast.587), kind=kOutput, calls=%fused_computation.1 | convolution fusion | flops 1073741824 | bytes 5242880 | tf_op jit(solution)/shard_map/dot_general | solution.py:210
  337.2 2.9 copy.460
  341.5 2.3 fusion.97
  343.8 1.4 fusion.98
  345.2 1.3 fusion.99
  346.5 1.3 fusion.100
  347.9 1.4 convolution_add_fusion.1
  349.2 2.3 convolution_convert_fusion
  351.6 3.7 all-to-all-start.1
  355.3 3.0 fusion.12
  359.4 1.6 copy.462
  361.0 2.4 copy.463
  363.4 2.8 multiply_add_fusion
  366.2 3.4 all-to-all-done.1
  370.7 2.8 collective-permute-start.12
  374.1 1.3 mul.602
  375.4 2.5 mul.603
  379.1 2.9 fusion.88
  382.0 5.1 %collective-permute-done.12 = bf16[128,4096]{1,0:T(8,128)(2,1)} collective-permute-done((bf16[128,4096]{1,0:T(8,128)(2,1)}, bf16[128,4096]{1,0:T(8,128)(2,1)}, u32[]{:S(2)}, u32[]{:S(2)}) %collective-permute-start.12) | collective-permute-done | bytes 1048608 | tf_op jit(solution)/shard_map/ppermute | solution.py:32
  390.0 2.3 copy.472
  (230 shorter events, 39.9 us)
Async XLA Ops:
  7.2 39.0 %all-gather.3.cloned.1.call-start = ((), (), s32[]{:S(2)}) async-start(), calls=%async_computation.4 | async-start | bytes 1179648 | tf_op jit(solution)/shard_map/all_gather | solution.py:93
  8.8 134.7 %reduce-scatter.5.cloned.1.call-start = ((), (), s32[]{:S(2)}) async-start(), calls=%async_computation.5 | async-start | bytes 4718592 | tf_op jit(solution)/shard_map/reduce_scatter | solution.py:95
  32.8 17.9 %copy-start.29 = (bf16[8,128,512]{2,1,0:T(8,128)(2,1)}, bf16[8,128,512]{2,1,0:T(8,128)(2,1)S(1)}, u32[]{:S(2)}) copy-start(bf16[8,128,512]{2,1,0:T(8,128)(2,1)S(1)} %copy.261) | copy-start | bytes 3145732
  50.7 282.0 %all-gather.5.cloned.1.call-start = ((), (), s32[]{:S(2)}) async-start(), calls=%async_computation.6 | async-start | bytes 2359296 | tf_op jit(solution)/shard_map/all_gather | solution.py:208
  57.6 88.4 %copy-start.20 = (f32[128,64]{1,0:T(8,128)S(1)}, f32[128,64]{1,0:T(8,128)}, u32[]{:S(2)}) copy-start(f32[128,64]{1,0:T(8,128)} %copy-done.19) | copy-start | bytes 98308
  57.6 88.4 %copy-start.24 = (f32[128,64]{1,0:T(8,128)S(1)}, f32[128,64]{1,0:T(8,128)}, u32[]{:S(2)}) copy-start(f32[128,64]{1,0:T(8,128)} %copy-done.23) | copy-start | bytes 98308
  144.6 52.7 %copy-start.17 = (bf16[128,512]{0,1:T(8,128)(2,1)}, bf16[128,512]{0,1:T(8,128)(2,1)S(1)}, u32[]{:S(2)}) copy-start(bf16[128,512]{0,1:T(8,128)(2,1)S(1)} %slice.130) | copy-start | bytes 393220
  145.4 25.1 %copy-start.46 = (pred[128,128]{0,1:T(8,128)(4,1)S(1)}, pred[128,128]{0,1:T(8,128)(4,1)}, u32[]{:S(2)}) copy-start(pred[128,128]{0,1:T(8,128)(4,1)} %get-tuple-element.62) | copy-start | bytes 49156
  146.2 28.5 %copy-start.14 = (bf16[128,4,64]{2,0,1:T(8,128)(2,1)}, bf16[128,4,64]{2,0,1:T(8,128)(2,1)S(1)}, u32[]{:S(2)}) copy-start(bf16[128,4,64]{2,0,1:T(8,128)(2,1)S(1)} %get-tuple-element.35) | copy-start | bytes 196612
  146.3 28.4 %copy-start.45 = (pred[128,128]{0,1:T(8,128)(4,1)S(1)}, pred[128,128]{0,1:T(8,128)(4,1)}, u32[]{:S(2)}) copy-start(pred[128,128]{0,1:T(8,128)(4,1)} %get-tuple-element.59) | copy-start | bytes 49156
  146.4 24.5 %collective-permute-start = (bf16[2,128,4,128]{3,1,2,0:T(8,128)(2,1)S(1)}, bf16[2,128,4,128]{3,1,2,0:T(8,128)(2,1)S(1)}, u32[]{:S(2)}, u32[]{:S(2)}) collective-permute-start(bf16[2,128,4,128]{3,1,2,0:T(8,128)(2,1)S(1)} %pad_maximum_fusion.2), channel_id=1, source_target_pairs={{0,4},{4,8},{8,12},{12,16},{16,20},{20,24},{24,28},{28,32},{32,36}... | collective-permute-start | bytes 786440 | tf_op jit(solution)/shard_map/ppermute | solution.py:27
  149.6 25.0 %collective-permute-start.2 = (bf16[2,128,4,128]{3,1,2,0:T(8,128)(2,1)S(1)}, bf16[2,128,4,128]{3,1,2,0:T(8,128)(2,1)S(1)}, u32[]{:S(2)}, u32[]{:S(2)}) collective-permute-start(bf16[2,128,4,128]{3,1,2,0:T(8,128)(2,1)S(1)} %pad_maximum_fusion.2), channel_id=1, source_target_pairs={{0,12},{4,16},{8,20},{12,24},{16,28},{20,32},{24,36},{28,40},{32,4... | collective-permute-start | bytes 786440 | tf_op jit(solution)/shard_map/ppermute | solution.py:27
  155.1 20.0 %collective-permute-start.3 = (bf16[2,128,4,128]{3,1,2,0:T(8,128)(2,1)S(1)}, bf16[2,128,4,128]{3,1,2,0:T(8,128)(2,1)S(1)}, u32[]{:S(2)}, u32[]{:S(2)}) collective-permute-start(bf16[2,128,4,128]{3,1,2,0:T(8,128)(2,1)S(1)} %pad_maximum_fusion.2), channel_id=1, source_target_pairs={{0,16},{4,20},{8,24},{12,28},{16,32},{20,36},{24,40},{28,44},{32,4... | collective-permute-start | bytes 786440 | tf_op jit(solution)/shard_map/ppermute | solution.py:27
  157.8 20.5 %collective-permute-start.4 = (bf16[2,128,4,128]{3,1,2,0:T(8,128)(2,1)S(1)}, bf16[2,128,4,128]{3,1,2,0:T(8,128)(2,1)S(1)}, u32[]{:S(2)}, u32[]{:S(2)}) collective-permute-start(bf16[2,128,4,128]{3,1,2,0:T(8,128)(2,1)S(1)} %pad_maximum_fusion.2), channel_id=1, source_target_pairs={{0,20},{4,24},{8,28},{12,32},{16,36},{20,40},{24,44},{28,48},{32,5... | collective-permute-start | bytes 786440 | tf_op jit(solution)/shard_map/ppermute | solution.py:27
  163.5 24.1 %collective-permute-start.5 = (bf16[2,128,4,128]{3,1,2,0:T(8,128)(2,1)S(1)}, bf16[2,128,4,128]{3,1,2,0:T(8,128)(2,1)S(1)}, u32[]{:S(2)}, u32[]{:S(2)}) collective-permute-start(bf16[2,128,4,128]{3,1,2,0:T(8,128)(2,1)S(1)} %pad_maximum_fusion.2), channel_id=1, source_target_pairs={{0,24},{4,28},{8,32},{12,36},{16,40},{20,44},{24,48},{28,52},{32,5... | collective-permute-start | bytes 786440 | tf_op jit(solution)/shard_map/ppermute | solution.py:27
  170.9 4.2 %copy-start.44 = (pred[128,128]{0,1:T(8,128)(4,1)S(1)}, pred[128,128]{0,1:T(8,128)(4,1)}, u32[]{:S(2)}) copy-start(pred[128,128]{0,1:T(8,128)(4,1)} %get-tuple-element.60) | copy-start | bytes 49156
  170.9 29.1 %copy-start.39 = (bf16[2,128,4,128]{3,1,2,0:T(8,128)(2,1)}, bf16[2,128,4,128]{3,1,2,0:T(8,128)(2,1)S(1)}, u32[]{:S(2)}) copy-start(bf16[2,128,4,128]{3,1,2,0:T(8,128)(2,1)S(1)} %collective-permute-done) | copy-start | bytes 786436
  170.9 23.1 %collective-permute-start.1 = (bf16[2,128,4,128]{3,1,2,0:T(8,128)(2,1)S(1)}, bf16[2,128,4,128]{3,1,2,0:T(8,128)(2,1)S(1)}, u32[]{:S(2)}, u32[]{:S(2)}) collective-permute-start(bf16[2,128,4,128]{3,1,2,0:T(8,128)(2,1)S(1)} %pad_maximum_fusion.2), channel_id=1, source_target_pairs={{0,8},{4,12},{8,16},{12,20},{16,24},{20,28},{24,32},{28,36},{32,40... | collective-permute-start | bytes 786440 | tf_op jit(solution)/shard_map/ppermute | solution.py:27
  174.6 3.7 copy-start.43
  174.7 34.2 %copy-start.32 = (bf16[2,128,4,128]{3,1,2,0:T(8,128)(2,1)}, bf16[2,128,4,128]{3,1,2,0:T(8,128)(2,1)S(1)}, u32[]{:S(2)}) copy-start(bf16[2,128,4,128]{3,1,2,0:T(8,128)(2,1)S(1)} %collective-permute-done.2) | copy-start | bytes 786436
  175.1 35.8 %copy-start.33 = (bf16[2,128,4,128]{3,1,2,0:T(8,128)(2,1)}, bf16[2,128,4,128]{3,1,2,0:T(8,128)(2,1)S(1)}, u32[]{:S(2)}) copy-start(bf16[2,128,4,128]{3,1,2,0:T(8,128)(2,1)S(1)} %collective-permute-done.3) | copy-start | bytes 786436
  175.5 18.6 %copy-start.42 = (pred[128,128]{0,1:T(8,128)(4,1)S(1)}, pred[128,128]{0,1:T(8,128)(4,1)}, u32[]{:S(2)}) copy-start(pred[128,128]{0,1:T(8,128)(4,1)} %get-tuple-element.58) | copy-start | bytes 49156
  178.3 34.5 %copy-start.35 = (bf16[2,128,4,128]{3,1,2,0:T(8,128)(2,1)}, bf16[2,128,4,128]{3,1,2,0:T(8,128)(2,1)S(1)}, u32[]{:S(2)}) copy-start(bf16[2,128,4,128]{3,1,2,0:T(8,128)(2,1)S(1)} %collective-permute-done.4) | copy-start | bytes 786436
  187.6 27.4 %copy-start.37 = (bf16[2,128,4,128]{3,1,2,0:T(8,128)(2,1)}, bf16[2,128,4,128]{3,1,2,0:T(8,128)(2,1)S(1)}, u32[]{:S(2)}) copy-start(bf16[2,128,4,128]{3,1,2,0:T(8,128)(2,1)S(1)} %collective-permute-done.5) | copy-start | bytes 786436
  194.0 12.9 %copy-start.30 = (bf16[2,128,4,128]{3,1,2,0:T(8,128)(2,1)}, bf16[2,128,4,128]{3,1,2,0:T(8,128)(2,1)S(1)}, u32[]{:S(2)}) copy-start(bf16[2,128,4,128]{3,1,2,0:T(8,128)(2,1)S(1)} %collective-permute-done.1) | copy-start | bytes 786436
  200.3 7.3 %copy-start.6 = (bf16[4,4,128,128]{2,3,1,0:T(8,128)(2,1)}, bf16[4,4,128,128]{2,3,1,0:T(8,128)(2,1)S(1)}, u32[]{:S(2)}) copy-start(bf16[4,4,128,128]{2,3,1,0:T(8,128)(2,1)S(1)} %fusion.47) | copy-start | bytes 1572868
  200.6 15.8 %collective-permute-start.6 = (bf16[2,128,4,128]{3,1,2,0:T(8,128)(2,1)S(1)}, bf16[2,128,4,128]{3,1,2,0:T(8,128)(2,1)S(1)}, u32[]{:S(2)}, u32[]{:S(2)}) collective-permute-start(bf16[2,128,4,128]{3,1,2,0:T(8,128)(2,1)S(1)} %pad_maximum_fusion.3), channel_id=1, source_target_pairs={{4,0},{8,4},{12,8},{16,12},{20,16},{24,20},{28,24},{32,28},{36,32}... | collective-permute-start | bytes 786440 | tf_op jit(solution)/shard_map/ppermute | solution.py:27
  207.6 16.3 %collective-permute-start.7 = (bf16[2,128,4,128]{3,1,2,0:T(8,128)(2,1)S(1)}, bf16[2,128,4,128]{3,1,2,0:T(8,128)(2,1)S(1)}, u32[]{:S(2)}, u32[]{:S(2)}) collective-permute-start(bf16[2,128,4,128]{3,1,2,0:T(8,128)(2,1)S(1)} %pad_maximum_fusion.4), channel_id=1, source_target_pairs={{8,0},{12,4},{16,8},{20,12},{24,16},{28,20},{32,24},{36,28},{40,32... | collective-permute-start | bytes 786440 | tf_op jit(solution)/shard_map/ppermute | solution.py:27
  209.5 29.9 %collective-permute-start.8 = (bf16[2,128,4,128]{3,1,2,0:T(8,128)(2,1)S(1)}, bf16[2,128,4,128]{3,1,2,0:T(8,128)(2,1)S(1)}, u32[]{:S(2)}, u32[]{:S(2)}) collective-permute-start(bf16[2,128,4,128]{3,1,2,0:T(8,128)(2,1)S(1)} %pad_maximum_fusion.5), channel_id=1, source_target_pairs={{12,0},{16,4},{20,8},{24,12},{28,16},{32,20},{36,24},{40,28},{44,3... | collective-permute-start | bytes 786440 | tf_op jit(solution)/shard_map/ppermute | solution.py:27
  211.5 45.9 %collective-permute-start.9 = (bf16[2,128,4,128]{3,1,2,0:T(8,128)(2,1)S(1)}, bf16[2,128,4,128]{3,1,2,0:T(8,128)(2,1)S(1)}, u32[]{:S(2)}, u32[]{:S(2)}) collective-permute-start(bf16[2,128,4,128]{3,1,2,0:T(8,128)(2,1)S(1)} %pad_maximum_fusion.6), channel_id=1, source_target_pairs={{16,0},{20,4},{24,8},{28,12},{32,16},{36,20},{40,24},{44,28},{48,3... | collective-permute-start | bytes 786440 | tf_op jit(solution)/shard_map/ppermute | solution.py:27
  213.5 43.9 %collective-permute-start.10 = (bf16[2,128,4,128]{3,1,2,0:T(8,128)(2,1)S(1)}, bf16[2,128,4,128]{3,1,2,0:T(8,128)(2,1)S(1)}, u32[]{:S(2)}, u32[]{:S(2)}) collective-permute-start(bf16[2,128,4,128]{3,1,2,0:T(8,128)(2,1)S(1)} %pad_maximum_fusion.7), channel_id=1, source_target_pairs={{20,0},{24,4},{28,8},{32,12},{36,16},{40,20},{44,24},{48,28},{52,3... | collective-permute-start | bytes 786440 | tf_op jit(solution)/shard_map/ppermute | solution.py:27
  216.4 44.7 %collective-permute-start.11 = (bf16[2,128,4,128]{3,1,2,0:T(8,128)(2,1)S(1)}, bf16[2,128,4,128]{3,1,2,0:T(8,128)(2,1)S(1)}, u32[]{:S(2)}, u32[]{:S(2)}) collective-permute-start(bf16[2,128,4,128]{3,1,2,0:T(8,128)(2,1)S(1)} %pad_maximum_fusion.8), channel_id=1, source_target_pairs={{24,0},{28,4},{32,8},{36,12},{40,16},{44,20},{48,24},{52,28},{56,3... | collective-permute-start | bytes 786440 | tf_op jit(solution)/shard_map/ppermute | solution.py:27
  218.0 44.1 %copy-start.21 = (f32[128,64]{1,0:T(8,128)S(1)}, f32[128,64]{1,0:T(8,128)}, u32[]{:S(2)}) copy-start(f32[128,64]{1,0:T(8,128)} %copy-done.19) | copy-start | bytes 98308
  218.0 44.1 %copy-start.25 = (f32[128,64]{1,0:T(8,128)S(1)}, f32[128,64]{1,0:T(8,128)}, u32[]{:S(2)}) copy-start(f32[128,64]{1,0:T(8,128)} %copy-done.23) | copy-start | bytes 98308
  218.3 43.9 %copy-start.52 = (f32[1,128]{1,0:T(1,128)S(1)}, f32[1,128]{1,0:T(1,128)}, u32[]{:S(2)}) copy-start(f32[1,128]{1,0:T(1,128)} %param.15) | copy-start | bytes 1540
  264.6 122.5 %reduce-scatter.7.cloned.1.call-start = ((), (), s32[]{:S(2)}) async-start(), calls=%async_computation.7 | async-start | bytes 2359296
  341.5 3.7 copy-start.3
  341.5 3.7 copy-start.36
  351.5 3.7 copy-start.9
  351.5 3.7 copy-start.31
  351.6 18.0 %all-to-all-start.1 = ((bf16[8,128,512]{2,1,0:T(8,128)(2,1)}), bf16[8,128,512]{2,1,0:T(8,128)(2,1)S(1)}, u32[]{:S(2)}, u32[]{:S(2)}) async-start(bf16[8,128,512]{2,1,0:T(8,128)(2,1)} %bitcast.588), calls=%async_computation.2 | async-start | bytes 2097152 | tf_op jit(solution)/shard_map/all_to_all | solution.py:220
  359.4 4.0 %copy-start.22 = (f32[128,64]{1,0:T(8,128)S(1)}, f32[128,64]{1,0:T(8,128)}, u32[]{:S(2)}) copy-start(f32[128,64]{1,0:T(8,128)} %copy-done.19) | copy-start | bytes 98308
  359.4 4.0 %copy-start.26 = (f32[128,64]{1,0:T(8,128)S(1)}, f32[128,64]{1,0:T(8,128)}, u32[]{:S(2)}) copy-start(f32[128,64]{1,0:T(8,128)} %copy-done.23) | copy-start | bytes 98308
  369.6 3.9 copy-start.12
  369.6 3.9 copy-start.13
  370.7 16.5 %collective-permute-start.12 = (bf16[128,4096]{1,0:T(8,128)(2,1)}, bf16[128,4096]{1,0:T(8,128)(2,1)}, u32[]{:S(2)}, u32[]{:S(2)}) collective-permute-start(bf16[128,4096]{1,0:T(8,128)(2,1)} %bitcast.231), channel_id=1, source_target_pairs={{0,3},{1,0},{2,1},{3,2},{4,7},{5,4},{6,5},{7,6},{8,11},{9,8},{10,9... | collective-permute-start | bytes 3145736 | tf_op jit(solution)/shard_map/ppermute | solution.py:32
  375.4 3.7 copy-start.10
  375.4 3.7 copy-start.11
  (27 other events, 54.7 us)
Sparse Core Ops, SparseCore 0:
  10.3 35.8 all-gather.2
  50.9 92.5 reduce-scatter.4
  264.8 67.9 all-gather.4
  340.3 37.8 reduce-scatter.6

commit v2 on v1

--- a/solution.py
+++ b/solution.py
@@ -72,6 +72,18 @@
     scaled = upstream * gain_row
     cubed = inverse * inverse * inverse
     return inverse * scaled - values * cubed * jnp.mean(values * scaled, -1, keepdims=True)
+
+
+def gathered(block, axis, parts):
+    copies = jnp.broadcast_to(block[None], (parts,) + block.shape)
+    received = lax.all_to_all(copies, axis, 0, 0, tiled=True)
+    return received.reshape((parts * block.shape[0],) + block.shape[1:])
+
+
+def summed_over(partial, axis, parts, sent_as):
+    pieces = partial.astype(sent_as).reshape((parts, partial.shape[0] // parts) + partial.shape[1:])
+    received = lax.all_to_all(pieces, axis, 0, 0, tiled=True)
+    return jnp.sum(received.astype(jnp.float32), 0)
 
 
 def guarded(tile_work, operands):
@@ -90,13 +102,13 @@
     col_index = lax.axis_index("cz")
     ctx_index = lax.axis_index("cb") * col_parts + col_index
     both_rows = jnp.concatenate([w_key[0], w_value[0]], 1)
-    weight_slice = lax.all_gather(both_rows, "cz", axis=0, tiled=True)
+    weight_slice = gathered(both_rows, "cz", col_parts)
     inputs_slice = lax.all_to_all(tokens_here, "cb", 1, 0, tiled=True)
-    projected = lax.psum_scatter(
+    projected = summed_over(
         jnp.dot(inputs_slice, weight_slice, preferred_element_type=jnp.float32),
         "cb",
-        scatter_dimension=0,
-        tiled=True,
+        row_parts,
+        jnp.bfloat16,
     )
     key_raw = projected[:, :kv_width].astype(jnp.bfloat16)
     value_own = projected[:, kv_width:].astype(jnp.bfloat16).reshape(tok_rows, kv_heads, HEAD)
@@ -205,14 +217,14 @@
     key_back = key_back.reshape(tok_rows, kv_width).astype(jnp.bfloat16)
     value_back = kv_total[1].reshape(tok_rows, kv_width).astype(jnp.bfloat16)
     both_back = jnp.concatenate([key_back, value_back], 1)
-    group_back = lax.all_gather(both_back, "cb", axis=0, tiled=True)
-    grad_rows = lax.psum_scatter(
+    group_back = gathered(both_back, "cb", row_parts)
+    grad_rows = summed_over(
         lax.dot_general(
             inputs_slice, group_back, (((0,), (0,)), ((), ())), preferred_element_type=jnp.float32
         ),
         "cz",
-        scatter_dimension=0,
-        tiled=True,
+        col_parts,
+        jnp.float32,
     )
     slice_grad = lax.dot_general(
         group_back, weight_slice, (((1,), (1,)), ((), ())), preferred_element_type=jnp.float32

time: 401 us -> 358 us (0.89)
  the two profiles are of different devices: /device:TPU:33 before, /device:TPU:1 now
where the time goes in v2:
time: 358 us; the launch traced here: 356 us
  waiting for transfers between devices  146 us (41%)
  starting transfers between devices  68.9 us (19%)
  blocking collectives  44 us (12%)
  matrix products  39.9 us (11%)
  local copies, waits for them, and re-layouts  39.4 us (11%)
  other arithmetic  16.4 us (5%)
    ppermute x12, waiting for transfers between devices, passed_along(): return lax.ppermute(block, axis, route)  53.2 us
    all_to_all x2, waiting for transfers between devices, summed_over(): received = lax.all_to_all(pieces, axis, 0, 0, tiled=True)  45.6 us
    all_to_all x1, blocking collectives, gathered(): received = lax.all_to_all(copies, axis, 0, 0, tiled=True)  44 us
    ppermute x12, starting transfers between devices, passed_along(): return lax.ppermute(block, axis, route)  29.3 us
    all_to_all x1, waiting for transfers between devices, gathered(): received = lax.all_to_all(copies, axis, 0, 0, tiled=True)  25.3 us
    all_to_all x2, starting transfers between devices, summed_over(): received = lax.all_to_all(pieces, axis, 0, 0, tiled=True)  16.7 us
    all_to_all x1, waiting for transfers between devices, local(): inputs_slice = lax.all_to_all(tokens_here, 'cb', 1, 0, tiled=True)  15.6 us
    unnamed x104, local copies, waits for them, and re-layouts  12.5 us
  transfers between devices with their start and end apart: 18, of which 11 were waited for; matrix products, arithmetic and copies ran while one was open for 16% of the time, Pallas kernels for 0%

profile of v2, /device:TPU:1, one launch (start us, length us, event | category | flops | bytes accessed | tf_op | source)
XLA Modules:
  0.0 356.5 jit_solution(13802278240123801361)
XLA Ops:
  0.7 2.3 copy.172
  3.0 7.5 %all-to-all-start.1 = ((bf16[128,8,512]{0,2,1:T(8,128)(2,1)}), bf16[128,8,512]{0,2,1:T(8,128)(2,1)S(1)}, u32[]{:S(2)}, u32[]{:S(2)}) async-start(bf16[128,8,512]{0,2,1:T(8,128)(2,1)} %bitcast.3), calls=%async_computation.1 | async-start | bytes 2097152 | tf_op jit(solution)/shard_map/all_to_all | solution.py:106
  10.5 15.6 %all-to-all-done.1 = bf16[128,8,512]{0,2,1:T(8,128)(2,1)S(1)} async-done(((bf16[128,8,512]{0,2,1:T(8,128)(2,1)}), bf16[128,8,512]{0,2,1:T(8,128)(2,1)S(1)}, u32[]{:S(2)}, u32[]{:S(2)}) %all-to-all-start.1) | async-done | bytes 1048608 | tf_op jit(solution)/shard_map/all_to_all | solution.py:106
  27.3 8.2 %all-to-all-start = ((bf16[8,64,1024]{2,1,0:T(8,128)(2,1)}), bf16[8,64,1024]{2,1,0:T(8,128)(2,1)}, u32[]{:S(2)}, u32[]{:S(2)}) async-start(bf16[8,64,1024]{2,1,0:T(8,128)(2,1)} %broadcast_in_dim.56), calls=%async_computation | async-start | bytes 2097152 | tf_op jit(solution)/shard_map/all_to_all | solution.py:79
  38.1 1.3 copy.173
  39.4 25.3 %all-to-all-done = bf16[8,64,1024]{2,1,0:T(8,128)(2,1)} async-done(((bf16[8,64,1024]{2,1,0:T(8,128)(2,1)}), bf16[8,64,1024]{2,1,0:T(8,128)(2,1)}, u32[]{:S(2)}, u32[]{:S(2)}) %all-to-all-start) | async-done | bytes 1048608 | tf_op jit(solution)/shard_map/all_to_all | solution.py:79
  64.8 4.2 %convolution_convert_fusion = bf16[1024,1024]{0,1:T(8,128)(2,1)} fusion(bf16[1024,512]{1,0:T(8,128)(2,1)} %bitcast.592, bf16[512,1024]{1,0:T(8,128)(2,1)} %bitcast.2), kind=kOutput, calls=%fused_computation | convolution fusion | flops 1074790400 | bytes 4194304 | tf_op jit(solution)/shard_map/dot_general | solution.py:108
  68.9 4.3 %all-to-all-start.2 = ((bf16[8,128,1024]{2,1,0:T(8,128)(2,1)}), bf16[8,128,1024]{2,1,0:T(8,128)(2,1)}, u32[]{:S(2)}, u32[]{:S(2)}) async-start(bf16[8,128,1024]{2,1,0:T(8,128)(2,1)} %bitcast.584), calls=%async_computation.2 | async-start | bytes 4194304 | tf_op jit(solution)/shard_map/all_to_all | solution.py:85
  74.1 1.3 copy.181
  78.7 25.6 %all-to-all-done.2 = bf16[8,128,1024]{2,1,0:T(8,128)(2,1)} async-done(((bf16[8,128,1024]{2,1,0:T(8,128)(2,1)}), bf16[8,128,1024]{2,1,0:T(8,128)(2,1)}, u32[]{:S(2)}, u32[]{:S(2)}) %all-to-all-start.2) | async-done | bytes 2097184 | tf_op jit(solution)/shard_map/all_to_all | solution.py:85
  104.3 2.0 reduce
  109.7 2.0 collective-permute-start
  113.0 9.7 %collective-permute-start.3 = (bf16[2,128,4,128]{3,1,2,0:T(8,128)(2,1)}, bf16[2,128,4,128]{3,1,2,0:T(8,128)(2,1)S(1)}, u32[]{:S(2)}, u32[]{:S(2)}) collective-permute-start(bf16[2,128,4,128]{3,1,2,0:T(8,128)(2,1)} %pad_maximum_fusion.2), channel_id=1, source_target_pairs={{0,16},{4,20},{8,24},{12,28},{16,32},{20,36},{24,40},{28,44},{32,4... | collective-permute-start | bytes 786440 | tf_op jit(solution)/shard_map/ppermute | solution.py:27
  122.8 2.0 collective-permute-start.4
  124.8 4.4 %collective-permute-start.5 = (bf16[2,128,4,128]{3,1,2,0:T(8,128)(2,1)}, bf16[2,128,4,128]{3,1,2,0:T(8,128)(2,1)}, u32[]{:S(2)}, u32[]{:S(2)}) collective-permute-start(bf16[2,128,4,128]{3,1,2,0:T(8,128)(2,1)} %pad_maximum_fusion.2), channel_id=1, source_target_pairs={{0,24},{4,28},{8,32},{12,36},{16,40},{20,44},{24,48},{28,52},{32,5... | collective-permute-start | bytes 786440 | tf_op jit(solution)/shard_map/ppermute | solution.py:27
  130.7 1.4 copy.252
  133.3 2.1 collective-permute-start.1
  137.5 13.0 %collective-permute-done.4 = bf16[2,128,4,128]{3,1,2,0:T(8,128)(2,1)} collective-permute-done((bf16[2,128,4,128]{3,1,2,0:T(8,128)(2,1)}, bf16[2,128,4,128]{3,1,2,0:T(8,128)(2,1)}, u32[]{:S(2)}, u32[]{:S(2)}) %collective-permute-start.4) | collective-permute-done | bytes 262176 | tf_op jit(solution)/shard_map/ppermute | solution.py:27
  151.8 10.7 %collective-permute-done.5 = bf16[2,128,4,128]{3,1,2,0:T(8,128)(2,1)} collective-permute-done((bf16[2,128,4,128]{3,1,2,0:T(8,128)(2,1)}, bf16[2,128,4,128]{3,1,2,0:T(8,128)(2,1)}, u32[]{:S(2)}, u32[]{:S(2)}) %collective-permute-start.5) | collective-permute-done | bytes 262176 | tf_op jit(solution)/shard_map/ppermute | solution.py:27
  182.8 1.4 collective-permute-start.10
  188.5 3.9 %collective-permute-done.7 = bf16[2,128,4,128]{3,1,2,0:T(8,128)(2,1)S(1)} collective-permute-done((bf16[2,128,4,128]{3,1,2,0:T(8,128)(2,1)S(1)}, bf16[2,128,4,128]{3,1,2,0:T(8,128)(2,1)S(1)}, u32[]{:S(2)}, u32[]{:S(2)}) %collective-permute-start.7) | collective-permute-done | bytes 262176 | tf_op jit(solution)/shard_map/ppermute | solution.py:27
  192.5 14.1 %collective-permute-done.8 = bf16[2,128,4,128]{3,1,2,0:T(8,128)(2,1)S(1)} collective-permute-done((bf16[2,128,4,128]{3,1,2,0:T(8,128)(2,1)S(1)}, bf16[2,128,4,128]{3,1,2,0:T(8,128)(2,1)S(1)}, u32[]{:S(2)}, u32[]{:S(2)}) %collective-permute-start.8) | collective-permute-done | bytes 262176 | tf_op jit(solution)/shard_map/ppermute | solution.py:27
  206.6 11.4 %collective-permute-done.11 = bf16[2,128,4,128]{3,1,2,0:T(8,128)(2,1)S(1)} collective-permute-done((bf16[2,128,4,128]{3,1,2,0:T(8,128)(2,1)S(1)}, bf16[2,128,4,128]{3,1,2,0:T(8,128)(2,1)S(1)}, u32[]{:S(2)}, u32[]{:S(2)}) %collective-permute-start.11) | collective-permute-done | bytes 262176 | tf_op jit(solution)/shard_map/ppermute | solution.py:27
  222.6 44.0 %all_to_all.58 = bf16[8,128,1024]{2,1,0:T(8,128)(2,1)S(1)} all-to-all(bf16[8,128,1024]{2,1,0:T(8,128)(2,1)S(1)} %broadcast_in_dim.65), channel_id=1, replica_groups=mesh['cb'=8,'cz'=8,'pipe'=4] {'cb'}, dimensions={0} | all-to-all | bytes 4194304 | tf_op jit(solution)/shard_map/all_to_all | solution.py:79
  266.6 4.3 %convolution_convert_fusion.1 = bf16[1024,512]{1,0:T(8,128)(2,1)} fusion(bf16[1024,1024]{1,0:T(8,128)(2,1)S(1)} %bitcast.586, bf16[512,1024]{1,0:T(8,128)(2,1)} %bitcast.2), kind=kOutput, calls=%fused_computation.1 | convolution fusion | flops 1074266112 | bytes 4194304 | tf_op jit(solution)/shard_map/dot_general | solution.py:229
  270.9 4.4 %all-to-all-start.5 = ((bf16[8,128,512]{2,1,0:T(8,128)(2,1)}), bf16[8,128,512]{2,1,0:T(8,128)(2,1)}, u32[]{:S(2)}, u32[]{:S(2)}) async-start(bf16[8,128,512]{2,1,0:T(8,128)(2,1)} %bitcast.159), calls=%async_computation.5 | async-start | bytes 2097152 | tf_op jit(solution)/shard_map/all_to_all | solution.py:232
  275.3 1.3 mul.517
  276.6 1.4 mul.518
  278.0 1.3 mul.597
  279.3 2.4 mul.598
  281.7 4.5 %fusion.136 = f32[1024,512,1]{0,1,2:T(8,128)} fusion(bf16[8,128,1024]{2,1,0:T(8,128)(2,1)} %copy-done.15, bf16[128,8,512]{0,2,1:T(8,128)(2,1)} %copy-done.11), kind=kOutput, calls=%fused_computation.274 | convolution fusion | flops 1073741824 | bytes 5242880 | tf_op jit(solution)/shard_map/dot_general | solution.py:222
  286.2 1.4 all-to-all-done.5
  287.6 12.4 %all-to-all-start.4 = ((f32[8,64,1024]{2,1,0:T(8,128)}), f32[8,64,1024]{2,1,0:T(8,128)}, u32[]{:S(2)}, u32[]{:S(2)}) async-start(f32[8,64,1024]{2,1,0:T(8,128)} %bitcast.585), calls=%async_computation.4 | async-start | bytes 4194304 | tf_op jit(solution)/shard_map/all_to_all | solution.py:85
  300.4 1.3 fusion.96
  302.1 1.3 fusion.98
  303.5 1.3 fusion.99
  307.7 1.6 copy.378
  309.3 2.4 copy.379
  311.7 1.4 multiply_add_fusion
  313.2 2.4 copy.383
  315.5 2.8 collective-permute-start.12
  319.1 1.3 mul.602
  320.4 2.5 mul.603
  324.0 2.9 fusion.88
  326.9 4.8 %collective-permute-done.12 = bf16[128,4096]{1,0:T(8,128)(2,1)} collective-permute-done((bf16[128,4096]{1,0:T(8,128)(2,1)}, bf16[128,4096]{1,0:T(8,128)(2,1)}, u32[]{:S(2)}, u32[]{:S(2)}) %collective-permute-start.12) | collective-permute-done | bytes 1048608 | tf_op jit(solution)/shard_map/ppermute | solution.py:32
  331.7 20.0 %all-to-all-done.4 = f32[8,64,1024]{2,1,0:T(8,128)} async-done(((f32[8,64,1024]{2,1,0:T(8,128)}), f32[8,64,1024]{2,1,0:T(8,128)}, u32[]{:S(2)}, u32[]{:S(2)}) %all-to-all-start.4) | async-done | bytes 2097184 | tf_op jit(solution)/shard_map/all_to_all | solution.py:85
  351.7 1.7 reduce_sum.139
  354.2 2.3 copy.390
  (218 shorter events, 53.3 us)
Async XLA Ops:
  0.6 9.8 %copy-start.42 = (bf16[1,64,512]{2,1,0:T(8,128)(2,1)S(1)}, bf16[1,64,512]{2,1,0:T(8,128)(2,1)}, u32[]{:S(2)}) copy-start(bf16[1,64,512]{2,1,0:T(8,128)(2,1)} %param.12) | copy-start | bytes 196612
  0.6 9.8 %copy-start.41 = (bf16[1,64,512]{2,1,0:T(8,128)(2,1)S(1)}, bf16[1,64,512]{2,1,0:T(8,128)(2,1)}, u32[]{:S(2)}) copy-start(bf16[1,64,512]{2,1,0:T(8,128)(2,1)} %param.13) | copy-start | bytes 196612
  3.0 23.1 %all-to-all-start.1 = ((bf16[128,8,512]{0,2,1:T(8,128)(2,1)}), bf16[128,8,512]{0,2,1:T(8,128)(2,1)S(1)}, u32[]{:S(2)}, u32[]{:S(2)}) async-start(bf16[128,8,512]{0,2,1:T(8,128)(2,1)} %bitcast.3), calls=%async_computation.1 | async-start | bytes 2097152 | tf_op jit(solution)/shard_map/all_to_all | solution.py:106
  10.4 25.0 %copy-start.14 = (bf16[1,128,2048]{2,1,0:T(8,128)(2,1)S(1)}, bf16[1,128,2048]{2,1,0:T(8,128)(2,1)}, u32[]{:S(2)}) copy-start(bf16[1,128,2048]{2,1,0:T(8,128)(2,1)} %param.9) | copy-start | bytes 1572868
  26.0 12.1 %copy-start.11 = (bf16[128,8,512]{0,2,1:T(8,128)(2,1)}, bf16[128,8,512]{0,2,1:T(8,128)(2,1)S(1)}, u32[]{:S(2)}) copy-start(bf16[128,8,512]{0,2,1:T(8,128)(2,1)S(1)} %all-to-all-done.1) | copy-start | bytes 3145732
  27.3 37.5 %all-to-all-start = ((bf16[8,64,1024]{2,1,0:T(8,128)(2,1)}), bf16[8,64,1024]{2,1,0:T(8,128)(2,1)}, u32[]{:S(2)}, u32[]{:S(2)}) async-start(bf16[8,64,1024]{2,1,0:T(8,128)(2,1)} %broadcast_in_dim.56), calls=%async_computation | async-start | bytes 2097152 | tf_op jit(solution)/shard_map/all_to_all | solution.py:79
  36.5 36.8 %copy-start.18 = (f32[128,64]{1,0:T(8,128)}, f32[128,64]{1,0:T(8,128)S(1)}, u32[]{:S(2)}) copy-start(f32[128,64]{1,0:T(8,128)S(1)} %get-tuple-element.47) | copy-start | bytes 98308
  36.5 36.8 %copy-start.22 = (f32[128,64]{1,0:T(8,128)}, f32[128,64]{1,0:T(8,128)S(1)}, u32[]{:S(2)}) copy-start(f32[128,64]{1,0:T(8,128)S(1)} %get-tuple-element.48) | copy-start | bytes 98308
  68.9 35.4 %all-to-all-start.2 = ((bf16[8,128,1024]{2,1,0:T(8,128)(2,1)}), bf16[8,128,1024]{2,1,0:T(8,128)(2,1)}, u32[]{:S(2)}, u32[]{:S(2)}) async-start(bf16[8,128,1024]{2,1,0:T(8,128)(2,1)} %bitcast.584), calls=%async_computation.2 | async-start | bytes 4194304 | tf_op jit(solution)/shard_map/all_to_all | solution.py:85
  78.7 29.8 %copy-start.19 = (f32[128,64]{1,0:T(8,128)S(1)}, f32[128,64]{1,0:T(8,128)}, u32[]{:S(2)}) copy-start(f32[128,64]{1,0:T(8,128)} %copy-done.18) | copy-start | bytes 98308
  78.7 29.8 %copy-start.23 = (f32[128,64]{1,0:T(8,128)S(1)}, f32[128,64]{1,0:T(8,128)}, u32[]{:S(2)}) copy-start(f32[128,64]{1,0:T(8,128)} %copy-done.22) | copy-start | bytes 98308
  108.6 28.0 %copy-start.12 = (bf16[128,4,64]{2,0,1:T(8,128)(2,1)}, bf16[128,4,64]{2,0,1:T(8,128)(2,1)S(1)}, u32[]{:S(2)}) copy-start(bf16[128,4,64]{2,0,1:T(8,128)(2,1)S(1)} %get-tuple-element.17) | copy-start | bytes 196612
  108.8 58.3 %copy-start.16 = (bf16[128,512]{0,1:T(8,128)(2,1)}, bf16[128,512]{0,1:T(8,128)(2,1)S(1)}, u32[]{:S(2)}) copy-start(bf16[128,512]{0,1:T(8,128)(2,1)S(1)} %copy.178) | copy-start | bytes 393220
  109.7 23.5 %collective-permute-start = (bf16[2,128,4,128]{3,1,2,0:T(8,128)(2,1)}, bf16[2,128,4,128]{3,1,2,0:T(8,128)(2,1)}, u32[]{:S(2)}, u32[]{:S(2)}) collective-permute-start(bf16[2,128,4,128]{3,1,2,0:T(8,128)(2,1)} %pad_maximum_fusion.2), channel_id=1, source_target_pairs={{0,4},{4,8},{8,12},{12,16},{16,20},{20,24},{24,28},{28,32},{32,36}... | collective-permute-start | bytes 786440 | tf_op jit(solution)/shard_map/ppermute | solution.py:27
  111.7 24.9 %collective-permute-start.2 = (bf16[2,128,4,128]{3,1,2,0:T(8,128)(2,1)}, bf16[2,128,4,128]{3,1,2,0:T(8,128)(2,1)S(1)}, u32[]{:S(2)}, u32[]{:S(2)}) collective-permute-start(bf16[2,128,4,128]{3,1,2,0:T(8,128)(2,1)} %pad_maximum_fusion.2), channel_id=1, source_target_pairs={{0,12},{4,16},{8,20},{12,24},{16,28},{20,32},{24,36},{28,40},{32,4... | collective-permute-start | bytes 786440 | tf_op jit(solution)/shard_map/ppermute | solution.py:27
  113.0 24.0 %collective-permute-start.3 = (bf16[2,128,4,128]{3,1,2,0:T(8,128)(2,1)}, bf16[2,128,4,128]{3,1,2,0:T(8,128)(2,1)S(1)}, u32[]{:S(2)}, u32[]{:S(2)}) collective-permute-start(bf16[2,128,4,128]{3,1,2,0:T(8,128)(2,1)} %pad_maximum_fusion.2), channel_id=1, source_target_pairs={{0,16},{4,20},{8,24},{12,28},{16,32},{20,36},{24,40},{28,44},{32,4... | collective-permute-start | bytes 786440 | tf_op jit(solution)/shard_map/ppermute | solution.py:27
  122.8 27.7 %collective-permute-start.4 = (bf16[2,128,4,128]{3,1,2,0:T(8,128)(2,1)}, bf16[2,128,4,128]{3,1,2,0:T(8,128)(2,1)}, u32[]{:S(2)}, u32[]{:S(2)}) collective-permute-start(bf16[2,128,4,128]{3,1,2,0:T(8,128)(2,1)} %pad_maximum_fusion.2), channel_id=1, source_target_pairs={{0,20},{4,24},{8,28},{12,32},{16,36},{20,40},{24,44},{28,48},{32,5... | collective-permute-start | bytes 786440 | tf_op jit(solution)/shard_map/ppermute | solution.py:27
  124.8 37.8 %collective-permute-start.5 = (bf16[2,128,4,128]{3,1,2,0:T(8,128)(2,1)}, bf16[2,128,4,128]{3,1,2,0:T(8,128)(2,1)}, u32[]{:S(2)}, u32[]{:S(2)}) collective-permute-start(bf16[2,128,4,128]{3,1,2,0:T(8,128)(2,1)} %pad_maximum_fusion.2), channel_id=1, source_target_pairs={{0,24},{4,28},{8,32},{12,36},{16,40},{20,44},{24,48},{28,52},{32,5... | collective-permute-start | bytes 786440 | tf_op jit(solution)/shard_map/ppermute | solution.py:27
  132.1 4.6 %copy-start.40 = (pred[128,128]{0,1:T(8,128)(4,1)S(1)}, pred[128,128]{0,1:T(8,128)(4,1)}, u32[]{:S(2)}) copy-start(pred[128,128]{0,1:T(8,128)(4,1)} %get-tuple-element.43) | copy-start | bytes 49156
  133.3 3.8 %copy-start.39 = (pred[128,128]{0,1:T(8,128)(4,1)S(1)}, pred[128,128]{0,1:T(8,128)(4,1)}, u32[]{:S(2)}) copy-start(pred[128,128]{0,1:T(8,128)(4,1)} %get-tuple-element.44) | copy-start | bytes 49156
  133.3 30.5 %collective-permute-start.1 = (bf16[2,128,4,128]{3,1,2,0:T(8,128)(2,1)}, bf16[2,128,4,128]{3,1,2,0:T(8,128)(2,1)S(1)}, u32[]{:S(2)}, u32[]{:S(2)}) collective-permute-start(bf16[2,128,4,128]{3,1,2,0:T(8,128)(2,1)} %pad_maximum_fusion.2), channel_id=1, source_target_pairs={{0,8},{4,12},{8,16},{12,20},{16,24},{20,28},{24,32},{28,36},{32,40... | collective-permute-start | bytes 786440 | tf_op jit(solution)/shard_map/ppermute | solution.py:27
  136.6 13.9 %copy-start.38 = (pred[128,128]{0,1:T(8,128)(4,1)S(1)}, pred[128,128]{0,1:T(8,128)(4,1)}, u32[]{:S(2)}) copy-start(pred[128,128]{0,1:T(8,128)(4,1)} %get-tuple-element.45) | copy-start | bytes 49156
  136.7 40.7 %copy-start.31 = (bf16[2,128,4,128]{3,1,2,0:T(8,128)(2,1)}, bf16[2,128,4,128]{3,1,2,0:T(8,128)(2,1)S(1)}, u32[]{:S(2)}) copy-start(bf16[2,128,4,128]{3,1,2,0:T(8,128)(2,1)S(1)} %collective-permute-done.2) | copy-start | bytes 786436
  137.1 42.2 %copy-start.32 = (bf16[2,128,4,128]{3,1,2,0:T(8,128)(2,1)}, bf16[2,128,4,128]{3,1,2,0:T(8,128)(2,1)S(1)}, u32[]{:S(2)}) copy-start(bf16[2,128,4,128]{3,1,2,0:T(8,128)(2,1)S(1)} %collective-permute-done.3) | copy-start | bytes 786436
  137.5 26.4 %copy-start.37 = (pred[128,128]{0,1:T(8,128)(4,1)S(1)}, pred[128,128]{0,1:T(8,128)(4,1)}, u32[]{:S(2)}) copy-start(pred[128,128]{0,1:T(8,128)(4,1)} %get-tuple-element.42) | copy-start | bytes 49156
  163.8 11.5 %copy-start.29 = (bf16[2,128,4,128]{3,1,2,0:T(8,128)(2,1)}, bf16[2,128,4,128]{3,1,2,0:T(8,128)(2,1)S(1)}, u32[]{:S(2)}) copy-start(bf16[2,128,4,128]{3,1,2,0:T(8,128)(2,1)S(1)} %collective-permute-done.1) | copy-start | bytes 786436
  174.1 12.6 %collective-permute-start.6 = (bf16[2,128,4,128]{3,1,2,0:T(8,128)(2,1)S(1)}, bf16[2,128,4,128]{3,1,2,0:T(8,128)(2,1)S(1)}, u32[]{:S(2)}, u32[]{:S(2)}) collective-permute-start(bf16[2,128,4,128]{3,1,2,0:T(8,128)(2,1)S(1)} %pad_maximum_fusion.3), channel_id=1, source_target_pairs={{4,0},{8,4},{12,8},{16,12},{20,16},{24,20},{28,24},{32,28},{36,32}... | collective-permute-start | bytes 786440 | tf_op jit(solution)/shard_map/ppermute | solution.py:27
  176.0 16.4 %collective-permute-start.7 = (bf16[2,128,4,128]{3,1,2,0:T(8,128)(2,1)S(1)}, bf16[2,128,4,128]{3,1,2,0:T(8,128)(2,1)S(1)}, u32[]{:S(2)}, u32[]{:S(2)}) collective-permute-start(bf16[2,128,4,128]{3,1,2,0:T(8,128)(2,1)S(1)} %pad_maximum_fusion.4), channel_id=1, source_target_pairs={{8,0},{12,4},{16,8},{20,12},{24,16},{28,20},{32,24},{36,28},{40,32... | collective-permute-start | bytes 786440 | tf_op jit(solution)/shard_map/ppermute | solution.py:27
  178.0 28.6 %collective-permute-start.8 = (bf16[2,128,4,128]{3,1,2,0:T(8,128)(2,1)S(1)}, bf16[2,128,4,128]{3,1,2,0:T(8,128)(2,1)S(1)}, u32[]{:S(2)}, u32[]{:S(2)}) collective-permute-start(bf16[2,128,4,128]{3,1,2,0:T(8,128)(2,1)S(1)} %pad_maximum_fusion.5), channel_id=1, source_target_pairs={{12,0},{16,4},{20,8},{24,12},{28,16},{32,20},{36,24},{40,28},{44,3... | collective-permute-start | bytes 786440 | tf_op jit(solution)/shard_map/ppermute | solution.py:27
  179.9 26.6 %collective-permute-start.9 = (bf16[2,128,4,128]{3,1,2,0:T(8,128)(2,1)S(1)}, bf16[2,128,4,128]{3,1,2,0:T(8,128)(2,1)S(1)}, u32[]{:S(2)}, u32[]{:S(2)}) collective-permute-start(bf16[2,128,4,128]{3,1,2,0:T(8,128)(2,1)S(1)} %pad_maximum_fusion.6), channel_id=1, source_target_pairs={{16,0},{20,4},{24,8},{28,12},{32,16},{36,20},{40,24},{44,28},{48,3... | collective-permute-start | bytes 786440 | tf_op jit(solution)/shard_map/ppermute | solution.py:27
  182.8 23.8 %collective-permute-start.10 = (bf16[2,128,4,128]{3,1,2,0:T(8,128)(2,1)S(1)}, bf16[2,128,4,128]{3,1,2,0:T(8,128)(2,1)S(1)}, u32[]{:S(2)}, u32[]{:S(2)}) collective-permute-start(bf16[2,128,4,128]{3,1,2,0:T(8,128)(2,1)S(1)} %pad_maximum_fusion.7), channel_id=1, source_target_pairs={{20,0},{24,4},{28,8},{32,12},{36,16},{40,20},{44,24},{48,28},{52,3... | collective-permute-start | bytes 786440 | tf_op jit(solution)/shard_map/ppermute | solution.py:27
  186.6 31.4 %collective-permute-start.11 = (bf16[2,128,4,128]{3,1,2,0:T(8,128)(2,1)S(1)}, bf16[2,128,4,128]{3,1,2,0:T(8,128)(2,1)S(1)}, u32[]{:S(2)}, u32[]{:S(2)}) collective-permute-start(bf16[2,128,4,128]{3,1,2,0:T(8,128)(2,1)S(1)} %pad_maximum_fusion.8), channel_id=1, source_target_pairs={{24,0},{28,4},{32,8},{36,12},{40,16},{44,20},{48,24},{52,28},{56,3... | collective-permute-start | bytes 786440 | tf_op jit(solution)/shard_map/ppermute | solution.py:27
  188.2 30.1 %copy-start.20 = (f32[128,64]{1,0:T(8,128)S(1)}, f32[128,64]{1,0:T(8,128)}, u32[]{:S(2)}) copy-start(f32[128,64]{1,0:T(8,128)} %copy-done.18) | copy-start | bytes 98308
  188.2 30.1 %copy-start.24 = (f32[128,64]{1,0:T(8,128)S(1)}, f32[128,64]{1,0:T(8,128)}, u32[]{:S(2)}) copy-start(f32[128,64]{1,0:T(8,128)} %copy-done.22) | copy-start | bytes 98308
  188.5 30.0 %copy-start.46 = (f32[1,128]{1,0:T(1,128)S(1)}, f32[1,128]{1,0:T(1,128)}, u32[]{:S(2)}) copy-start(f32[1,128]{1,0:T(1,128)} %param.15) | copy-start | bytes 1540
  218.3 3.8 %copy-start.27 = (bf16[128,1024]{1,0:T(8,128)(2,1)S(1)}, bf16[128,1024]{1,0:T(8,128)(2,1)}, u32[]{:S(2)}) copy-start(bf16[128,1024]{1,0:T(8,128)(2,1)} %copy-done.26) | copy-start | bytes 786436
  218.3 3.8 %copy-start.28 = (f32[128,512]{1,0:T(8,128)S(1)}, f32[128,512]{1,0:T(8,128)}, u32[]{:S(2)}) copy-start(f32[128,512]{1,0:T(8,128)} %copy.251) | copy-start | bytes 786436
  218.3 3.8 %copy-start.44 = (f32[512]{0:T(512)S(1)}, f32[512]{0:T(512)}, u32[]{:S(2)}) copy-start(f32[512]{0:T(512)} %broadcast_bitcast_fusion.1) | copy-start | bytes 6148
  266.6 4.3 %copy-start.15 = (bf16[8,128,1024]{2,1,0:T(8,128)(2,1)}, bf16[8,128,1024]{2,1,0:T(8,128)(2,1)S(1)}, u32[]{:S(2)}) copy-start(bf16[8,128,1024]{2,1,0:T(8,128)(2,1)S(1)} %all_to_all.58) | copy-start | bytes 6291460
  270.9 4.4 %copy-start.35 = (f32[128,16]{1,0:T(8,128)S(1)}, f32[128,16]{1,0:T(8,128)}, u32[]{:S(2)}) copy-start(f32[128,16]{1,0:T(8,128)} %copy-done.34) | copy-start | bytes 24580
  270.9 16.7 %all-to-all-start.5 = ((bf16[8,128,512]{2,1,0:T(8,128)(2,1)}), bf16[8,128,512]{2,1,0:T(8,128)(2,1)}, u32[]{:S(2)}, u32[]{:S(2)}) async-start(bf16[8,128,512]{2,1,0:T(8,128)(2,1)} %bitcast.159), calls=%async_computation.5 | async-start | bytes 2097152 | tf_op jit(solution)/shard_map/all_to_all | solution.py:232
  278.0 3.7 %copy-start.48 = (f32[1,128]{1,0:T(1,128)S(1)}, f32[1,128]{1,0:T(1,128)}, u32[]{:S(2)}) copy-start(f32[1,128]{1,0:T(1,128)} %param.14) | copy-start | bytes 1540
  287.6 12.4 %copy-start.13 = (bf16[128,4,64]{2,0,1:T(8,128)(2,1)S(1)}, bf16[128,4,64]{2,0,1:T(8,128)(2,1)}, u32[]{:S(2)}) copy-start(bf16[128,4,64]{2,0,1:T(8,128)(2,1)} %copy-done.12) | copy-start | bytes 196612
  287.6 64.1 %all-to-all-start.4 = ((f32[8,64,1024]{2,1,0:T(8,128)}), f32[8,64,1024]{2,1,0:T(8,128)}, u32[]{:S(2)}, u32[]{:S(2)}) async-start(f32[8,64,1024]{2,1,0:T(8,128)} %bitcast.585), calls=%async_computation.4 | async-start | bytes 4194304 | tf_op jit(solution)/shard_map/all_to_all | solution.py:85
  307.7 4.0 %copy-start.21 = (f32[128,64]{1,0:T(8,128)S(1)}, f32[128,64]{1,0:T(8,128)}, u32[]{:S(2)}) copy-start(f32[128,64]{1,0:T(8,128)} %copy-done.18) | copy-start | bytes 98308
  307.7 4.0 %copy-start.25 = (f32[128,64]{1,0:T(8,128)S(1)}, f32[128,64]{1,0:T(8,128)}, u32[]{:S(2)}) copy-start(f32[128,64]{1,0:T(8,128)} %copy-done.22) | copy-start | bytes 98308
  315.5 16.2 %collective-permute-start.12 = (bf16[128,4096]{1,0:T(8,128)(2,1)}, bf16[128,4096]{1,0:T(8,128)(2,1)}, u32[]{:S(2)}, u32[]{:S(2)}) collective-permute-start(bf16[128,4096]{1,0:T(8,128)(2,1)} %bitcast.236), channel_id=1, source_target_pairs={{0,3},{1,0},{2,1},{3,2},{4,7},{5,4},{6,5},{7,6},{8,11},{9,8},{10,9... | collective-permute-start | bytes 3145736 | tf_op jit(solution)/shard_map/ppermute | solution.py:32
  320.4 3.6 %copy-start.10 = (f32[1,128,2048]{2,1,0:T(8,128)S(1)}, f32[1,128,2048]{2,1,0:T(8,128)}, u32[]{:S(2)}) copy-start(f32[1,128,2048]{2,1,0:T(8,128)} %mul.598) | copy-start | bytes 3145732
  (19 other events, 39.9 us)

commit v3 on v2

--- a/solution.py
+++ b/solution.py
@@ -102,7 +102,7 @@
     col_index = lax.axis_index("cz")
     ctx_index = lax.axis_index("cb") * col_parts + col_index
     both_rows = jnp.concatenate([w_key[0], w_value[0]], 1)
-    weight_slice = gathered(both_rows, "cz", col_parts)
+    weight_slice = lax.all_gather(both_rows, "cz", axis=0, tiled=True)
     inputs_slice = lax.all_to_all(tokens_here, "cb", 1, 0, tiled=True)
     projected = summed_over(
         jnp.dot(inputs_slice, weight_slice, preferred_element_type=jnp.float32),
@@ -218,13 +218,13 @@
     value_back = kv_total[1].reshape(tok_rows, kv_width).astype(jnp.bfloat16)
     both_back = jnp.concatenate([key_back, value_back], 1)
     group_back = gathered(both_back, "cb", row_parts)
-    grad_rows = summed_over(
+    grad_rows = lax.psum_scatter(
         lax.dot_general(
             inputs_slice, group_back, (((0,), (0,)), ((), ())), preferred_element_type=jnp.float32
         ),
         "cz",
-        col_parts,
-        jnp.float32,
+        scatter_dimension=0,
+        tiled=True,
     )
     slice_grad = lax.dot_general(
         group_back, weight_slice, (((1,), (1,)), ((), ())), preferred_element_type=jnp.float32

time: 358 us -> 331 us (0.925)
  the two profiles are of different devices: /device:TPU:1 before, /device:TPU:33 now
where the time goes in v3:
time: 331 us; the launch traced here: 329 us
  waiting for transfers between devices  134 us (40%)
  starting transfers between devices  73 us (22%)
  matrix products  45.1 us (14%)
  local copies, waits for them, and re-layouts  43.1 us (13%)
  other arithmetic  18.3 us (6%)
  between operations  15.3 us (5%)
    ppermute x12, waiting for transfers between devices, passed_along(): return lax.ppermute(block, axis, route)  51.8 us
    ppermute x12, starting transfers between devices, passed_along(): return lax.ppermute(block, axis, route)  37.2 us
    all_to_all x1, waiting for transfers between devices, gathered(): received = lax.all_to_all(copies, axis, 0, 0, tiled=True)  27.8 us
    all_to_all x1, waiting for transfers between devices, summed_over(): received = lax.all_to_all(pieces, axis, 0, 0, tiled=True)  19.7 us
    all_to_all x1, starting transfers between devices, gathered(): received = lax.all_to_all(copies, axis, 0, 0, tiled=True)  17.7 us
    unnamed x113, local copies, waits for them, and re-layouts  16.4 us
    all_to_all x1, waiting for transfers between devices, local(): inputs_slice = lax.all_to_all(tokens_here, 'cb', 1, 0, tiled=True)  13 us
    dot_general x7, matrix products, grad_block(): jnp.einsum('grqk,kgd->qgrd', score_grad, key_pair[0], preferred_element_t...  12.9 us
  transfers between devices with their start and end apart: 19, of which 10 were waited for; matrix products, arithmetic and copies ran while one was open for 20% of the time, Pallas kernels for 0%

profile of v3, /device:TPU:33, one launch (start us, length us, event | category | flops | bytes accessed | tf_op | source)
XLA Modules:
  0.0 328.5 jit_solution(2538978641647127066)
XLA Ops:
  7.2 1.5 pad_maximum_fusion.11
  8.8 1.6 copy.173
  10.4 1.3 copy.174
  11.7 6.7 %all-to-all-start = ((bf16[128,8,512]{2,0,1:T(8,128)(2,1)}), bf16[128,8,512]{2,0,1:T(8,128)(2,1)S(1)}, u32[]{:S(2)}, u32[]{:S(2)}) async-start(bf16[128,8,512]{2,0,1:T(8,128)(2,1)} %copy.174), calls=%async_computation | async-start | bytes 2097152 | tf_op jit(solution)/shard_map/all_to_all | solution.py:106
  21.0 13.0 %all-to-all-done = bf16[128,8,512]{2,0,1:T(8,128)(2,1)S(1)} async-done(((bf16[128,8,512]{2,0,1:T(8,128)(2,1)}), bf16[128,8,512]{2,0,1:T(8,128)(2,1)S(1)}, u32[]{:S(2)}, u32[]{:S(2)}) %all-to-all-start) | async-done | bytes 1048608 | tf_op jit(solution)/shard_map/all_to_all | solution.py:106
  34.0 12.2 %all-gather.2.cloned.1.call-done = bf16[512,1024]{1,0:T(8,128)(2,1)} async-done(((bf16[64,1024]{1,0:T(8,128)(2,1)}), bf16[512,1024]{1,0:T(8,128)(2,1)}) %all-gather.2.cloned.1.call-update) | async-done | bytes 1048592 | tf_op jit(solution)/shard_map/all_gather | solution.py:105
  46.2 3.8 %convolution_convert_fusion = bf16[1024,1024]{0,1:T(8,128)(2,1)} fusion(bf16[1024,512]{1,0:T(8,128)(2,1)S(1)} %bitcast.592, bf16[512,1024]{1,0:T(8,128)(2,1)} %all-gather.2.cloned.1.call-done), kind=kOutput, calls=%fused_computation | convolution fusion | flops 1074790400 | bytes 4194304 | tf_op jit(solution)/shard_map/dot_general | solution.py:108
  50.1 6.4 %all-to-all-start.1 = ((bf16[8,128,1024]{2,1,0:T(8,128)(2,1)}), bf16[8,128,1024]{2,1,0:T(8,128)(2,1)}, u32[]{:S(2)}, u32[]{:S(2)}) async-start(bf16[8,128,1024]{2,1,0:T(8,128)(2,1)} %bitcast.583), calls=%async_computation.1 | async-start | bytes 4194304 | tf_op jit(solution)/shard_map/all_to_all | solution.py:85
  62.6 19.7 %all-to-all-done.1 = bf16[8,128,1024]{2,1,0:T(8,128)(2,1)} async-done(((bf16[8,128,1024]{2,1,0:T(8,128)(2,1)}), bf16[8,128,1024]{2,1,0:T(8,128)(2,1)}, u32[]{:S(2)}, u32[]{:S(2)}) %all-to-all-start.1) | async-done | bytes 2097184 | tf_op jit(solution)/shard_map/all_to_all | solution.py:85
  82.3 2.0 reduce
  87.8 2.3 collective-permute-start
  90.1 4.2 %collective-permute-start.2 = (bf16[2,128,4,128]{3,1,2,0:T(8,128)(2,1)}, bf16[2,128,4,128]{3,1,2,0:T(8,128)(2,1)S(1)}, u32[]{:S(2)}, u32[]{:S(2)}) collective-permute-start(bf16[2,128,4,128]{3,1,2,0:T(8,128)(2,1)} %pad_maximum_fusion.2), channel_id=1, source_target_pairs={{0,12},{4,16},{8,20},{12,24},{16,28},{20,32},{24,36},{28,40},{32,4... | collective-permute-start | bytes 786440 | tf_op jit(solution)/shard_map/ppermute | solution.py:27
  94.3 3.2 collective-permute-start.3
  97.5 4.4 %collective-permute-start.4 = (bf16[2,128,4,128]{3,1,2,0:T(8,128)(2,1)}, bf16[2,128,4,128]{3,1,2,0:T(8,128)(2,1)}, u32[]{:S(2)}, u32[]{:S(2)}) collective-permute-start(bf16[2,128,4,128]{3,1,2,0:T(8,128)(2,1)} %pad_maximum_fusion.2), channel_id=1, source_target_pairs={{0,20},{4,24},{8,28},{12,32},{16,36},{20,40},{24,44},{28,48},{32,5... | collective-permute-start | bytes 786440 | tf_op jit(solution)/shard_map/ppermute | solution.py:27
  101.9 7.0 %collective-permute-start.5 = (bf16[2,128,4,128]{3,1,2,0:T(8,128)(2,1)}, bf16[2,128,4,128]{3,1,2,0:T(8,128)(2,1)}, u32[]{:S(2)}, u32[]{:S(2)}) collective-permute-start(bf16[2,128,4,128]{3,1,2,0:T(8,128)(2,1)} %pad_maximum_fusion.2), channel_id=1, source_target_pairs={{0,24},{4,28},{8,32},{12,36},{16,40},{20,44},{24,48},{28,52},{32,5... | collective-permute-start | bytes 786440 | tf_op jit(solution)/shard_map/ppermute | solution.py:27
  110.5 1.4 copy.253
  113.0 3.3 %collective-permute-start.1 = (bf16[2,128,4,128]{3,1,2,0:T(8,128)(2,1)}, bf16[2,128,4,128]{3,1,2,0:T(8,128)(2,1)S(1)}, u32[]{:S(2)}, u32[]{:S(2)}) collective-permute-start(bf16[2,128,4,128]{3,1,2,0:T(8,128)(2,1)} %pad_maximum_fusion.2), channel_id=1, source_target_pairs={{0,8},{4,12},{8,16},{12,20},{16,24},{20,28},{24,32},{28,36},{32,40... | collective-permute-start | bytes 786440 | tf_op jit(solution)/shard_map/ppermute | solution.py:27
  119.8 9.9 %collective-permute-done.5 = bf16[2,128,4,128]{3,1,2,0:T(8,128)(2,1)} collective-permute-done((bf16[2,128,4,128]{3,1,2,0:T(8,128)(2,1)}, bf16[2,128,4,128]{3,1,2,0:T(8,128)(2,1)}, u32[]{:S(2)}, u32[]{:S(2)}) %collective-permute-start.5) | collective-permute-done | bytes 262176 | tf_op jit(solution)/shard_map/ppermute | solution.py:27
  141.2 6.0 %collective-permute-start.6 = (bf16[2,128,4,128]{3,1,2,0:T(8,128)(2,1)S(1)}, bf16[2,128,4,128]{3,1,2,0:T(8,128)(2,1)S(1)}, u32[]{:S(2)}, u32[]{:S(2)}) collective-permute-start(bf16[2,128,4,128]{3,1,2,0:T(8,128)(2,1)S(1)} %pad_maximum_fusion.3), channel_id=1, source_target_pairs={{4,0},{8,4},{12,8},{16,12},{20,16},{24,20},{28,24},{32,28},{36,32}... | collective-permute-start | bytes 786440 | tf_op jit(solution)/shard_map/ppermute | solution.py:27
  147.9 1.3 collective-permute-start.7
  154.7 1.4 collective-permute-start.10
  158.5 1.5 collective-permute-start.11
  160.6 15.4 %collective-permute-done.8 = bf16[2,128,4,128]{3,1,2,0:T(8,128)(2,1)S(1)} collective-permute-done((bf16[2,128,4,128]{3,1,2,0:T(8,128)(2,1)S(1)}, bf16[2,128,4,128]{3,1,2,0:T(8,128)(2,1)S(1)}, u32[]{:S(2)}, u32[]{:S(2)}) %collective-permute-start.8) | collective-permute-done | bytes 262176 | tf_op jit(solution)/shard_map/ppermute | solution.py:27
  176.0 21.4 %collective-permute-done.9 = bf16[2,128,4,128]{3,1,2,0:T(8,128)(2,1)S(1)} collective-permute-done((bf16[2,128,4,128]{3,1,2,0:T(8,128)(2,1)S(1)}, bf16[2,128,4,128]{3,1,2,0:T(8,128)(2,1)S(1)}, u32[]{:S(2)}, u32[]{:S(2)}) %collective-permute-start.9) | collective-permute-done | bytes 262176 | tf_op jit(solution)/shard_map/ppermute | solution.py:27
  197.4 5.2 %collective-permute-done.11 = bf16[2,128,4,128]{3,1,2,0:T(8,128)(2,1)S(1)} collective-permute-done((bf16[2,128,4,128]{3,1,2,0:T(8,128)(2,1)S(1)}, bf16[2,128,4,128]{3,1,2,0:T(8,128)(2,1)S(1)}, u32[]{:S(2)}, u32[]{:S(2)}) %collective-permute-start.11) | collective-permute-done | bytes 262176 | tf_op jit(solution)/shard_map/ppermute | solution.py:27
  207.1 1.6 broadcast_in_dim.62
  208.7 17.7 %all-to-all-start.2 = ((bf16[8,128,1024]{1,2,0:T(8,128)(2,1)}), bf16[8,128,1024]{1,2,0:T(8,128)(2,1)}, u32[]{:S(2)}, u32[]{:S(2)}) async-start(bf16[8,128,1024]{1,2,0:T(8,128)(2,1)} %broadcast_in_dim.62), calls=%async_computation.2 | async-start | bytes 4194304 | tf_op jit(solution)/shard_map/all_to_all | solution.py:79
  229.5 27.8 %all-to-all-done.2 = bf16[8,128,1024]{1,2,0:T(8,128)(2,1)} async-done(((bf16[8,128,1024]{1,2,0:T(8,128)(2,1)}), bf16[8,128,1024]{1,2,0:T(8,128)(2,1)}, u32[]{:S(2)}, u32[]{:S(2)}) %all-to-all-start.2) | async-done | bytes 2097184 | tf_op jit(solution)/shard_map/all_to_all | solution.py:79
  257.3 4.5 %convolution_bitcast_fusion = f32[512,1024]{0,1:T(8,128)} fusion(bf16[8,128,1024]{1,2,0:T(8,128)(2,1)} %all-to-all-done.2, bf16[128,8,512]{2,0,1:T(8,128)(2,1)} %copy-done.30), kind=kOutput, calls=%fused_computation.1 | convolution fusion | flops 1073741824 | bytes 5242880 | tf_op jit(solution)/shard_map/dot_general | solution.py:222
  261.7 2.9 copy.383
  266.0 1.4 fusion.97
  267.4 1.4 fusion.98
  268.7 2.3 fusion.99
  271.0 2.2 fusion.100
  273.2 2.2 convolution_add_fusion.1
  275.5 2.9 copy.259
  278.3 3.5 %convolution_convert_fusion.1 = bf16[1024,512]{1,0:T(8,128)(2,1)} fusion(bf16[1024,1024]{1,0:T(8,128)(2,1)S(1)} %bitcast.584, bf16[512,1024]{1,0:T(8,128)(2,1)} %all-gather.2.cloned.1.call-done), kind=kOutput, calls=%fused_computation.2 | convolution fusion | flops 1074266112 | bytes 4194304 | tf_op jit(solution)/shard_map/dot_general | solution.py:229
  281.8 3.7 %all-to-all-start.3 = ((bf16[8,128,512]{2,1,0:T(8,128)(2,1)}), bf16[8,128,512]{2,1,0:T(8,128)(2,1)S(1)}, u32[]{:S(2)}, u32[]{:S(2)}) async-start(bf16[8,128,512]{2,1,0:T(8,128)(2,1)} %bitcast.593), calls=%async_computation.3 | async-start | bytes 2097152 | tf_op jit(solution)/shard_map/all_to_all | solution.py:232
  285.6 3.0 fusion.12
  289.7 1.6 copy.385
  291.3 2.4 copy.386
  293.7 2.8 multiply_add_fusion
  296.5 4.5 %all-to-all-done.3 = bf16[8,128,512]{2,1,0:T(8,128)(2,1)S(1)} async-done(((bf16[8,128,512]{2,1,0:T(8,128)(2,1)}), bf16[8,128,512]{2,1,0:T(8,128)(2,1)S(1)}, u32[]{:S(2)}, u32[]{:S(2)}) %all-to-all-start.3) | async-done | bytes 1048608 | tf_op jit(solution)/shard_map/all_to_all | solution.py:232
  304.0 1.3 mul.602
  305.3 2.5 mul.603
  309.0 2.9 fusion.88
  311.9 4.7 %collective-permute-done.12 = bf16[128,4096]{1,0:T(8,128)(2,1)} collective-permute-done((bf16[128,4096]{1,0:T(8,128)(2,1)}, bf16[128,4096]{1,0:T(8,128)(2,1)}, u32[]{:S(2)}, u32[]{:S(2)}) %collective-permute-start.12) | collective-permute-done | bytes 1048608 | tf_op jit(solution)/shard_map/ppermute | solution.py:32
  319.4 2.3 copy.399
  (230 shorter events, 55.2 us)
Async XLA Ops:
  7.2 39.0 %all-gather.2.cloned.1.call-start = ((), (), s32[]{:S(2)}) async-start(), calls=%async_computation.5 | async-start | bytes 1179648 | tf_op jit(solution)/shard_map/all_gather | solution.py:105
  10.4 8.0 %copy-start.16 = (bf16[1,128,2048]{2,1,0:T(8,128)(2,1)S(1)}, bf16[1,128,2048]{2,1,0:T(8,128)(2,1)}, u32[]{:S(2)}) copy-start(bf16[1,128,2048]{2,1,0:T(8,128)(2,1)} %param.9) | copy-start | bytes 1572868
  11.7 22.3 %all-to-all-start = ((bf16[128,8,512]{2,0,1:T(8,128)(2,1)}), bf16[128,8,512]{2,0,1:T(8,128)(2,1)S(1)}, u32[]{:S(2)}, u32[]{:S(2)}) async-start(bf16[128,8,512]{2,0,1:T(8,128)(2,1)} %copy.174), calls=%async_computation | async-start | bytes 2097152 | tf_op jit(solution)/shard_map/all_to_all | solution.py:106
  19.4 37.1 %copy-start.19 = (f32[128,64]{1,0:T(8,128)}, f32[128,64]{1,0:T(8,128)S(1)}, u32[]{:S(2)}) copy-start(f32[128,64]{1,0:T(8,128)S(1)} %get-tuple-element.59) | copy-start | bytes 98308
  19.4 37.1 %copy-start.23 = (f32[128,64]{1,0:T(8,128)}, f32[128,64]{1,0:T(8,128)S(1)}, u32[]{:S(2)}) copy-start(f32[128,64]{1,0:T(8,128)S(1)} %get-tuple-element.60) | copy-start | bytes 98308
  34.0 16.1 %copy-start.30 = (bf16[128,8,512]{2,0,1:T(8,128)(2,1)}, bf16[128,8,512]{2,0,1:T(8,128)(2,1)S(1)}, u32[]{:S(2)}) copy-start(bf16[128,8,512]{2,0,1:T(8,128)(2,1)S(1)} %all-to-all-done) | copy-start | bytes 3145732
  50.1 32.2 %all-to-all-start.1 = ((bf16[8,128,1024]{2,1,0:T(8,128)(2,1)}), bf16[8,128,1024]{2,1,0:T(8,128)(2,1)}, u32[]{:S(2)}, u32[]{:S(2)}) async-start(bf16[8,128,1024]{2,1,0:T(8,128)(2,1)} %bitcast.583), calls=%async_computation.1 | async-start | bytes 4194304 | tf_op jit(solution)/shard_map/all_to_all | solution.py:85
  62.6 23.9 %copy-start.20 = (f32[128,64]{1,0:T(8,128)S(1)}, f32[128,64]{1,0:T(8,128)}, u32[]{:S(2)}) copy-start(f32[128,64]{1,0:T(8,128)} %copy-done.19) | copy-start | bytes 98308
  62.6 23.9 %copy-start.24 = (f32[128,64]{1,0:T(8,128)S(1)}, f32[128,64]{1,0:T(8,128)}, u32[]{:S(2)}) copy-start(f32[128,64]{1,0:T(8,128)} %copy-done.23) | copy-start | bytes 98308
  86.7 31.0 %copy-start.14 = (bf16[128,4,64]{2,0,1:T(8,128)(2,1)}, bf16[128,4,64]{2,0,1:T(8,128)(2,1)S(1)}, u32[]{:S(2)}) copy-start(bf16[128,4,64]{2,0,1:T(8,128)(2,1)S(1)} %get-tuple-element.29) | copy-start | bytes 196612
  86.8 47.5 %copy-start.17 = (bf16[128,512]{0,1:T(8,128)(2,1)}, bf16[128,512]{0,1:T(8,128)(2,1)S(1)}, u32[]{:S(2)}) copy-start(bf16[128,512]{0,1:T(8,128)(2,1)S(1)} %copy.179) | copy-start | bytes 393220
  87.8 25.3 %collective-permute-start = (bf16[2,128,4,128]{3,1,2,0:T(8,128)(2,1)}, bf16[2,128,4,128]{3,1,2,0:T(8,128)(2,1)}, u32[]{:S(2)}, u32[]{:S(2)}) collective-permute-start(bf16[2,128,4,128]{3,1,2,0:T(8,128)(2,1)} %pad_maximum_fusion.2), channel_id=1, source_target_pairs={{0,4},{4,8},{8,12},{12,16},{16,20},{20,24},{24,28},{28,32},{32,36}... | collective-permute-start | bytes 786440 | tf_op jit(solution)/shard_map/ppermute | solution.py:27
  90.1 27.6 %collective-permute-start.2 = (bf16[2,128,4,128]{3,1,2,0:T(8,128)(2,1)}, bf16[2,128,4,128]{3,1,2,0:T(8,128)(2,1)S(1)}, u32[]{:S(2)}, u32[]{:S(2)}) collective-permute-start(bf16[2,128,4,128]{3,1,2,0:T(8,128)(2,1)} %pad_maximum_fusion.2), channel_id=1, source_target_pairs={{0,12},{4,16},{8,20},{12,24},{16,28},{20,32},{24,36},{28,40},{32,4... | collective-permute-start | bytes 786440 | tf_op jit(solution)/shard_map/ppermute | solution.py:27
  94.3 23.8 %collective-permute-start.3 = (bf16[2,128,4,128]{3,1,2,0:T(8,128)(2,1)}, bf16[2,128,4,128]{3,1,2,0:T(8,128)(2,1)S(1)}, u32[]{:S(2)}, u32[]{:S(2)}) collective-permute-start(bf16[2,128,4,128]{3,1,2,0:T(8,128)(2,1)} %pad_maximum_fusion.2), channel_id=1, source_target_pairs={{0,16},{4,20},{8,24},{12,28},{16,32},{20,36},{24,40},{28,44},{32,4... | collective-permute-start | bytes 786440 | tf_op jit(solution)/shard_map/ppermute | solution.py:27
  97.5 21.1 %collective-permute-start.4 = (bf16[2,128,4,128]{3,1,2,0:T(8,128)(2,1)}, bf16[2,128,4,128]{3,1,2,0:T(8,128)(2,1)}, u32[]{:S(2)}, u32[]{:S(2)}) collective-permute-start(bf16[2,128,4,128]{3,1,2,0:T(8,128)(2,1)} %pad_maximum_fusion.2), channel_id=1, source_target_pairs={{0,20},{4,24},{8,28},{12,32},{16,36},{20,40},{24,44},{28,48},{32,5... | collective-permute-start | bytes 786440 | tf_op jit(solution)/shard_map/ppermute | solution.py:27
  101.9 27.8 %collective-permute-start.5 = (bf16[2,128,4,128]{3,1,2,0:T(8,128)(2,1)}, bf16[2,128,4,128]{3,1,2,0:T(8,128)(2,1)}, u32[]{:S(2)}, u32[]{:S(2)}) collective-permute-start(bf16[2,128,4,128]{3,1,2,0:T(8,128)(2,1)} %pad_maximum_fusion.2), channel_id=1, source_target_pairs={{0,24},{4,28},{8,32},{12,36},{16,40},{20,44},{24,48},{28,52},{32,5... | collective-permute-start | bytes 786440 | tf_op jit(solution)/shard_map/ppermute | solution.py:27
  111.9 5.9 %copy-start.44 = (pred[128,128]{0,1:T(8,128)(4,1)S(1)}, pred[128,128]{0,1:T(8,128)(4,1)}, u32[]{:S(2)}) copy-start(pred[128,128]{0,1:T(8,128)(4,1)} %get-tuple-element.55) | copy-start | bytes 49156
  113.0 5.1 %copy-start.43 = (pred[128,128]{0,1:T(8,128)(4,1)S(1)}, pred[128,128]{0,1:T(8,128)(4,1)}, u32[]{:S(2)}) copy-start(pred[128,128]{0,1:T(8,128)(4,1)} %get-tuple-element.56) | copy-start | bytes 49156
  113.0 18.0 %collective-permute-start.1 = (bf16[2,128,4,128]{3,1,2,0:T(8,128)(2,1)}, bf16[2,128,4,128]{3,1,2,0:T(8,128)(2,1)S(1)}, u32[]{:S(2)}, u32[]{:S(2)}) collective-permute-start(bf16[2,128,4,128]{3,1,2,0:T(8,128)(2,1)} %pad_maximum_fusion.2), channel_id=1, source_target_pairs={{0,8},{4,12},{8,16},{12,20},{16,24},{20,28},{24,32},{28,36},{32,40... | collective-permute-start | bytes 786440 | tf_op jit(solution)/shard_map/ppermute | solution.py:27
  117.7 31.5 %copy-start.33 = (bf16[2,128,4,128]{3,1,2,0:T(8,128)(2,1)}, bf16[2,128,4,128]{3,1,2,0:T(8,128)(2,1)S(1)}, u32[]{:S(2)}) copy-start(bf16[2,128,4,128]{3,1,2,0:T(8,128)(2,1)S(1)} %collective-permute-done.2) | copy-start | bytes 786436
  118.1 33.0 %copy-start.35 = (bf16[2,128,4,128]{3,1,2,0:T(8,128)(2,1)}, bf16[2,128,4,128]{3,1,2,0:T(8,128)(2,1)S(1)}, u32[]{:S(2)}) copy-start(bf16[2,128,4,128]{3,1,2,0:T(8,128)(2,1)S(1)} %collective-permute-done.3) | copy-start | bytes 786436
  118.5 12.5 %copy-start.41 = (pred[128,128]{0,1:T(8,128)(4,1)S(1)}, pred[128,128]{0,1:T(8,128)(4,1)}, u32[]{:S(2)}) copy-start(pred[128,128]{0,1:T(8,128)(4,1)} %get-tuple-element.54) | copy-start | bytes 49156
  131.0 16.2 %copy-start.31 = (bf16[2,128,4,128]{3,1,2,0:T(8,128)(2,1)}, bf16[2,128,4,128]{3,1,2,0:T(8,128)(2,1)S(1)}, u32[]{:S(2)}) copy-start(bf16[2,128,4,128]{3,1,2,0:T(8,128)(2,1)S(1)} %collective-permute-done.1) | copy-start | bytes 786436
  140.9 6.9 %copy-start.6 = (bf16[4,4,128,128]{2,3,1,0:T(8,128)(2,1)}, bf16[4,4,128,128]{2,3,1,0:T(8,128)(2,1)S(1)}, u32[]{:S(2)}) copy-start(bf16[4,4,128,128]{2,3,1,0:T(8,128)(2,1)S(1)} %fusion.47) | copy-start | bytes 1572868
  141.2 17.2 %collective-permute-start.6 = (bf16[2,128,4,128]{3,1,2,0:T(8,128)(2,1)S(1)}, bf16[2,128,4,128]{3,1,2,0:T(8,128)(2,1)S(1)}, u32[]{:S(2)}, u32[]{:S(2)}) collective-permute-start(bf16[2,128,4,128]{3,1,2,0:T(8,128)(2,1)S(1)} %pad_maximum_fusion.3), channel_id=1, source_target_pairs={{4,0},{8,4},{12,8},{16,12},{20,16},{24,20},{28,24},{32,28},{36,32}... | collective-permute-start | bytes 786440 | tf_op jit(solution)/shard_map/ppermute | solution.py:27
  147.9 12.8 %collective-permute-start.7 = (bf16[2,128,4,128]{3,1,2,0:T(8,128)(2,1)S(1)}, bf16[2,128,4,128]{3,1,2,0:T(8,128)(2,1)S(1)}, u32[]{:S(2)}, u32[]{:S(2)}) collective-permute-start(bf16[2,128,4,128]{3,1,2,0:T(8,128)(2,1)S(1)} %pad_maximum_fusion.4), channel_id=1, source_target_pairs={{8,0},{12,4},{16,8},{20,12},{24,16},{28,20},{32,24},{36,28},{40,32... | collective-permute-start | bytes 786440 | tf_op jit(solution)/shard_map/ppermute | solution.py:27
  149.8 26.2 %collective-permute-start.8 = (bf16[2,128,4,128]{3,1,2,0:T(8,128)(2,1)S(1)}, bf16[2,128,4,128]{3,1,2,0:T(8,128)(2,1)S(1)}, u32[]{:S(2)}, u32[]{:S(2)}) collective-permute-start(bf16[2,128,4,128]{3,1,2,0:T(8,128)(2,1)S(1)} %pad_maximum_fusion.5), channel_id=1, source_target_pairs={{12,0},{16,4},{20,8},{24,12},{28,16},{32,20},{36,24},{40,28},{44,3... | collective-permute-start | bytes 786440 | tf_op jit(solution)/shard_map/ppermute | solution.py:27
  151.8 45.6 %collective-permute-start.9 = (bf16[2,128,4,128]{3,1,2,0:T(8,128)(2,1)S(1)}, bf16[2,128,4,128]{3,1,2,0:T(8,128)(2,1)S(1)}, u32[]{:S(2)}, u32[]{:S(2)}) collective-permute-start(bf16[2,128,4,128]{3,1,2,0:T(8,128)(2,1)S(1)} %pad_maximum_fusion.6), channel_id=1, source_target_pairs={{16,0},{20,4},{24,8},{28,12},{32,16},{36,20},{40,24},{44,28},{48,3... | collective-permute-start | bytes 786440 | tf_op jit(solution)/shard_map/ppermute | solution.py:27
  154.7 42.7 %collective-permute-start.10 = (bf16[2,128,4,128]{3,1,2,0:T(8,128)(2,1)S(1)}, bf16[2,128,4,128]{3,1,2,0:T(8,128)(2,1)S(1)}, u32[]{:S(2)}, u32[]{:S(2)}) collective-permute-start(bf16[2,128,4,128]{3,1,2,0:T(8,128)(2,1)S(1)} %pad_maximum_fusion.7), channel_id=1, source_target_pairs={{20,0},{24,4},{28,8},{32,12},{36,16},{40,20},{44,24},{48,28},{52,3... | collective-permute-start | bytes 786440 | tf_op jit(solution)/shard_map/ppermute | solution.py:27
  158.5 44.1 %collective-permute-start.11 = (bf16[2,128,4,128]{3,1,2,0:T(8,128)(2,1)S(1)}, bf16[2,128,4,128]{3,1,2,0:T(8,128)(2,1)S(1)}, u32[]{:S(2)}, u32[]{:S(2)}) collective-permute-start(bf16[2,128,4,128]{3,1,2,0:T(8,128)(2,1)S(1)} %pad_maximum_fusion.8), channel_id=1, source_target_pairs={{24,0},{28,4},{32,8},{36,12},{40,16},{44,20},{48,24},{52,28},{56,3... | collective-permute-start | bytes 786440 | tf_op jit(solution)/shard_map/ppermute | solution.py:27
  160.3 42.6 %copy-start.21 = (f32[128,64]{1,0:T(8,128)S(1)}, f32[128,64]{1,0:T(8,128)}, u32[]{:S(2)}) copy-start(f32[128,64]{1,0:T(8,128)} %copy-done.19) | copy-start | bytes 98308
  160.3 42.6 %copy-start.25 = (f32[128,64]{1,0:T(8,128)S(1)}, f32[128,64]{1,0:T(8,128)}, u32[]{:S(2)}) copy-start(f32[128,64]{1,0:T(8,128)} %copy-done.23) | copy-start | bytes 98308
  160.6 42.5 %copy-start.48 = (f32[1,128]{1,0:T(1,128)S(1)}, f32[1,128]{1,0:T(1,128)}, u32[]{:S(2)}) copy-start(f32[1,128]{1,0:T(1,128)} %param.15) | copy-start | bytes 1540
  202.9 3.8 %copy-start.28 = (bf16[128,1024]{1,0:T(8,128)(2,1)S(1)}, bf16[128,1024]{1,0:T(8,128)(2,1)}, u32[]{:S(2)}) copy-start(bf16[128,1024]{1,0:T(8,128)(2,1)} %copy-done.27) | copy-start | bytes 786436
  202.9 3.8 %copy-start.29 = (f32[128,512]{1,0:T(8,128)S(1)}, f32[128,512]{1,0:T(8,128)}, u32[]{:S(2)}) copy-start(f32[128,512]{1,0:T(8,128)} %copy.252) | copy-start | bytes 786436
  202.9 3.8 %copy-start.46 = (f32[512]{0:T(512)S(1)}, f32[512]{0:T(512)}, u32[]{:S(2)}) copy-start(f32[512]{0:T(512)} %broadcast_bitcast_fusion.1) | copy-start | bytes 6148
  208.7 17.7 %copy-start.38 = (f32[128,16]{1,0:T(8,128)S(1)}, f32[128,16]{1,0:T(8,128)}, u32[]{:S(2)}) copy-start(f32[128,16]{1,0:T(8,128)} %copy-done.37) | copy-start | bytes 24580
  208.7 48.6 %all-to-all-start.2 = ((bf16[8,128,1024]{1,2,0:T(8,128)(2,1)}), bf16[8,128,1024]{1,2,0:T(8,128)(2,1)}, u32[]{:S(2)}, u32[]{:S(2)}) async-start(bf16[8,128,1024]{1,2,0:T(8,128)(2,1)} %broadcast_in_dim.62), calls=%async_computation.2 | async-start | bytes 4194304 | tf_op jit(solution)/shard_map/all_to_all | solution.py:79
  226.4 90.2 %reduce-scatter.4.cloned.1.call-start = ((), (), s32[]{:S(2)}) async-start(), calls=%async_computation.6 | async-start | bytes 2359296
  268.7 4.5 %copy-start.7 = (bf16[4,4,128,128]{2,3,1,0:T(8,128)(2,1)S(1)}, bf16[4,4,128,128]{2,3,1,0:T(8,128)(2,1)}, u32[]{:S(2)}) copy-start(bf16[4,4,128,128]{2,3,1,0:T(8,128)(2,1)} %copy-done.6) | copy-start | bytes 1572868
  281.8 3.7 %copy-start.9 = (bf16[4,4,128,128]{2,3,1,0:T(8,128)(2,1)S(1)}, bf16[4,4,128,128]{2,3,1,0:T(8,128)(2,1)}, u32[]{:S(2)}) copy-start(bf16[4,4,128,128]{2,3,1,0:T(8,128)(2,1)} %copy-done.8) | copy-start | bytes 1572868
  281.8 3.7 %copy-start.32 = (bf16[2,128,4,128]{3,1,2,0:T(8,128)(2,1)S(1)}, bf16[2,128,4,128]{3,1,2,0:T(8,128)(2,1)}, u32[]{:S(2)}) copy-start(bf16[2,128,4,128]{3,1,2,0:T(8,128)(2,1)} %copy-done.31) | copy-start | bytes 786436
  281.8 19.1 %all-to-all-start.3 = ((bf16[8,128,512]{2,1,0:T(8,128)(2,1)}), bf16[8,128,512]{2,1,0:T(8,128)(2,1)S(1)}, u32[]{:S(2)}, u32[]{:S(2)}) async-start(bf16[8,128,512]{2,1,0:T(8,128)(2,1)} %bitcast.593), calls=%async_computation.3 | async-start | bytes 2097152 | tf_op jit(solution)/shard_map/all_to_all | solution.py:232
  289.7 4.0 %copy-start.22 = (f32[128,64]{1,0:T(8,128)S(1)}, f32[128,64]{1,0:T(8,128)}, u32[]{:S(2)}) copy-start(f32[128,64]{1,0:T(8,128)} %copy-done.19) | copy-start | bytes 98308
  289.7 4.0 %copy-start.26 = (f32[128,64]{1,0:T(8,128)S(1)}, f32[128,64]{1,0:T(8,128)}, u32[]{:S(2)}) copy-start(f32[128,64]{1,0:T(8,128)} %copy-done.23) | copy-start | bytes 98308
  302.1 14.5 %collective-permute-start.12 = (bf16[128,4096]{1,0:T(8,128)(2,1)}, bf16[128,4096]{1,0:T(8,128)(2,1)}, u32[]{:S(2)}, u32[]{:S(2)}) collective-permute-start(bf16[128,4096]{1,0:T(8,128)(2,1)} %bitcast.235), channel_id=1, source_target_pairs={{0,3},{1,0},{2,1},{3,2},{4,7},{5,4},{6,5},{7,6},{8,11},{9,8},{10,9... | collective-permute-start | bytes 3145736 | tf_op jit(solution)/shard_map/ppermute | solution.py:32
  305.3 3.7 %copy-start.10 = (f32[1,128,2048]{2,1,0:T(8,128)S(1)}, f32[1,128,2048]{2,1,0:T(8,128)}, u32[]{:S(2)}) copy-start(f32[1,128,2048]{2,1,0:T(8,128)} %mul.518) | copy-start | bytes 3145732
  305.3 3.7 %copy-start.11 = (f32[1,128,2048]{2,1,0:T(8,128)S(1)}, f32[1,128,2048]{2,1,0:T(8,128)}, u32[]{:S(2)}) copy-start(f32[1,128,2048]{2,1,0:T(8,128)} %mul.598) | copy-start | bytes 3145732
  (22 other events, 42.1 us)
Sparse Core Ops, SparseCore 0:
  10.3 35.8 all-gather.1
  264.8 35.5 reduce-scatter.3

commit v4 on v3

--- a/solution.py
+++ b/solution.py
@@ -143,69 +143,41 @@
         allowed_list.append(allowed)
     q_group = query_rot.reshape(tok_rows, kv_heads, group, HEAD)
     out_grad = grad_out[0].reshape(tok_rows, kv_heads, group, HEAD)
-
-    def exp_block(key_pair, allowed):
-        scores = (
-            jnp.einsum("qgrd,kgd->grqk", q_group, key_pair[0], preferred_element_type=jnp.float32)
-            * score_scale
-        )
-        return jnp.where(allowed, jnp.exp(scores), 0.0)
-
-    def total_block(key_pair, allowed):
-        return jnp.sum(exp_block(key_pair, allowed), -1)
-
-    zero_total = jnp.zeros((kv_heads, group, tok_rows), jnp.float32)
-    row_total = zero_total
-    for distance in range(reach_blocks + 1):
-        row_total = row_total + guarded(total_block, (key_blocks[distance], allowed_list[distance]))
-
-    def prob_block(key_pair, allowed):
-        prob_tile = (exp_block(key_pair, allowed) / row_total[..., None]).astype(jnp.bfloat16)
-        out_tile = jnp.einsum(
-            "grqk,kgd->qgrd", prob_tile, key_pair[1], preferred_element_type=jnp.float32
-        )
-        return (prob_tile, out_tile)
-
-    zero_query = jnp.zeros((tok_rows, kv_heads, group, HEAD), jnp.float32)
-    prob_list = []
-    attn_out = zero_query
-    for distance in range(reach_blocks + 1):
-        prob_tile, out_tile = guarded(prob_block, (key_blocks[distance], allowed_list[distance]))
-        prob_list.append(prob_tile)
-        attn_out = attn_out + out_tile
+    pairs = jnp.concatenate(key_blocks, 1)
+    keys, values = pairs[0], pairs[1]
+    allowed = jnp.concatenate(allowed_list, 1)
+    scores = (
+        jnp.einsum("qgrd,kgd->grqk", q_group, keys, preferred_element_type=jnp.float32)
+        * score_scale
+    )
+    exp_score = jnp.where(allowed, jnp.exp(scores), 0.0)
+    row_total = jnp.sum(exp_score, -1, keepdims=True)
+    prob_tile = (exp_score / row_total).astype(jnp.bfloat16)
+    attn_out = jnp.einsum(
+        "grqk,kgd->qgrd", prob_tile, values, preferred_element_type=jnp.float32
+    )
     row_delta = jnp.sum(out_grad.astype(jnp.float32) * attn_out, -1).transpose(1, 2, 0)[..., None]
-
-    def grad_block(key_pair, prob_tile):
-        prob_grad = jnp.einsum(
-            "qgrd,kgd->grqk", out_grad, key_pair[1], preferred_element_type=jnp.float32
-        )
-        score_grad = (prob_tile.astype(jnp.float32) * (prob_grad - row_delta)).astype(jnp.bfloat16)
-        value_grad = jnp.einsum(
-            "grqk,qgrd->kgd", prob_tile, out_grad, preferred_element_type=jnp.float32
-        )
-        key_grad = (
-            jnp.einsum("grqk,qgrd->kgd", score_grad, q_group, preferred_element_type=jnp.float32)
-            * score_scale
-        )
-        query_part = (
-            jnp.einsum(
-                "grqk,kgd->qgrd", score_grad, key_pair[0], preferred_element_type=jnp.float32
-            )
-            * score_scale
-        )
-        return (query_part, jnp.stack([key_grad, value_grad]))
-
-    zero_pair = jnp.zeros((2, tok_rows, kv_heads, HEAD), jnp.float32)
-    query_rot_grad = zero_query
-    kv_total = zero_pair
-    for distance in range(reach_blocks + 1):
-        query_part, kv_part = guarded(grad_block, (key_blocks[distance], prob_list[distance]))
-        query_rot_grad = query_rot_grad + query_part
-        if distance == 0:
-            kv_total = kv_part
-        else:
-            returned = passed_along(kv_part.astype(jnp.bfloat16), CTX, -distance)
-            kv_total = kv_total + returned.astype(jnp.float32)
+    prob_grad = jnp.einsum(
+        "qgrd,kgd->grqk", out_grad, values, preferred_element_type=jnp.float32
+    )
+    score_grad = (prob_tile.astype(jnp.float32) * (prob_grad - row_delta)).astype(jnp.bfloat16)
+    value_grad = jnp.einsum(
+        "grqk,qgrd->kgd", prob_tile, out_grad, preferred_element_type=jnp.float32
+    )
+    key_grad = (
+        jnp.einsum("grqk,qgrd->kgd", score_grad, q_group, preferred_element_type=jnp.float32)
+        * score_scale
+    )
+    query_rot_grad = (
+        jnp.einsum("grqk,kgd->qgrd", score_grad, keys, preferred_element_type=jnp.float32)
+        * score_scale
+    )
+    kv_parts = jnp.stack([key_grad, value_grad])
+    kv_total = kv_parts[:, :tok_rows]
+    for distance in range(1, reach_blocks + 1):
+        kv_part = kv_parts[:, distance * tok_rows : (distance + 1) * tok_rows]
+        returned = passed_along(kv_part.astype(jnp.bfloat16), CTX, -distance)
+        kv_total = kv_total + returned.astype(jnp.float32)
     query_grad = normalize_back(
         query_in,
         query_inv,

time: 331 us -> 340 us (1.027)
  blocking collectives: 0 us -> 44.1 us
  matrix products: 45.1 us -> 21.4 us
  starting transfers between devices: 73 us -> 62.9 us
  waiting for transfers between devices: 134 us -> 126 us
  local copies, waits for them, and re-layouts: 43.1 us -> 48.1 us
    all_to_all x0 -> x1, blocking collectives: none -> 44.1 us  [gathered(): received = lax.all_to_all(copies, axis, 0, 0, tiled=True)]
    all_to_all x1 -> x0, waiting for transfers between devices: 27.8 us -> none  [gathered(): received = lax.all_to_all(copies, axis, 0, 0, tiled=True)]
    dot_general x42 -> x6, matrix products: 33.3 us -> 9.3 us  [the longest x1 3.15 us: local(): jnp.einsum('grqk,kgd->qgrd', score_grad, keys, preferred_element_type=jnp...]
    all_to_all x1 -> x0, starting transfers between devices: 17.7 us -> none  [gathered(): received = lax.all_to_all(copies, axis, 0, 0, tiled=True)]
    all_gather x1, waiting for transfers between devices: 12.2 us -> 23.7 us  [local(): weight_slice = lax.all_gather(both_rows, 'cz', axis=0, tiled=True)]
    ppermute x12, waiting for transfers between devices: 51.8 us -> 59.4 us  [passed_along(): return lax.ppermute(block, axis, route)]
    ppermute x12, starting transfers between devices: 37.2 us -> 41.6 us  [passed_along(): return lax.ppermute(block, axis, route)]
    unnamed x113 -> x72, local copies, waits for them, and re-layouts: 16.4 us -> 19.9 us
  transfers between devices with their start and end apart: 19 -> 18, of which waited for: 10 -> 11; matrix products, arithmetic and copies ran while one was open for 20% -> 15% of each run, Pallas kernels for 0% -> 0%
where the time goes in v4:
time: 340 us; the launch traced here: 338 us
  waiting for transfers between devices  126 us (37%)
  starting transfers between devices  62.9 us (18%)
  local copies, waits for them, and re-layouts  48.1 us (14%)
  blocking collectives  44.1 us (13%)
  matrix products  21.4 us (6%)
  other arithmetic  21.3 us (6%)
  between operations  14.9 us (4%)
    ppermute x12, waiting for transfers between devices, passed_along(): return lax.ppermute(block, axis, route)  59.4 us
    all_to_all x1, blocking collectives, gathered(): received = lax.all_to_all(copies, axis, 0, 0, tiled=True)  44.1 us
    ppermute x12, starting transfers between devices, passed_along(): return lax.ppermute(block, axis, route)  41.6 us
    all_gather x1, waiting for transfers between devices, local(): weight_slice = lax.all_gather(both_rows, 'cz', axis=0, tiled=True)  23.7 us
    all_to_all x1, waiting for transfers between devices, summed_over(): received = lax.all_to_all(pieces, axis, 0, 0, tiled=True)  22 us
    unnamed x72, local copies, waits for them, and re-layouts  19.9 us
    all_to_all x1, waiting for transfers between devices, local(): inputs_slice = lax.all_to_all(tokens_here, 'cb', 1, 0, tiled=True)  12 us
    mul x6, local copies, waits for them, and re-layouts, normalize_back(): values * cubed * jnp.mean(values * scaled, -1, keepdims=True)  7.91 us
  transfers between devices with their start and end apart: 18, of which 11 were waited for; matrix products, arithmetic and copies ran while one was open for 15% of the time, Pallas kernels for 0%

profile of v4, /device:TPU:33, one launch (start us, length us, event | category | flops | bytes accessed | tf_op | source)
XLA Modules:
  0.0 338.3 jit_solution(5620152722793849660)
XLA Ops:
  7.2 1.6 copy.65
  8.8 1.3 copy.66
  10.1 6.7 %all-to-all-start = ((bf16[128,8,512]{2,0,1:T(8,128)(2,1)}), bf16[128,8,512]{2,0,1:T(8,128)(2,1)}, u32[]{:S(2)}, u32[]{:S(2)}) async-start(bf16[128,8,512]{2,0,1:T(8,128)(2,1)} %copy.66), calls=%async_computation | async-start | bytes 2097152 | tf_op jit(solution)/shard_map/all_to_all | solution.py:106
  18.7 1.5 fusion.58
  20.5 12.0 %all-to-all-done = bf16[128,8,512]{2,0,1:T(8,128)(2,1)} async-done(((bf16[128,8,512]{2,0,1:T(8,128)(2,1)}), bf16[128,8,512]{2,0,1:T(8,128)(2,1)}, u32[]{:S(2)}, u32[]{:S(2)}) %all-to-all-start) | async-done | bytes 1048608 | tf_op jit(solution)/shard_map/all_to_all | solution.py:106
  32.5 23.7 %all-gather.2.cloned.1.call-done = bf16[512,1024]{1,0:T(8,128)(2,1)} async-done(((bf16[64,1024]{1,0:T(8,128)(2,1)}), bf16[512,1024]{1,0:T(8,128)(2,1)}) %all-gather.2.cloned.1.call-update) | async-done | bytes 1048592 | tf_op jit(solution)/shard_map/all_gather | solution.py:105
  56.2 4.1 %convolution_convert_fusion = bf16[1024,1024]{0,1:T(8,128)(2,1)} fusion(bf16[1024,512]{1,0:T(8,128)(2,1)} %bitcast.4, bf16[512,1024]{1,0:T(8,128)(2,1)} %all-gather.2.cloned.1.call-done), kind=kOutput, calls=%fused_computation.10 | convolution fusion | flops 1074790400 | bytes 4194304 | tf_op jit(solution)/shard_map/dot_general | solution.py:108
  60.3 6.6 %all-to-all-start.1 = ((bf16[8,128,1024]{2,1,0:T(8,128)(2,1)}), bf16[8,128,1024]{2,1,0:T(8,128)(2,1)S(1)}, u32[]{:S(2)}, u32[]{:S(2)}) async-start(bf16[8,128,1024]{2,1,0:T(8,128)(2,1)} %bitcast.162), calls=%async_computation.1 | async-start | bytes 4194304 | tf_op jit(solution)/shard_map/all_to_all | solution.py:85
  69.0 1.5 subtract_convert_fusion
  70.5 22.0 %all-to-all-done.1 = bf16[8,128,1024]{2,1,0:T(8,128)(2,1)S(1)} async-done(((bf16[8,128,1024]{2,1,0:T(8,128)(2,1)}), bf16[8,128,1024]{2,1,0:T(8,128)(2,1)S(1)}, u32[]{:S(2)}, u32[]{:S(2)}) %all-to-all-start.1) | async-done | bytes 2097184 | tf_op jit(solution)/shard_map/all_to_all | solution.py:85
  96.4 1.9 constant_dynamic-update-slice_fusion.6
  98.3 2.7 collective-permute-start
  101.0 4.9 %collective-permute-start.1 = (bf16[2,128,4,128]{3,1,2,0:T(8,128)(2,1)}, bf16[2,128,4,128]{3,1,2,0:T(8,128)(2,1)}, u32[]{:S(2)}, u32[]{:S(2)}) collective-permute-start(bf16[2,128,4,128]{3,1,2,0:T(8,128)(2,1)} %get-tuple-element.21), channel_id=1, source_target_pairs={{0,8},{4,12},{8,16},{12,20},{16,24},{20,28},{24,32},{28,36},{32,40... | collective-permute-start | bytes 786440 | tf_op jit(solution)/shard_map/ppermute | solution.py:27
  105.9 2.7 collective-permute-start.2
  108.5 1.4 fusion.50
  109.9 2.0 copy.71
  112.9 1.3 copy.73
  114.2 1.9 collective-permute-start.3
  116.2 8.4 %collective-permute-start.4 = (bf16[2,128,4,128]{3,1,2,0:T(8,128)(2,1)}, bf16[2,128,4,128]{3,1,2,0:T(8,128)(2,1)S(1)}, u32[]{:S(2)}, u32[]{:S(2)}) collective-permute-start(bf16[2,128,4,128]{3,1,2,0:T(8,128)(2,1)} %get-tuple-element.21), channel_id=1, source_target_pairs={{0,20},{4,24},{8,28},{12,32},{16,36},{20,40},{24,44},{28,48},{32,5... | collective-permute-start | bytes 786440 | tf_op jit(solution)/shard_map/ppermute | solution.py:27
  124.6 3.1 collective-permute-start.5
  129.7 3.4 %collective-permute-done.2 = bf16[2,128,4,128]{3,1,2,0:T(8,128)(2,1)} collective-permute-done((bf16[2,128,4,128]{3,1,2,0:T(8,128)(2,1)}, bf16[2,128,4,128]{3,1,2,0:T(8,128)(2,1)}, u32[]{:S(2)}, u32[]{:S(2)}) %collective-permute-start.2) | collective-permute-done | bytes 262176 | tf_op jit(solution)/shard_map/ppermute | solution.py:27
  134.1 1.8 collective-permute-done.4
  135.9 11.4 %collective-permute-done.5 = bf16[2,128,4,128]{3,1,2,0:T(8,128)(2,1)S(1)} collective-permute-done((bf16[2,128,4,128]{3,1,2,0:T(8,128)(2,1)}, bf16[2,128,4,128]{3,1,2,0:T(8,128)(2,1)S(1)}, u32[]{:S(2)}, u32[]{:S(2)}) %collective-permute-start.5) | collective-permute-done | bytes 262176 | tf_op jit(solution)/shard_map/ppermute | solution.py:27
  147.4 1.9 fusion.2
  149.3 1.6 divide_convert_fusion
  161.0 11.5 %collective-permute-start.6 = (bf16[2,128,4,128]{3,1,2,0:T(8,128)(2,1)}, bf16[2,128,4,128]{3,1,2,0:T(8,128)(2,1)}, u32[]{:S(2)}, u32[]{:S(2)}) collective-permute-start(bf16[2,128,4,128]{3,1,2,0:T(8,128)(2,1)} %get-tuple-element.24), channel_id=1, source_target_pairs={{4,0},{8,4},{12,8},{16,12},{20,16},{24,20},{28,24},{32,28},{36,32}... | collective-permute-start | bytes 786440 | tf_op jit(solution)/shard_map/ppermute | solution.py:27
  175.1 9.8 %collective-permute-done.10 = bf16[2,128,4,128]{3,1,2,0:T(8,128)(2,1)S(1)} collective-permute-done((bf16[2,128,4,128]{3,1,2,0:T(8,128)(2,1)S(1)}, bf16[2,128,4,128]{3,1,2,0:T(8,128)(2,1)S(1)}, u32[]{:S(2)}, u32[]{:S(2)}) %collective-permute-start.10) | collective-permute-done | bytes 262176 | tf_op jit(solution)/shard_map/ppermute | solution.py:27
  187.9 20.6 %collective-permute-done.11 = bf16[2,128,4,128]{3,1,2,0:T(8,128)(2,1)} collective-permute-done((bf16[2,128,4,128]{3,1,2,0:T(8,128)(2,1)}, bf16[2,128,4,128]{3,1,2,0:T(8,128)(2,1)}, u32[]{:S(2)}, u32[]{:S(2)}) %collective-permute-start.11) | collective-permute-done | bytes 262176 | tf_op jit(solution)/shard_map/ppermute | solution.py:27
  208.5 12.4 %collective-permute-done.9 = bf16[2,128,4,128]{3,1,2,0:T(8,128)(2,1)} collective-permute-done((bf16[2,128,4,128]{3,1,2,0:T(8,128)(2,1)S(1)}, bf16[2,128,4,128]{3,1,2,0:T(8,128)(2,1)}, u32[]{:S(2)}, u32[]{:S(2)}) %collective-permute-start.9) | collective-permute-done | bytes 262176 | tf_op jit(solution)/shard_map/ppermute | solution.py:27
  220.9 1.7 fusion.18
  225.5 44.1 %all_to_all.48 = bf16[8,128,1024]{1,2,0:T(8,128)(2,1)S(1)} all-to-all(bf16[8,128,1024]{1,2,0:T(8,128)(2,1)S(1)} %broadcast_in_dim.16), channel_id=1, replica_groups=mesh['cb'=8,'cz'=8,'pipe'=4] {'cb'}, dimensions={0} | all-to-all | bytes 4194304 | tf_op jit(solution)/shard_map/all_to_all | solution.py:79
  269.6 3.8 %convolution_bitcast_fusion = f32[512,1024]{0,1:T(8,128)} fusion(bf16[8,128,1024]{1,2,0:T(8,128)(2,1)S(1)} %all_to_all.48, bf16[128,8,512]{2,0,1:T(8,128)(2,1)} %all-to-all-done), kind=kOutput, calls=%fused_computation.13 | convolution fusion | flops 1073741824 | bytes 5242880 | tf_op jit(solution)/shard_map/dot_general | solution.py:194
  273.4 2.9 copy.118
  278.5 2.4 mul.414
  282.2 2.4 mul.476
  284.6 2.7 copy.96
  287.3 4.1 %convolution_convert_fusion.1 = bf16[1024,512]{1,0:T(8,128)(2,1)} fusion(bf16[1024,1024]{1,0:T(8,128)(2,1)} %bitcast.163, bf16[512,1024]{1,0:T(8,128)(2,1)} %all-gather.2.cloned.1.call-done), kind=kOutput, calls=%fused_computation.15 | convolution fusion | flops 1074266112 | bytes 4194304 | tf_op jit(solution)/shard_map/dot_general | solution.py:201
  291.4 3.7 %all-to-all-start.3 = ((bf16[8,128,512]{2,1,0:T(8,128)(2,1)}), bf16[8,128,512]{2,1,0:T(8,128)(2,1)S(1)}, u32[]{:S(2)}, u32[]{:S(2)}) async-start(bf16[8,128,512]{2,1,0:T(8,128)(2,1)} %bitcast.56), calls=%async_computation.3 | async-start | bytes 2097152 | tf_op jit(solution)/shard_map/all_to_all | solution.py:204
  295.1 3.1 convolution_multiply_fusion
  298.4 1.4 copy.120
  299.8 1.4 copy.121
  301.2 2.8 multiply_add_fusion
  303.9 4.1 %all-to-all-done.3 = bf16[8,128,512]{2,1,0:T(8,128)(2,1)S(1)} async-done(((bf16[8,128,512]{2,1,0:T(8,128)(2,1)}), bf16[8,128,512]{2,1,0:T(8,128)(2,1)S(1)}, u32[]{:S(2)}, u32[]{:S(2)}) %all-to-all-start.3) | async-done | bytes 1048608 | tf_op jit(solution)/shard_map/all_to_all | solution.py:204
  309.1 4.3 %collective-permute-start.12 = (bf16[128,4096]{1,0:T(8,128)(2,1)}, bf16[128,4096]{1,0:T(8,128)(2,1)}, u32[]{:S(2)}, u32[]{:S(2)}) collective-permute-start(bf16[128,4096]{1,0:T(8,128)(2,1)} %bitcast.75), channel_id=1, source_target_pairs={{0,3},{1,0},{2,1},{3,2},{4,7},{5,4},{6,5},{7,6},{8,11},{9,8},{10,9... | collective-permute-start | bytes 3145736 | tf_op jit(solution)/shard_map/ppermute | solution.py:32
  315.4 2.5 mul.481
  319.0 2.9 fusion.9
  321.9 4.4 %collective-permute-done.12 = bf16[128,4096]{1,0:T(8,128)(2,1)} collective-permute-done((bf16[128,4096]{1,0:T(8,128)(2,1)}, bf16[128,4096]{1,0:T(8,128)(2,1)}, u32[]{:S(2)}, u32[]{:S(2)}) %collective-permute-start.12) | collective-permute-done | bytes 1048608 | tf_op jit(solution)/shard_map/ppermute | solution.py:32
  329.2 2.3 copy.146
  (154 shorter events, 40.9 us)
Async XLA Ops:
  8.8 8.0 %copy-start.23 = (bf16[1,64,512]{2,1,0:T(8,128)(2,1)S(1)}, bf16[1,64,512]{2,1,0:T(8,128)(2,1)}, u32[]{:S(2)}) copy-start(bf16[1,64,512]{2,1,0:T(8,128)(2,1)} %param.13) | copy-start | bytes 196612
  8.8 8.0 %copy-start.24 = (bf16[1,64,512]{2,1,0:T(8,128)(2,1)S(1)}, bf16[1,64,512]{2,1,0:T(8,128)(2,1)}, u32[]{:S(2)}) copy-start(bf16[1,64,512]{2,1,0:T(8,128)(2,1)} %param.12) | copy-start | bytes 196612
  8.8 8.9 %copy-start.9 = (bf16[1,128,2048]{2,1,0:T(8,128)(2,1)S(1)}, bf16[1,128,2048]{2,1,0:T(8,128)(2,1)}, u32[]{:S(2)}) copy-start(bf16[1,128,2048]{2,1,0:T(8,128)(2,1)} %param.9) | copy-start | bytes 1572868
  10.1 22.4 %all-to-all-start = ((bf16[128,8,512]{2,0,1:T(8,128)(2,1)}), bf16[128,8,512]{2,0,1:T(8,128)(2,1)}, u32[]{:S(2)}, u32[]{:S(2)}) async-start(bf16[128,8,512]{2,0,1:T(8,128)(2,1)} %copy.66), calls=%async_computation | async-start | bytes 2097152 | tf_op jit(solution)/shard_map/all_to_all | solution.py:106
  16.8 39.4 %all-gather.2.cloned.1.call-start = ((), (), s32[]{:S(2)}) async-start(), calls=%async_computation.5 | async-start | bytes 1179648 | tf_op jit(solution)/shard_map/all_gather | solution.py:105
  60.3 8.3 %copy-start.26 = (f32[1,128]{1,0:T(1,128)S(1)}, f32[1,128]{1,0:T(1,128)}, u32[]{:S(2)}) copy-start(f32[1,128]{1,0:T(1,128)} %param.14) | copy-start | bytes 1540
  60.3 32.2 %all-to-all-start.1 = ((bf16[8,128,1024]{2,1,0:T(8,128)(2,1)}), bf16[8,128,1024]{2,1,0:T(8,128)(2,1)S(1)}, u32[]{:S(2)}, u32[]{:S(2)}) async-start(bf16[8,128,1024]{2,1,0:T(8,128)(2,1)} %bitcast.162), calls=%async_computation.1 | async-start | bytes 4194304 | tf_op jit(solution)/shard_map/all_to_all | solution.py:85
  66.9 259.5 %reduce-scatter.4.cloned.1.call-start = ((), (), s32[]{:S(2)}) async-start(), calls=%async_computation.6 | async-start | bytes 2359296
  67.7 2.8 copy-start.21
  68.7 1.9 copy-start.16
  92.9 0.7 copy-start.13
  93.7 2.7 copy-start.7
  93.8 18.2 %copy-start.12 = (bf16[128,16,64]{2,1,0:T(8,128)(2,1)S(1)}, bf16[128,16,64]{2,1,0:T(8,128)(2,1)}, u32[]{:S(2)}) copy-start(bf16[128,16,64]{2,1,0:T(8,128)(2,1)} %get-tuple-element.31) | copy-start | bytes 786436
  98.3 26.3 %collective-permute-start = (bf16[2,128,4,128]{3,1,2,0:T(8,128)(2,1)}, bf16[2,128,4,128]{3,1,2,0:T(8,128)(2,1)}, u32[]{:S(2)}, u32[]{:S(2)}) collective-permute-start(bf16[2,128,4,128]{3,1,2,0:T(8,128)(2,1)} %get-tuple-element.21), channel_id=1, source_target_pairs={{0,4},{4,8},{8,12},{12,16},{16,20},{20,24},{24,28},{28,32},{32,36}... | collective-permute-start | bytes 786440 | tf_op jit(solution)/shard_map/ppermute | solution.py:27
  101.0 27.7 %collective-permute-start.1 = (bf16[2,128,4,128]{3,1,2,0:T(8,128)(2,1)}, bf16[2,128,4,128]{3,1,2,0:T(8,128)(2,1)}, u32[]{:S(2)}, u32[]{:S(2)}) collective-permute-start(bf16[2,128,4,128]{3,1,2,0:T(8,128)(2,1)} %get-tuple-element.21), channel_id=1, source_target_pairs={{0,8},{4,12},{8,16},{12,20},{16,24},{20,28},{24,32},{28,36},{32,40... | collective-permute-start | bytes 786440 | tf_op jit(solution)/shard_map/ppermute | solution.py:27
  105.9 27.2 %collective-permute-start.2 = (bf16[2,128,4,128]{3,1,2,0:T(8,128)(2,1)}, bf16[2,128,4,128]{3,1,2,0:T(8,128)(2,1)}, u32[]{:S(2)}, u32[]{:S(2)}) collective-permute-start(bf16[2,128,4,128]{3,1,2,0:T(8,128)(2,1)} %get-tuple-element.21), channel_id=1, source_target_pairs={{0,12},{4,16},{8,20},{12,24},{16,28},{20,32},{24,36},{28,40},{32,4... | collective-permute-start | bytes 786440 | tf_op jit(solution)/shard_map/ppermute | solution.py:27
  114.2 33.2 %copy-start.10 = (bf16[128,16,64]{2,0,1:T(8,128)(2,1)S(1)}, bf16[128,16,64]{2,0,1:T(8,128)(2,1)}, u32[]{:S(2)}) copy-start(bf16[128,16,64]{2,0,1:T(8,128)(2,1)} %copy.71) | copy-start | bytes 786436
  114.2 33.2 %copy-start.11 = (bf16[128,16,64]{2,0,1:T(8,128)(2,1)S(1)}, bf16[128,16,64]{2,0,1:T(8,128)(2,1)}, u32[]{:S(2)}) copy-start(bf16[128,16,64]{2,0,1:T(8,128)(2,1)} %copy.72) | copy-start | bytes 786436
  114.2 33.2 %copy-start.22 = (pred[128,896]{0,1:T(8,128)(4,1)S(1)}, pred[128,896]{0,1:T(8,128)(4,1)}, u32[]{:S(2)}) copy-start(pred[128,896]{0,1:T(8,128)(4,1)} %fusion.50) | copy-start | bytes 344068
  114.2 19.9 %collective-permute-start.3 = (bf16[2,128,4,128]{3,1,2,0:T(8,128)(2,1)}, bf16[2,128,4,128]{3,1,2,0:T(8,128)(2,1)S(1)}, u32[]{:S(2)}, u32[]{:S(2)}) collective-permute-start(bf16[2,128,4,128]{3,1,2,0:T(8,128)(2,1)} %get-tuple-element.21), channel_id=1, source_target_pairs={{0,16},{4,20},{8,24},{12,28},{16,32},{20,36},{24,40},{28,44},{32,4... | collective-permute-start | bytes 786440 | tf_op jit(solution)/shard_map/ppermute | solution.py:27
  116.2 19.7 %collective-permute-start.4 = (bf16[2,128,4,128]{3,1,2,0:T(8,128)(2,1)}, bf16[2,128,4,128]{3,1,2,0:T(8,128)(2,1)S(1)}, u32[]{:S(2)}, u32[]{:S(2)}) collective-permute-start(bf16[2,128,4,128]{3,1,2,0:T(8,128)(2,1)} %get-tuple-element.21), channel_id=1, source_target_pairs={{0,20},{4,24},{8,28},{12,32},{16,36},{20,40},{24,44},{28,48},{32,5... | collective-permute-start | bytes 786440 | tf_op jit(solution)/shard_map/ppermute | solution.py:27
  124.6 22.8 %collective-permute-start.5 = (bf16[2,128,4,128]{3,1,2,0:T(8,128)(2,1)}, bf16[2,128,4,128]{3,1,2,0:T(8,128)(2,1)S(1)}, u32[]{:S(2)}, u32[]{:S(2)}) collective-permute-start(bf16[2,128,4,128]{3,1,2,0:T(8,128)(2,1)} %get-tuple-element.21), channel_id=1, source_target_pairs={{0,24},{4,28},{8,32},{12,36},{16,40},{20,44},{24,48},{28,52},{32,5... | collective-permute-start | bytes 786440 | tf_op jit(solution)/shard_map/ppermute | solution.py:27
  147.4 3.6 %copy-start.5 = (bf16[2,896,4,128]{3,1,2,0:T(8,128)(2,1)}, bf16[2,896,4,128]{3,1,2,0:T(8,128)(2,1)S(1)}, u32[]{:S(2)}) copy-start(bf16[2,896,4,128]{3,1,2,0:T(8,128)(2,1)S(1)} %constant_dynamic-update-slice_fusion) | copy-start | bytes 5505028
  151.8 1.5 copy-start.6
  154.4 1.8 copy-start
  156.2 1.2 copy-start.1
  157.4 28.8 %copy-start.25 = (f32[1,128]{1,0:T(1,128)S(1)}, f32[1,128]{1,0:T(1,128)}, u32[]{:S(2)}) copy-start(f32[1,128]{1,0:T(1,128)} %param.15) | copy-start | bytes 1540
  158.5 26.5 %collective-permute-start.10 = (bf16[2,128,4,128]{3,1,2,0:T(8,128)(2,1)S(1)}, bf16[2,128,4,128]{3,1,2,0:T(8,128)(2,1)S(1)}, u32[]{:S(2)}, u32[]{:S(2)}) collective-permute-start(bf16[2,128,4,128]{3,1,2,0:T(8,128)(2,1)S(1)} %get-tuple-element.26), channel_id=1, source_target_pairs={{20,0},{24,4},{28,8},{32,12},{36,16},{40,20},{44,24},{48,28},{52,3... | collective-permute-start | bytes 786440 | tf_op jit(solution)/shard_map/ppermute | solution.py:27
  159.7 48.8 %collective-permute-start.11 = (bf16[2,128,4,128]{3,1,2,0:T(8,128)(2,1)}, bf16[2,128,4,128]{3,1,2,0:T(8,128)(2,1)}, u32[]{:S(2)}, u32[]{:S(2)}) collective-permute-start(bf16[2,128,4,128]{3,1,2,0:T(8,128)(2,1)} %get-tuple-element.25), channel_id=1, source_target_pairs={{24,0},{28,4},{32,8},{36,12},{40,16},{44,20},{48,24},{52,28},{56,3... | collective-permute-start | bytes 786440 | tf_op jit(solution)/shard_map/ppermute | solution.py:27
  161.0 47.5 %collective-permute-start.6 = (bf16[2,128,4,128]{3,1,2,0:T(8,128)(2,1)}, bf16[2,128,4,128]{3,1,2,0:T(8,128)(2,1)}, u32[]{:S(2)}, u32[]{:S(2)}) collective-permute-start(bf16[2,128,4,128]{3,1,2,0:T(8,128)(2,1)} %get-tuple-element.24), channel_id=1, source_target_pairs={{4,0},{8,4},{12,8},{16,12},{20,16},{24,20},{28,24},{32,28},{36,32}... | collective-permute-start | bytes 786440 | tf_op jit(solution)/shard_map/ppermute | solution.py:27
  172.5 36.0 %collective-permute-start.7 = (bf16[2,128,4,128]{3,1,2,0:T(8,128)(2,1)}, bf16[2,128,4,128]{3,1,2,0:T(8,128)(2,1)}, u32[]{:S(2)}, u32[]{:S(2)}) collective-permute-start(bf16[2,128,4,128]{3,1,2,0:T(8,128)(2,1)} %get-tuple-element.29), channel_id=1, source_target_pairs={{8,0},{12,4},{16,8},{20,12},{24,16},{28,20},{32,24},{36,28},{40,32... | collective-permute-start | bytes 786440 | tf_op jit(solution)/shard_map/ppermute | solution.py:27
  173.8 34.7 %collective-permute-start.8 = (bf16[2,128,4,128]{3,1,2,0:T(8,128)(2,1)}, bf16[2,128,4,128]{3,1,2,0:T(8,128)(2,1)}, u32[]{:S(2)}, u32[]{:S(2)}) collective-permute-start(bf16[2,128,4,128]{3,1,2,0:T(8,128)(2,1)} %get-tuple-element.28), channel_id=1, source_target_pairs={{12,0},{16,4},{20,8},{24,12},{28,16},{32,20},{36,24},{40,28},{44,3... | collective-permute-start | bytes 786440 | tf_op jit(solution)/shard_map/ppermute | solution.py:27
  185.0 1.3 copy-start.18
  185.0 35.9 %collective-permute-start.9 = (bf16[2,128,4,128]{3,1,2,0:T(8,128)(2,1)S(1)}, bf16[2,128,4,128]{3,1,2,0:T(8,128)(2,1)}, u32[]{:S(2)}, u32[]{:S(2)}) collective-permute-start(bf16[2,128,4,128]{3,1,2,0:T(8,128)(2,1)S(1)} %get-tuple-element.27), channel_id=1, source_target_pairs={{16,0},{20,4},{24,8},{28,12},{32,16},{36,20},{40,24},{44,28},{48,3... | collective-permute-start | bytes 786440 | tf_op jit(solution)/shard_map/ppermute | solution.py:27
  222.6 1.0 copy-start.8
  222.6 2.0 copy-start.20
  222.7 2.2 copy-start.14
  222.7 2.2 copy-start.15
  276.4 0.8 copy-start.17
  277.2 3.7 %copy-start.19 = (f32[128,16]{1,0:T(8,128)S(1)}, f32[128,16]{1,0:T(8,128)}, u32[]{:S(2)}) copy-start(f32[128,16]{1,0:T(8,128)} %get-tuple-element.42) | copy-start | bytes 24580
  280.9 3.7 %copy-start.27 = (f32[1,128]{1,0:T(1,128)S(1)}, f32[1,128]{1,0:T(1,128)}, u32[]{:S(2)}) copy-start(f32[1,128]{1,0:T(1,128)} %param.14) | copy-start | bytes 1540
  291.4 16.6 %all-to-all-start.3 = ((bf16[8,128,512]{2,1,0:T(8,128)(2,1)}), bf16[8,128,512]{2,1,0:T(8,128)(2,1)S(1)}, u32[]{:S(2)}, u32[]{:S(2)}) async-start(bf16[8,128,512]{2,1,0:T(8,128)(2,1)} %bitcast.56), calls=%async_computation.3 | async-start | bytes 2097152 | tf_op jit(solution)/shard_map/all_to_all | solution.py:204
  308.0 5.4 %copy-start.4 = (f32[128,16,64]{2,1,0:T(8,128)S(1)}, f32[128,16,64]{2,1,0:T(8,128)}, u32[]{:S(2)}) copy-start(f32[128,16,64]{2,1,0:T(8,128)} %get-tuple-element.23) | copy-start | bytes 1572868
  309.1 17.3 %collective-permute-start.12 = (bf16[128,4096]{1,0:T(8,128)(2,1)}, bf16[128,4096]{1,0:T(8,128)(2,1)}, u32[]{:S(2)}, u32[]{:S(2)}) collective-permute-start(bf16[128,4096]{1,0:T(8,128)(2,1)} %bitcast.75), channel_id=1, source_target_pairs={{0,3},{1,0},{2,1},{3,2},{4,7},{5,4},{6,5},{7,6},{8,11},{9,8},{10,9... | collective-permute-start | bytes 3145736 | tf_op jit(solution)/shard_map/ppermute | solution.py:32
  315.4 3.6 %copy-start.2 = (f32[1,128,2048]{2,1,0:T(8,128)S(1)}, f32[1,128,2048]{2,1,0:T(8,128)}, u32[]{:S(2)}) copy-start(f32[1,128,2048]{2,1,0:T(8,128)} %mul.414) | copy-start | bytes 3145732
  315.4 3.6 %copy-start.3 = (f32[1,128,2048]{2,1,0:T(8,128)S(1)}, f32[1,128,2048]{2,1,0:T(8,128)}, u32[]{:S(2)}) copy-start(f32[1,128,2048]{2,1,0:T(8,128)} %mul.476) | copy-start | bytes 3145732
Sparse Core Ops, SparseCore 0:
  20.0 36.1 all-gather.1
  276.5 36.3 reduce-scatter.3

commit v5 on v4

--- a/solution.py
+++ b/solution.py
@@ -84,6 +84,38 @@
     pieces = partial.astype(sent_as).reshape((parts, partial.shape[0] // parts) + partial.shape[1:])
     received = lax.all_to_all(pieces, axis, 0, 0, tiled=True)
     return jnp.sum(received.astype(jnp.float32), 0)
+
+
+def relayed_blocks(own_pair, reach_blocks):
+    blocks = [own_pair]
+    step = 1
+    while len(blocks) <= reach_blocks:
+        sent = jnp.stack(blocks[: min(step, reach_blocks + 1 - step)])
+        arrived = passed_along(sent, CTX, step)
+        blocks = blocks + [arrived[k] for k in range(arrived.shape[0])]
+        step *= 2
+    return blocks[: reach_blocks + 1]
+
+
+def relayed_sums(kv_parts, tok_rows, reach_blocks):
+    sums = [kv_parts[:, :tok_rows]] + [
+        kv_parts[:, d * tok_rows : (d + 1) * tok_rows].astype(jnp.bfloat16).astype(jnp.float32)
+        for d in range(1, reach_blocks + 1)
+    ]
+    first = True
+    step = 1
+    while step * 2 <= reach_blocks:
+        step *= 2
+    while step >= 1:
+        count = len(sums) - step
+        sent = jnp.stack(sums[step:])
+        if first:
+            sent = sent.astype(jnp.bfloat16)
+        arrived = passed_along(sent, CTX, -step).astype(jnp.float32)
+        sums = [sums[k] + arrived[k] if k < count else sums[k] for k in range(step)]
+        first = False
+        step //= 2
+    return sums[0]
 
 
 def guarded(tile_work, operands):
@@ -122,9 +154,7 @@
     key_norm, key_inv = normalize(key_in, k_gain[0])
     key_rot = rotate(key_norm, cosine, sine_table).astype(jnp.bfloat16)
     own_pair = jnp.stack([key_rot, value_own])
-    key_blocks = [own_pair]
-    for distance in range(1, reach_blocks + 1):
-        key_blocks.append(passed_along(own_pair, CTX, distance))
+    key_blocks = relayed_blocks(own_pair, reach_blocks)
     seg_all = segments[0]
     seg_query = lax.dynamic_slice_in_dim(seg_all, ctx_index * tok_rows, tok_rows)
     allowed_list = []
@@ -173,11 +203,7 @@
         * score_scale
     )
     kv_parts = jnp.stack([key_grad, value_grad])
-    kv_total = kv_parts[:, :tok_rows]
-    for distance in range(1, reach_blocks + 1):
-        kv_part = kv_parts[:, distance * tok_rows : (distance + 1) * tok_rows]
-        returned = passed_along(kv_part.astype(jnp.bfloat16), CTX, -distance)
-        kv_total = kv_total + returned.astype(jnp.float32)
+    kv_total = relayed_sums(kv_parts, tok_rows, reach_blocks)
     query_grad = normalize_back(
         query_in,
         query_inv,

time: 340 us -> 385 us (1.13); the launches traced: 338 us -> 379 us
  waiting for transfers between devices: 126 us -> 162 us
    ppermute x12 -> x6, waiting for transfers between devices: 59.4 us -> 106 us  [passed_along(): return lax.ppermute(block, axis, route)]
    all_gather x1, waiting for transfers between devices: 23.7 us -> 12.4 us  [local(): weight_slice = lax.all_gather(both_rows, 'cz', axis=0, tiled=True)]
    unnamed x72 -> x82, local copies, waits for them, and re-layouts: 19.9 us -> 21.5 us
    ppermute x12 -> x6, starting transfers between devices: 41.6 us -> 42.2 us  [passed_along(): return lax.ppermute(block, axis, route)]
  transfers between devices with their start and end apart: 18 -> 12, of which waited for: 11 -> 11; matrix products, arithmetic and copies ran while one was open for 15% -> 14% of each run, Pallas kernels for 0% -> 0%
where the time goes in v5:
time: 385 us; the launch traced here: 379 us
  waiting for transfers between devices  162 us (42%)
  starting transfers between devices  62 us (16%)
  local copies, waits for them, and re-layouts  48.6 us (13%)
  blocking collectives  46.5 us (12%)
  other arithmetic  23.2 us (6%)
  matrix products  21.4 us (6%)
  between operations  14.9 us (4%)
    ppermute x6, waiting for transfers between devices, passed_along(): return lax.ppermute(block, axis, route)  106 us
    all_to_all x1, blocking collectives, gathered(): received = lax.all_to_all(copies, axis, 0, 0, tiled=True)  46.5 us
    ppermute x6, starting transfers between devices, passed_along(): return lax.ppermute(block, axis, route)  42.2 us
    all_to_all x1, waiting for transfers between devices, summed_over(): received = lax.all_to_all(pieces, axis, 0, 0, tiled=True)  23.3 us
    unnamed x82, local copies, waits for them, and re-layouts  21.5 us
    all_gather x1, waiting for transfers between devices, local(): weight_slice = lax.all_gather(both_rows, 'cz', axis=0, tiled=True)  12.4 us
    all_to_all x1, waiting for transfers between devices, local(): inputs_slice = lax.all_to_all(tokens_here, 'cb', 1, 0, tiled=True)  12.1 us
    mul x6, local copies, waits for them, and re-layouts, normalize_back(): values * cubed * jnp.mean(values * scaled, -1, keepdims=True)  7.88 us
  transfers between devices with their start and end apart: 12, of which 11 were waited for; matrix products, arithmetic and copies ran while one was open for 14% of the time, Pallas kernels for 0%

profile of v5, /device:TPU:33, one launch (start us, length us, event | category | flops | bytes accessed | tf_op | source)
XLA Modules:
  0.0 379.1 jit_solution(13788744153831585452)
XLA Ops:
  7.2 1.5 pad_maximum_fusion.10
  8.8 1.6 copy.65
  10.4 1.3 copy.66
  11.7 6.7 %all-to-all-start = ((bf16[128,8,512]{2,0,1:T(8,128)(2,1)}), bf16[128,8,512]{2,0,1:T(8,128)(2,1)}, u32[]{:S(2)}, u32[]{:S(2)}) async-start(bf16[128,8,512]{2,0,1:T(8,128)(2,1)} %copy.66), calls=%async_computation | async-start | bytes 2097152 | tf_op jit(solution)/shard_map/all_to_all | solution.py:138
  20.5 1.5 fusion.67
  22.0 12.1 %all-to-all-done = bf16[128,8,512]{2,0,1:T(8,128)(2,1)} async-done(((bf16[128,8,512]{2,0,1:T(8,128)(2,1)}), bf16[128,8,512]{2,0,1:T(8,128)(2,1)}, u32[]{:S(2)}, u32[]{:S(2)}) %all-to-all-start) | async-done | bytes 1048608 | tf_op jit(solution)/shard_map/all_to_all | solution.py:138
  34.1 12.4 %all-gather.2.cloned.1.call-done = bf16[512,1024]{1,0:T(8,128)(2,1)} async-done(((bf16[64,1024]{1,0:T(8,128)(2,1)}), bf16[512,1024]{1,0:T(8,128)(2,1)}) %all-gather.2.cloned.1.call-update) | async-done | bytes 1048592 | tf_op jit(solution)/shard_map/all_gather | solution.py:137
  46.5 4.1 %convolution_convert_fusion = bf16[1024,1024]{0,1:T(8,128)(2,1)} fusion(bf16[1024,512]{1,0:T(8,128)(2,1)} %bitcast.4, bf16[512,1024]{1,0:T(8,128)(2,1)} %all-gather.2.cloned.1.call-done), kind=kOutput, calls=%fused_computation.10 | convolution fusion | flops 1074790400 | bytes 4194304 | tf_op jit(solution)/shard_map/dot_general | solution.py:140
  50.6 6.1 %all-to-all-start.1 = ((bf16[8,128,1024]{2,1,0:T(8,128)(2,1)}), bf16[8,128,1024]{2,1,0:T(8,128)(2,1)S(1)}, u32[]{:S(2)}, u32[]{:S(2)}) async-start(bf16[8,128,1024]{2,1,0:T(8,128)(2,1)} %bitcast.227), calls=%async_computation.1 | async-start | bytes 4194304 | tf_op jit(solution)/shard_map/all_to_all | solution.py:85
  59.1 23.3 %all-to-all-done.1 = bf16[8,128,1024]{2,1,0:T(8,128)(2,1)S(1)} async-done(((bf16[8,128,1024]{2,1,0:T(8,128)(2,1)}), bf16[8,128,1024]{2,1,0:T(8,128)(2,1)S(1)}, u32[]{:S(2)}, u32[]{:S(2)}) %all-to-all-start.1) | async-done | bytes 2097184 | tf_op jit(solution)/shard_map/all_to_all | solution.py:85
  86.1 3.4 collective-permute-start
  89.9 3.4 collective-permute-done
  93.3 4.3 %collective-permute-start.1 = (bf16[2,2,128,4,128]{4,2,3,1,0:T(8,128)(2,1)S(1)}, bf16[2,2,128,4,128]{4,2,3,1,0:T(8,128)(2,1)S(1)}, u32[]{:S(2)}, u32[]{:S(2)}) collective-permute-start(bf16[2,2,128,4,128]{4,2,3,1,0:T(8,128)(2,1)S(1)} %pad_maximum_fusion.5), channel_id=1, source_target_pairs={{0,8},{4,12},{8,16},{12,20},{16,24},{20,28},{24,32},{28,36},{32,40... | collective-permute-start | bytes 1572872 | tf_op jit(solution)/shard_map/ppermute | solution.py:27
  99.0 16.4 %collective-permute-done.1 = bf16[2,2,128,4,128]{4,2,3,1,0:T(8,128)(2,1)S(1)} collective-permute-done((bf16[2,2,128,4,128]{4,2,3,1,0:T(8,128)(2,1)S(1)}, bf16[2,2,128,4,128]{4,2,3,1,0:T(8,128)(2,1)S(1)}, u32[]{:S(2)}, u32[]{:S(2)}) %collective-permute-start.1) | collective-permute-done | bytes 524320 | tf_op jit(solution)/shard_map/ppermute | solution.py:27
  116.4 5.1 %collective-permute-start.2 = (bf16[3,2,128,4,128]{4,2,3,1,0:T(8,128)(2,1)}, bf16[3,2,128,4,128]{4,2,3,1,0:T(8,128)(2,1)}, u32[]{:S(2)}, u32[]{:S(2)}) collective-permute-start(bf16[3,2,128,4,128]{4,2,3,1,0:T(8,128)(2,1)} %pad_maximum_fusion.3), channel_id=1, source_target_pairs={{0,16},{4,20},{8,24},{12,28},{16,32},{20,36},{24,40},{28,44},{32,4... | collective-permute-start | bytes 2359304 | tf_op jit(solution)/shard_map/ppermute | solution.py:27
  124.1 1.3 copy.73
  128.5 24.3 %collective-permute-done.2 = bf16[3,2,128,4,128]{4,2,3,1,0:T(8,128)(2,1)} collective-permute-done((bf16[3,2,128,4,128]{4,2,3,1,0:T(8,128)(2,1)}, bf16[3,2,128,4,128]{4,2,3,1,0:T(8,128)(2,1)}, u32[]{:S(2)}, u32[]{:S(2)}) %collective-permute-start.2) | collective-permute-done | bytes 786464 | tf_op jit(solution)/shard_map/ppermute | solution.py:27
  155.9 1.9 fusion.2
  157.8 1.6 divide_convert_fusion
  162.9 1.2 fusion.4
  166.1 1.3 collective-permute-start.3
  167.4 22.2 %collective-permute-done.3 = bf16[3,2,128,4,128]{4,2,3,1,0:T(8,128)(2,1)S(1)} collective-permute-done((bf16[3,2,128,4,128]{4,2,3,1,0:T(8,128)(2,1)S(1)}, bf16[3,2,128,4,128]{4,2,3,1,0:T(8,128)(2,1)S(1)}, u32[]{:S(2)}, u32[]{:S(2)}) %collective-permute-start.3) | collective-permute-done | bytes 786464 | tf_op jit(solution)/shard_map/ppermute | solution.py:27
  190.0 1.3 collective-permute-start.4
  191.3 22.7 %collective-permute-done.4 = f32[2,2,128,4,128]{4,2,3,1,0:T(8,128)S(1)} collective-permute-done((f32[2,2,128,4,128]{4,2,3,1,0:T(8,128)S(1)}, f32[2,2,128,4,128]{4,2,3,1,0:T(8,128)S(1)}, u32[]{:S(2)}, u32[]{:S(2)}) %collective-permute-start.4) | collective-permute-done | bytes 1048608 | tf_op jit(solution)/shard_map/ppermute | solution.py:27
  215.0 26.8 %collective-permute-start.5 = (f32[1,2,128,4,128]{4,2,3,1,0:T(8,128)}, f32[1,2,128,4,128]{4,2,3,1,0:T(8,128)}, u32[]{:S(2)}, u32[]{:S(2)}) collective-permute-start(f32[1,2,128,4,128]{4,2,3,1,0:T(8,128)} %fusion.17), channel_id=1, source_target_pairs={{4,0},{8,4},{12,8},{16,12},{20,16},{24,20},{28,24},{32,28},{36,32}... | collective-permute-start | bytes 1572872 | tf_op jit(solution)/shard_map/ppermute | solution.py:27
  243.4 16.7 %collective-permute-done.5 = f32[1,2,128,4,128]{4,2,3,1,0:T(8,128)} collective-permute-done((f32[1,2,128,4,128]{4,2,3,1,0:T(8,128)}, f32[1,2,128,4,128]{4,2,3,1,0:T(8,128)}, u32[]{:S(2)}, u32[]{:S(2)}) %collective-permute-start.5) | collective-permute-done | bytes 524320 | tf_op jit(solution)/shard_map/ppermute | solution.py:27
  260.1 1.5 fusion.15
  264.3 46.5 %all_to_all.48 = bf16[8,128,1024]{1,2,0:T(8,128)(2,1)S(1)} all-to-all(bf16[8,128,1024]{1,2,0:T(8,128)(2,1)S(1)} %broadcast_in_dim.16), channel_id=1, replica_groups=mesh['cb'=8,'cz'=8,'pipe'=4] {'cb'}, dimensions={0} | all-to-all | bytes 4194304 | tf_op jit(solution)/shard_map/all_to_all | solution.py:79
  310.8 3.8 %convolution_bitcast_fusion = f32[512,1024]{0,1:T(8,128)} fusion(bf16[8,128,1024]{1,2,0:T(8,128)(2,1)S(1)} %all_to_all.48, bf16[128,8,512]{2,0,1:T(8,128)(2,1)} %all-to-all-done), kind=kOutput, calls=%fused_computation.13 | convolution fusion | flops 1073741824 | bytes 5242880 | tf_op jit(solution)/shard_map/dot_general | solution.py:220
  314.7 2.9 copy.118
  318.4 1.3 mul.475
  319.7 2.4 mul.476
  322.1 1.3 mul.413
  323.4 2.4 mul.414
  325.8 2.7 copy.96
  328.5 4.1 %convolution_convert_fusion.1 = bf16[1024,512]{1,0:T(8,128)(2,1)} fusion(bf16[1024,1024]{1,0:T(8,128)(2,1)} %bitcast.228, bf16[512,1024]{1,0:T(8,128)(2,1)} %all-gather.2.cloned.1.call-done), kind=kOutput, calls=%fused_computation.15 | convolution fusion | flops 1074266112 | bytes 4194304 | tf_op jit(solution)/shard_map/dot_general | solution.py:227
  332.6 3.6 all-to-all-start.3
  336.2 3.1 convolution_multiply_fusion
  339.4 1.4 copy.121
  340.8 1.4 copy.120
  342.2 2.7 multiply_add_fusion
  345.0 4.7 %all-to-all-done.3 = bf16[8,128,512]{2,1,0:T(8,128)(2,1)S(1)} async-done(((bf16[8,128,512]{2,1,0:T(8,128)(2,1)}), bf16[8,128,512]{2,1,0:T(8,128)(2,1)S(1)}, u32[]{:S(2)}, u32[]{:S(2)}) %all-to-all-start.3) | async-done | bytes 1048608 | tf_op jit(solution)/shard_map/all_to_all | solution.py:230
  350.8 3.5 collective-permute-start.6
  355.0 1.3 mul.480
  356.3 2.5 mul.481
  360.0 2.9 fusion.9
  362.9 4.2 %collective-permute-done.6 = bf16[128,4096]{1,0:T(8,128)(2,1)} collective-permute-done((bf16[128,4096]{1,0:T(8,128)(2,1)}, bf16[128,4096]{1,0:T(8,128)(2,1)}, u32[]{:S(2)}, u32[]{:S(2)}) %collective-permute-start.6) | collective-permute-done | bytes 1048608 | tf_op jit(solution)/shard_map/ppermute | solution.py:32
  369.9 2.3 copy.146
  (160 shorter events, 37.1 us)
Async XLA Ops:
  7.2 39.3 %all-gather.2.cloned.1.call-start = ((), (), s32[]{:S(2)}) async-start(), calls=%async_computation.5 | async-start | bytes 1179648 | tf_op jit(solution)/shard_map/all_gather | solution.py:137
  10.4 8.0 %copy-start.11 = (bf16[1,128,2048]{2,1,0:T(8,128)(2,1)S(1)}, bf16[1,128,2048]{2,1,0:T(8,128)(2,1)}, u32[]{:S(2)}) copy-start(bf16[1,128,2048]{2,1,0:T(8,128)(2,1)} %param.9) | copy-start | bytes 1572868
  11.7 22.4 %all-to-all-start = ((bf16[128,8,512]{2,0,1:T(8,128)(2,1)}), bf16[128,8,512]{2,0,1:T(8,128)(2,1)}, u32[]{:S(2)}, u32[]{:S(2)}) async-start(bf16[128,8,512]{2,0,1:T(8,128)(2,1)} %copy.66), calls=%async_computation | async-start | bytes 2097152 | tf_op jit(solution)/shard_map/all_to_all | solution.py:138
  50.6 31.8 %all-to-all-start.1 = ((bf16[8,128,1024]{2,1,0:T(8,128)(2,1)}), bf16[8,128,1024]{2,1,0:T(8,128)(2,1)S(1)}, u32[]{:S(2)}, u32[]{:S(2)}) async-start(bf16[8,128,1024]{2,1,0:T(8,128)(2,1)} %bitcast.227), calls=%async_computation.1 | async-start | bytes 4194304 | tf_op jit(solution)/shard_map/all_to_all | solution.py:85
  56.7 310.4 %reduce-scatter.4.cloned.1.call-start = ((), (), s32[]{:S(2)}) async-start(), calls=%async_computation.6 | async-start | bytes 2359296
  57.8 0.7 copy-start.23
  82.8 3.4 copy-start.14
  82.8 6.7 %copy-start.19 = (f32[128,16]{1,0:T(8,128)S(1)}, f32[128,16]{1,0:T(8,128)}, u32[]{:S(2)}) copy-start(f32[128,16]{1,0:T(8,128)} %get-tuple-element.41) | copy-start | bytes 24580
  82.8 6.7 %copy-start.26 = (f32[1,128]{1,0:T(1,128)S(1)}, f32[1,128]{1,0:T(1,128)}, u32[]{:S(2)}) copy-start(f32[1,128]{1,0:T(1,128)} %param.14) | copy-start | bytes 1540
  84.0 1.0 copy-start.8
  85.0 12.6 %copy-start.29 = (s32[128]{0:T(128)S(1)}, s32[128]{0:T(128)}, u32[]{:S(2)}) copy-start(s32[128]{0:T(128)} %get-tuple-element.49) | copy-start | bytes 1540
  85.1 12.6 %copy-start.31 = (pred[128]{0:T(512)(128)(4,1)S(1)}, pred[128]{0:T(512)(128)(4,1)}, u32[]{:S(2)}) copy-start(pred[128]{0:T(512)(128)(4,1)} %get-tuple-element.56) | copy-start | bytes 388
  85.1 12.6 %copy-start.32 = (s32[128]{0:T(128)S(1)}, s32[128]{0:T(128)}, u32[]{:S(2)}) copy-start(s32[128]{0:T(128)} %iota_add_fusion.1) | copy-start | bytes 1540
  86.1 7.1 %collective-permute-start = (bf16[1,2,128,4,128]{4,2,3,1,0:T(8,128)(2,1)S(1)}, bf16[1,2,128,4,128]{4,2,3,1,0:T(8,128)(2,1)S(1)}, u32[]{:S(2)}, u32[]{:S(2)}) collective-permute-start(bf16[1,2,128,4,128]{4,2,3,1,0:T(8,128)(2,1)S(1)} %get-tuple-element.32), channel_id=1, source_target_pairs={{0,4},{4,8},{8,12},{12,16},{16,20},{20,24},{24,28},{28,32},{32,36}... | collective-permute-start | bytes 786440 | tf_op jit(solution)/shard_map/ppermute | solution.py:27
  93.3 22.1 %copy-start.10 = (bf16[1,2,128,4,128]{4,2,3,1,0:T(8,128)(2,1)}, bf16[1,2,128,4,128]{4,2,3,1,0:T(8,128)(2,1)S(1)}, u32[]{:S(2)}) copy-start(bf16[1,2,128,4,128]{4,2,3,1,0:T(8,128)(2,1)S(1)} %collective-permute-done) | copy-start | bytes 786436
  93.3 22.0 %collective-permute-start.1 = (bf16[2,2,128,4,128]{4,2,3,1,0:T(8,128)(2,1)S(1)}, bf16[2,2,128,4,128]{4,2,3,1,0:T(8,128)(2,1)S(1)}, u32[]{:S(2)}, u32[]{:S(2)}) collective-permute-start(bf16[2,2,128,4,128]{4,2,3,1,0:T(8,128)(2,1)S(1)} %pad_maximum_fusion.5), channel_id=1, source_target_pairs={{0,8},{4,12},{8,16},{12,20},{16,24},{20,28},{24,32},{28,36},{32,40... | collective-permute-start | bytes 1572872 | tf_op jit(solution)/shard_map/ppermute | solution.py:27
  98.4 23.1 %copy-start.28 = (s32[128]{0:T(128)S(1)}, s32[128]{0:T(128)}, u32[]{:S(2)}) copy-start(s32[128]{0:T(128)} %get-tuple-element.42) | copy-start | bytes 1540
  98.4 23.1 %copy-start.30 = (s32[128]{0:T(128)S(1)}, s32[128]{0:T(128)}, u32[]{:S(2)}) copy-start(s32[128]{0:T(128)} %get-tuple-element.62) | copy-start | bytes 1540
  115.3 7.9 %copy-start.16 = (bf16[2,2,128,4,128]{4,2,3,1,0:T(8,128)(2,1)}, bf16[2,2,128,4,128]{4,2,3,1,0:T(8,128)(2,1)S(1)}, u32[]{:S(2)}) copy-start(bf16[2,2,128,4,128]{4,2,3,1,0:T(8,128)(2,1)S(1)} %collective-permute-done.1) | copy-start | bytes 1572868
  116.4 36.5 %collective-permute-start.2 = (bf16[3,2,128,4,128]{4,2,3,1,0:T(8,128)(2,1)}, bf16[3,2,128,4,128]{4,2,3,1,0:T(8,128)(2,1)}, u32[]{:S(2)}, u32[]{:S(2)}) collective-permute-start(bf16[3,2,128,4,128]{4,2,3,1,0:T(8,128)(2,1)} %pad_maximum_fusion.3), channel_id=1, source_target_pairs={{0,16},{4,20},{8,24},{12,28},{16,32},{20,36},{24,40},{28,44},{32,4... | collective-permute-start | bytes 2359304 | tf_op jit(solution)/shard_map/ppermute | solution.py:27
  125.4 30.4 %copy-start.12 = (bf16[128,16,64]{2,0,1:T(8,128)(2,1)S(1)}, bf16[128,16,64]{2,0,1:T(8,128)(2,1)}, u32[]{:S(2)}) copy-start(bf16[128,16,64]{2,0,1:T(8,128)(2,1)} %copy.72) | copy-start | bytes 786436
  125.5 30.4 %copy-start.13 = (bf16[128,16,64]{2,0,1:T(8,128)(2,1)S(1)}, bf16[128,16,64]{2,0,1:T(8,128)(2,1)}, u32[]{:S(2)}) copy-start(bf16[128,16,64]{2,0,1:T(8,128)(2,1)} %copy.71) | copy-start | bytes 786436
  125.5 30.4 %copy-start.24 = (pred[128,896]{0,1:T(8,128)(4,1)S(1)}, pred[128,896]{0,1:T(8,128)(4,1)}, u32[]{:S(2)}) copy-start(pred[128,896]{0,1:T(8,128)(4,1)} %fusion.57) | copy-start | bytes 344068
  155.8 3.6 copy-start.6
  160.2 1.5 copy-start.7
  162.9 1.8 copy-start
  164.7 1.2 copy-start.1
  166.1 23.5 %collective-permute-start.3 = (bf16[3,2,128,4,128]{4,2,3,1,0:T(8,128)(2,1)S(1)}, bf16[3,2,128,4,128]{4,2,3,1,0:T(8,128)(2,1)S(1)}, u32[]{:S(2)}, u32[]{:S(2)}) collective-permute-start(bf16[3,2,128,4,128]{4,2,3,1,0:T(8,128)(2,1)S(1)} %pad_maximum_fusion.4), channel_id=1, source_target_pairs={{16,0},{20,4},{24,8},{28,12},{32,16},{36,20},{40,24},{44,28},{48,3... | collective-permute-start | bytes 2359304 | tf_op jit(solution)/shard_map/ppermute | solution.py:27
  189.8 25.2 %copy-start.2 = (f32[3,2,128,4,128]{4,2,3,1,0:T(8,128)}, f32[3,2,128,4,128]{4,2,3,1,0:T(8,128)S(1)}, u32[]{:S(2)}) copy-start(f32[3,2,128,4,128]{4,2,3,1,0:T(8,128)S(1)} %convert_element_type.109) | copy-start | bytes 4718596
  189.9 51.9 %copy-start.25 = (f32[1,128]{1,0:T(1,128)S(1)}, f32[1,128]{1,0:T(1,128)}, u32[]{:S(2)}) copy-start(f32[1,128]{1,0:T(1,128)} %param.15) | copy-start | bytes 1540
  190.0 24.0 %collective-permute-start.4 = (f32[2,2,128,4,128]{4,2,3,1,0:T(8,128)S(1)}, f32[2,2,128,4,128]{4,2,3,1,0:T(8,128)S(1)}, u32[]{:S(2)}, u32[]{:S(2)}) collective-permute-start(f32[2,2,128,4,128]{4,2,3,1,0:T(8,128)S(1)} %pad_maximum_fusion.2), channel_id=1, source_target_pairs={{8,0},{12,4},{16,8},{20,12},{24,16},{28,20},{32,24},{36,28},{40,32... | collective-permute-start | bytes 3145736 | tf_op jit(solution)/shard_map/ppermute | solution.py:27
  213.9 27.8 %copy-start.18 = (f32[2,2,128,4,128]{4,2,3,1,0:T(8,128)}, f32[2,2,128,4,128]{4,2,3,1,0:T(8,128)S(1)}, u32[]{:S(2)}) copy-start(f32[2,2,128,4,128]{4,2,3,1,0:T(8,128)S(1)} %collective-permute-done.4) | copy-start | bytes 3145732
  215.0 45.1 %collective-permute-start.5 = (f32[1,2,128,4,128]{4,2,3,1,0:T(8,128)}, f32[1,2,128,4,128]{4,2,3,1,0:T(8,128)}, u32[]{:S(2)}, u32[]{:S(2)}) collective-permute-start(f32[1,2,128,4,128]{4,2,3,1,0:T(8,128)} %fusion.17), channel_id=1, source_target_pairs={{4,0},{8,4},{12,8},{16,12},{20,16},{24,20},{28,24},{32,28},{36,32}... | collective-permute-start | bytes 1572872 | tf_op jit(solution)/shard_map/ppermute | solution.py:27
  261.6 1.0 copy-start.9
  261.7 1.7 copy-start.22
  261.9 1.8 copy-start.15
  261.9 1.8 copy-start.17
  317.6 0.8 copy-start.21
  317.6 4.5 %copy-start.20 = (f32[128,16]{1,0:T(8,128)S(1)}, f32[128,16]{1,0:T(8,128)}, u32[]{:S(2)}) copy-start(f32[128,16]{1,0:T(8,128)} %get-tuple-element.41) | copy-start | bytes 24580
  322.1 3.7 copy-start.27
  332.6 17.1 %all-to-all-start.3 = ((bf16[8,128,512]{2,1,0:T(8,128)(2,1)}), bf16[8,128,512]{2,1,0:T(8,128)(2,1)S(1)}, u32[]{:S(2)}, u32[]{:S(2)}) async-start(bf16[8,128,512]{2,1,0:T(8,128)(2,1)} %bitcast.75), calls=%async_computation.3 | async-start | bytes 2097152 | tf_op jit(solution)/shard_map/all_to_all | solution.py:230
  349.7 4.7 %copy-start.5 = (f32[128,16,64]{2,1,0:T(8,128)S(1)}, f32[128,16,64]{2,1,0:T(8,128)}, u32[]{:S(2)}) copy-start(f32[128,16,64]{2,1,0:T(8,128)} %get-tuple-element.21) | copy-start | bytes 1572868
  350.8 16.3 %collective-permute-start.6 = (bf16[128,4096]{1,0:T(8,128)(2,1)}, bf16[128,4096]{1,0:T(8,128)(2,1)}, u32[]{:S(2)}, u32[]{:S(2)}) collective-permute-start(bf16[128,4096]{1,0:T(8,128)(2,1)} %bitcast.95), channel_id=1, source_target_pairs={{0,3},{1,0},{2,1},{3,2},{4,7},{5,4},{6,5},{7,6},{8,11},{9,8},{10,9... | collective-permute-start | bytes 3145736 | tf_op jit(solution)/shard_map/ppermute | solution.py:32
  356.3 3.7 copy-start.3
  356.3 3.7 copy-start.4
Sparse Core Ops, SparseCore 0:
  10.3 36.1 all-gather.1
  317.7 39.5 reduce-scatter.3

commit v6 on v3

--- a/solution.py
+++ b/solution.py
@@ -187,32 +187,19 @@
             jnp.einsum("grqk,qgrd->kgd", score_grad, q_group, preferred_element_type=jnp.float32)
             * score_scale
         )
-        query_part = (
-            jnp.einsum(
-                "grqk,kgd->qgrd", score_grad, key_pair[0], preferred_element_type=jnp.float32
-            )
-            * score_scale
-        )
-        return (query_part, jnp.stack([key_grad, value_grad]))
+        return (score_grad, jnp.stack([key_grad, value_grad]))
 
     zero_pair = jnp.zeros((2, tok_rows, kv_heads, HEAD), jnp.float32)
-    query_rot_grad = zero_query
     kv_total = zero_pair
-    for distance in range(reach_blocks + 1):
-        query_part, kv_part = guarded(grad_block, (key_blocks[distance], prob_list[distance]))
-        query_rot_grad = query_rot_grad + query_part
+    score_list = []
+    for distance in range(reach_blocks + 1):
+        score_grad, kv_part = guarded(grad_block, (key_blocks[distance], prob_list[distance]))
+        score_list.append(score_grad)
         if distance == 0:
             kv_total = kv_part
         else:
             returned = passed_along(kv_part.astype(jnp.bfloat16), CTX, -distance)
             kv_total = kv_total + returned.astype(jnp.float32)
-    query_grad = normalize_back(
-        query_in,
-        query_inv,
-        q_gain[0],
-        unrotate(query_rot_grad.reshape(tok_rows, q_heads, HEAD), cosine, sine_table),
-    )
-    query_grad = query_grad.reshape(tok_rows, q_heads * HEAD).astype(jnp.bfloat16)
     key_back = normalize_back(key_in, key_inv, k_gain[0], unrotate(kv_total[0], cosine, sine_table))
     key_back = key_back.reshape(tok_rows, kv_width).astype(jnp.bfloat16)
     value_back = kv_total[1].reshape(tok_rows, kv_width).astype(jnp.bfloat16)
@@ -229,7 +216,27 @@
     slice_grad = lax.dot_general(
         group_back, weight_slice, (((1,), (1,)), ((), ())), preferred_element_type=jnp.float32
     ).astype(jnp.bfloat16)
+    score_list, slice_grad = lax.optimization_barrier((score_list, slice_grad))
     input_grad = lax.all_to_all(slice_grad, "cb", 0, 1, tiled=True)
+    query_rot_grad = zero_query
+    for distance in range(reach_blocks + 1):
+        query_part = (
+            jnp.einsum(
+                "grqk,kgd->qgrd",
+                score_list[distance],
+                key_blocks[distance][0],
+                preferred_element_type=jnp.float32,
+            )
+            * score_scale
+        )
+        query_rot_grad = query_rot_grad + query_part
+    query_grad = normalize_back(
+        query_in,
+        query_inv,
+        q_gain[0],
+        unrotate(query_rot_grad.reshape(tok_rows, q_heads, HEAD), cosine, sine_table),
+    )
+    query_grad = query_grad.reshape(tok_rows, q_heads * HEAD).astype(jnp.bfloat16)
     passed = shifted(input_grad, "pipe", -1)
     return (
         query_grad[None],

time: 331 us -> 325 us (0.982)
  waiting for transfers between devices: 134 us -> 127 us
  matrix products: 45.1 us -> 39.3 us
  local copies, waits for them, and re-layouts: 43.1 us -> 48.6 us
    dot_general x7, matrix products: 12.9 us -> 6.48 us  [local(): jnp.einsum('grqk,kgd->qgrd', score_list[distance], key_blocks[distance][0...]
    all_to_all x1, waiting for transfers between devices: 4.48 us -> 0.95 us  [local(): input_grad = lax.all_to_all(slice_grad, 'cb', 0, 1, tiled=True)]
    all_to_all x1, waiting for transfers between devices: 27.8 us -> 24.5 us  [gathered(): received = lax.all_to_all(copies, axis, 0, 0, tiled=True)]
    unnamed x113 -> x109, local copies, waits for them, and re-layouts: 16.4 us -> 16.1 us
where the time goes in v6:
time: 325 us; the launch traced here: 322 us
  waiting for transfers between devices  127 us (39%)
  starting transfers between devices  73.7 us (23%)
  local copies, waits for them, and re-layouts  48.6 us (15%)
  matrix products  39.3 us (12%)
  other arithmetic  18.3 us (6%)
  between operations  15.4 us (5%)
    ppermute x12, waiting for transfers between devices, passed_along(): return lax.ppermute(block, axis, route)  51.8 us
    ppermute x12, starting transfers between devices, passed_along(): return lax.ppermute(block, axis, route)  37.3 us
    all_to_all x1, waiting for transfers between devices, gathered(): received = lax.all_to_all(copies, axis, 0, 0, tiled=True)  24.5 us
    all_to_all x1, waiting for transfers between devices, summed_over(): received = lax.all_to_all(pieces, axis, 0, 0, tiled=True)  19.7 us
    all_to_all x1, starting transfers between devices, gathered(): received = lax.all_to_all(copies, axis, 0, 0, tiled=True)  17.7 us
    unnamed x109, local copies, waits for them, and re-layouts  16.1 us
    all_to_all x1, waiting for transfers between devices, local(): inputs_slice = lax.all_to_all(tokens_here, 'cb', 1, 0, tiled=True)  13 us
    all_gather x1, waiting for transfers between devices, local(): weight_slice = lax.all_gather(both_rows, 'cz', axis=0, tiled=True)  12.2 us
  transfers between devices with their start and end apart: 19, of which 10 were waited for; matrix products, arithmetic and copies ran while one was open for 20% of the time, Pallas kernels for 0%

profile of v6, /device:TPU:33, one launch (start us, length us, event | category | flops | bytes accessed | tf_op | source)
XLA Modules:
  0.0 322.2 jit_solution(15076816846011760403)
XLA Ops:
  7.2 1.5 pad_maximum_fusion.11
  8.8 1.6 copy.173
  10.4 1.3 copy.174
  11.7 6.7 %all-to-all-start = ((bf16[128,8,512]{2,0,1:T(8,128)(2,1)}), bf16[128,8,512]{2,0,1:T(8,128)(2,1)S(1)}, u32[]{:S(2)}, u32[]{:S(2)}) async-start(bf16[128,8,512]{2,0,1:T(8,128)(2,1)} %copy.174), calls=%async_computation | async-start | bytes 2097152 | tf_op jit(solution)/shard_map/all_to_all | solution.py:106
  21.0 13.0 %all-to-all-done = bf16[128,8,512]{2,0,1:T(8,128)(2,1)S(1)} async-done(((bf16[128,8,512]{2,0,1:T(8,128)(2,1)}), bf16[128,8,512]{2,0,1:T(8,128)(2,1)S(1)}, u32[]{:S(2)}, u32[]{:S(2)}) %all-to-all-start) | async-done | bytes 1048608 | tf_op jit(solution)/shard_map/all_to_all | solution.py:106
  34.0 12.2 %all-gather.2.cloned.1.call-done = bf16[512,1024]{1,0:T(8,128)(2,1)} async-done(((bf16[64,1024]{1,0:T(8,128)(2,1)}), bf16[512,1024]{1,0:T(8,128)(2,1)}) %all-gather.2.cloned.1.call-update) | async-done | bytes 1048592 | tf_op jit(solution)/shard_map/all_gather | solution.py:105
  46.2 3.9 %convolution_convert_fusion = bf16[1024,1024]{0,1:T(8,128)(2,1)} fusion(bf16[1024,512]{1,0:T(8,128)(2,1)S(1)} %bitcast.591, bf16[512,1024]{1,0:T(8,128)(2,1)} %all-gather.2.cloned.1.call-done), kind=kOutput, calls=%fused_computation | convolution fusion | flops 1074790400 | bytes 4194304 | tf_op jit(solution)/shard_map/dot_general | solution.py:108
  50.1 6.4 %all-to-all-start.1 = ((bf16[8,128,1024]{2,1,0:T(8,128)(2,1)}), bf16[8,128,1024]{2,1,0:T(8,128)(2,1)}, u32[]{:S(2)}, u32[]{:S(2)}) async-start(bf16[8,128,1024]{2,1,0:T(8,128)(2,1)} %bitcast.582), calls=%async_computation.1 | async-start | bytes 4194304 | tf_op jit(solution)/shard_map/all_to_all | solution.py:85
  62.6 19.7 %all-to-all-done.1 = bf16[8,128,1024]{2,1,0:T(8,128)(2,1)} async-done(((bf16[8,128,1024]{2,1,0:T(8,128)(2,1)}), bf16[8,128,1024]{2,1,0:T(8,128)(2,1)}, u32[]{:S(2)}, u32[]{:S(2)}) %all-to-all-start.1) | async-done | bytes 2097184 | tf_op jit(solution)/shard_map/all_to_all | solution.py:85
  82.3 2.0 reduce
  87.8 2.3 collective-permute-start
  90.1 4.2 %collective-permute-start.2 = (bf16[2,128,4,128]{3,1,2,0:T(8,128)(2,1)}, bf16[2,128,4,128]{3,1,2,0:T(8,128)(2,1)S(1)}, u32[]{:S(2)}, u32[]{:S(2)}) collective-permute-start(bf16[2,128,4,128]{3,1,2,0:T(8,128)(2,1)} %pad_maximum_fusion.2), channel_id=1, source_target_pairs={{0,12},{4,16},{8,20},{12,24},{16,28},{20,32},{24,36},{28,40},{32,4... | collective-permute-start | bytes 786440 | tf_op jit(solution)/shard_map/ppermute | solution.py:27
  94.3 3.2 collective-permute-start.3
  97.4 4.4 %collective-permute-start.4 = (bf16[2,128,4,128]{3,1,2,0:T(8,128)(2,1)}, bf16[2,128,4,128]{3,1,2,0:T(8,128)(2,1)}, u32[]{:S(2)}, u32[]{:S(2)}) collective-permute-start(bf16[2,128,4,128]{3,1,2,0:T(8,128)(2,1)} %pad_maximum_fusion.2), channel_id=1, source_target_pairs={{0,20},{4,24},{8,28},{12,32},{16,36},{20,40},{24,44},{28,48},{32,5... | collective-permute-start | bytes 786440 | tf_op jit(solution)/shard_map/ppermute | solution.py:27
  101.9 7.0 %collective-permute-start.5 = (bf16[2,128,4,128]{3,1,2,0:T(8,128)(2,1)}, bf16[2,128,4,128]{3,1,2,0:T(8,128)(2,1)}, u32[]{:S(2)}, u32[]{:S(2)}) collective-permute-start(bf16[2,128,4,128]{3,1,2,0:T(8,128)(2,1)} %pad_maximum_fusion.2), channel_id=1, source_target_pairs={{0,24},{4,28},{8,32},{12,36},{16,40},{20,44},{24,48},{28,52},{32,5... | collective-permute-start | bytes 786440 | tf_op jit(solution)/shard_map/ppermute | solution.py:27
  110.4 1.4 copy.237
  113.0 3.4 %collective-permute-start.1 = (bf16[2,128,4,128]{3,1,2,0:T(8,128)(2,1)}, bf16[2,128,4,128]{3,1,2,0:T(8,128)(2,1)S(1)}, u32[]{:S(2)}, u32[]{:S(2)}) collective-permute-start(bf16[2,128,4,128]{3,1,2,0:T(8,128)(2,1)} %pad_maximum_fusion.2), channel_id=1, source_target_pairs={{0,8},{4,12},{8,16},{12,20},{16,24},{20,28},{24,32},{28,36},{32,40... | collective-permute-start | bytes 786440 | tf_op jit(solution)/shard_map/ppermute | solution.py:27
  119.8 9.9 %collective-permute-done.5 = bf16[2,128,4,128]{3,1,2,0:T(8,128)(2,1)} collective-permute-done((bf16[2,128,4,128]{3,1,2,0:T(8,128)(2,1)}, bf16[2,128,4,128]{3,1,2,0:T(8,128)(2,1)}, u32[]{:S(2)}, u32[]{:S(2)}) %collective-permute-start.5) | collective-permute-done | bytes 262176 | tf_op jit(solution)/shard_map/ppermute | solution.py:27
  141.2 6.0 %collective-permute-start.6 = (bf16[2,128,4,128]{3,1,2,0:T(8,128)(2,1)S(1)}, bf16[2,128,4,128]{3,1,2,0:T(8,128)(2,1)S(1)}, u32[]{:S(2)}, u32[]{:S(2)}) collective-permute-start(bf16[2,128,4,128]{3,1,2,0:T(8,128)(2,1)S(1)} %pad_maximum_fusion.3), channel_id=1, source_target_pairs={{4,0},{8,4},{12,8},{16,12},{20,16},{24,20},{28,24},{32,28},{36,32}... | collective-permute-start | bytes 786440 | tf_op jit(solution)/shard_map/ppermute | solution.py:27
  154.6 1.4 collective-permute-start.10
  158.5 1.5 collective-permute-start.11
  160.6 15.3 %collective-permute-done.8 = bf16[2,128,4,128]{3,1,2,0:T(8,128)(2,1)S(1)} collective-permute-done((bf16[2,128,4,128]{3,1,2,0:T(8,128)(2,1)S(1)}, bf16[2,128,4,128]{3,1,2,0:T(8,128)(2,1)S(1)}, u32[]{:S(2)}, u32[]{:S(2)}) %collective-permute-start.8) | collective-permute-done | bytes 262176 | tf_op jit(solution)/shard_map/ppermute | solution.py:27
  175.9 21.4 %collective-permute-done.9 = bf16[2,128,4,128]{3,1,2,0:T(8,128)(2,1)S(1)} collective-permute-done((bf16[2,128,4,128]{3,1,2,0:T(8,128)(2,1)S(1)}, bf16[2,128,4,128]{3,1,2,0:T(8,128)(2,1)S(1)}, u32[]{:S(2)}, u32[]{:S(2)}) %collective-permute-start.9) | collective-permute-done | bytes 262176 | tf_op jit(solution)/shard_map/ppermute | solution.py:27
  197.3 5.2 %collective-permute-done.11 = bf16[2,128,4,128]{3,1,2,0:T(8,128)(2,1)S(1)} collective-permute-done((bf16[2,128,4,128]{3,1,2,0:T(8,128)(2,1)S(1)}, bf16[2,128,4,128]{3,1,2,0:T(8,128)(2,1)S(1)}, u32[]{:S(2)}, u32[]{:S(2)}) %collective-permute-start.11) | collective-permute-done | bytes 262176 | tf_op jit(solution)/shard_map/ppermute | solution.py:27
  207.1 1.6 broadcast_in_dim.62
  208.7 17.7 %all-to-all-start.2 = ((bf16[8,128,1024]{1,2,0:T(8,128)(2,1)}), bf16[8,128,1024]{1,2,0:T(8,128)(2,1)}, u32[]{:S(2)}, u32[]{:S(2)}) async-start(bf16[8,128,1024]{1,2,0:T(8,128)(2,1)} %broadcast_in_dim.62), calls=%async_computation.2 | async-start | bytes 4194304 | tf_op jit(solution)/shard_map/all_to_all | solution.py:79
  226.4 1.3 mul.517
  227.8 1.4 mul.518
  229.2 1.3 mul.631
  230.5 2.4 mul.632
  232.8 24.5 %all-to-all-done.2 = bf16[8,128,1024]{1,2,0:T(8,128)(2,1)} async-done(((bf16[8,128,1024]{1,2,0:T(8,128)(2,1)}), bf16[8,128,1024]{1,2,0:T(8,128)(2,1)}, u32[]{:S(2)}, u32[]{:S(2)}) %all-to-all-start.2) | async-done | bytes 2097184 | tf_op jit(solution)/shard_map/all_to_all | solution.py:79
  257.3 4.5 %convolution_bitcast_fusion = f32[512,1024]{0,1:T(8,128)} fusion(bf16[8,128,1024]{1,2,0:T(8,128)(2,1)} %all-to-all-done.2, bf16[128,8,512]{2,0,1:T(8,128)(2,1)} %copy-done.29), kind=kOutput, calls=%fused_computation.1 | convolution fusion | flops 1073741824 | bytes 5242880 | tf_op jit(solution)/shard_map/dot_general | solution.py:209
  261.7 2.9 copy.383
  265.3 3.9 %copy.243 = bf16[8,128,1024]{2,1,0:T(8,128)(2,1)} copy(bf16[8,128,1024]{1,2,0:T(8,128)(2,1)} %all-to-all-done.2) | data formatting | bytes 4194304 | tf_op jit(solution)/shard_map/all_to_all | solution.py:79
  269.3 4.1 %convolution_convert_fusion.1 = bf16[1024,512]{1,0:T(8,128)(2,1)} fusion(bf16[1024,1024]{1,0:T(8,128)(2,1)} %bitcast.583, bf16[512,1024]{1,0:T(8,128)(2,1)} %all-gather.2.cloned.1.call-done), kind=kOutput, calls=%fused_computation.2 | convolution fusion | flops 1074266112 | bytes 4194304 | tf_op jit(solution)/shard_map/dot_general | solution.py:216
  273.4 4.4 %all-to-all-start.3 = ((bf16[8,128,512]{2,1,0:T(8,128)(2,1)}), bf16[8,128,512]{2,1,0:T(8,128)(2,1)}, u32[]{:S(2)}, u32[]{:S(2)}) async-start(bf16[8,128,512]{2,1,0:T(8,128)(2,1)} %bitcast.592), calls=%async_computation.3 | async-start | bytes 2097152 | tf_op jit(solution)/shard_map/all_to_all | solution.py:220
  278.2 1.3 fusion.97
  279.9 1.3 fusion.99
  281.3 1.3 fusion.100
  285.5 1.6 copy.385
  287.1 2.4 copy.386
  289.5 2.8 multiply_add_fusion
  293.3 2.5 copy.392
  297.7 1.3 mul.636
  299.0 2.5 mul.637
  302.6 2.9 fusion.88
  305.5 4.8 %collective-permute-done.12 = bf16[128,4096]{1,0:T(8,128)(2,1)} collective-permute-done((bf16[128,4096]{1,0:T(8,128)(2,1)}, bf16[128,4096]{1,0:T(8,128)(2,1)}, u32[]{:S(2)}, u32[]{:S(2)}) %collective-permute-start.12) | collective-permute-done | bytes 1048608 | tf_op jit(solution)/shard_map/ppermute | solution.py:32
  313.1 2.3 copy.399
  (226 shorter events, 55.1 us)
Async XLA Ops:
  7.2 39.0 %all-gather.2.cloned.1.call-start = ((), (), s32[]{:S(2)}) async-start(), calls=%async_computation.5 | async-start | bytes 1179648 | tf_op jit(solution)/shard_map/all_gather | solution.py:105
  10.4 8.0 %copy-start.15 = (bf16[1,128,2048]{2,1,0:T(8,128)(2,1)S(1)}, bf16[1,128,2048]{2,1,0:T(8,128)(2,1)}, u32[]{:S(2)}) copy-start(bf16[1,128,2048]{2,1,0:T(8,128)(2,1)} %param.9) | copy-start | bytes 1572868
  11.7 22.3 %all-to-all-start = ((bf16[128,8,512]{2,0,1:T(8,128)(2,1)}), bf16[128,8,512]{2,0,1:T(8,128)(2,1)S(1)}, u32[]{:S(2)}, u32[]{:S(2)}) async-start(bf16[128,8,512]{2,0,1:T(8,128)(2,1)} %copy.174), calls=%async_computation | async-start | bytes 2097152 | tf_op jit(solution)/shard_map/all_to_all | solution.py:106
  19.4 37.1 %copy-start.18 = (f32[128,64]{1,0:T(8,128)}, f32[128,64]{1,0:T(8,128)S(1)}, u32[]{:S(2)}) copy-start(f32[128,64]{1,0:T(8,128)S(1)} %get-tuple-element.75) | copy-start | bytes 98308
  19.4 37.1 %copy-start.22 = (f32[128,64]{1,0:T(8,128)}, f32[128,64]{1,0:T(8,128)S(1)}, u32[]{:S(2)}) copy-start(f32[128,64]{1,0:T(8,128)S(1)} %get-tuple-element.76) | copy-start | bytes 98308
  34.0 16.1 %copy-start.29 = (bf16[128,8,512]{2,0,1:T(8,128)(2,1)}, bf16[128,8,512]{2,0,1:T(8,128)(2,1)S(1)}, u32[]{:S(2)}) copy-start(bf16[128,8,512]{2,0,1:T(8,128)(2,1)S(1)} %all-to-all-done) | copy-start | bytes 3145732
  50.1 32.2 %all-to-all-start.1 = ((bf16[8,128,1024]{2,1,0:T(8,128)(2,1)}), bf16[8,128,1024]{2,1,0:T(8,128)(2,1)}, u32[]{:S(2)}, u32[]{:S(2)}) async-start(bf16[8,128,1024]{2,1,0:T(8,128)(2,1)} %bitcast.582), calls=%async_computation.1 | async-start | bytes 4194304 | tf_op jit(solution)/shard_map/all_to_all | solution.py:85
  62.6 23.9 %copy-start.19 = (f32[128,64]{1,0:T(8,128)S(1)}, f32[128,64]{1,0:T(8,128)}, u32[]{:S(2)}) copy-start(f32[128,64]{1,0:T(8,128)} %copy-done.18) | copy-start | bytes 98308
  62.6 23.9 %copy-start.23 = (f32[128,64]{1,0:T(8,128)S(1)}, f32[128,64]{1,0:T(8,128)}, u32[]{:S(2)}) copy-start(f32[128,64]{1,0:T(8,128)} %copy-done.22) | copy-start | bytes 98308
  86.6 31.0 %copy-start.13 = (bf16[128,4,64]{2,0,1:T(8,128)(2,1)}, bf16[128,4,64]{2,0,1:T(8,128)(2,1)S(1)}, u32[]{:S(2)}) copy-start(bf16[128,4,64]{2,0,1:T(8,128)(2,1)S(1)} %get-tuple-element.45) | copy-start | bytes 196612
  86.8 47.5 %copy-start.16 = (bf16[128,512]{0,1:T(8,128)(2,1)}, bf16[128,512]{0,1:T(8,128)(2,1)S(1)}, u32[]{:S(2)}) copy-start(bf16[128,512]{0,1:T(8,128)(2,1)S(1)} %copy.179) | copy-start | bytes 393220
  87.8 25.2 %collective-permute-start = (bf16[2,128,4,128]{3,1,2,0:T(8,128)(2,1)}, bf16[2,128,4,128]{3,1,2,0:T(8,128)(2,1)}, u32[]{:S(2)}, u32[]{:S(2)}) collective-permute-start(bf16[2,128,4,128]{3,1,2,0:T(8,128)(2,1)} %pad_maximum_fusion.2), channel_id=1, source_target_pairs={{0,4},{4,8},{8,12},{12,16},{16,20},{20,24},{24,28},{28,32},{32,36}... | collective-permute-start | bytes 786440 | tf_op jit(solution)/shard_map/ppermute | solution.py:27
  90.1 27.6 %collective-permute-start.2 = (bf16[2,128,4,128]{3,1,2,0:T(8,128)(2,1)}, bf16[2,128,4,128]{3,1,2,0:T(8,128)(2,1)S(1)}, u32[]{:S(2)}, u32[]{:S(2)}) collective-permute-start(bf16[2,128,4,128]{3,1,2,0:T(8,128)(2,1)} %pad_maximum_fusion.2), channel_id=1, source_target_pairs={{0,12},{4,16},{8,20},{12,24},{16,28},{20,32},{24,36},{28,40},{32,4... | collective-permute-start | bytes 786440 | tf_op jit(solution)/shard_map/ppermute | solution.py:27
  94.3 23.8 %collective-permute-start.3 = (bf16[2,128,4,128]{3,1,2,0:T(8,128)(2,1)}, bf16[2,128,4,128]{3,1,2,0:T(8,128)(2,1)S(1)}, u32[]{:S(2)}, u32[]{:S(2)}) collective-permute-start(bf16[2,128,4,128]{3,1,2,0:T(8,128)(2,1)} %pad_maximum_fusion.2), channel_id=1, source_target_pairs={{0,16},{4,20},{8,24},{12,28},{16,32},{20,36},{24,40},{28,44},{32,4... | collective-permute-start | bytes 786440 | tf_op jit(solution)/shard_map/ppermute | solution.py:27
  97.4 21.1 %collective-permute-start.4 = (bf16[2,128,4,128]{3,1,2,0:T(8,128)(2,1)}, bf16[2,128,4,128]{3,1,2,0:T(8,128)(2,1)}, u32[]{:S(2)}, u32[]{:S(2)}) collective-permute-start(bf16[2,128,4,128]{3,1,2,0:T(8,128)(2,1)} %pad_maximum_fusion.2), channel_id=1, source_target_pairs={{0,20},{4,24},{8,28},{12,32},{16,36},{20,40},{24,44},{28,48},{32,5... | collective-permute-start | bytes 786440 | tf_op jit(solution)/shard_map/ppermute | solution.py:27
  101.9 27.8 %collective-permute-start.5 = (bf16[2,128,4,128]{3,1,2,0:T(8,128)(2,1)}, bf16[2,128,4,128]{3,1,2,0:T(8,128)(2,1)}, u32[]{:S(2)}, u32[]{:S(2)}) collective-permute-start(bf16[2,128,4,128]{3,1,2,0:T(8,128)(2,1)} %pad_maximum_fusion.2), channel_id=1, source_target_pairs={{0,24},{4,28},{8,32},{12,36},{16,40},{20,44},{24,48},{28,52},{32,5... | collective-permute-start | bytes 786440 | tf_op jit(solution)/shard_map/ppermute | solution.py:27
  111.8 5.9 %copy-start.42 = (pred[128,128]{0,1:T(8,128)(4,1)S(1)}, pred[128,128]{0,1:T(8,128)(4,1)}, u32[]{:S(2)}) copy-start(pred[128,128]{0,1:T(8,128)(4,1)} %get-tuple-element.71) | copy-start | bytes 49156
  113.0 5.1 %copy-start.41 = (pred[128,128]{0,1:T(8,128)(4,1)S(1)}, pred[128,128]{0,1:T(8,128)(4,1)}, u32[]{:S(2)}) copy-start(pred[128,128]{0,1:T(8,128)(4,1)} %get-tuple-element.72) | copy-start | bytes 49156
  113.0 18.0 %collective-permute-start.1 = (bf16[2,128,4,128]{3,1,2,0:T(8,128)(2,1)}, bf16[2,128,4,128]{3,1,2,0:T(8,128)(2,1)S(1)}, u32[]{:S(2)}, u32[]{:S(2)}) collective-permute-start(bf16[2,128,4,128]{3,1,2,0:T(8,128)(2,1)} %pad_maximum_fusion.2), channel_id=1, source_target_pairs={{0,8},{4,12},{8,16},{12,20},{16,24},{20,28},{24,32},{28,36},{32,40... | collective-permute-start | bytes 786440 | tf_op jit(solution)/shard_map/ppermute | solution.py:27
  117.7 31.5 %copy-start.32 = (bf16[2,128,4,128]{3,1,2,0:T(8,128)(2,1)}, bf16[2,128,4,128]{3,1,2,0:T(8,128)(2,1)S(1)}, u32[]{:S(2)}) copy-start(bf16[2,128,4,128]{3,1,2,0:T(8,128)(2,1)S(1)} %collective-permute-done.2) | copy-start | bytes 786436
  118.1 33.0 %copy-start.33 = (bf16[2,128,4,128]{3,1,2,0:T(8,128)(2,1)}, bf16[2,128,4,128]{3,1,2,0:T(8,128)(2,1)S(1)}, u32[]{:S(2)}) copy-start(bf16[2,128,4,128]{3,1,2,0:T(8,128)(2,1)S(1)} %collective-permute-done.3) | copy-start | bytes 786436
  118.5 12.5 %copy-start.39 = (pred[128,128]{0,1:T(8,128)(4,1)S(1)}, pred[128,128]{0,1:T(8,128)(4,1)}, u32[]{:S(2)}) copy-start(pred[128,128]{0,1:T(8,128)(4,1)} %get-tuple-element.70) | copy-start | bytes 49156
  131.0 16.2 %copy-start.30 = (bf16[2,128,4,128]{3,1,2,0:T(8,128)(2,1)}, bf16[2,128,4,128]{3,1,2,0:T(8,128)(2,1)S(1)}, u32[]{:S(2)}) copy-start(bf16[2,128,4,128]{3,1,2,0:T(8,128)(2,1)S(1)} %collective-permute-done.1) | copy-start | bytes 786436
  140.9 7.0 %copy-start.6 = (bf16[4,4,128,128]{2,3,1,0:T(8,128)(2,1)}, bf16[4,4,128,128]{2,3,1,0:T(8,128)(2,1)S(1)}, u32[]{:S(2)}) copy-start(bf16[4,4,128,128]{2,3,1,0:T(8,128)(2,1)S(1)} %fusion.47) | copy-start | bytes 1572868
  141.2 17.2 %collective-permute-start.6 = (bf16[2,128,4,128]{3,1,2,0:T(8,128)(2,1)S(1)}, bf16[2,128,4,128]{3,1,2,0:T(8,128)(2,1)S(1)}, u32[]{:S(2)}, u32[]{:S(2)}) collective-permute-start(bf16[2,128,4,128]{3,1,2,0:T(8,128)(2,1)S(1)} %pad_maximum_fusion.3), channel_id=1, source_target_pairs={{4,0},{8,4},{12,8},{16,12},{20,16},{24,20},{28,24},{32,28},{36,32}... | collective-permute-start | bytes 786440 | tf_op jit(solution)/shard_map/ppermute | solution.py:27
  147.9 12.7 %collective-permute-start.7 = (bf16[2,128,4,128]{3,1,2,0:T(8,128)(2,1)S(1)}, bf16[2,128,4,128]{3,1,2,0:T(8,128)(2,1)S(1)}, u32[]{:S(2)}, u32[]{:S(2)}) collective-permute-start(bf16[2,128,4,128]{3,1,2,0:T(8,128)(2,1)S(1)} %pad_maximum_fusion.4), channel_id=1, source_target_pairs={{8,0},{12,4},{16,8},{20,12},{24,16},{28,20},{32,24},{36,28},{40,32... | collective-permute-start | bytes 786440 | tf_op jit(solution)/shard_map/ppermute | solution.py:27
  149.8 26.1 %collective-permute-start.8 = (bf16[2,128,4,128]{3,1,2,0:T(8,128)(2,1)S(1)}, bf16[2,128,4,128]{3,1,2,0:T(8,128)(2,1)S(1)}, u32[]{:S(2)}, u32[]{:S(2)}) collective-permute-start(bf16[2,128,4,128]{3,1,2,0:T(8,128)(2,1)S(1)} %pad_maximum_fusion.5), channel_id=1, source_target_pairs={{12,0},{16,4},{20,8},{24,12},{28,16},{32,20},{36,24},{40,28},{44,3... | collective-permute-start | bytes 786440 | tf_op jit(solution)/shard_map/ppermute | solution.py:27
  151.8 45.6 %collective-permute-start.9 = (bf16[2,128,4,128]{3,1,2,0:T(8,128)(2,1)S(1)}, bf16[2,128,4,128]{3,1,2,0:T(8,128)(2,1)S(1)}, u32[]{:S(2)}, u32[]{:S(2)}) collective-permute-start(bf16[2,128,4,128]{3,1,2,0:T(8,128)(2,1)S(1)} %pad_maximum_fusion.6), channel_id=1, source_target_pairs={{16,0},{20,4},{24,8},{28,12},{32,16},{36,20},{40,24},{44,28},{48,3... | collective-permute-start | bytes 786440 | tf_op jit(solution)/shard_map/ppermute | solution.py:27
  154.6 3.5 %copy-start.17 = (bf16[128,512]{0,1:T(8,128)(2,1)S(1)}, bf16[128,512]{0,1:T(8,128)(2,1)}, u32[]{:S(2)}) copy-start(bf16[128,512]{0,1:T(8,128)(2,1)} %copy-done.16) | copy-start | bytes 393220
  154.6 42.7 %collective-permute-start.10 = (bf16[2,128,4,128]{3,1,2,0:T(8,128)(2,1)S(1)}, bf16[2,128,4,128]{3,1,2,0:T(8,128)(2,1)S(1)}, u32[]{:S(2)}, u32[]{:S(2)}) collective-permute-start(bf16[2,128,4,128]{3,1,2,0:T(8,128)(2,1)S(1)} %pad_maximum_fusion.7), channel_id=1, source_target_pairs={{20,0},{24,4},{28,8},{32,12},{36,16},{40,20},{44,24},{48,28},{52,3... | collective-permute-start | bytes 786440 | tf_op jit(solution)/shard_map/ppermute | solution.py:27
  158.5 44.1 %collective-permute-start.11 = (bf16[2,128,4,128]{3,1,2,0:T(8,128)(2,1)S(1)}, bf16[2,128,4,128]{3,1,2,0:T(8,128)(2,1)S(1)}, u32[]{:S(2)}, u32[]{:S(2)}) collective-permute-start(bf16[2,128,4,128]{3,1,2,0:T(8,128)(2,1)S(1)} %pad_maximum_fusion.8), channel_id=1, source_target_pairs={{24,0},{28,4},{32,8},{36,12},{40,16},{44,20},{48,24},{52,28},{56,3... | collective-permute-start | bytes 786440 | tf_op jit(solution)/shard_map/ppermute | solution.py:27
  160.3 42.6 %copy-start.20 = (f32[128,64]{1,0:T(8,128)S(1)}, f32[128,64]{1,0:T(8,128)}, u32[]{:S(2)}) copy-start(f32[128,64]{1,0:T(8,128)} %copy-done.18) | copy-start | bytes 98308
  160.3 42.6 %copy-start.24 = (f32[128,64]{1,0:T(8,128)S(1)}, f32[128,64]{1,0:T(8,128)}, u32[]{:S(2)}) copy-start(f32[128,64]{1,0:T(8,128)} %copy-done.22) | copy-start | bytes 98308
  160.6 42.5 %copy-start.46 = (f32[1,128]{1,0:T(1,128)S(1)}, f32[1,128]{1,0:T(1,128)}, u32[]{:S(2)}) copy-start(f32[1,128]{1,0:T(1,128)} %param.15) | copy-start | bytes 1540
  202.9 3.8 %copy-start.27 = (bf16[128,1024]{1,0:T(8,128)(2,1)S(1)}, bf16[128,1024]{1,0:T(8,128)(2,1)}, u32[]{:S(2)}) copy-start(bf16[128,1024]{1,0:T(8,128)(2,1)} %copy-done.26) | copy-start | bytes 786436
  202.9 3.8 %copy-start.28 = (f32[128,512]{1,0:T(8,128)S(1)}, f32[128,512]{1,0:T(8,128)}, u32[]{:S(2)}) copy-start(f32[128,512]{1,0:T(8,128)} %copy.236) | copy-start | bytes 786436
  202.9 3.8 %copy-start.44 = (f32[512]{0:T(512)S(1)}, f32[512]{0:T(512)}, u32[]{:S(2)}) copy-start(f32[512]{0:T(512)} %broadcast_bitcast_fusion.1) | copy-start | bytes 6148
  208.7 17.7 %copy-start.36 = (f32[128,16]{1,0:T(8,128)S(1)}, f32[128,16]{1,0:T(8,128)}, u32[]{:S(2)}) copy-start(f32[128,16]{1,0:T(8,128)} %copy-done.35) | copy-start | bytes 24580
  208.7 48.6 %all-to-all-start.2 = ((bf16[8,128,1024]{1,2,0:T(8,128)(2,1)}), bf16[8,128,1024]{1,2,0:T(8,128)(2,1)}, u32[]{:S(2)}, u32[]{:S(2)}) async-start(bf16[8,128,1024]{1,2,0:T(8,128)(2,1)} %broadcast_in_dim.62), calls=%async_computation.2 | async-start | bytes 4194304 | tf_op jit(solution)/shard_map/all_to_all | solution.py:79
  226.4 83.9 %reduce-scatter.4.cloned.1.call-start = ((), (), s32[]{:S(2)}) async-start(), calls=%async_computation.6 | async-start | bytes 2359296
  273.4 4.4 %copy-start.14 = (bf16[128,4,64]{2,0,1:T(8,128)(2,1)S(1)}, bf16[128,4,64]{2,0,1:T(8,128)(2,1)}, u32[]{:S(2)}) copy-start(bf16[128,4,64]{2,0,1:T(8,128)(2,1)} %copy-done.13) | copy-start | bytes 196612
  273.4 19.9 %all-to-all-start.3 = ((bf16[8,128,512]{2,1,0:T(8,128)(2,1)}), bf16[8,128,512]{2,1,0:T(8,128)(2,1)}, u32[]{:S(2)}, u32[]{:S(2)}) async-start(bf16[8,128,512]{2,1,0:T(8,128)(2,1)} %bitcast.592), calls=%async_computation.3 | async-start | bytes 2097152 | tf_op jit(solution)/shard_map/all_to_all | solution.py:220
  285.5 4.0 %copy-start.21 = (f32[128,64]{1,0:T(8,128)S(1)}, f32[128,64]{1,0:T(8,128)}, u32[]{:S(2)}) copy-start(f32[128,64]{1,0:T(8,128)} %copy-done.18) | copy-start | bytes 98308
  285.5 4.0 %copy-start.25 = (f32[128,64]{1,0:T(8,128)S(1)}, f32[128,64]{1,0:T(8,128)}, u32[]{:S(2)}) copy-start(f32[128,64]{1,0:T(8,128)} %copy-done.22) | copy-start | bytes 98308
  293.3 3.7 %copy-start.11 = (f32[128,16,64]{2,1,0:T(8,128)S(1)}, f32[128,16,64]{2,1,0:T(8,128)}, u32[]{:S(2)}) copy-start(f32[128,16,64]{2,1,0:T(8,128)} %get-tuple-element.36) | copy-start | bytes 1572868
  293.3 3.7 %copy-start.12 = (f32[128,16,64]{2,1,0:T(8,128)S(1)}, f32[128,16,64]{2,1,0:T(8,128)}, u32[]{:S(2)}) copy-start(f32[128,16,64]{2,1,0:T(8,128)} %get-tuple-element.37) | copy-start | bytes 1572868
  295.8 14.5 %collective-permute-start.12 = (bf16[128,4096]{1,0:T(8,128)(2,1)}, bf16[128,4096]{1,0:T(8,128)(2,1)}, u32[]{:S(2)}, u32[]{:S(2)}) collective-permute-start(bf16[128,4096]{1,0:T(8,128)(2,1)} %bitcast.235), channel_id=1, source_target_pairs={{0,3},{1,0},{2,1},{3,2},{4,7},{5,4},{6,5},{7,6},{8,11},{9,8},{10,9... | collective-permute-start | bytes 3145736 | tf_op jit(solution)/shard_map/ppermute | solution.py:32
  299.0 3.6 %copy-start.10 = (f32[1,128,2048]{2,1,0:T(8,128)S(1)}, f32[1,128,2048]{2,1,0:T(8,128)}, u32[]{:S(2)}) copy-start(f32[1,128,2048]{2,1,0:T(8,128)} %mul.632) | copy-start | bytes 3145732
  (20 other events, 37.0 us)
Sparse Core Ops, SparseCore 0:
  10.3 35.8 all-gather.1
  264.8 35.9 reduce-scatter.3

commit v7 on v6

--- a/solution.py
+++ b/solution.py
@@ -208,16 +208,18 @@
     grad_rows = lax.psum_scatter(
         lax.dot_general(
             inputs_slice, group_back, (((0,), (0,)), ((), ())), preferred_element_type=jnp.float32
-        ),
+        ).astype(jnp.bfloat16),
         "cz",
         scatter_dimension=0,
         tiled=True,
-    )
+    ).astype(jnp.float32)
     slice_grad = lax.dot_general(
         group_back, weight_slice, (((1,), (1,)), ((), ())), preferred_element_type=jnp.float32
     ).astype(jnp.bfloat16)
     score_list, slice_grad = lax.optimization_barrier((score_list, slice_grad))
-    input_grad = lax.all_to_all(slice_grad, "cb", 0, 1, tiled=True)
+    input_grad = lax.all_to_all(
+        slice_grad.reshape(row_parts, tok_rows, slice_grad.shape[1]), "cb", 0, 0, tiled=True
+    )
     query_rot_grad = zero_query
     for distance in range(reach_blocks + 1):
         query_part = (
@@ -237,7 +239,7 @@
         unrotate(query_rot_grad.reshape(tok_rows, q_heads, HEAD), cosine, sine_table),
     )
     query_grad = query_grad.reshape(tok_rows, q_heads * HEAD).astype(jnp.bfloat16)
-    passed = shifted(input_grad, "pipe", -1)
+    passed = shifted(input_grad, "pipe", -1).transpose(1, 0, 2).reshape(tok_rows, -1)
     return (
         query_grad[None],
         grad_rows[:, :kv_width][None],

time: 325 us -> 330 us (1.015)
  the two profiles are of different devices: /device:TPU:33 before, /device:TPU:10 now
where the time goes in v7:
time: 330 us; the launch traced here: 328 us
  waiting for transfers between devices  143 us (43%)
  starting transfers between devices  73.2 us (22%)
  local copies, waits for them, and re-layouts  39 us (12%)
  matrix products  38.6 us (12%)
  other arithmetic  19.1 us (6%)
  between operations  15.3 us (5%)
    ppermute x12, waiting for transfers between devices, passed_along(): return lax.ppermute(block, axis, route)  47.5 us
    ppermute x12, starting transfers between devices, passed_along(): return lax.ppermute(block, axis, route)  44.3 us
    unnamed x3, waiting for transfers between devices  23.9 us
    all_to_all x1, waiting for transfers between devices, gathered(): received = lax.all_to_all(copies, axis, 0, 0, tiled=True)  21.2 us
    all_gather x1, waiting for transfers between devices, local(): weight_slice = lax.all_gather(both_rows, 'cz', axis=0, tiled=True)  18.8 us
    all_to_all x1, waiting for transfers between devices, summed_over(): received = lax.all_to_all(pieces, axis, 0, 0, tiled=True)  16.6 us
    all_to_all x1, waiting for transfers between devices, local(): inputs_slice = lax.all_to_all(tokens_here, 'cb', 1, 0, tiled=True)  11.9 us
    unnamed x113, local copies, waits for them, and re-layouts  11.3 us
  transfers between devices with their start and end apart: 19, of which 13 were waited for; matrix products, arithmetic and copies ran while one was open for 17% of the time, Pallas kernels for 0%

profile of v7, /device:TPU:10, one launch (start us, length us, event | category | flops | bytes accessed | tf_op | source)
XLA Modules:
  0.0 328.0 jit_solution(10427440552770527923)
XLA Ops:
  7.2 1.5 pad_maximum_fusion.11
  8.8 1.6 copy.173
  11.7 6.6 %all-to-all-start = ((bf16[128,8,512]{2,0,1:T(8,128)(2,1)}), bf16[128,8,512]{2,0,1:T(8,128)(2,1)S(1)}, u32[]{:S(2)}, u32[]{:S(2)}) async-start(bf16[128,8,512]{2,0,1:T(8,128)(2,1)} %copy.174), calls=%async_computation | async-start | bytes 2097152 | tf_op jit(solution)/shard_map/all_to_all | solution.py:106
  20.9 11.9 %all-to-all-done = bf16[128,8,512]{2,0,1:T(8,128)(2,1)S(1)} async-done(((bf16[128,8,512]{2,0,1:T(8,128)(2,1)}), bf16[128,8,512]{2,0,1:T(8,128)(2,1)S(1)}, u32[]{:S(2)}, u32[]{:S(2)}) %all-to-all-start) | async-done | bytes 1048608 | tf_op jit(solution)/shard_map/all_to_all | solution.py:106
  32.8 18.8 %all-gather.2.cloned.1.call-done = bf16[512,1024]{1,0:T(8,128)(2,1)} async-done(((bf16[64,1024]{1,0:T(8,128)(2,1)}), bf16[512,1024]{1,0:T(8,128)(2,1)}) %all-gather.2.cloned.1.call-update) | async-done | bytes 1048592 | tf_op jit(solution)/shard_map/all_gather | solution.py:105
  51.6 3.8 %convolution_convert_fusion = bf16[1024,1024]{0,1:T(8,128)(2,1)} fusion(bf16[1024,512]{1,0:T(8,128)(2,1)S(1)} %bitcast.590, bf16[512,1024]{1,0:T(8,128)(2,1)} %all-gather.2.cloned.1.call-done), kind=kOutput, calls=%fused_computation.1 | convolution fusion | flops 1074790400 | bytes 4194304 | tf_op jit(solution)/shard_map/dot_general | solution.py:108
  55.5 6.4 %all-to-all-start.1 = ((bf16[8,128,1024]{2,1,0:T(8,128)(2,1)}), bf16[8,128,1024]{2,1,0:T(8,128)(2,1)}, u32[]{:S(2)}, u32[]{:S(2)}) async-start(bf16[8,128,1024]{2,1,0:T(8,128)(2,1)} %bitcast.583), calls=%async_computation.1 | async-start | bytes 4194304 | tf_op jit(solution)/shard_map/all_to_all | solution.py:85
  67.9 16.6 %all-to-all-done.1 = bf16[8,128,1024]{2,1,0:T(8,128)(2,1)} async-done(((bf16[8,128,1024]{2,1,0:T(8,128)(2,1)}), bf16[8,128,1024]{2,1,0:T(8,128)(2,1)}, u32[]{:S(2)}, u32[]{:S(2)}) %all-to-all-start.1) | async-done | bytes 2097184 | tf_op jit(solution)/shard_map/all_to_all | solution.py:85
  84.4 2.0 reduce
  89.8 2.8 collective-permute-start
  92.6 4.4 %collective-permute-start.2 = (bf16[2,128,4,128]{3,1,2,0:T(8,128)(2,1)}, bf16[2,128,4,128]{3,1,2,0:T(8,128)(2,1)S(1)}, u32[]{:S(2)}, u32[]{:S(2)}) collective-permute-start(bf16[2,128,4,128]{3,1,2,0:T(8,128)(2,1)} %pad_maximum_fusion.2), channel_id=1, source_target_pairs={{0,12},{4,16},{8,20},{12,24},{16,28},{20,32},{24,36},{28,40},{32,4... | collective-permute-start | bytes 786440 | tf_op jit(solution)/shard_map/ppermute | solution.py:27
  97.0 7.4 %collective-permute-start.3 = (bf16[2,128,4,128]{3,1,2,0:T(8,128)(2,1)}, bf16[2,128,4,128]{3,1,2,0:T(8,128)(2,1)}, u32[]{:S(2)}, u32[]{:S(2)}) collective-permute-start(bf16[2,128,4,128]{3,1,2,0:T(8,128)(2,1)} %pad_maximum_fusion.2), channel_id=1, source_target_pairs={{0,16},{4,20},{8,24},{12,28},{16,32},{20,36},{24,40},{28,44},{32,4... | collective-permute-start | bytes 786440 | tf_op jit(solution)/shard_map/ppermute | solution.py:27
  104.4 4.3 %collective-permute-start.4 = (bf16[2,128,4,128]{3,1,2,0:T(8,128)(2,1)}, bf16[2,128,4,128]{3,1,2,0:T(8,128)(2,1)}, u32[]{:S(2)}, u32[]{:S(2)}) collective-permute-start(bf16[2,128,4,128]{3,1,2,0:T(8,128)(2,1)} %pad_maximum_fusion.2), channel_id=1, source_target_pairs={{0,20},{4,24},{8,28},{12,32},{16,36},{20,40},{24,44},{28,48},{32,5... | collective-permute-start | bytes 786440 | tf_op jit(solution)/shard_map/ppermute | solution.py:27
  108.7 4.0 %collective-permute-start.5 = (bf16[2,128,4,128]{3,1,2,0:T(8,128)(2,1)}, bf16[2,128,4,128]{3,1,2,0:T(8,128)(2,1)S(1)}, u32[]{:S(2)}, u32[]{:S(2)}) collective-permute-start(bf16[2,128,4,128]{3,1,2,0:T(8,128)(2,1)} %pad_maximum_fusion.2), channel_id=1, source_target_pairs={{0,24},{4,28},{8,32},{12,36},{16,40},{20,44},{24,48},{28,52},{32,5... | collective-permute-start | bytes 786440 | tf_op jit(solution)/shard_map/ppermute | solution.py:27
  114.2 1.4 copy.237
  116.8 2.6 collective-permute-start.1
  120.7 5.6 %collective-permute-done.2 = bf16[2,128,4,128]{3,1,2,0:T(8,128)(2,1)S(1)} collective-permute-done((bf16[2,128,4,128]{3,1,2,0:T(8,128)(2,1)}, bf16[2,128,4,128]{3,1,2,0:T(8,128)(2,1)S(1)}, u32[]{:S(2)}, u32[]{:S(2)}) %collective-permute-start.2) | collective-permute-done | bytes 262176 | tf_op jit(solution)/shard_map/ppermute | solution.py:27
  126.7 10.2 %collective-permute-done.3 = bf16[2,128,4,128]{3,1,2,0:T(8,128)(2,1)} collective-permute-done((bf16[2,128,4,128]{3,1,2,0:T(8,128)(2,1)}, bf16[2,128,4,128]{3,1,2,0:T(8,128)(2,1)}, u32[]{:S(2)}, u32[]{:S(2)}) %collective-permute-start.3) | collective-permute-done | bytes 262176 | tf_op jit(solution)/shard_map/ppermute | solution.py:27
  139.5 4.8 %collective-permute-done.5 = bf16[2,128,4,128]{3,1,2,0:T(8,128)(2,1)S(1)} collective-permute-done((bf16[2,128,4,128]{3,1,2,0:T(8,128)(2,1)}, bf16[2,128,4,128]{3,1,2,0:T(8,128)(2,1)S(1)}, u32[]{:S(2)}, u32[]{:S(2)}) %collective-permute-start.5) | collective-permute-done | bytes 262176 | tf_op jit(solution)/shard_map/ppermute | solution.py:27
  154.8 1.9 collective-permute-start.6
  157.4 3.1 collective-permute-start.7
  161.2 6.3 %collective-permute-start.8 = (bf16[2,128,4,128]{3,1,2,0:T(8,128)(2,1)S(1)}, bf16[2,128,4,128]{3,1,2,0:T(8,128)(2,1)S(1)}, u32[]{:S(2)}, u32[]{:S(2)}) collective-permute-start(bf16[2,128,4,128]{3,1,2,0:T(8,128)(2,1)S(1)} %pad_maximum_fusion.5), channel_id=1, source_target_pairs={{12,0},{16,4},{20,8},{24,12},{28,16},{32,20},{36,24},{40,28},{44,3... | collective-permute-start | bytes 786440 | tf_op jit(solution)/shard_map/ppermute | solution.py:27
  169.0 3.4 %collective-permute-start.9 = (bf16[2,128,4,128]{3,1,2,0:T(8,128)(2,1)S(1)}, bf16[2,128,4,128]{3,1,2,0:T(8,128)(2,1)S(1)}, u32[]{:S(2)}, u32[]{:S(2)}) collective-permute-start(bf16[2,128,4,128]{3,1,2,0:T(8,128)(2,1)S(1)} %pad_maximum_fusion.6), channel_id=1, source_target_pairs={{16,0},{20,4},{24,8},{28,12},{32,16},{36,20},{40,24},{44,28},{48,3... | collective-permute-start | bytes 786440 | tf_op jit(solution)/shard_map/ppermute | solution.py:27
  173.9 2.1 collective-permute-start.10
  177.5 2.1 collective-permute-start.11
  180.3 11.7 %collective-permute-done.8 = bf16[2,128,4,128]{3,1,2,0:T(8,128)(2,1)S(1)} collective-permute-done((bf16[2,128,4,128]{3,1,2,0:T(8,128)(2,1)S(1)}, bf16[2,128,4,128]{3,1,2,0:T(8,128)(2,1)S(1)}, u32[]{:S(2)}, u32[]{:S(2)}) %collective-permute-start.8) | collective-permute-done | bytes 262176 | tf_op jit(solution)/shard_map/ppermute | solution.py:27
  191.9 2.4 collective-permute-done.9
  194.3 8.2 %collective-permute-done.10 = bf16[2,128,4,128]{3,1,2,0:T(8,128)(2,1)S(1)} collective-permute-done((bf16[2,128,4,128]{3,1,2,0:T(8,128)(2,1)S(1)}, bf16[2,128,4,128]{3,1,2,0:T(8,128)(2,1)S(1)}, u32[]{:S(2)}, u32[]{:S(2)}) %collective-permute-start.10) | collective-permute-done | bytes 262176 | tf_op jit(solution)/shard_map/ppermute | solution.py:27
  202.5 4.8 %collective-permute-done.11 = bf16[2,128,4,128]{3,1,2,0:T(8,128)(2,1)S(1)} collective-permute-done((bf16[2,128,4,128]{3,1,2,0:T(8,128)(2,1)S(1)}, bf16[2,128,4,128]{3,1,2,0:T(8,128)(2,1)S(1)}, u32[]{:S(2)}, u32[]{:S(2)}) %collective-permute-start.11) | collective-permute-done | bytes 262176 | tf_op jit(solution)/shard_map/ppermute | solution.py:27
  211.8 1.6 broadcast_in_dim.60
  213.4 9.4 %all-to-all-start.2 = ((bf16[8,128,1024]{1,2,0:T(8,128)(2,1)}), bf16[8,128,1024]{1,2,0:T(8,128)(2,1)}, u32[]{:S(2)}, u32[]{:S(2)}) async-start(bf16[8,128,1024]{1,2,0:T(8,128)(2,1)} %broadcast_in_dim.60), calls=%async_computation.2 | async-start | bytes 4194304 | tf_op jit(solution)/shard_map/all_to_all | solution.py:79
  225.8 21.2 %all-to-all-done.2 = bf16[8,128,1024]{1,2,0:T(8,128)(2,1)} async-done(((bf16[8,128,1024]{1,2,0:T(8,128)(2,1)}), bf16[8,128,1024]{1,2,0:T(8,128)(2,1)}, u32[]{:S(2)}, u32[]{:S(2)}) %all-to-all-start.2) | async-done | bytes 2097184 | tf_op jit(solution)/shard_map/all_to_all | solution.py:79
  247.0 3.9 %copy.243 = bf16[8,128,1024]{2,1,0:T(8,128)(2,1)} copy(bf16[8,128,1024]{1,2,0:T(8,128)(2,1)} %all-to-all-done.2) | data formatting | bytes 4194304 | tf_op jit(solution)/shard_map/all_to_all | solution.py:79
  250.9 3.9 %convolution_convert_fusion.1 = bf16[1024,512]{1,0:T(8,128)(2,1)} fusion(bf16[1024,1024]{1,0:T(8,128)(2,1)} %bitcast.584, bf16[512,1024]{1,0:T(8,128)(2,1)S(1)} %copy-done.51), kind=kOutput, calls=%fused_computation.2 | convolution fusion | flops 1074266112 | bytes 4194304 | tf_op jit(solution)/shard_map/dot_general | solution.py:216
  254.9 1.4 fusion.127
  256.3 6.6 %all-to-all-start.3 = ((bf16[8,128,512]{2,1,0:T(8,128)(2,1)}), bf16[8,128,512]{2,1,0:T(8,128)(2,1)}, u32[]{:S(2)}, u32[]{:S(2)}) async-start(bf16[8,128,512]{2,1,0:T(8,128)(2,1)} %bitcast.591), calls=%async_computation.3 | async-start | bytes 2097152 | tf_op jit(solution)/shard_map/all_to_all | solution.py:220
  262.9 3.8 %fusion = bf16[512,1024]{0,1:T(8,128)(2,1)} fusion(bf16[8,128,1024]{1,2,0:T(8,128)(2,1)} %all-to-all-done.2, bf16[128,8,512]{2,0,1:T(8,128)(2,1)S(1)} %copy-done.30), kind=kOutput, calls=%fused_computation.3 | convolution fusion | flops 1074266112 | bytes 4194304 | tf_op jit(solution)/shard_map/dot_general | solution.py:209
  266.7 2.3 copy.383
  269.4 1.4 fusion.99
  272.2 1.3 convolution_add_fusion.1
  275.0 1.4 copy.386
  276.4 2.4 multiply_add_fusion
  278.8 1.9 multiply_reduce_fusion
  282.0 2.5 mul.637
  285.7 2.9 fusion.89
  288.6 2.9 collective-permute-done.12
  291.5 1.8 copy.260
  294.6 23.9 %reduce-scatter.4.cloned.1.call-done = bf16[64,1024]{1,0:T(8,128)(2,1)} async-done(((bf16[512,1024]{1,0:T(8,128)(2,1)}), bf16[64,1024]{1,0:T(8,128)(2,1)}) %reduce-scatter.4.cloned.1.call-update) | async-done | bytes 131088
  (232 shorter events, 53.9 us)
Async XLA Ops:
  7.2 44.5 %all-gather.2.cloned.1.call-start = ((), (), s32[]{:S(2)}) async-start(), calls=%async_computation.5 | async-start | bytes 1179648 | tf_op jit(solution)/shard_map/all_gather | solution.py:105
  10.4 7.9 %copy-start.15 = (bf16[1,128,2048]{2,1,0:T(8,128)(2,1)S(1)}, bf16[1,128,2048]{2,1,0:T(8,128)(2,1)}, u32[]{:S(2)}) copy-start(bf16[1,128,2048]{2,1,0:T(8,128)(2,1)} %param.9) | copy-start | bytes 1572868
  11.7 21.1 %all-to-all-start = ((bf16[128,8,512]{2,0,1:T(8,128)(2,1)}), bf16[128,8,512]{2,0,1:T(8,128)(2,1)S(1)}, u32[]{:S(2)}, u32[]{:S(2)}) async-start(bf16[128,8,512]{2,0,1:T(8,128)(2,1)} %copy.174), calls=%async_computation | async-start | bytes 2097152 | tf_op jit(solution)/shard_map/all_to_all | solution.py:106
  19.3 42.5 %copy-start.18 = (f32[128,64]{1,0:T(8,128)}, f32[128,64]{1,0:T(8,128)S(1)}, u32[]{:S(2)}) copy-start(f32[128,64]{1,0:T(8,128)S(1)} %get-tuple-element.75) | copy-start | bytes 98308
  19.3 42.5 %copy-start.22 = (f32[128,64]{1,0:T(8,128)}, f32[128,64]{1,0:T(8,128)S(1)}, u32[]{:S(2)}) copy-start(f32[128,64]{1,0:T(8,128)S(1)} %get-tuple-element.76) | copy-start | bytes 98308
  32.8 22.6 %copy-start.29 = (bf16[128,8,512]{2,0,1:T(8,128)(2,1)}, bf16[128,8,512]{2,0,1:T(8,128)(2,1)S(1)}, u32[]{:S(2)}) copy-start(bf16[128,8,512]{2,0,1:T(8,128)(2,1)S(1)} %all-to-all-done) | copy-start | bytes 3145732
  55.5 29.0 %all-to-all-start.1 = ((bf16[8,128,1024]{2,1,0:T(8,128)(2,1)}), bf16[8,128,1024]{2,1,0:T(8,128)(2,1)}, u32[]{:S(2)}, u32[]{:S(2)}) async-start(bf16[8,128,1024]{2,1,0:T(8,128)(2,1)} %bitcast.583), calls=%async_computation.1 | async-start | bytes 4194304 | tf_op jit(solution)/shard_map/all_to_all | solution.py:85
  67.8 20.7 %copy-start.19 = (f32[128,64]{1,0:T(8,128)S(1)}, f32[128,64]{1,0:T(8,128)}, u32[]{:S(2)}) copy-start(f32[128,64]{1,0:T(8,128)} %copy-done.18) | copy-start | bytes 98308
  67.9 20.7 %copy-start.23 = (f32[128,64]{1,0:T(8,128)S(1)}, f32[128,64]{1,0:T(8,128)}, u32[]{:S(2)}) copy-start(f32[128,64]{1,0:T(8,128)} %copy-done.22) | copy-start | bytes 98308
  88.7 32.0 %copy-start.13 = (bf16[128,4,64]{2,0,1:T(8,128)(2,1)}, bf16[128,4,64]{2,0,1:T(8,128)(2,1)S(1)}, u32[]{:S(2)}) copy-start(bf16[128,4,64]{2,0,1:T(8,128)(2,1)S(1)} %get-tuple-element.47) | copy-start | bytes 196612
  88.9 59.0 %copy-start.16 = (bf16[128,512]{0,1:T(8,128)(2,1)}, bf16[128,512]{0,1:T(8,128)(2,1)S(1)}, u32[]{:S(2)}) copy-start(bf16[128,512]{0,1:T(8,128)(2,1)S(1)} %copy.179) | copy-start | bytes 393220
  89.8 27.0 %collective-permute-start = (bf16[2,128,4,128]{3,1,2,0:T(8,128)(2,1)}, bf16[2,128,4,128]{3,1,2,0:T(8,128)(2,1)}, u32[]{:S(2)}, u32[]{:S(2)}) collective-permute-start(bf16[2,128,4,128]{3,1,2,0:T(8,128)(2,1)} %pad_maximum_fusion.2), channel_id=1, source_target_pairs={{0,4},{4,8},{8,12},{12,16},{16,20},{20,24},{24,28},{28,32},{32,36}... | collective-permute-start | bytes 786440 | tf_op jit(solution)/shard_map/ppermute | solution.py:27
  92.6 33.7 %collective-permute-start.2 = (bf16[2,128,4,128]{3,1,2,0:T(8,128)(2,1)}, bf16[2,128,4,128]{3,1,2,0:T(8,128)(2,1)S(1)}, u32[]{:S(2)}, u32[]{:S(2)}) collective-permute-start(bf16[2,128,4,128]{3,1,2,0:T(8,128)(2,1)} %pad_maximum_fusion.2), channel_id=1, source_target_pairs={{0,12},{4,16},{8,20},{12,24},{16,28},{20,32},{24,36},{28,40},{32,4... | collective-permute-start | bytes 786440 | tf_op jit(solution)/shard_map/ppermute | solution.py:27
  97.0 39.9 %collective-permute-start.3 = (bf16[2,128,4,128]{3,1,2,0:T(8,128)(2,1)}, bf16[2,128,4,128]{3,1,2,0:T(8,128)(2,1)}, u32[]{:S(2)}, u32[]{:S(2)}) collective-permute-start(bf16[2,128,4,128]{3,1,2,0:T(8,128)(2,1)} %pad_maximum_fusion.2), channel_id=1, source_target_pairs={{0,16},{4,20},{8,24},{12,28},{16,32},{20,36},{24,40},{28,44},{32,4... | collective-permute-start | bytes 786440 | tf_op jit(solution)/shard_map/ppermute | solution.py:27
  104.4 33.8 %collective-permute-start.4 = (bf16[2,128,4,128]{3,1,2,0:T(8,128)(2,1)}, bf16[2,128,4,128]{3,1,2,0:T(8,128)(2,1)}, u32[]{:S(2)}, u32[]{:S(2)}) collective-permute-start(bf16[2,128,4,128]{3,1,2,0:T(8,128)(2,1)} %pad_maximum_fusion.2), channel_id=1, source_target_pairs={{0,20},{4,24},{8,28},{12,32},{16,36},{20,40},{24,44},{28,48},{32,5... | collective-permute-start | bytes 786440 | tf_op jit(solution)/shard_map/ppermute | solution.py:27
  108.7 35.5 %collective-permute-start.5 = (bf16[2,128,4,128]{3,1,2,0:T(8,128)(2,1)}, bf16[2,128,4,128]{3,1,2,0:T(8,128)(2,1)S(1)}, u32[]{:S(2)}, u32[]{:S(2)}) collective-permute-start(bf16[2,128,4,128]{3,1,2,0:T(8,128)(2,1)} %pad_maximum_fusion.2), channel_id=1, source_target_pairs={{0,24},{4,28},{8,32},{12,36},{16,40},{20,44},{24,48},{28,52},{32,5... | collective-permute-start | bytes 786440 | tf_op jit(solution)/shard_map/ppermute | solution.py:27
  115.6 10.7 %copy-start.44 = (pred[128,128]{0,1:T(8,128)(4,1)S(1)}, pred[128,128]{0,1:T(8,128)(4,1)}, u32[]{:S(2)}) copy-start(pred[128,128]{0,1:T(8,128)(4,1)} %get-tuple-element.71) | copy-start | bytes 49156
  116.8 20.1 %copy-start.43 = (pred[128,128]{0,1:T(8,128)(4,1)S(1)}, pred[128,128]{0,1:T(8,128)(4,1)}, u32[]{:S(2)}) copy-start(pred[128,128]{0,1:T(8,128)(4,1)} %get-tuple-element.72) | copy-start | bytes 49156
  116.8 27.8 %collective-permute-start.1 = (bf16[2,128,4,128]{3,1,2,0:T(8,128)(2,1)}, bf16[2,128,4,128]{3,1,2,0:T(8,128)(2,1)S(1)}, u32[]{:S(2)}, u32[]{:S(2)}) collective-permute-start(bf16[2,128,4,128]{3,1,2,0:T(8,128)(2,1)} %pad_maximum_fusion.2), channel_id=1, source_target_pairs={{0,8},{4,12},{8,16},{12,20},{16,24},{20,28},{24,32},{28,36},{32,40... | collective-permute-start | bytes 786440 | tf_op jit(solution)/shard_map/ppermute | solution.py:27
  120.7 17.5 %copy-start.42 = (pred[128,128]{0,1:T(8,128)(4,1)S(1)}, pred[128,128]{0,1:T(8,128)(4,1)}, u32[]{:S(2)}) copy-start(pred[128,128]{0,1:T(8,128)(4,1)} %get-tuple-element.73) | copy-start | bytes 49156
  126.3 34.2 %copy-start.35 = (bf16[2,128,4,128]{3,1,2,0:T(8,128)(2,1)}, bf16[2,128,4,128]{3,1,2,0:T(8,128)(2,1)S(1)}, u32[]{:S(2)}) copy-start(bf16[2,128,4,128]{3,1,2,0:T(8,128)(2,1)S(1)} %collective-permute-done.2) | copy-start | bytes 786436
  138.2 6.5 %copy-start.41 = (pred[128,128]{0,1:T(8,128)(4,1)S(1)}, pred[128,128]{0,1:T(8,128)(4,1)}, u32[]{:S(2)}) copy-start(pred[128,128]{0,1:T(8,128)(4,1)} %get-tuple-element.70) | copy-start | bytes 49156
  144.2 31.8 %copy-start.33 = (bf16[2,128,4,128]{3,1,2,0:T(8,128)(2,1)}, bf16[2,128,4,128]{3,1,2,0:T(8,128)(2,1)S(1)}, u32[]{:S(2)}) copy-start(bf16[2,128,4,128]{3,1,2,0:T(8,128)(2,1)S(1)} %collective-permute-done.5) | copy-start | bytes 786436
  144.6 12.2 %copy-start.31 = (bf16[2,128,4,128]{3,1,2,0:T(8,128)(2,1)}, bf16[2,128,4,128]{3,1,2,0:T(8,128)(2,1)S(1)}, u32[]{:S(2)}) copy-start(bf16[2,128,4,128]{3,1,2,0:T(8,128)(2,1)S(1)} %collective-permute-done.1) | copy-start | bytes 786436
  154.8 22.6 %collective-permute-start.6 = (bf16[2,128,4,128]{3,1,2,0:T(8,128)(2,1)S(1)}, bf16[2,128,4,128]{3,1,2,0:T(8,128)(2,1)S(1)}, u32[]{:S(2)}, u32[]{:S(2)}) collective-permute-start(bf16[2,128,4,128]{3,1,2,0:T(8,128)(2,1)S(1)} %pad_maximum_fusion.3), channel_id=1, source_target_pairs={{4,0},{8,4},{12,8},{16,12},{20,16},{24,20},{28,24},{32,28},{36,32}... | collective-permute-start | bytes 786440 | tf_op jit(solution)/shard_map/ppermute | solution.py:27
  157.1 4.0 %copy-start.8 = (bf16[4,4,128,128]{2,3,1,0:T(8,128)(2,1)}, bf16[4,4,128,128]{2,3,1,0:T(8,128)(2,1)S(1)}, u32[]{:S(2)}) copy-start(bf16[4,4,128,128]{2,3,1,0:T(8,128)(2,1)S(1)} %fusion.49) | copy-start | bytes 1572868
  157.4 22.8 %collective-permute-start.7 = (bf16[2,128,4,128]{3,1,2,0:T(8,128)(2,1)S(1)}, bf16[2,128,4,128]{3,1,2,0:T(8,128)(2,1)S(1)}, u32[]{:S(2)}, u32[]{:S(2)}) collective-permute-start(bf16[2,128,4,128]{3,1,2,0:T(8,128)(2,1)S(1)} %pad_maximum_fusion.4), channel_id=1, source_target_pairs={{8,0},{12,4},{16,8},{20,12},{24,16},{28,20},{32,24},{36,28},{40,32... | collective-permute-start | bytes 786440 | tf_op jit(solution)/shard_map/ppermute | solution.py:27
  161.2 30.8 %collective-permute-start.8 = (bf16[2,128,4,128]{3,1,2,0:T(8,128)(2,1)S(1)}, bf16[2,128,4,128]{3,1,2,0:T(8,128)(2,1)S(1)}, u32[]{:S(2)}, u32[]{:S(2)}) collective-permute-start(bf16[2,128,4,128]{3,1,2,0:T(8,128)(2,1)S(1)} %pad_maximum_fusion.5), channel_id=1, source_target_pairs={{12,0},{16,4},{20,8},{24,12},{28,16},{32,20},{36,24},{40,28},{44,3... | collective-permute-start | bytes 786440 | tf_op jit(solution)/shard_map/ppermute | solution.py:27
  168.6 5.2 %copy-start = (bf16[4,4,128,128]{2,3,1,0:T(8,128)(2,1)}, bf16[4,4,128,128]{2,3,1,0:T(8,128)(2,1)S(1)}, u32[]{:S(2)}) copy-start(bf16[4,4,128,128]{2,3,1,0:T(8,128)(2,1)S(1)} %fusion.51) | copy-start | bytes 1572868
  169.0 25.3 %collective-permute-start.9 = (bf16[2,128,4,128]{3,1,2,0:T(8,128)(2,1)S(1)}, bf16[2,128,4,128]{3,1,2,0:T(8,128)(2,1)S(1)}, u32[]{:S(2)}, u32[]{:S(2)}) collective-permute-start(bf16[2,128,4,128]{3,1,2,0:T(8,128)(2,1)S(1)} %pad_maximum_fusion.6), channel_id=1, source_target_pairs={{16,0},{20,4},{24,8},{28,12},{32,16},{36,20},{40,24},{44,28},{48,3... | collective-permute-start | bytes 786440 | tf_op jit(solution)/shard_map/ppermute | solution.py:27
  173.9 28.5 %collective-permute-start.10 = (bf16[2,128,4,128]{3,1,2,0:T(8,128)(2,1)S(1)}, bf16[2,128,4,128]{3,1,2,0:T(8,128)(2,1)S(1)}, u32[]{:S(2)}, u32[]{:S(2)}) collective-permute-start(bf16[2,128,4,128]{3,1,2,0:T(8,128)(2,1)S(1)} %pad_maximum_fusion.7), channel_id=1, source_target_pairs={{20,0},{24,4},{28,8},{32,12},{36,16},{40,20},{44,24},{48,28},{52,3... | collective-permute-start | bytes 786440 | tf_op jit(solution)/shard_map/ppermute | solution.py:27
  177.5 29.8 %collective-permute-start.11 = (bf16[2,128,4,128]{3,1,2,0:T(8,128)(2,1)S(1)}, bf16[2,128,4,128]{3,1,2,0:T(8,128)(2,1)S(1)}, u32[]{:S(2)}, u32[]{:S(2)}) collective-permute-start(bf16[2,128,4,128]{3,1,2,0:T(8,128)(2,1)S(1)} %pad_maximum_fusion.8), channel_id=1, source_target_pairs={{24,0},{28,4},{32,8},{36,12},{40,16},{44,20},{48,24},{52,28},{56,3... | collective-permute-start | bytes 786440 | tf_op jit(solution)/shard_map/ppermute | solution.py:27
  179.9 27.6 %copy-start.20 = (f32[128,64]{1,0:T(8,128)S(1)}, f32[128,64]{1,0:T(8,128)}, u32[]{:S(2)}) copy-start(f32[128,64]{1,0:T(8,128)} %copy-done.18) | copy-start | bytes 98308
  179.9 27.6 %copy-start.24 = (f32[128,64]{1,0:T(8,128)S(1)}, f32[128,64]{1,0:T(8,128)}, u32[]{:S(2)}) copy-start(f32[128,64]{1,0:T(8,128)} %copy-done.22) | copy-start | bytes 98308
  180.3 27.5 %copy-start.48 = (f32[1,128]{1,0:T(1,128)S(1)}, f32[1,128]{1,0:T(1,128)}, u32[]{:S(2)}) copy-start(f32[1,128]{1,0:T(1,128)} %param.15) | copy-start | bytes 1540
  207.6 3.8 %copy-start.27 = (bf16[128,1024]{1,0:T(8,128)(2,1)S(1)}, bf16[128,1024]{1,0:T(8,128)(2,1)}, u32[]{:S(2)}) copy-start(bf16[128,1024]{1,0:T(8,128)(2,1)} %copy-done.26) | copy-start | bytes 786436
  207.6 3.8 %copy-start.28 = (f32[128,512]{1,0:T(8,128)S(1)}, f32[128,512]{1,0:T(8,128)}, u32[]{:S(2)}) copy-start(f32[128,512]{1,0:T(8,128)} %copy.236) | copy-start | bytes 786436
  207.6 3.8 %copy-start.46 = (f32[512]{0:T(512)S(1)}, f32[512]{0:T(512)}, u32[]{:S(2)}) copy-start(f32[512]{0:T(512)} %broadcast_bitcast_fusion.1) | copy-start | bytes 6148
  213.4 9.4 %copy-start.38 = (f32[128,16]{1,0:T(8,128)S(1)}, f32[128,16]{1,0:T(8,128)}, u32[]{:S(2)}) copy-start(f32[128,16]{1,0:T(8,128)} %copy-done.37) | copy-start | bytes 24580
  213.4 33.6 %all-to-all-start.2 = ((bf16[8,128,1024]{1,2,0:T(8,128)(2,1)}), bf16[8,128,1024]{1,2,0:T(8,128)(2,1)}, u32[]{:S(2)}, u32[]{:S(2)}) async-start(bf16[8,128,1024]{1,2,0:T(8,128)(2,1)} %broadcast_in_dim.60), calls=%async_computation.2 | async-start | bytes 4194304 | tf_op jit(solution)/shard_map/all_to_all | solution.py:79
  225.8 25.1 %copy-start.51 = (bf16[512,1024]{1,0:T(8,128)(2,1)S(1)}, bf16[512,1024]{1,0:T(8,128)(2,1)}, u32[]{:S(2)}) copy-start(bf16[512,1024]{1,0:T(8,128)(2,1)} %all-gather.2.cloned.1.call-done) | copy-start | bytes 3145732
  250.9 3.9 %copy-start.14 = (bf16[128,4,64]{2,0,1:T(8,128)(2,1)S(1)}, bf16[128,4,64]{2,0,1:T(8,128)(2,1)}, u32[]{:S(2)}) copy-start(bf16[128,4,64]{2,0,1:T(8,128)(2,1)} %copy-done.13) | copy-start | bytes 196612
  254.9 8.0 %copy-start.30 = (bf16[128,8,512]{2,0,1:T(8,128)(2,1)S(1)}, bf16[128,8,512]{2,0,1:T(8,128)(2,1)}, u32[]{:S(2)}) copy-start(bf16[128,8,512]{2,0,1:T(8,128)(2,1)} %copy-done.29) | copy-start | bytes 3145732
  256.3 22.6 %all-to-all-start.3 = ((bf16[8,128,512]{2,1,0:T(8,128)(2,1)}), bf16[8,128,512]{2,1,0:T(8,128)(2,1)}, u32[]{:S(2)}, u32[]{:S(2)}) async-start(bf16[8,128,512]{2,1,0:T(8,128)(2,1)} %bitcast.591), calls=%async_computation.3 | async-start | bytes 2097152 | tf_op jit(solution)/shard_map/all_to_all | solution.py:220
  262.9 55.6 %reduce-scatter.4.cloned.1.call-start = ((), (), s32[]{:S(2)}) async-start(), calls=%async_computation.6 | async-start | bytes 1179648
  278.8 12.6 %collective-permute-start.12 = (bf16[8,128,512]{2,1,0:T(8,128)(2,1)}, bf16[8,128,512]{2,1,0:T(8,128)(2,1)}, u32[]{:S(2)}, u32[]{:S(2)}) collective-permute-start(bf16[8,128,512]{2,1,0:T(8,128)(2,1)} %all-to-all-done.3), channel_id=1, source_target_pairs={{0,3},{1,0},{2,1},{3,2},{4,7},{5,4},{6,5},{7,6},{8,11},{9,8},{10,9... | collective-permute-start | bytes 3145736 | tf_op jit(solution)/shard_map/ppermute | solution.py:32
  282.0 3.6 %copy-start.10 = (f32[1,128,2048]{2,1,0:T(8,128)S(1)}, f32[1,128,2048]{2,1,0:T(8,128)}, u32[]{:S(2)}) copy-start(f32[1,128,2048]{2,1,0:T(8,128)} %mul.518) | copy-start | bytes 3145732
  282.0 3.6 %copy-start.11 = (f32[1,128,2048]{2,1,0:T(8,128)S(1)}, f32[1,128,2048]{2,1,0:T(8,128)}, u32[]{:S(2)}) copy-start(f32[1,128,2048]{2,1,0:T(8,128)} %mul.632) | copy-start | bytes 3145732
  (23 other events, 46.2 us)
Sparse Core Ops, SparseCore 0:
  10.3 41.2 all-gather.1
  269.2 49.2 reduce-scatter.3

commit v8 on v7

--- a/solution.py
+++ b/solution.py
@@ -205,14 +205,11 @@
     value_back = kv_total[1].reshape(tok_rows, kv_width).astype(jnp.bfloat16)
     both_back = jnp.concatenate([key_back, value_back], 1)
     group_back = gathered(both_back, "cb", row_parts)
-    grad_rows = lax.psum_scatter(
-        lax.dot_general(
-            inputs_slice, group_back, (((0,), (0,)), ((), ())), preferred_element_type=jnp.float32
-        ).astype(jnp.bfloat16),
-        "cz",
-        scatter_dimension=0,
-        tiled=True,
-    ).astype(jnp.float32)
+    weight_part = lax.dot_general(
+        inputs_slice, group_back, (((0,), (0,)), ((), ())), preferred_element_type=jnp.float32
+    )
+    weight_part, group_back = lax.optimization_barrier((weight_part, group_back))
+    grad_rows = lax.psum_scatter(weight_part, "cz", scatter_dimension=0, tiled=True)
     slice_grad = lax.dot_general(
         group_back, weight_slice, (((1,), (1,)), ((), ())), preferred_element_type=jnp.float32
     ).astype(jnp.bfloat16)

time: 330 us -> 323 us (0.979)
  the two profiles are of different devices: /device:TPU:10 before, /device:TPU:33 now
where the time goes in v8:
time: 323 us; the launch traced here: 321 us
  waiting for transfers between devices  126 us (39%)
  starting transfers between devices  73.7 us (23%)
  local copies, waits for them, and re-layouts  46.9 us (15%)
  matrix products  39.4 us (12%)
  other arithmetic  19.9 us (6%)
  between operations  15.4 us (5%)
    ppermute x12, waiting for transfers between devices, passed_along(): return lax.ppermute(block, axis, route)  51.8 us
    ppermute x12, starting transfers between devices, passed_along(): return lax.ppermute(block, axis, route)  37.2 us
    all_to_all x1, waiting for transfers between devices, gathered(): received = lax.all_to_all(copies, axis, 0, 0, tiled=True)  24.5 us
    all_to_all x1, waiting for transfers between devices, summed_over(): received = lax.all_to_all(pieces, axis, 0, 0, tiled=True)  19.8 us
    all_to_all x1, starting transfers between devices, gathered(): received = lax.all_to_all(copies, axis, 0, 0, tiled=True)  17.7 us
    unnamed x104, local copies, waits for them, and re-layouts  13.8 us
    all_to_all x1, waiting for transfers between devices, local(): inputs_slice = lax.all_to_all(tokens_here, 'cb', 1, 0, tiled=True)  13 us
    all_gather x1, waiting for transfers between devices, local(): weight_slice = lax.all_gather(both_rows, 'cz', axis=0, tiled=True)  12.2 us
  transfers between devices with their start and end apart: 19, of which 10 were waited for; matrix products, arithmetic and copies ran while one was open for 20% of the time, Pallas kernels for 0%

profile of v8, /device:TPU:33, one launch (start us, length us, event | category | flops | bytes accessed | tf_op | source)
XLA Modules:
  0.0 320.9 jit_solution(2434407535018803221)
XLA Ops:
  7.2 1.5 pad_maximum_fusion.11
  8.8 1.6 copy.173
  10.4 1.3 copy.174
  11.7 6.7 %all-to-all-start = ((bf16[128,8,512]{2,0,1:T(8,128)(2,1)}), bf16[128,8,512]{2,0,1:T(8,128)(2,1)S(1)}, u32[]{:S(2)}, u32[]{:S(2)}) async-start(bf16[128,8,512]{2,0,1:T(8,128)(2,1)} %copy.174), calls=%async_computation | async-start | bytes 2097152 | tf_op jit(solution)/shard_map/all_to_all | solution.py:106
  21.0 13.0 %all-to-all-done = bf16[128,8,512]{2,0,1:T(8,128)(2,1)S(1)} async-done(((bf16[128,8,512]{2,0,1:T(8,128)(2,1)}), bf16[128,8,512]{2,0,1:T(8,128)(2,1)S(1)}, u32[]{:S(2)}, u32[]{:S(2)}) %all-to-all-start) | async-done | bytes 1048608 | tf_op jit(solution)/shard_map/all_to_all | solution.py:106
  34.0 12.2 %all-gather.2.cloned.1.call-done = bf16[512,1024]{1,0:T(8,128)(2,1)} async-done(((bf16[64,1024]{1,0:T(8,128)(2,1)}), bf16[512,1024]{1,0:T(8,128)(2,1)}) %all-gather.2.cloned.1.call-update) | async-done | bytes 1048592 | tf_op jit(solution)/shard_map/all_gather | solution.py:105
  46.2 3.9 %convolution_convert_fusion = bf16[1024,1024]{0,1:T(8,128)(2,1)} fusion(bf16[1024,512]{1,0:T(8,128)(2,1)S(1)} %bitcast.588, bf16[512,1024]{1,0:T(8,128)(2,1)} %all-gather.2.cloned.1.call-done), kind=kOutput, calls=%fused_computation | convolution fusion | flops 1074790400 | bytes 4194304 | tf_op jit(solution)/shard_map/dot_general | solution.py:108
  50.1 6.4 %all-to-all-start.1 = ((bf16[8,128,1024]{2,1,0:T(8,128)(2,1)}), bf16[8,128,1024]{2,1,0:T(8,128)(2,1)}, u32[]{:S(2)}, u32[]{:S(2)}) async-start(bf16[8,128,1024]{2,1,0:T(8,128)(2,1)} %bitcast.579), calls=%async_computation.1 | async-start | bytes 4194304 | tf_op jit(solution)/shard_map/all_to_all | solution.py:85
  62.6 19.8 %all-to-all-done.1 = bf16[8,128,1024]{2,1,0:T(8,128)(2,1)} async-done(((bf16[8,128,1024]{2,1,0:T(8,128)(2,1)}), bf16[8,128,1024]{2,1,0:T(8,128)(2,1)}, u32[]{:S(2)}, u32[]{:S(2)}) %all-to-all-start.1) | async-done | bytes 2097184 | tf_op jit(solution)/shard_map/all_to_all | solution.py:85
  82.3 2.0 reduce
  87.8 2.3 collective-permute-start
  90.1 4.2 %collective-permute-start.2 = (bf16[2,128,4,128]{3,1,2,0:T(8,128)(2,1)}, bf16[2,128,4,128]{3,1,2,0:T(8,128)(2,1)S(1)}, u32[]{:S(2)}, u32[]{:S(2)}) collective-permute-start(bf16[2,128,4,128]{3,1,2,0:T(8,128)(2,1)} %pad_maximum_fusion.2), channel_id=1, source_target_pairs={{0,12},{4,16},{8,20},{12,24},{16,28},{20,32},{24,36},{28,40},{32,4... | collective-permute-start | bytes 786440 | tf_op jit(solution)/shard_map/ppermute | solution.py:27
  94.3 3.2 collective-permute-start.3
  97.4 4.4 %collective-permute-start.4 = (bf16[2,128,4,128]{3,1,2,0:T(8,128)(2,1)}, bf16[2,128,4,128]{3,1,2,0:T(8,128)(2,1)}, u32[]{:S(2)}, u32[]{:S(2)}) collective-permute-start(bf16[2,128,4,128]{3,1,2,0:T(8,128)(2,1)} %pad_maximum_fusion.2), channel_id=1, source_target_pairs={{0,20},{4,24},{8,28},{12,32},{16,36},{20,40},{24,44},{28,48},{32,5... | collective-permute-start | bytes 786440 | tf_op jit(solution)/shard_map/ppermute | solution.py:27
  101.9 7.0 %collective-permute-start.5 = (bf16[2,128,4,128]{3,1,2,0:T(8,128)(2,1)}, bf16[2,128,4,128]{3,1,2,0:T(8,128)(2,1)}, u32[]{:S(2)}, u32[]{:S(2)}) collective-permute-start(bf16[2,128,4,128]{3,1,2,0:T(8,128)(2,1)} %pad_maximum_fusion.2), channel_id=1, source_target_pairs={{0,24},{4,28},{8,32},{12,36},{16,40},{20,44},{24,48},{28,52},{32,5... | collective-permute-start | bytes 786440 | tf_op jit(solution)/shard_map/ppermute | solution.py:27
  110.4 1.4 copy.237
  113.0 3.4 %collective-permute-start.1 = (bf16[2,128,4,128]{3,1,2,0:T(8,128)(2,1)}, bf16[2,128,4,128]{3,1,2,0:T(8,128)(2,1)S(1)}, u32[]{:S(2)}, u32[]{:S(2)}) collective-permute-start(bf16[2,128,4,128]{3,1,2,0:T(8,128)(2,1)} %pad_maximum_fusion.2), channel_id=1, source_target_pairs={{0,8},{4,12},{8,16},{12,20},{16,24},{20,28},{24,32},{28,36},{32,40... | collective-permute-start | bytes 786440 | tf_op jit(solution)/shard_map/ppermute | solution.py:27
  119.8 9.9 %collective-permute-done.5 = bf16[2,128,4,128]{3,1,2,0:T(8,128)(2,1)} collective-permute-done((bf16[2,128,4,128]{3,1,2,0:T(8,128)(2,1)}, bf16[2,128,4,128]{3,1,2,0:T(8,128)(2,1)}, u32[]{:S(2)}, u32[]{:S(2)}) %collective-permute-start.5) | collective-permute-done | bytes 262176 | tf_op jit(solution)/shard_map/ppermute | solution.py:27
  141.2 6.0 %collective-permute-start.6 = (bf16[2,128,4,128]{3,1,2,0:T(8,128)(2,1)S(1)}, bf16[2,128,4,128]{3,1,2,0:T(8,128)(2,1)S(1)}, u32[]{:S(2)}, u32[]{:S(2)}) collective-permute-start(bf16[2,128,4,128]{3,1,2,0:T(8,128)(2,1)S(1)} %pad_maximum_fusion.3), channel_id=1, source_target_pairs={{4,0},{8,4},{12,8},{16,12},{20,16},{24,20},{28,24},{32,28},{36,32}... | collective-permute-start | bytes 786440 | tf_op jit(solution)/shard_map/ppermute | solution.py:27
  154.6 1.4 collective-permute-start.10
  158.5 1.5 collective-permute-start.11
  160.6 15.4 %collective-permute-done.8 = bf16[2,128,4,128]{3,1,2,0:T(8,128)(2,1)S(1)} collective-permute-done((bf16[2,128,4,128]{3,1,2,0:T(8,128)(2,1)S(1)}, bf16[2,128,4,128]{3,1,2,0:T(8,128)(2,1)S(1)}, u32[]{:S(2)}, u32[]{:S(2)}) %collective-permute-start.8) | collective-permute-done | bytes 262176 | tf_op jit(solution)/shard_map/ppermute | solution.py:27
  176.0 21.4 %collective-permute-done.9 = bf16[2,128,4,128]{3,1,2,0:T(8,128)(2,1)S(1)} collective-permute-done((bf16[2,128,4,128]{3,1,2,0:T(8,128)(2,1)S(1)}, bf16[2,128,4,128]{3,1,2,0:T(8,128)(2,1)S(1)}, u32[]{:S(2)}, u32[]{:S(2)}) %collective-permute-start.9) | collective-permute-done | bytes 262176 | tf_op jit(solution)/shard_map/ppermute | solution.py:27
  197.4 5.2 %collective-permute-done.11 = bf16[2,128,4,128]{3,1,2,0:T(8,128)(2,1)S(1)} collective-permute-done((bf16[2,128,4,128]{3,1,2,0:T(8,128)(2,1)S(1)}, bf16[2,128,4,128]{3,1,2,0:T(8,128)(2,1)S(1)}, u32[]{:S(2)}, u32[]{:S(2)}) %collective-permute-start.11) | collective-permute-done | bytes 262176 | tf_op jit(solution)/shard_map/ppermute | solution.py:27
  207.1 1.6 broadcast_in_dim.60
  208.7 17.7 %all-to-all-start.2 = ((bf16[8,128,1024]{1,2,0:T(8,128)(2,1)}), bf16[8,128,1024]{1,2,0:T(8,128)(2,1)}, u32[]{:S(2)}, u32[]{:S(2)}) async-start(bf16[8,128,1024]{1,2,0:T(8,128)(2,1)} %broadcast_in_dim.60), calls=%async_computation.2 | async-start | bytes 4194304 | tf_op jit(solution)/shard_map/all_to_all | solution.py:79
  226.5 1.3 mul.517
  227.8 1.4 mul.518
  229.2 1.3 mul.631
  230.5 2.3 mul.632
  232.8 24.5 %all-to-all-done.2 = bf16[8,128,1024]{1,2,0:T(8,128)(2,1)} async-done(((bf16[8,128,1024]{1,2,0:T(8,128)(2,1)}), bf16[8,128,1024]{1,2,0:T(8,128)(2,1)}, u32[]{:S(2)}, u32[]{:S(2)}) %all-to-all-start.2) | async-done | bytes 2097184 | tf_op jit(solution)/shard_map/all_to_all | solution.py:79
  257.3 3.9 %copy.243 = bf16[8,128,1024]{2,1,0:T(8,128)(2,1)} copy(bf16[8,128,1024]{1,2,0:T(8,128)(2,1)} %all-to-all-done.2) | data formatting | bytes 4194304 | tf_op jit(solution)/shard_map/all_to_all | solution.py:79
  261.2 4.5 %convolution_bitcast_fusion = f32[512,1024]{0,1:T(8,128)} fusion(bf16[8,128,1024]{1,2,0:T(8,128)(2,1)} %all-to-all-done.2, bf16[128,8,512]{2,0,1:T(8,128)(2,1)} %copy-done.27), kind=kOutput, calls=%fused_computation.1 | convolution fusion | flops 1073741824 | bytes 5242880 | tf_op jit(solution)/shard_map/dot_general | solution.py:208
  265.7 2.9 copy.383
  269.2 4.2 %convolution_convert_fusion.1 = bf16[1024,512]{1,0:T(8,128)(2,1)} fusion(bf16[1024,1024]{1,0:T(8,128)(2,1)} %bitcast.580, bf16[512,1024]{1,0:T(8,128)(2,1)} %all-gather.2.cloned.1.call-done), kind=kOutput, calls=%fused_computation.2 | convolution fusion | flops 1074266112 | bytes 4194304 | tf_op jit(solution)/shard_map/dot_general | solution.py:213
  273.4 4.4 %all-to-all-start.3 = ((bf16[8,128,512]{2,1,0:T(8,128)(2,1)}), bf16[8,128,512]{2,1,0:T(8,128)(2,1)}, u32[]{:S(2)}, u32[]{:S(2)}) async-start(bf16[8,128,512]{2,1,0:T(8,128)(2,1)} %bitcast.589), calls=%async_computation.3 | async-start | bytes 2097152 | tf_op jit(solution)/shard_map/all_to_all | solution.py:217
  278.3 1.3 fusion.97
  281.4 1.3 fusion.100
  285.6 1.6 copy.385
  287.2 2.4 copy.386
  289.6 2.8 multiply_add_fusion
  294.6 2.2 multiply_reduce_fusion
  296.8 1.3 mul.636
  298.1 2.5 mul.637
  301.7 3.0 fusion.88
  304.7 3.5 %collective-permute-done.12 = bf16[8,128,512]{2,1,0:T(8,128)(2,1)} collective-permute-done((bf16[8,128,512]{2,1,0:T(8,128)(2,1)}, bf16[8,128,512]{2,1,0:T(8,128)(2,1)}, u32[]{:S(2)}, u32[]{:S(2)}) %collective-permute-start.12) | collective-permute-done | bytes 1048608 | tf_op jit(solution)/shard_map/ppermute | solution.py:32
  308.2 1.8 copy.260
  310.0 1.3 broadcast_in_dim_reshape.3
  (222 shorter events, 55.7 us)
Async XLA Ops:
  7.2 39.0 %all-gather.2.cloned.1.call-start = ((), (), s32[]{:S(2)}) async-start(), calls=%async_computation.5 | async-start | bytes 1179648 | tf_op jit(solution)/shard_map/all_gather | solution.py:105
  10.4 8.0 %copy-start.13 = (bf16[1,128,2048]{2,1,0:T(8,128)(2,1)S(1)}, bf16[1,128,2048]{2,1,0:T(8,128)(2,1)}, u32[]{:S(2)}) copy-start(bf16[1,128,2048]{2,1,0:T(8,128)(2,1)} %param.9) | copy-start | bytes 1572868
  11.7 22.3 %all-to-all-start = ((bf16[128,8,512]{2,0,1:T(8,128)(2,1)}), bf16[128,8,512]{2,0,1:T(8,128)(2,1)S(1)}, u32[]{:S(2)}, u32[]{:S(2)}) async-start(bf16[128,8,512]{2,0,1:T(8,128)(2,1)} %copy.174), calls=%async_computation | async-start | bytes 2097152 | tf_op jit(solution)/shard_map/all_to_all | solution.py:106
  19.4 37.1 %copy-start.16 = (f32[128,64]{1,0:T(8,128)}, f32[128,64]{1,0:T(8,128)S(1)}, u32[]{:S(2)}) copy-start(f32[128,64]{1,0:T(8,128)S(1)} %get-tuple-element.79) | copy-start | bytes 98308
  19.4 37.1 %copy-start.20 = (f32[128,64]{1,0:T(8,128)}, f32[128,64]{1,0:T(8,128)S(1)}, u32[]{:S(2)}) copy-start(f32[128,64]{1,0:T(8,128)S(1)} %get-tuple-element.80) | copy-start | bytes 98308
  34.0 16.1 %copy-start.27 = (bf16[128,8,512]{2,0,1:T(8,128)(2,1)}, bf16[128,8,512]{2,0,1:T(8,128)(2,1)S(1)}, u32[]{:S(2)}) copy-start(bf16[128,8,512]{2,0,1:T(8,128)(2,1)S(1)} %all-to-all-done) | copy-start | bytes 3145732
  50.1 32.2 %all-to-all-start.1 = ((bf16[8,128,1024]{2,1,0:T(8,128)(2,1)}), bf16[8,128,1024]{2,1,0:T(8,128)(2,1)}, u32[]{:S(2)}, u32[]{:S(2)}) async-start(bf16[8,128,1024]{2,1,0:T(8,128)(2,1)} %bitcast.579), calls=%async_computation.1 | async-start | bytes 4194304 | tf_op jit(solution)/shard_map/all_to_all | solution.py:85
  62.6 23.9 %copy-start.17 = (f32[128,64]{1,0:T(8,128)S(1)}, f32[128,64]{1,0:T(8,128)}, u32[]{:S(2)}) copy-start(f32[128,64]{1,0:T(8,128)} %copy-done.16) | copy-start | bytes 98308
  62.6 23.9 %copy-start.21 = (f32[128,64]{1,0:T(8,128)S(1)}, f32[128,64]{1,0:T(8,128)}, u32[]{:S(2)}) copy-start(f32[128,64]{1,0:T(8,128)} %copy-done.20) | copy-start | bytes 98308
  86.7 31.0 %copy-start.11 = (bf16[128,4,64]{2,0,1:T(8,128)(2,1)}, bf16[128,4,64]{2,0,1:T(8,128)(2,1)S(1)}, u32[]{:S(2)}) copy-start(bf16[128,4,64]{2,0,1:T(8,128)(2,1)S(1)} %get-tuple-element.49) | copy-start | bytes 196612
  86.8 47.5 %copy-start.14 = (bf16[128,512]{0,1:T(8,128)(2,1)}, bf16[128,512]{0,1:T(8,128)(2,1)S(1)}, u32[]{:S(2)}) copy-start(bf16[128,512]{0,1:T(8,128)(2,1)S(1)} %copy.179) | copy-start | bytes 393220
  87.8 25.2 %collective-permute-start = (bf16[2,128,4,128]{3,1,2,0:T(8,128)(2,1)}, bf16[2,128,4,128]{3,1,2,0:T(8,128)(2,1)}, u32[]{:S(2)}, u32[]{:S(2)}) collective-permute-start(bf16[2,128,4,128]{3,1,2,0:T(8,128)(2,1)} %pad_maximum_fusion.2), channel_id=1, source_target_pairs={{0,4},{4,8},{8,12},{12,16},{16,20},{20,24},{24,28},{28,32},{32,36}... | collective-permute-start | bytes 786440 | tf_op jit(solution)/shard_map/ppermute | solution.py:27
  90.1 27.6 %collective-permute-start.2 = (bf16[2,128,4,128]{3,1,2,0:T(8,128)(2,1)}, bf16[2,128,4,128]{3,1,2,0:T(8,128)(2,1)S(1)}, u32[]{:S(2)}, u32[]{:S(2)}) collective-permute-start(bf16[2,128,4,128]{3,1,2,0:T(8,128)(2,1)} %pad_maximum_fusion.2), channel_id=1, source_target_pairs={{0,12},{4,16},{8,20},{12,24},{16,28},{20,32},{24,36},{28,40},{32,4... | collective-permute-start | bytes 786440 | tf_op jit(solution)/shard_map/ppermute | solution.py:27
  94.3 23.8 %collective-permute-start.3 = (bf16[2,128,4,128]{3,1,2,0:T(8,128)(2,1)}, bf16[2,128,4,128]{3,1,2,0:T(8,128)(2,1)S(1)}, u32[]{:S(2)}, u32[]{:S(2)}) collective-permute-start(bf16[2,128,4,128]{3,1,2,0:T(8,128)(2,1)} %pad_maximum_fusion.2), channel_id=1, source_target_pairs={{0,16},{4,20},{8,24},{12,28},{16,32},{20,36},{24,40},{28,44},{32,4... | collective-permute-start | bytes 786440 | tf_op jit(solution)/shard_map/ppermute | solution.py:27
  97.4 21.1 %collective-permute-start.4 = (bf16[2,128,4,128]{3,1,2,0:T(8,128)(2,1)}, bf16[2,128,4,128]{3,1,2,0:T(8,128)(2,1)}, u32[]{:S(2)}, u32[]{:S(2)}) collective-permute-start(bf16[2,128,4,128]{3,1,2,0:T(8,128)(2,1)} %pad_maximum_fusion.2), channel_id=1, source_target_pairs={{0,20},{4,24},{8,28},{12,32},{16,36},{20,40},{24,44},{28,48},{32,5... | collective-permute-start | bytes 786440 | tf_op jit(solution)/shard_map/ppermute | solution.py:27
  101.9 27.8 %collective-permute-start.5 = (bf16[2,128,4,128]{3,1,2,0:T(8,128)(2,1)}, bf16[2,128,4,128]{3,1,2,0:T(8,128)(2,1)}, u32[]{:S(2)}, u32[]{:S(2)}) collective-permute-start(bf16[2,128,4,128]{3,1,2,0:T(8,128)(2,1)} %pad_maximum_fusion.2), channel_id=1, source_target_pairs={{0,24},{4,28},{8,32},{12,36},{16,40},{20,44},{24,48},{28,52},{32,5... | collective-permute-start | bytes 786440 | tf_op jit(solution)/shard_map/ppermute | solution.py:27
  111.8 5.9 %copy-start.40 = (pred[128,128]{0,1:T(8,128)(4,1)S(1)}, pred[128,128]{0,1:T(8,128)(4,1)}, u32[]{:S(2)}) copy-start(pred[128,128]{0,1:T(8,128)(4,1)} %get-tuple-element.75) | copy-start | bytes 49156
  113.0 5.1 %copy-start.39 = (pred[128,128]{0,1:T(8,128)(4,1)S(1)}, pred[128,128]{0,1:T(8,128)(4,1)}, u32[]{:S(2)}) copy-start(pred[128,128]{0,1:T(8,128)(4,1)} %get-tuple-element.76) | copy-start | bytes 49156
  113.0 18.0 %collective-permute-start.1 = (bf16[2,128,4,128]{3,1,2,0:T(8,128)(2,1)}, bf16[2,128,4,128]{3,1,2,0:T(8,128)(2,1)S(1)}, u32[]{:S(2)}, u32[]{:S(2)}) collective-permute-start(bf16[2,128,4,128]{3,1,2,0:T(8,128)(2,1)} %pad_maximum_fusion.2), channel_id=1, source_target_pairs={{0,8},{4,12},{8,16},{12,20},{16,24},{20,28},{24,32},{28,36},{32,40... | collective-permute-start | bytes 786440 | tf_op jit(solution)/shard_map/ppermute | solution.py:27
  117.7 31.5 %copy-start.30 = (bf16[2,128,4,128]{3,1,2,0:T(8,128)(2,1)}, bf16[2,128,4,128]{3,1,2,0:T(8,128)(2,1)S(1)}, u32[]{:S(2)}) copy-start(bf16[2,128,4,128]{3,1,2,0:T(8,128)(2,1)S(1)} %collective-permute-done.2) | copy-start | bytes 786436
  118.1 33.0 %copy-start.31 = (bf16[2,128,4,128]{3,1,2,0:T(8,128)(2,1)}, bf16[2,128,4,128]{3,1,2,0:T(8,128)(2,1)S(1)}, u32[]{:S(2)}) copy-start(bf16[2,128,4,128]{3,1,2,0:T(8,128)(2,1)S(1)} %collective-permute-done.3) | copy-start | bytes 786436
  118.5 12.5 %copy-start.37 = (pred[128,128]{0,1:T(8,128)(4,1)S(1)}, pred[128,128]{0,1:T(8,128)(4,1)}, u32[]{:S(2)}) copy-start(pred[128,128]{0,1:T(8,128)(4,1)} %get-tuple-element.74) | copy-start | bytes 49156
  131.0 16.2 %copy-start.28 = (bf16[2,128,4,128]{3,1,2,0:T(8,128)(2,1)}, bf16[2,128,4,128]{3,1,2,0:T(8,128)(2,1)S(1)}, u32[]{:S(2)}) copy-start(bf16[2,128,4,128]{3,1,2,0:T(8,128)(2,1)S(1)} %collective-permute-done.1) | copy-start | bytes 786436
  140.9 6.9 %copy-start.6 = (bf16[4,4,128,128]{2,3,1,0:T(8,128)(2,1)}, bf16[4,4,128,128]{2,3,1,0:T(8,128)(2,1)S(1)}, u32[]{:S(2)}) copy-start(bf16[4,4,128,128]{2,3,1,0:T(8,128)(2,1)S(1)} %fusion.47) | copy-start | bytes 1572868
  141.2 17.2 %collective-permute-start.6 = (bf16[2,128,4,128]{3,1,2,0:T(8,128)(2,1)S(1)}, bf16[2,128,4,128]{3,1,2,0:T(8,128)(2,1)S(1)}, u32[]{:S(2)}, u32[]{:S(2)}) collective-permute-start(bf16[2,128,4,128]{3,1,2,0:T(8,128)(2,1)S(1)} %pad_maximum_fusion.3), channel_id=1, source_target_pairs={{4,0},{8,4},{12,8},{16,12},{20,16},{24,20},{28,24},{32,28},{36,32}... | collective-permute-start | bytes 786440 | tf_op jit(solution)/shard_map/ppermute | solution.py:27
  147.9 12.7 %collective-permute-start.7 = (bf16[2,128,4,128]{3,1,2,0:T(8,128)(2,1)S(1)}, bf16[2,128,4,128]{3,1,2,0:T(8,128)(2,1)S(1)}, u32[]{:S(2)}, u32[]{:S(2)}) collective-permute-start(bf16[2,128,4,128]{3,1,2,0:T(8,128)(2,1)S(1)} %pad_maximum_fusion.4), channel_id=1, source_target_pairs={{8,0},{12,4},{16,8},{20,12},{24,16},{28,20},{32,24},{36,28},{40,32... | collective-permute-start | bytes 786440 | tf_op jit(solution)/shard_map/ppermute | solution.py:27
  149.8 26.2 %collective-permute-start.8 = (bf16[2,128,4,128]{3,1,2,0:T(8,128)(2,1)S(1)}, bf16[2,128,4,128]{3,1,2,0:T(8,128)(2,1)S(1)}, u32[]{:S(2)}, u32[]{:S(2)}) collective-permute-start(bf16[2,128,4,128]{3,1,2,0:T(8,128)(2,1)S(1)} %pad_maximum_fusion.5), channel_id=1, source_target_pairs={{12,0},{16,4},{20,8},{24,12},{28,16},{32,20},{36,24},{40,28},{44,3... | collective-permute-start | bytes 786440 | tf_op jit(solution)/shard_map/ppermute | solution.py:27
  151.4 3.2 copy-start
  151.8 45.6 %collective-permute-start.9 = (bf16[2,128,4,128]{3,1,2,0:T(8,128)(2,1)S(1)}, bf16[2,128,4,128]{3,1,2,0:T(8,128)(2,1)S(1)}, u32[]{:S(2)}, u32[]{:S(2)}) collective-permute-start(bf16[2,128,4,128]{3,1,2,0:T(8,128)(2,1)S(1)} %pad_maximum_fusion.6), channel_id=1, source_target_pairs={{16,0},{20,4},{24,8},{28,12},{32,16},{36,20},{40,24},{44,28},{48,3... | collective-permute-start | bytes 786440 | tf_op jit(solution)/shard_map/ppermute | solution.py:27
  154.3 3.3 %copy-start.2 = (bf16[4,4,128,128]{2,3,1,0:T(8,128)(2,1)}, bf16[4,4,128,128]{2,3,1,0:T(8,128)(2,1)S(1)}, u32[]{:S(2)}) copy-start(bf16[4,4,128,128]{2,3,1,0:T(8,128)(2,1)S(1)} %fusion.51) | copy-start | bytes 1572868
  154.6 3.5 %copy-start.15 = (bf16[128,512]{0,1:T(8,128)(2,1)S(1)}, bf16[128,512]{0,1:T(8,128)(2,1)}, u32[]{:S(2)}) copy-start(bf16[128,512]{0,1:T(8,128)(2,1)} %copy-done.14) | copy-start | bytes 393220
  154.6 42.7 %collective-permute-start.10 = (bf16[2,128,4,128]{3,1,2,0:T(8,128)(2,1)S(1)}, bf16[2,128,4,128]{3,1,2,0:T(8,128)(2,1)S(1)}, u32[]{:S(2)}, u32[]{:S(2)}) collective-permute-start(bf16[2,128,4,128]{3,1,2,0:T(8,128)(2,1)S(1)} %pad_maximum_fusion.7), channel_id=1, source_target_pairs={{20,0},{24,4},{28,8},{32,12},{36,16},{40,20},{44,24},{48,28},{52,3... | collective-permute-start | bytes 786440 | tf_op jit(solution)/shard_map/ppermute | solution.py:27
  158.5 44.1 %collective-permute-start.11 = (bf16[2,128,4,128]{3,1,2,0:T(8,128)(2,1)S(1)}, bf16[2,128,4,128]{3,1,2,0:T(8,128)(2,1)S(1)}, u32[]{:S(2)}, u32[]{:S(2)}) collective-permute-start(bf16[2,128,4,128]{3,1,2,0:T(8,128)(2,1)S(1)} %pad_maximum_fusion.8), channel_id=1, source_target_pairs={{24,0},{28,4},{32,8},{36,12},{40,16},{44,20},{48,24},{52,28},{56,3... | collective-permute-start | bytes 786440 | tf_op jit(solution)/shard_map/ppermute | solution.py:27
  160.3 42.6 %copy-start.18 = (f32[128,64]{1,0:T(8,128)S(1)}, f32[128,64]{1,0:T(8,128)}, u32[]{:S(2)}) copy-start(f32[128,64]{1,0:T(8,128)} %copy-done.16) | copy-start | bytes 98308
  160.3 42.6 %copy-start.22 = (f32[128,64]{1,0:T(8,128)S(1)}, f32[128,64]{1,0:T(8,128)}, u32[]{:S(2)}) copy-start(f32[128,64]{1,0:T(8,128)} %copy-done.20) | copy-start | bytes 98308
  160.6 42.5 %copy-start.44 = (f32[1,128]{1,0:T(1,128)S(1)}, f32[1,128]{1,0:T(1,128)}, u32[]{:S(2)}) copy-start(f32[1,128]{1,0:T(1,128)} %param.15) | copy-start | bytes 1540
  202.9 3.8 %copy-start.25 = (bf16[128,1024]{1,0:T(8,128)(2,1)S(1)}, bf16[128,1024]{1,0:T(8,128)(2,1)}, u32[]{:S(2)}) copy-start(bf16[128,1024]{1,0:T(8,128)(2,1)} %copy-done.24) | copy-start | bytes 786436
  202.9 3.8 %copy-start.26 = (f32[128,512]{1,0:T(8,128)S(1)}, f32[128,512]{1,0:T(8,128)}, u32[]{:S(2)}) copy-start(f32[128,512]{1,0:T(8,128)} %copy.236) | copy-start | bytes 786436
  202.9 3.8 %copy-start.42 = (f32[512]{0:T(512)S(1)}, f32[512]{0:T(512)}, u32[]{:S(2)}) copy-start(f32[512]{0:T(512)} %broadcast_bitcast_fusion.1) | copy-start | bytes 6148
  208.7 17.7 %copy-start.34 = (f32[128,16]{1,0:T(8,128)S(1)}, f32[128,16]{1,0:T(8,128)}, u32[]{:S(2)}) copy-start(f32[128,16]{1,0:T(8,128)} %copy-done.33) | copy-start | bytes 24580
  208.7 48.6 %all-to-all-start.2 = ((bf16[8,128,1024]{1,2,0:T(8,128)(2,1)}), bf16[8,128,1024]{1,2,0:T(8,128)(2,1)}, u32[]{:S(2)}, u32[]{:S(2)}) async-start(bf16[8,128,1024]{1,2,0:T(8,128)(2,1)} %broadcast_in_dim.60), calls=%async_computation.2 | async-start | bytes 4194304 | tf_op jit(solution)/shard_map/all_to_all | solution.py:79
  226.4 84.9 %reduce-scatter.4.cloned.1.call-start = ((), (), s32[]{:S(2)}) async-start(), calls=%async_computation.6 | async-start | bytes 2359296
  273.4 4.4 %copy-start.12 = (bf16[128,4,64]{2,0,1:T(8,128)(2,1)S(1)}, bf16[128,4,64]{2,0,1:T(8,128)(2,1)}, u32[]{:S(2)}) copy-start(bf16[128,4,64]{2,0,1:T(8,128)(2,1)} %copy-done.11) | copy-start | bytes 196612
  273.4 19.9 %all-to-all-start.3 = ((bf16[8,128,512]{2,1,0:T(8,128)(2,1)}), bf16[8,128,512]{2,1,0:T(8,128)(2,1)}, u32[]{:S(2)}, u32[]{:S(2)}) async-start(bf16[8,128,512]{2,1,0:T(8,128)(2,1)} %bitcast.589), calls=%async_computation.3 | async-start | bytes 2097152 | tf_op jit(solution)/shard_map/all_to_all | solution.py:217
  285.6 4.0 %copy-start.19 = (f32[128,64]{1,0:T(8,128)S(1)}, f32[128,64]{1,0:T(8,128)}, u32[]{:S(2)}) copy-start(f32[128,64]{1,0:T(8,128)} %copy-done.16) | copy-start | bytes 98308
  285.6 4.0 %copy-start.23 = (f32[128,64]{1,0:T(8,128)S(1)}, f32[128,64]{1,0:T(8,128)}, u32[]{:S(2)}) copy-start(f32[128,64]{1,0:T(8,128)} %copy-done.20) | copy-start | bytes 98308
  293.3 14.8 %collective-permute-start.12 = (bf16[8,128,512]{2,1,0:T(8,128)(2,1)}, bf16[8,128,512]{2,1,0:T(8,128)(2,1)}, u32[]{:S(2)}, u32[]{:S(2)}) collective-permute-start(bf16[8,128,512]{2,1,0:T(8,128)(2,1)} %all-to-all-done.3), channel_id=1, source_target_pairs={{0,3},{1,0},{2,1},{3,2},{4,7},{5,4},{6,5},{7,6},{8,11},{9,8},{10,9... | collective-permute-start | bytes 3145736 | tf_op jit(solution)/shard_map/ppermute | solution.py:32
  298.1 3.6 %copy-start.10 = (f32[1,128,2048]{2,1,0:T(8,128)S(1)}, f32[1,128,2048]{2,1,0:T(8,128)}, u32[]{:S(2)}) copy-start(f32[1,128,2048]{2,1,0:T(8,128)} %mul.632) | copy-start | bytes 3145732
  (18 other events, 30.5 us)
Sparse Core Ops, SparseCore 0:
  10.3 35.8 all-gather.1
  268.7 35.9 reduce-scatter.3

commit v9 on v8

--- a/solution.py
+++ b/solution.py
@@ -167,12 +167,10 @@
         return (prob_tile, out_tile)
 
     zero_query = jnp.zeros((tok_rows, kv_heads, group, HEAD), jnp.float32)
-    prob_list = []
-    attn_out = zero_query
-    for distance in range(reach_blocks + 1):
-        prob_tile, out_tile = guarded(prob_block, (key_blocks[distance], allowed_list[distance]))
-        prob_list.append(prob_tile)
-        attn_out = attn_out + out_tile
+    prob_all, attn_out = prob_block(jnp.concatenate(key_blocks, 1), jnp.concatenate(allowed_list, 1))
+    prob_list = [
+        prob_all[..., d * tok_rows : (d + 1) * tok_rows] for d in range(reach_blocks + 1)
+    ]
     row_delta = jnp.sum(out_grad.astype(jnp.float32) * attn_out, -1).transpose(1, 2, 0)[..., None]
 
     def grad_block(key_pair, prob_tile):
@@ -191,10 +189,12 @@
 
     zero_pair = jnp.zeros((2, tok_rows, kv_heads, HEAD), jnp.float32)
     kv_total = zero_pair
-    score_list = []
+    score_all, kv_all = grad_block(jnp.concatenate(key_blocks, 1), prob_all)
+    score_list = [
+        score_all[..., d * tok_rows : (d + 1) * tok_rows] for d in range(reach_blocks + 1)
+    ]
     for distance in range(reach_blocks + 1):
-        score_grad, kv_part = guarded(grad_block, (key_blocks[distance], prob_list[distance]))
-        score_list.append(score_grad)
+        kv_part = kv_all[:, distance * tok_rows : (distance + 1) * tok_rows]
         if distance == 0:
             kv_total = kv_part
         else:
@@ -217,18 +217,15 @@
     input_grad = lax.all_to_all(
         slice_grad.reshape(row_parts, tok_rows, slice_grad.shape[1]), "cb", 0, 0, tiled=True
     )
-    query_rot_grad = zero_query
-    for distance in range(reach_blocks + 1):
-        query_part = (
-            jnp.einsum(
-                "grqk,kgd->qgrd",
-                score_list[distance],
-                key_blocks[distance][0],
-                preferred_element_type=jnp.float32,
-            )
-            * score_scale
-        )
-        query_rot_grad = query_rot_grad + query_part
+    query_rot_grad = (
+        jnp.einsum(
+            "grqk,kgd->qgrd",
+            jnp.concatenate(score_list, -1),
+            jnp.concatenate([pair[0] for pair in key_blocks], 0),
+            preferred_element_type=jnp.float32,
+        )
+        * score_scale
+    )
     query_grad = normalize_back(
         query_in,
         query_inv,

time: 323 us -> 331 us (1.025)
  matrix products: 39.4 us -> 22.4 us
  local copies, waits for them, and re-layouts: 46.9 us -> 60.1 us
  starting transfers between devices: 73.7 us -> 80.6 us
  waiting for transfers between devices: 126 us -> 130 us
    all_gather x1, waiting for transfers between devices: 12.2 us -> 23.8 us  [local(): weight_slice = lax.all_gather(both_rows, 'cz', axis=0, tiled=True)]
    all_to_all x1, waiting for transfers between devices: 24.5 us -> 15.3 us  [gathered(): received = lax.all_to_all(copies, axis, 0, 0, tiled=True)]
    unnamed x104 -> x106, local copies, waits for them, and re-layouts: 13.8 us -> 22 us
    all_to_all x1, waiting for transfers between devices: 19.8 us -> 13.6 us  [summed_over(): received = lax.all_to_all(pieces, axis, 0, 0, tiled=True)]
    unnamed x1 -> x9, other arithmetic: 0.09 us -> 5.36 us
    ppermute x12, waiting for transfers between devices: 51.8 us -> 57 us  [passed_along(): return lax.ppermute(block, axis, route)]
    all_to_all x1, waiting for transfers between devices: 0.93 us -> 5.9 us  [local(): lax.all_to_all(slice_grad.reshape(row_parts, tok_rows, slice_grad.shape[1...]
    ppermute x12, starting transfers between devices: 37.2 us -> 41.9 us  [passed_along(): return lax.ppermute(block, axis, route)]
  transfers between devices with their start and end apart: 19 -> 19, of which waited for: 10 -> 11; matrix products, arithmetic and copies ran while one was open for 20% -> 20% of each run, Pallas kernels for 0% -> 0%
where the time goes in v9:
time: 331 us; the launch traced here: 329 us
  waiting for transfers between devices  130 us (39%)
  starting transfers between devices  80.6 us (24%)
  local copies, waits for them, and re-layouts  60.1 us (18%)
  matrix products  22.4 us (7%)
  other arithmetic  20.8 us (6%)
  between operations  15.1 us (5%)
    ppermute x12, waiting for transfers between devices, passed_along(): return lax.ppermute(block, axis, route)  57 us
    ppermute x12, starting transfers between devices, passed_along(): return lax.ppermute(block, axis, route)  41.9 us
    all_gather x1, waiting for transfers between devices, local(): weight_slice = lax.all_gather(both_rows, 'cz', axis=0, tiled=True)  23.8 us
    unnamed x106, local copies, waits for them, and re-layouts  22 us
    all_to_all x1, starting transfers between devices, gathered(): received = lax.all_to_all(copies, axis, 0, 0, tiled=True)  19 us
    all_to_all x1, waiting for transfers between devices, gathered(): received = lax.all_to_all(copies, axis, 0, 0, tiled=True)  15.3 us
    all_to_all x1, waiting for transfers between devices, summed_over(): received = lax.all_to_all(pieces, axis, 0, 0, tiled=True)  13.6 us
    all_to_all x1, waiting for transfers between devices, local(): inputs_slice = lax.all_to_all(tokens_here, 'cb', 1, 0, tiled=True)  11.2 us
  transfers between devices with their start and end apart: 19, of which 11 were waited for; matrix products, arithmetic and copies ran while one was open for 20% of the time, Pallas kernels for 0%

profile of v9, /device:TPU:33, one launch (start us, length us, event | category | flops | bytes accessed | tf_op | source)
XLA Modules:
  0.0 329.0 jit_solution(15358538127846965591)
XLA Ops:
  7.2 1.6 copy.65
  10.1 6.7 %all-to-all-start = ((bf16[128,8,512]{2,0,1:T(8,128)(2,1)}), bf16[128,8,512]{2,0,1:T(8,128)(2,1)S(1)}, u32[]{:S(2)}, u32[]{:S(2)}) async-start(bf16[128,8,512]{2,0,1:T(8,128)(2,1)} %copy.66), calls=%async_computation | async-start | bytes 2097152 | tf_op jit(solution)/shard_map/all_to_all | solution.py:106
  21.2 11.2 %all-to-all-done = bf16[128,8,512]{2,0,1:T(8,128)(2,1)S(1)} async-done(((bf16[128,8,512]{2,0,1:T(8,128)(2,1)}), bf16[128,8,512]{2,0,1:T(8,128)(2,1)S(1)}, u32[]{:S(2)}, u32[]{:S(2)}) %all-to-all-start) | async-done | bytes 1048608 | tf_op jit(solution)/shard_map/all_to_all | solution.py:106
  32.4 23.8 %all-gather.2.cloned.1.call-done = bf16[512,1024]{1,0:T(8,128)(2,1)} async-done(((bf16[64,1024]{1,0:T(8,128)(2,1)}), bf16[512,1024]{1,0:T(8,128)(2,1)}) %all-gather.2.cloned.1.call-update) | async-done | bytes 1048592 | tf_op jit(solution)/shard_map/all_gather | solution.py:105
  56.2 3.8 %convolution_convert_fusion = bf16[1024,1024]{0,1:T(8,128)(2,1)} fusion(bf16[1024,512]{1,0:T(8,128)(2,1)S(1)} %bitcast.266, bf16[512,1024]{1,0:T(8,128)(2,1)} %all-gather.2.cloned.1.call-done), kind=kOutput, calls=%fused_computation.10 | convolution fusion | flops 1074790400 | bytes 4194304 | tf_op jit(solution)/shard_map/dot_general | solution.py:108
  60.0 6.4 %all-to-all-start.1 = ((bf16[8,128,1024]{2,1,0:T(8,128)(2,1)}), bf16[8,128,1024]{2,1,0:T(8,128)(2,1)S(1)}, u32[]{:S(2)}, u32[]{:S(2)}) async-start(bf16[8,128,1024]{2,1,0:T(8,128)(2,1)} %bitcast.258), calls=%async_computation.1 | async-start | bytes 4194304 | tf_op jit(solution)/shard_map/all_to_all | solution.py:85
  66.5 2.0 copy.71
  68.5 2.0 copy.72
  70.4 2.0 copy.73
  78.5 13.6 %all-to-all-done.1 = bf16[8,128,1024]{2,1,0:T(8,128)(2,1)S(1)} async-done(((bf16[8,128,1024]{2,1,0:T(8,128)(2,1)}), bf16[8,128,1024]{2,1,0:T(8,128)(2,1)S(1)}, u32[]{:S(2)}, u32[]{:S(2)}) %all-to-all-start.1) | async-done | bytes 2097184 | tf_op jit(solution)/shard_map/all_to_all | solution.py:85
  93.5 2.7 collective-permute-start
  96.6 4.2 %collective-permute-start.1 = (bf16[2,128,4,128]{3,1,2,0:T(8,128)(2,1)S(1)}, bf16[2,128,4,128]{3,1,2,0:T(8,128)(2,1)S(1)}, u32[]{:S(2)}, u32[]{:S(2)}) collective-permute-start(bf16[2,128,4,128]{3,1,2,0:T(8,128)(2,1)S(1)} %get-tuple-element.41), channel_id=1, source_target_pairs={{0,8},{4,12},{8,16},{12,20},{16,24},{20,28},{24,32},{28,36},{32,40... | collective-permute-start | bytes 786440 | tf_op jit(solution)/shard_map/ppermute | solution.py:27
  100.8 2.7 collective-permute-start.2
  103.5 2.5 collective-permute-start.3
  106.0 8.4 %collective-permute-start.4 = (bf16[2,128,4,128]{3,1,2,0:T(8,128)(2,1)S(1)}, bf16[2,128,4,128]{3,1,2,0:T(8,128)(2,1)S(1)}, u32[]{:S(2)}, u32[]{:S(2)}) collective-permute-start(bf16[2,128,4,128]{3,1,2,0:T(8,128)(2,1)S(1)} %get-tuple-element.41), channel_id=1, source_target_pairs={{0,20},{4,24},{8,28},{12,32},{16,36},{20,40},{24,44},{28,48},{32,5... | collective-permute-start | bytes 786440 | tf_op jit(solution)/shard_map/ppermute | solution.py:27
  115.6 3.1 collective-permute-start.5
  119.5 11.4 %collective-permute-done.2 = bf16[2,128,4,128]{3,1,2,0:T(8,128)(2,1)S(1)} collective-permute-done((bf16[2,128,4,128]{3,1,2,0:T(8,128)(2,1)S(1)}, bf16[2,128,4,128]{3,1,2,0:T(8,128)(2,1)S(1)}, u32[]{:S(2)}, u32[]{:S(2)}) %collective-permute-start.2) | collective-permute-done | bytes 262176 | tf_op jit(solution)/shard_map/ppermute | solution.py:27
  132.1 4.6 %collective-permute-done.5 = bf16[2,128,4,128]{3,1,2,0:T(8,128)(2,1)S(1)} collective-permute-done((bf16[2,128,4,128]{3,1,2,0:T(8,128)(2,1)S(1)}, bf16[2,128,4,128]{3,1,2,0:T(8,128)(2,1)S(1)}, u32[]{:S(2)}, u32[]{:S(2)}) %collective-permute-start.5) | collective-permute-done | bytes 262176 | tf_op jit(solution)/shard_map/ppermute | solution.py:27
  137.4 2.9 fusion.3
  150.1 12.0 %collective-permute-start.6 = (bf16[2,128,4,128]{3,1,2,0:T(8,128)(2,1)}, bf16[2,128,4,128]{3,1,2,0:T(8,128)(2,1)}, u32[]{:S(2)}, u32[]{:S(2)}) collective-permute-start(bf16[2,128,4,128]{3,1,2,0:T(8,128)(2,1)} %get-tuple-element.51), channel_id=1, source_target_pairs={{4,0},{8,4},{12,8},{16,12},{20,16},{24,20},{28,24},{32,28},{36,32}... | collective-permute-start | bytes 786440 | tf_op jit(solution)/shard_map/ppermute | solution.py:27
  164.7 10.4 %collective-permute-done.10 = bf16[2,128,4,128]{3,1,2,0:T(8,128)(2,1)} collective-permute-done((bf16[2,128,4,128]{3,1,2,0:T(8,128)(2,1)S(1)}, bf16[2,128,4,128]{3,1,2,0:T(8,128)(2,1)}, u32[]{:S(2)}, u32[]{:S(2)}) %collective-permute-start.10) | collective-permute-done | bytes 262176 | tf_op jit(solution)/shard_map/ppermute | solution.py:27
  177.0 1.8 copy.85
  179.6 15.9 %collective-permute-done.11 = bf16[2,128,4,128]{3,1,2,0:T(8,128)(2,1)} collective-permute-done((bf16[2,128,4,128]{3,1,2,0:T(8,128)(2,1)}, bf16[2,128,4,128]{3,1,2,0:T(8,128)(2,1)}, u32[]{:S(2)}, u32[]{:S(2)}) %collective-permute-start.11) | collective-permute-done | bytes 262176 | tf_op jit(solution)/shard_map/ppermute | solution.py:27
  195.5 14.7 %collective-permute-done.9 = bf16[2,128,4,128]{3,1,2,0:T(8,128)(2,1)} collective-permute-done((bf16[2,128,4,128]{3,1,2,0:T(8,128)(2,1)}, bf16[2,128,4,128]{3,1,2,0:T(8,128)(2,1)}, u32[]{:S(2)}, u32[]{:S(2)}) %collective-permute-start.9) | collective-permute-done | bytes 262176 | tf_op jit(solution)/shard_map/ppermute | solution.py:27
  210.2 1.7 fusion.47
  213.8 1.6 broadcast_in_dim.56
  215.4 19.0 %all-to-all-start.2 = ((bf16[8,128,1024]{1,2,0:T(8,128)(2,1)}), bf16[8,128,1024]{1,2,0:T(8,128)(2,1)S(1)}, u32[]{:S(2)}, u32[]{:S(2)}) async-start(bf16[8,128,1024]{1,2,0:T(8,128)(2,1)} %broadcast_in_dim.56), calls=%async_computation.2 | async-start | bytes 4194304 | tf_op jit(solution)/shard_map/all_to_all | solution.py:79
  235.9 2.4 mul.442
  238.4 2.2 mul.533
  240.5 2.4 mul.534
  243.7 1.6 bitcast_dynamic-update-slice_fusion.5
  245.3 1.6 bitcast_dynamic-update-slice_fusion.4
  248.4 15.3 %all-to-all-done.2 = bf16[8,128,1024]{1,2,0:T(8,128)(2,1)S(1)} async-done(((bf16[8,128,1024]{1,2,0:T(8,128)(2,1)}), bf16[8,128,1024]{1,2,0:T(8,128)(2,1)S(1)}, u32[]{:S(2)}, u32[]{:S(2)}) %all-to-all-start.2) | async-done | bytes 2097184 | tf_op jit(solution)/shard_map/all_to_all | solution.py:79
  263.8 2.7 copy.92
  266.4 3.9 %convolution_bitcast_fusion = f32[512,1024]{0,1:T(8,128)} fusion(bf16[8,128,1024]{1,2,0:T(8,128)(2,1)S(1)} %all-to-all-done.2, bf16[128,8,512]{2,0,1:T(8,128)(2,1)} %copy-done.15), kind=kOutput, calls=%fused_computation.13 | convolution fusion | flops 1073741824 | bytes 5242880 | tf_op jit(solution)/shard_map/dot_general | solution.py:208
  270.3 2.9 copy.125
  276.2 3.5 %fusion.94 = (bf16[4,4,128,128]{2,3,1,0:T(8,128)(2,1)S(1)}, bf16[4,4,128,128]{2,3,1,0:T(8,128)(2,1)S(1)}, bf16[4,4,128,128]{2,3,1,0:T(8,128)(2,1)S(1)}, bf16[4,4...) fusion(bf16[4,4,128,896]{2,3,1,0:T(8,128)(2,1)} %copy-done), kind=kLoop, calls=%fused_computation.219 | loop fusion | bytes 7340032 | tf_op jit(solution)/shard_map/slice | solution.py:194
  279.7 2.3 convolution_convert_fusion.1
  281.9 4.2 %all-to-all-start.3 = ((bf16[8,128,512]{2,1,0:T(8,128)(2,1)}), bf16[8,128,512]{2,1,0:T(8,128)(2,1)}, u32[]{:S(2)}, u32[]{:S(2)}) async-start(bf16[8,128,512]{2,1,0:T(8,128)(2,1)} %bitcast.267), calls=%async_computation.3 | async-start | bytes 2097152 | tf_op jit(solution)/shard_map/all_to_all | solution.py:217
  288.9 2.0 convolution_multiply_fusion
  292.9 2.4 multiply_add_fusion
  295.3 5.9 %all-to-all-done.3 = bf16[8,128,512]{2,1,0:T(8,128)(2,1)} async-done(((bf16[8,128,512]{2,1,0:T(8,128)(2,1)}), bf16[8,128,512]{2,1,0:T(8,128)(2,1)}, u32[]{:S(2)}, u32[]{:S(2)}) %all-to-all-start.3) | async-done | bytes 1048608 | tf_op jit(solution)/shard_map/all_to_all | solution.py:217
  301.2 2.1 collective-permute-start.12
  303.3 1.9 multiply_reduce_fusion
  306.5 2.5 mul.539
  310.1 2.9 fusion.38
  313.1 3.2 collective-permute-done.12
  316.3 1.8 copy.97
  (202 shorter events, 51.8 us)
Async XLA Ops:
  8.8 8.0 %copy-start.28 = (bf16[1,64,512]{2,1,0:T(8,128)(2,1)S(1)}, bf16[1,64,512]{2,1,0:T(8,128)(2,1)}, u32[]{:S(2)}) copy-start(bf16[1,64,512]{2,1,0:T(8,128)(2,1)} %param.13) | copy-start | bytes 196612
  8.8 8.0 %copy-start.29 = (bf16[1,64,512]{2,1,0:T(8,128)(2,1)S(1)}, bf16[1,64,512]{2,1,0:T(8,128)(2,1)}, u32[]{:S(2)}) copy-start(bf16[1,64,512]{2,1,0:T(8,128)(2,1)} %param.12) | copy-start | bytes 196612
  8.8 8.8 %copy-start.6 = (bf16[1,128,2048]{2,1,0:T(8,128)(2,1)S(1)}, bf16[1,128,2048]{2,1,0:T(8,128)(2,1)}, u32[]{:S(2)}) copy-start(bf16[1,128,2048]{2,1,0:T(8,128)(2,1)} %param.9) | copy-start | bytes 1572868
  10.1 22.3 %all-to-all-start = ((bf16[128,8,512]{2,0,1:T(8,128)(2,1)}), bf16[128,8,512]{2,0,1:T(8,128)(2,1)S(1)}, u32[]{:S(2)}, u32[]{:S(2)}) async-start(bf16[128,8,512]{2,0,1:T(8,128)(2,1)} %copy.66), calls=%async_computation | async-start | bytes 2097152 | tf_op jit(solution)/shard_map/all_to_all | solution.py:106
  16.8 39.4 %all-gather.2.cloned.1.call-start = ((), (), s32[]{:S(2)}) async-start(), calls=%async_computation.5 | async-start | bytes 1179648 | tf_op jit(solution)/shard_map/all_gather | solution.py:105
  32.4 27.6 %copy-start.15 = (bf16[128,8,512]{2,0,1:T(8,128)(2,1)}, bf16[128,8,512]{2,0,1:T(8,128)(2,1)S(1)}, u32[]{:S(2)}) copy-start(bf16[128,8,512]{2,0,1:T(8,128)(2,1)S(1)} %all-to-all-done) | copy-start | bytes 3145732
  60.0 32.1 %all-to-all-start.1 = ((bf16[8,128,1024]{2,1,0:T(8,128)(2,1)}), bf16[8,128,1024]{2,1,0:T(8,128)(2,1)S(1)}, u32[]{:S(2)}, u32[]{:S(2)}) async-start(bf16[8,128,1024]{2,1,0:T(8,128)(2,1)} %bitcast.258), calls=%async_computation.1 | async-start | bytes 4194304 | tf_op jit(solution)/shard_map/all_to_all | solution.py:85
  78.5 14.3 %copy-start.36 = (f32[1,128]{1,0:T(1,128)S(1)}, f32[1,128]{1,0:T(1,128)}, u32[]{:S(2)}) copy-start(f32[1,128]{1,0:T(1,128)} %param.15) | copy-start | bytes 1540
  92.5 3.8 %copy-start.7 = (bf16[128,16,64]{2,0,1:T(8,128)(2,1)S(1)}, bf16[128,16,64]{2,0,1:T(8,128)(2,1)}, u32[]{:S(2)}) copy-start(bf16[128,16,64]{2,0,1:T(8,128)(2,1)} %copy.71) | copy-start | bytes 786436
  92.5 3.8 %copy-start.8 = (bf16[128,16,64]{2,0,1:T(8,128)(2,1)S(1)}, bf16[128,16,64]{2,0,1:T(8,128)(2,1)}, u32[]{:S(2)}) copy-start(bf16[128,16,64]{2,0,1:T(8,128)(2,1)} %copy.72) | copy-start | bytes 786436
  93.1 22.4 %copy-start.10 = (bf16[128,4,64]{2,0,1:T(8,128)(2,1)}, bf16[128,4,64]{2,0,1:T(8,128)(2,1)S(1)}, u32[]{:S(2)}) copy-start(bf16[128,4,64]{2,0,1:T(8,128)(2,1)S(1)} %get-tuple-element.63) | copy-start | bytes 196612
  93.1 22.4 %copy-start.12 = (bf16[128,4,64]{2,0,1:T(8,128)(2,1)}, bf16[128,4,64]{2,0,1:T(8,128)(2,1)S(1)}, u32[]{:S(2)}) copy-start(bf16[128,4,64]{2,0,1:T(8,128)(2,1)S(1)} %get-tuple-element.64) | copy-start | bytes 196612
  93.4 25.3 %copy-start.30 = (pred[128,128]{0,1:T(8,128)(4,1)S(1)}, pred[128,128]{0,1:T(8,128)(4,1)}, u32[]{:S(2)}) copy-start(pred[128,128]{0,1:T(8,128)(4,1)} %get-tuple-element.90) | copy-start | bytes 49156
  93.5 22.0 %collective-permute-start = (bf16[2,128,4,128]{3,1,2,0:T(8,128)(2,1)S(1)}, bf16[2,128,4,128]{3,1,2,0:T(8,128)(2,1)S(1)}, u32[]{:S(2)}, u32[]{:S(2)}) collective-permute-start(bf16[2,128,4,128]{3,1,2,0:T(8,128)(2,1)S(1)} %get-tuple-element.41), channel_id=1, source_target_pairs={{0,4},{4,8},{8,12},{12,16},{16,20},{20,24},{24,28},{28,32},{32,36}... | collective-permute-start | bytes 786440 | tf_op jit(solution)/shard_map/ppermute | solution.py:27
  96.6 22.5 %copy-start.31 = (pred[128,128]{0,1:T(8,128)(4,1)S(1)}, pred[128,128]{0,1:T(8,128)(4,1)}, u32[]{:S(2)}) copy-start(pred[128,128]{0,1:T(8,128)(4,1)} %get-tuple-element.88) | copy-start | bytes 49156
  96.6 22.5 %collective-permute-start.1 = (bf16[2,128,4,128]{3,1,2,0:T(8,128)(2,1)S(1)}, bf16[2,128,4,128]{3,1,2,0:T(8,128)(2,1)S(1)}, u32[]{:S(2)}, u32[]{:S(2)}) collective-permute-start(bf16[2,128,4,128]{3,1,2,0:T(8,128)(2,1)S(1)} %get-tuple-element.41), channel_id=1, source_target_pairs={{0,8},{4,12},{8,16},{12,20},{16,24},{20,28},{24,32},{28,36},{32,40... | collective-permute-start | bytes 786440 | tf_op jit(solution)/shard_map/ppermute | solution.py:27
  100.8 30.1 %collective-permute-start.2 = (bf16[2,128,4,128]{3,1,2,0:T(8,128)(2,1)S(1)}, bf16[2,128,4,128]{3,1,2,0:T(8,128)(2,1)S(1)}, u32[]{:S(2)}, u32[]{:S(2)}) collective-permute-start(bf16[2,128,4,128]{3,1,2,0:T(8,128)(2,1)S(1)} %get-tuple-element.41), channel_id=1, source_target_pairs={{0,12},{4,16},{8,20},{12,24},{16,28},{20,32},{24,36},{28,40},{32,4... | collective-permute-start | bytes 786440 | tf_op jit(solution)/shard_map/ppermute | solution.py:27
  103.5 27.8 %collective-permute-start.3 = (bf16[2,128,4,128]{3,1,2,0:T(8,128)(2,1)S(1)}, bf16[2,128,4,128]{3,1,2,0:T(8,128)(2,1)S(1)}, u32[]{:S(2)}, u32[]{:S(2)}) collective-permute-start(bf16[2,128,4,128]{3,1,2,0:T(8,128)(2,1)S(1)} %get-tuple-element.41), channel_id=1, source_target_pairs={{0,16},{4,20},{8,24},{12,28},{16,32},{20,36},{24,40},{28,44},{32,4... | collective-permute-start | bytes 786440 | tf_op jit(solution)/shard_map/ppermute | solution.py:27
  106.0 25.7 %collective-permute-start.4 = (bf16[2,128,4,128]{3,1,2,0:T(8,128)(2,1)S(1)}, bf16[2,128,4,128]{3,1,2,0:T(8,128)(2,1)S(1)}, u32[]{:S(2)}, u32[]{:S(2)}) collective-permute-start(bf16[2,128,4,128]{3,1,2,0:T(8,128)(2,1)S(1)} %get-tuple-element.41), channel_id=1, source_target_pairs={{0,20},{4,24},{8,28},{12,32},{16,36},{20,40},{24,44},{28,48},{32,5... | collective-permute-start | bytes 786440 | tf_op jit(solution)/shard_map/ppermute | solution.py:27
  115.5 15.3 %copy-start.32 = (pred[128,128]{0,1:T(8,128)(4,1)S(1)}, pred[128,128]{0,1:T(8,128)(4,1)}, u32[]{:S(2)}) copy-start(pred[128,128]{0,1:T(8,128)(4,1)} %get-tuple-element.86) | copy-start | bytes 49156
  115.5 21.5 %copy-start.24 = (bf16[2,128,4,128]{3,1,2,0:T(8,128)(2,1)}, bf16[2,128,4,128]{3,1,2,0:T(8,128)(2,1)S(1)}, u32[]{:S(2)}) copy-start(bf16[2,128,4,128]{3,1,2,0:T(8,128)(2,1)S(1)} %collective-permute-done) | copy-start | bytes 786436
  115.6 21.1 %collective-permute-start.5 = (bf16[2,128,4,128]{3,1,2,0:T(8,128)(2,1)S(1)}, bf16[2,128,4,128]{3,1,2,0:T(8,128)(2,1)S(1)}, u32[]{:S(2)}, u32[]{:S(2)}) collective-permute-start(bf16[2,128,4,128]{3,1,2,0:T(8,128)(2,1)S(1)} %get-tuple-element.41), channel_id=1, source_target_pairs={{0,24},{4,28},{8,32},{12,36},{16,40},{20,44},{24,48},{28,52},{32,5... | collective-permute-start | bytes 786440 | tf_op jit(solution)/shard_map/ppermute | solution.py:27
  119.1 12.2 %copy-start.33 = (pred[128,128]{0,1:T(8,128)(4,1)S(1)}, pred[128,128]{0,1:T(8,128)(4,1)}, u32[]{:S(2)}) copy-start(pred[128,128]{0,1:T(8,128)(4,1)} %get-tuple-element.84) | copy-start | bytes 49156
  119.1 18.0 %copy-start.25 = (bf16[2,128,4,128]{3,1,2,0:T(8,128)(2,1)}, bf16[2,128,4,128]{3,1,2,0:T(8,128)(2,1)S(1)}, u32[]{:S(2)}) copy-start(bf16[2,128,4,128]{3,1,2,0:T(8,128)(2,1)S(1)} %collective-permute-done.1) | copy-start | bytes 786436
  119.5 12.2 %copy-start.34 = (pred[128,128]{0,1:T(8,128)(4,1)S(1)}, pred[128,128]{0,1:T(8,128)(4,1)}, u32[]{:S(2)}) copy-start(pred[128,128]{0,1:T(8,128)(4,1)} %get-tuple-element.82) | copy-start | bytes 49156
  130.9 6.3 %copy-start.26 = (bf16[2,128,4,128]{3,1,2,0:T(8,128)(2,1)}, bf16[2,128,4,128]{3,1,2,0:T(8,128)(2,1)S(1)}, u32[]{:S(2)}) copy-start(bf16[2,128,4,128]{3,1,2,0:T(8,128)(2,1)S(1)} %collective-permute-done.2) | copy-start | bytes 786436
  131.3 5.4 %copy-start.35 = (pred[128,128]{0,1:T(8,128)(4,1)S(1)}, pred[128,128]{0,1:T(8,128)(4,1)}, u32[]{:S(2)}) copy-start(pred[128,128]{0,1:T(8,128)(4,1)} %get-tuple-element.80) | copy-start | bytes 49156
  131.3 5.9 %copy-start.18 = (bf16[2,128,4,128]{3,1,2,0:T(8,128)(2,1)}, bf16[2,128,4,128]{3,1,2,0:T(8,128)(2,1)S(1)}, u32[]{:S(2)}) copy-start(bf16[2,128,4,128]{3,1,2,0:T(8,128)(2,1)S(1)} %collective-permute-done.3) | copy-start | bytes 786436
  131.7 5.6 %copy-start.20 = (bf16[2,128,4,128]{3,1,2,0:T(8,128)(2,1)}, bf16[2,128,4,128]{3,1,2,0:T(8,128)(2,1)S(1)}, u32[]{:S(2)}) copy-start(bf16[2,128,4,128]{3,1,2,0:T(8,128)(2,1)S(1)} %collective-permute-done.4) | copy-start | bytes 786436
  137.4 3.0 copy-start.2
  147.5 27.5 %collective-permute-start.10 = (bf16[2,128,4,128]{3,1,2,0:T(8,128)(2,1)S(1)}, bf16[2,128,4,128]{3,1,2,0:T(8,128)(2,1)}, u32[]{:S(2)}, u32[]{:S(2)}) collective-permute-start(bf16[2,128,4,128]{3,1,2,0:T(8,128)(2,1)S(1)} %get-tuple-element.53), channel_id=1, source_target_pairs={{20,0},{24,4},{28,8},{32,12},{36,16},{40,20},{44,24},{48,28},{52,3... | collective-permute-start | bytes 786440 | tf_op jit(solution)/shard_map/ppermute | solution.py:27
  148.8 46.7 %collective-permute-start.11 = (bf16[2,128,4,128]{3,1,2,0:T(8,128)(2,1)}, bf16[2,128,4,128]{3,1,2,0:T(8,128)(2,1)}, u32[]{:S(2)}, u32[]{:S(2)}) collective-permute-start(bf16[2,128,4,128]{3,1,2,0:T(8,128)(2,1)} %get-tuple-element.52), channel_id=1, source_target_pairs={{24,0},{28,4},{32,8},{36,12},{40,16},{44,20},{48,24},{52,28},{56,3... | collective-permute-start | bytes 786440 | tf_op jit(solution)/shard_map/ppermute | solution.py:27
  150.1 45.4 %collective-permute-start.6 = (bf16[2,128,4,128]{3,1,2,0:T(8,128)(2,1)}, bf16[2,128,4,128]{3,1,2,0:T(8,128)(2,1)}, u32[]{:S(2)}, u32[]{:S(2)}) collective-permute-start(bf16[2,128,4,128]{3,1,2,0:T(8,128)(2,1)} %get-tuple-element.51), channel_id=1, source_target_pairs={{4,0},{8,4},{12,8},{16,12},{20,16},{24,20},{28,24},{32,28},{36,32}... | collective-permute-start | bytes 786440 | tf_op jit(solution)/shard_map/ppermute | solution.py:27
  162.1 33.4 %collective-permute-start.7 = (bf16[2,128,4,128]{3,1,2,0:T(8,128)(2,1)}, bf16[2,128,4,128]{3,1,2,0:T(8,128)(2,1)}, u32[]{:S(2)}, u32[]{:S(2)}) collective-permute-start(bf16[2,128,4,128]{3,1,2,0:T(8,128)(2,1)} %get-tuple-element.56), channel_id=1, source_target_pairs={{8,0},{12,4},{16,8},{20,12},{24,16},{28,20},{32,24},{36,28},{40,32... | collective-permute-start | bytes 786440 | tf_op jit(solution)/shard_map/ppermute | solution.py:27
  163.4 32.1 %collective-permute-start.8 = (bf16[2,128,4,128]{3,1,2,0:T(8,128)(2,1)}, bf16[2,128,4,128]{3,1,2,0:T(8,128)(2,1)}, u32[]{:S(2)}, u32[]{:S(2)}) collective-permute-start(bf16[2,128,4,128]{3,1,2,0:T(8,128)(2,1)} %get-tuple-element.55), channel_id=1, source_target_pairs={{12,0},{16,4},{20,8},{24,12},{28,16},{32,20},{36,24},{40,28},{44,3... | collective-permute-start | bytes 786440 | tf_op jit(solution)/shard_map/ppermute | solution.py:27
  175.0 35.2 %collective-permute-start.9 = (bf16[2,128,4,128]{3,1,2,0:T(8,128)(2,1)}, bf16[2,128,4,128]{3,1,2,0:T(8,128)(2,1)}, u32[]{:S(2)}, u32[]{:S(2)}) collective-permute-start(bf16[2,128,4,128]{3,1,2,0:T(8,128)(2,1)} %get-tuple-element.54), channel_id=1, source_target_pairs={{16,0},{20,4},{24,8},{28,12},{32,16},{36,20},{40,24},{44,28},{48,3... | collective-permute-start | bytes 786440 | tf_op jit(solution)/shard_map/ppermute | solution.py:27
  215.4 19.2 %copy-start.17 = (f32[128,16]{1,0:T(8,128)S(1)}, f32[128,16]{1,0:T(8,128)}, u32[]{:S(2)}) copy-start(f32[128,16]{1,0:T(8,128)} %copy-done.16) | copy-start | bytes 24580
  215.4 48.4 %all-to-all-start.2 = ((bf16[8,128,1024]{1,2,0:T(8,128)(2,1)}), bf16[8,128,1024]{1,2,0:T(8,128)(2,1)S(1)}, u32[]{:S(2)}, u32[]{:S(2)}) async-start(bf16[8,128,1024]{1,2,0:T(8,128)(2,1)} %broadcast_in_dim.56), calls=%async_computation.2 | async-start | bytes 4194304 | tf_op jit(solution)/shard_map/all_to_all | solution.py:79
  234.4 85.0 %reduce-scatter.4.cloned.1.call-start = ((), (), s32[]{:S(2)}) async-start(), calls=%async_computation.6 | async-start | bytes 2359296
  238.3 4.6 %copy-start.38 = (f32[1,128]{1,0:T(1,128)S(1)}, f32[1,128]{1,0:T(1,128)}, u32[]{:S(2)}) copy-start(f32[1,128]{1,0:T(1,128)} %param.14) | copy-start | bytes 1540
  238.3 4.6 %copy-start.11 = (bf16[128,4,64]{2,0,1:T(8,128)(2,1)S(1)}, bf16[128,4,64]{2,0,1:T(8,128)(2,1)}, u32[]{:S(2)}) copy-start(bf16[128,4,64]{2,0,1:T(8,128)(2,1)} %copy-done.10) | copy-start | bytes 196612
  238.4 4.6 %copy-start.13 = (bf16[128,4,64]{2,0,1:T(8,128)(2,1)S(1)}, bf16[128,4,64]{2,0,1:T(8,128)(2,1)}, u32[]{:S(2)}) copy-start(bf16[128,4,64]{2,0,1:T(8,128)(2,1)} %copy-done.12) | copy-start | bytes 196612
  276.2 3.5 %copy-start.9 = (bf16[8,128,1024]{2,1,0:T(8,128)(2,1)S(1)}, bf16[8,128,1024]{2,1,0:T(8,128)(2,1)}, u32[]{:S(2)}) copy-start(bf16[8,128,1024]{2,1,0:T(8,128)(2,1)} %copy.92) | copy-start | bytes 6291460
  276.2 3.5 %copy-start.39 = (bf16[512,1024]{1,0:T(8,128)(2,1)S(1)}, bf16[512,1024]{1,0:T(8,128)(2,1)}, u32[]{:S(2)}) copy-start(bf16[512,1024]{1,0:T(8,128)(2,1)} %all-gather.2.cloned.1.call-done) | copy-start | bytes 3145732
  281.9 19.3 %all-to-all-start.3 = ((bf16[8,128,512]{2,1,0:T(8,128)(2,1)}), bf16[8,128,512]{2,1,0:T(8,128)(2,1)}, u32[]{:S(2)}, u32[]{:S(2)}) async-start(bf16[8,128,512]{2,1,0:T(8,128)(2,1)} %bitcast.267), calls=%async_computation.3 | async-start | bytes 2097152 | tf_op jit(solution)/shard_map/all_to_all | solution.py:217
  301.2 15.1 %collective-permute-start.12 = (bf16[8,128,512]{2,1,0:T(8,128)(2,1)}, bf16[8,128,512]{2,1,0:T(8,128)(2,1)}, u32[]{:S(2)}, u32[]{:S(2)}) collective-permute-start(bf16[8,128,512]{2,1,0:T(8,128)(2,1)} %all-to-all-done.3), channel_id=1, source_target_pairs={{0,3},{1,0},{2,1},{3,2},{4,7},{5,4},{6,5},{7,6},{8,11},{9,8},{10,9... | collective-permute-start | bytes 3145736 | tf_op jit(solution)/shard_map/ppermute | solution.py:32
  306.5 3.6 %copy-start.3 = (f32[1,128,2048]{2,1,0:T(8,128)S(1)}, f32[1,128,2048]{2,1,0:T(8,128)}, u32[]{:S(2)}) copy-start(f32[1,128,2048]{2,1,0:T(8,128)} %mul.442) | copy-start | bytes 3145732
  306.5 3.6 %copy-start.4 = (f32[1,128,2048]{2,1,0:T(8,128)S(1)}, f32[1,128,2048]{2,1,0:T(8,128)}, u32[]{:S(2)}) copy-start(f32[1,128,2048]{2,1,0:T(8,128)} %mul.534) | copy-start | bytes 3145732
  (11 other events, 17.2 us)
Sparse Core Ops, SparseCore 0:
  20.0 36.1 all-gather.1
  273.3 32.8 reduce-scatter.3

commit v10 on v9

--- a/solution.py
+++ b/solution.py
@@ -102,6 +102,7 @@
     col_index = lax.axis_index("cz")
     ctx_index = lax.axis_index("cb") * col_parts + col_index
     both_rows = jnp.concatenate([w_key[0], w_value[0]], 1)
+    both_rows, tokens_here = lax.optimization_barrier((both_rows, tokens_here))
     weight_slice = lax.all_gather(both_rows, "cz", axis=0, tiled=True)
     inputs_slice = lax.all_to_all(tokens_here, "cb", 1, 0, tiled=True)
     projected = summed_over(

time: 331 us -> 330 us (level)
  local copies, waits for them, and re-layouts: 60.1 us -> 55.9 us
    all_to_all x1, waiting for transfers between devices: 5.9 us -> 0.21 us  [local(): lax.all_to_all(slice_grad.reshape(row_parts, tok_rows, slice_grad.shape[1...]
    all_to_all x1, waiting for transfers between devices: 15.3 us -> 19.6 us  [gathered(): received = lax.all_to_all(copies, axis, 0, 0, tiled=True)]
    unnamed x106 -> x96, local copies, waits for them, and re-layouts: 22 us -> 20.3 us
  transfers between devices with their start and end apart: 19 -> 19, of which waited for: 11 -> 11; matrix products, arithmetic and copies ran while one was open for 20% -> 22% of each run, Pallas kernels for 0% -> 0%
where the time goes in v10:
time: 330 us; the launch traced here: 328 us
  waiting for transfers between devices  128 us (39%)
  starting transfers between devices  80.9 us (25%)
  local copies, waits for them, and re-layouts  55.9 us (17%)
  matrix products  24.6 us (7%)
  other arithmetic  23.3 us (7%)
  between operations  15.1 us (5%)
    ppermute x12, waiting for transfers between devices, passed_along(): return lax.ppermute(block, axis, route)  57 us
    ppermute x12, starting transfers between devices, passed_along(): return lax.ppermute(block, axis, route)  42 us
    all_gather x1, waiting for transfers between devices, local(): weight_slice = lax.all_gather(both_rows, 'cz', axis=0, tiled=True)  23.3 us
    unnamed x96, local copies, waits for them, and re-layouts  20.3 us
    all_to_all x1, waiting for transfers between devices, gathered(): received = lax.all_to_all(copies, axis, 0, 0, tiled=True)  19.6 us
    all_to_all x1, starting transfers between devices, gathered(): received = lax.all_to_all(copies, axis, 0, 0, tiled=True)  18.9 us
    all_to_all x1, waiting for transfers between devices, summed_over(): received = lax.all_to_all(pieces, axis, 0, 0, tiled=True)  13.6 us
    all_to_all x1, waiting for transfers between devices, local(): inputs_slice = lax.all_to_all(tokens_here, 'cb', 1, 0, tiled=True)  11.2 us
  transfers between devices with their start and end apart: 19, of which 11 were waited for; matrix products, arithmetic and copies ran while one was open for 22% of the time, Pallas kernels for 0%

profile of v10, /device:TPU:33, one launch (start us, length us, event | category | flops | bytes accessed | tf_op | source)
XLA Modules:
  0.0 327.8 jit_solution(13928130902214673328)
XLA Ops:
  8.7 2.3 copy.64
  11.0 6.7 %all-to-all-start = ((bf16[128,8,512]{0,2,1:T(8,128)(2,1)}), bf16[128,8,512]{0,2,1:T(8,128)(2,1)S(1)}, u32[]{:S(2)}, u32[]{:S(2)}) async-start(bf16[128,8,512]{0,2,1:T(8,128)(2,1)} %bitcast.3), calls=%async_computation | async-start | bytes 2097152 | tf_op jit(solution)/shard_map/all_to_all | solution.py:107
  22.1 11.2 %all-to-all-done = bf16[128,8,512]{0,2,1:T(8,128)(2,1)S(1)} async-done(((bf16[128,8,512]{0,2,1:T(8,128)(2,1)}), bf16[128,8,512]{0,2,1:T(8,128)(2,1)S(1)}, u32[]{:S(2)}, u32[]{:S(2)}) %all-to-all-start) | async-done | bytes 1048608 | tf_op jit(solution)/shard_map/all_to_all | solution.py:107
  33.8 23.3 %all-gather.2.cloned.1.call-done = bf16[512,1024]{1,0:T(8,128)(2,1)} async-done(((bf16[64,1024]{1,0:T(8,128)(2,1)}), bf16[512,1024]{1,0:T(8,128)(2,1)}) %all-gather.2.cloned.1.call-update) | async-done | bytes 1048592 | tf_op jit(solution)/shard_map/all_gather | solution.py:106
  57.1 3.8 %convolution_convert_fusion = bf16[1024,1024]{1,0:T(8,128)(2,1)} fusion(bf16[1024,512]{1,0:T(8,128)(2,1)S(1)} %bitcast.262, bf16[512,1024]{1,0:T(8,128)(2,1)} %all-gather.2.cloned.1.call-done), kind=kOutput, calls=%fused_computation.10 | convolution fusion | flops 1074790400 | bytes 4194304 | tf_op jit(solution)/shard_map/dot_general | solution.py:109
  60.9 6.4 %all-to-all-start.1 = ((bf16[8,128,1024]{2,1,0:T(8,128)(2,1)}), bf16[8,128,1024]{2,1,0:T(8,128)(2,1)S(1)}, u32[]{:S(2)}, u32[]{:S(2)}) async-start(bf16[8,128,1024]{2,1,0:T(8,128)(2,1)} %bitcast.255), calls=%async_computation.1 | async-start | bytes 4194304 | tf_op jit(solution)/shard_map/all_to_all | solution.py:85
  67.4 2.0 copy.70
  69.3 2.0 copy.71
  71.3 2.0 copy.72
  79.4 13.6 %all-to-all-done.1 = bf16[8,128,1024]{2,1,0:T(8,128)(2,1)S(1)} async-done(((bf16[8,128,1024]{2,1,0:T(8,128)(2,1)}), bf16[8,128,1024]{2,1,0:T(8,128)(2,1)S(1)}, u32[]{:S(2)}, u32[]{:S(2)}) %all-to-all-start.1) | async-done | bytes 2097184 | tf_op jit(solution)/shard_map/all_to_all | solution.py:85
  94.4 2.7 collective-permute-start
  97.5 4.2 %collective-permute-start.1 = (bf16[2,128,4,128]{3,1,2,0:T(8,128)(2,1)S(1)}, bf16[2,128,4,128]{3,1,2,0:T(8,128)(2,1)S(1)}, u32[]{:S(2)}, u32[]{:S(2)}) collective-permute-start(bf16[2,128,4,128]{3,1,2,0:T(8,128)(2,1)S(1)} %get-tuple-element.33), channel_id=1, source_target_pairs={{0,8},{4,12},{8,16},{12,20},{16,24},{20,28},{24,32},{28,36},{32,40... | collective-permute-start | bytes 786440 | tf_op jit(solution)/shard_map/ppermute | solution.py:27
  101.7 2.7 collective-permute-start.2
  104.4 2.5 collective-permute-start.3
  106.9 8.4 %collective-permute-start.4 = (bf16[2,128,4,128]{3,1,2,0:T(8,128)(2,1)S(1)}, bf16[2,128,4,128]{3,1,2,0:T(8,128)(2,1)S(1)}, u32[]{:S(2)}, u32[]{:S(2)}) collective-permute-start(bf16[2,128,4,128]{3,1,2,0:T(8,128)(2,1)S(1)} %get-tuple-element.33), channel_id=1, source_target_pairs={{0,20},{4,24},{8,28},{12,32},{16,36},{20,40},{24,44},{28,48},{32,5... | collective-permute-start | bytes 786440 | tf_op jit(solution)/shard_map/ppermute | solution.py:27
  116.5 3.1 collective-permute-start.5
  120.4 11.4 %collective-permute-done.2 = bf16[2,128,4,128]{3,1,2,0:T(8,128)(2,1)S(1)} collective-permute-done((bf16[2,128,4,128]{3,1,2,0:T(8,128)(2,1)S(1)}, bf16[2,128,4,128]{3,1,2,0:T(8,128)(2,1)S(1)}, u32[]{:S(2)}, u32[]{:S(2)}) %collective-permute-start.2) | collective-permute-done | bytes 262176 | tf_op jit(solution)/shard_map/ppermute | solution.py:27
  132.9 4.6 %collective-permute-done.5 = bf16[2,128,4,128]{3,1,2,0:T(8,128)(2,1)S(1)} collective-permute-done((bf16[2,128,4,128]{3,1,2,0:T(8,128)(2,1)S(1)}, bf16[2,128,4,128]{3,1,2,0:T(8,128)(2,1)S(1)}, u32[]{:S(2)}, u32[]{:S(2)}) %collective-permute-start.5) | collective-permute-done | bytes 262176 | tf_op jit(solution)/shard_map/ppermute | solution.py:27
  138.3 2.9 fusion.3
  151.0 12.0 %collective-permute-start.6 = (bf16[2,128,4,128]{3,1,2,0:T(8,128)(2,1)}, bf16[2,128,4,128]{3,1,2,0:T(8,128)(2,1)}, u32[]{:S(2)}, u32[]{:S(2)}) collective-permute-start(bf16[2,128,4,128]{3,1,2,0:T(8,128)(2,1)} %get-tuple-element.43), channel_id=1, source_target_pairs={{4,0},{8,4},{12,8},{16,12},{20,16},{24,20},{28,24},{32,28},{36,32}... | collective-permute-start | bytes 786440 | tf_op jit(solution)/shard_map/ppermute | solution.py:27
  165.5 10.4 %collective-permute-done.10 = bf16[2,128,4,128]{3,1,2,0:T(8,128)(2,1)} collective-permute-done((bf16[2,128,4,128]{3,1,2,0:T(8,128)(2,1)S(1)}, bf16[2,128,4,128]{3,1,2,0:T(8,128)(2,1)}, u32[]{:S(2)}, u32[]{:S(2)}) %collective-permute-start.10) | collective-permute-done | bytes 262176 | tf_op jit(solution)/shard_map/ppermute | solution.py:27
  177.9 1.8 copy.84
  180.5 15.9 %collective-permute-done.11 = bf16[2,128,4,128]{3,1,2,0:T(8,128)(2,1)} collective-permute-done((bf16[2,128,4,128]{3,1,2,0:T(8,128)(2,1)}, bf16[2,128,4,128]{3,1,2,0:T(8,128)(2,1)}, u32[]{:S(2)}, u32[]{:S(2)}) %collective-permute-start.11) | collective-permute-done | bytes 262176 | tf_op jit(solution)/shard_map/ppermute | solution.py:27
  196.4 14.7 %collective-permute-done.9 = bf16[2,128,4,128]{3,1,2,0:T(8,128)(2,1)} collective-permute-done((bf16[2,128,4,128]{3,1,2,0:T(8,128)(2,1)}, bf16[2,128,4,128]{3,1,2,0:T(8,128)(2,1)}, u32[]{:S(2)}, u32[]{:S(2)}) %collective-permute-start.9) | collective-permute-done | bytes 262176 | tf_op jit(solution)/shard_map/ppermute | solution.py:27
  211.1 1.7 fusion.46
  214.5 1.6 broadcast_in_dim.56
  216.1 18.9 %all-to-all-start.2 = ((bf16[8,128,1024]{2,1,0:T(8,128)(2,1)}), bf16[8,128,1024]{2,1,0:T(8,128)(2,1)}, u32[]{:S(2)}, u32[]{:S(2)}) async-start(bf16[8,128,1024]{2,1,0:T(8,128)(2,1)} %broadcast_in_dim.56), calls=%async_computation.2 | async-start | bytes 4194304 | tf_op jit(solution)/shard_map/all_to_all | solution.py:79
  235.9 2.2 mul.533
  240.2 1.6 bitcast_dynamic-update-slice_fusion.5
  241.8 1.6 bitcast_dynamic-update-slice_fusion.4
  243.4 1.6 bitcast_dynamic-update-slice_fusion.3
  245.0 19.6 %all-to-all-done.2 = bf16[8,128,1024]{2,1,0:T(8,128)(2,1)} async-done(((bf16[8,128,1024]{2,1,0:T(8,128)(2,1)}), bf16[8,128,1024]{2,1,0:T(8,128)(2,1)}, u32[]{:S(2)}, u32[]{:S(2)}) %all-to-all-start.2) | async-done | bytes 2097184 | tf_op jit(solution)/shard_map/all_to_all | solution.py:79
  264.5 4.5 %convolution_bitcast_fusion = f32[512,1024]{1,0:T(8,128)} fusion(bf16[8,128,1024]{2,1,0:T(8,128)(2,1)} %all-to-all-done.2, bf16[128,8,512]{0,2,1:T(8,128)(2,1)} %copy-done.4), kind=kOutput, calls=%fused_computation.13 | convolution fusion | flops 1073741824 | bytes 5242880 | tf_op jit(solution)/shard_map/dot_general | solution.py:209
  270.7 1.6 bitcast_dynamic-update-slice_fusion.1
  273.9 4.0 %fusion.94 = (bf16[4,4,128,128]{2,3,1,0:T(8,128)(2,1)}, bf16[4,4,128,128]{2,3,1,0:T(8,128)(2,1)}, bf16[4,4,128,128]{2,3,1,0:T(8,128)(2,1)}, bf16[4,4,128,128]{2,...) fusion(bf16[4,4,128,896]{2,3,1,0:T(8,128)(2,1)} %copy-done), kind=kLoop, calls=%fused_computation.221 | loop fusion | bytes 7340032 | tf_op jit(solution)/shard_map/slice | solution.py:195
  277.8 3.9 %convolution_convert_fusion.1 = bf16[1024,512]{1,0:T(8,128)(2,1)} fusion(bf16[1024,1024]{1,0:T(8,128)(2,1)} %bitcast.75, bf16[512,1024]{1,0:T(8,128)(2,1)S(1)} %copy-done.37), kind=kOutput, calls=%fused_computation.15 | convolution fusion | flops 1074266112 | bytes 4194304 | tf_op jit(solution)/shard_map/dot_general | solution.py:214
  281.7 4.2 %all-to-all-start.3 = ((bf16[8,128,512]{2,1,0:T(8,128)(2,1)}), bf16[8,128,512]{2,1,0:T(8,128)(2,1)}, u32[]{:S(2)}, u32[]{:S(2)}) async-start(bf16[8,128,512]{2,1,0:T(8,128)(2,1)} %bitcast.261), calls=%async_computation.4 | async-start | bytes 2097152 | tf_op jit(solution)/shard_map/all_to_all | solution.py:218
  289.5 2.0 convolution_multiply_fusion
  292.6 2.4 copy.120
  295.0 2.4 copy.121
  297.4 3.1 multiply_add_fusion
  300.7 2.4 collective-permute-start.12
  303.1 2.8 multiply_reduce_fusion
  307.3 2.4 mul.539
  310.8 2.9 fusion.38
  313.7 2.4 collective-permute-done.12
  316.1 1.8 copy.94
  319.3 1.7 slice_bitcast_fusion.6
  (191 shorter events, 48.8 us)
Async XLA Ops:
  8.7 9.8 %copy-start.10 = (bf16[1,128,2048]{2,1,0:T(8,128)(2,1)S(1)}, bf16[1,128,2048]{2,1,0:T(8,128)(2,1)}, u32[]{:S(2)}) copy-start(bf16[1,128,2048]{2,1,0:T(8,128)(2,1)} %param.9) | copy-start | bytes 1572868
  11.0 22.3 %all-to-all-start = ((bf16[128,8,512]{0,2,1:T(8,128)(2,1)}), bf16[128,8,512]{0,2,1:T(8,128)(2,1)S(1)}, u32[]{:S(2)}, u32[]{:S(2)}) async-start(bf16[128,8,512]{0,2,1:T(8,128)(2,1)} %bitcast.3), calls=%async_computation | async-start | bytes 2097152 | tf_op jit(solution)/shard_map/all_to_all | solution.py:107
  17.7 39.4 %all-gather.2.cloned.1.call-start = ((), (), s32[]{:S(2)}) async-start(), calls=%async_computation.5 | async-start | bytes 1179648 | tf_op jit(solution)/shard_map/all_gather | solution.py:106
  20.2 1.9 copy-start.18
  33.3 27.6 %copy-start.4 = (bf16[128,8,512]{0,2,1:T(8,128)(2,1)}, bf16[128,8,512]{0,2,1:T(8,128)(2,1)S(1)}, u32[]{:S(2)}) copy-start(bf16[128,8,512]{0,2,1:T(8,128)(2,1)S(1)} %all-to-all-done) | copy-start | bytes 3145732
  60.9 32.1 %all-to-all-start.1 = ((bf16[8,128,1024]{2,1,0:T(8,128)(2,1)}), bf16[8,128,1024]{2,1,0:T(8,128)(2,1)S(1)}, u32[]{:S(2)}, u32[]{:S(2)}) async-start(bf16[8,128,1024]{2,1,0:T(8,128)(2,1)} %bitcast.255), calls=%async_computation.1 | async-start | bytes 4194304 | tf_op jit(solution)/shard_map/all_to_all | solution.py:85
  79.3 14.4 %copy-start.34 = (f32[1,128]{1,0:T(1,128)S(1)}, f32[1,128]{1,0:T(1,128)}, u32[]{:S(2)}) copy-start(f32[1,128]{1,0:T(1,128)} %param.15) | copy-start | bytes 1540
  93.4 3.8 %copy-start.11 = (bf16[128,16,64]{2,0,1:T(8,128)(2,1)S(1)}, bf16[128,16,64]{2,0,1:T(8,128)(2,1)}, u32[]{:S(2)}) copy-start(bf16[128,16,64]{2,0,1:T(8,128)(2,1)} %copy.70) | copy-start | bytes 786436
  93.4 3.8 %copy-start.12 = (bf16[128,16,64]{2,0,1:T(8,128)(2,1)S(1)}, bf16[128,16,64]{2,0,1:T(8,128)(2,1)}, u32[]{:S(2)}) copy-start(bf16[128,16,64]{2,0,1:T(8,128)(2,1)} %copy.71) | copy-start | bytes 786436
  94.0 22.4 %copy-start.13 = (bf16[128,4,64]{2,0,1:T(8,128)(2,1)}, bf16[128,4,64]{2,0,1:T(8,128)(2,1)S(1)}, u32[]{:S(2)}) copy-start(bf16[128,4,64]{2,0,1:T(8,128)(2,1)S(1)} %get-tuple-element.55) | copy-start | bytes 196612
  94.0 22.4 %copy-start.15 = (bf16[128,4,64]{2,0,1:T(8,128)(2,1)}, bf16[128,4,64]{2,0,1:T(8,128)(2,1)S(1)}, u32[]{:S(2)}) copy-start(bf16[128,4,64]{2,0,1:T(8,128)(2,1)S(1)} %get-tuple-element.56) | copy-start | bytes 196612
  94.3 25.3 %copy-start.28 = (pred[128,128]{0,1:T(8,128)(4,1)S(1)}, pred[128,128]{0,1:T(8,128)(4,1)}, u32[]{:S(2)}) copy-start(pred[128,128]{0,1:T(8,128)(4,1)} %get-tuple-element.82) | copy-start | bytes 49156
  94.4 22.0 %collective-permute-start = (bf16[2,128,4,128]{3,1,2,0:T(8,128)(2,1)S(1)}, bf16[2,128,4,128]{3,1,2,0:T(8,128)(2,1)S(1)}, u32[]{:S(2)}, u32[]{:S(2)}) collective-permute-start(bf16[2,128,4,128]{3,1,2,0:T(8,128)(2,1)S(1)} %get-tuple-element.33), channel_id=1, source_target_pairs={{0,4},{4,8},{8,12},{12,16},{16,20},{20,24},{24,28},{28,32},{32,36}... | collective-permute-start | bytes 786440 | tf_op jit(solution)/shard_map/ppermute | solution.py:27
  97.5 22.5 %copy-start.29 = (pred[128,128]{0,1:T(8,128)(4,1)S(1)}, pred[128,128]{0,1:T(8,128)(4,1)}, u32[]{:S(2)}) copy-start(pred[128,128]{0,1:T(8,128)(4,1)} %get-tuple-element.80) | copy-start | bytes 49156
  97.5 22.5 %collective-permute-start.1 = (bf16[2,128,4,128]{3,1,2,0:T(8,128)(2,1)S(1)}, bf16[2,128,4,128]{3,1,2,0:T(8,128)(2,1)S(1)}, u32[]{:S(2)}, u32[]{:S(2)}) collective-permute-start(bf16[2,128,4,128]{3,1,2,0:T(8,128)(2,1)S(1)} %get-tuple-element.33), channel_id=1, source_target_pairs={{0,8},{4,12},{8,16},{12,20},{16,24},{20,28},{24,32},{28,36},{32,40... | collective-permute-start | bytes 786440 | tf_op jit(solution)/shard_map/ppermute | solution.py:27
  101.7 30.1 %collective-permute-start.2 = (bf16[2,128,4,128]{3,1,2,0:T(8,128)(2,1)S(1)}, bf16[2,128,4,128]{3,1,2,0:T(8,128)(2,1)S(1)}, u32[]{:S(2)}, u32[]{:S(2)}) collective-permute-start(bf16[2,128,4,128]{3,1,2,0:T(8,128)(2,1)S(1)} %get-tuple-element.33), channel_id=1, source_target_pairs={{0,12},{4,16},{8,20},{12,24},{16,28},{20,32},{24,36},{28,40},{32,4... | collective-permute-start | bytes 786440 | tf_op jit(solution)/shard_map/ppermute | solution.py:27
  104.4 27.8 %collective-permute-start.3 = (bf16[2,128,4,128]{3,1,2,0:T(8,128)(2,1)S(1)}, bf16[2,128,4,128]{3,1,2,0:T(8,128)(2,1)S(1)}, u32[]{:S(2)}, u32[]{:S(2)}) collective-permute-start(bf16[2,128,4,128]{3,1,2,0:T(8,128)(2,1)S(1)} %get-tuple-element.33), channel_id=1, source_target_pairs={{0,16},{4,20},{8,24},{12,28},{16,32},{20,36},{24,40},{28,44},{32,4... | collective-permute-start | bytes 786440 | tf_op jit(solution)/shard_map/ppermute | solution.py:27
  106.9 25.7 %collective-permute-start.4 = (bf16[2,128,4,128]{3,1,2,0:T(8,128)(2,1)S(1)}, bf16[2,128,4,128]{3,1,2,0:T(8,128)(2,1)S(1)}, u32[]{:S(2)}, u32[]{:S(2)}) collective-permute-start(bf16[2,128,4,128]{3,1,2,0:T(8,128)(2,1)S(1)} %get-tuple-element.33), channel_id=1, source_target_pairs={{0,20},{4,24},{8,28},{12,32},{16,36},{20,40},{24,44},{28,48},{32,5... | collective-permute-start | bytes 786440 | tf_op jit(solution)/shard_map/ppermute | solution.py:27
  116.4 15.3 %copy-start.30 = (pred[128,128]{0,1:T(8,128)(4,1)S(1)}, pred[128,128]{0,1:T(8,128)(4,1)}, u32[]{:S(2)}) copy-start(pred[128,128]{0,1:T(8,128)(4,1)} %get-tuple-element.78) | copy-start | bytes 49156
  116.4 21.5 %copy-start.24 = (bf16[2,128,4,128]{3,1,2,0:T(8,128)(2,1)}, bf16[2,128,4,128]{3,1,2,0:T(8,128)(2,1)S(1)}, u32[]{:S(2)}) copy-start(bf16[2,128,4,128]{3,1,2,0:T(8,128)(2,1)S(1)} %collective-permute-done) | copy-start | bytes 786436
  116.5 21.1 %collective-permute-start.5 = (bf16[2,128,4,128]{3,1,2,0:T(8,128)(2,1)S(1)}, bf16[2,128,4,128]{3,1,2,0:T(8,128)(2,1)S(1)}, u32[]{:S(2)}, u32[]{:S(2)}) collective-permute-start(bf16[2,128,4,128]{3,1,2,0:T(8,128)(2,1)S(1)} %get-tuple-element.33), channel_id=1, source_target_pairs={{0,24},{4,28},{8,32},{12,36},{16,40},{20,44},{24,48},{28,52},{32,5... | collective-permute-start | bytes 786440 | tf_op jit(solution)/shard_map/ppermute | solution.py:27
  119.9 12.2 %copy-start.31 = (pred[128,128]{0,1:T(8,128)(4,1)S(1)}, pred[128,128]{0,1:T(8,128)(4,1)}, u32[]{:S(2)}) copy-start(pred[128,128]{0,1:T(8,128)(4,1)} %get-tuple-element.76) | copy-start | bytes 49156
  120.0 18.0 %copy-start.25 = (bf16[2,128,4,128]{3,1,2,0:T(8,128)(2,1)}, bf16[2,128,4,128]{3,1,2,0:T(8,128)(2,1)S(1)}, u32[]{:S(2)}) copy-start(bf16[2,128,4,128]{3,1,2,0:T(8,128)(2,1)S(1)} %collective-permute-done.1) | copy-start | bytes 786436
  120.4 12.2 %copy-start.32 = (pred[128,128]{0,1:T(8,128)(4,1)S(1)}, pred[128,128]{0,1:T(8,128)(4,1)}, u32[]{:S(2)}) copy-start(pred[128,128]{0,1:T(8,128)(4,1)} %get-tuple-element.74) | copy-start | bytes 49156
  131.8 6.3 %copy-start.26 = (bf16[2,128,4,128]{3,1,2,0:T(8,128)(2,1)}, bf16[2,128,4,128]{3,1,2,0:T(8,128)(2,1)S(1)}, u32[]{:S(2)}) copy-start(bf16[2,128,4,128]{3,1,2,0:T(8,128)(2,1)S(1)} %collective-permute-done.2) | copy-start | bytes 786436
  132.1 5.4 %copy-start.33 = (pred[128,128]{0,1:T(8,128)(4,1)S(1)}, pred[128,128]{0,1:T(8,128)(4,1)}, u32[]{:S(2)}) copy-start(pred[128,128]{0,1:T(8,128)(4,1)} %get-tuple-element.72) | copy-start | bytes 49156
  132.1 5.9 %copy-start.20 = (bf16[2,128,4,128]{3,1,2,0:T(8,128)(2,1)}, bf16[2,128,4,128]{3,1,2,0:T(8,128)(2,1)S(1)}, u32[]{:S(2)}) copy-start(bf16[2,128,4,128]{3,1,2,0:T(8,128)(2,1)S(1)} %collective-permute-done.3) | copy-start | bytes 786436
  132.6 5.6 %copy-start.22 = (bf16[2,128,4,128]{3,1,2,0:T(8,128)(2,1)}, bf16[2,128,4,128]{3,1,2,0:T(8,128)(2,1)S(1)}, u32[]{:S(2)}) copy-start(bf16[2,128,4,128]{3,1,2,0:T(8,128)(2,1)S(1)} %collective-permute-done.4) | copy-start | bytes 786436
  138.3 3.0 copy-start.2
  148.4 27.5 %collective-permute-start.10 = (bf16[2,128,4,128]{3,1,2,0:T(8,128)(2,1)S(1)}, bf16[2,128,4,128]{3,1,2,0:T(8,128)(2,1)}, u32[]{:S(2)}, u32[]{:S(2)}) collective-permute-start(bf16[2,128,4,128]{3,1,2,0:T(8,128)(2,1)S(1)} %get-tuple-element.45), channel_id=1, source_target_pairs={{20,0},{24,4},{28,8},{32,12},{36,16},{40,20},{44,24},{48,28},{52,3... | collective-permute-start | bytes 786440 | tf_op jit(solution)/shard_map/ppermute | solution.py:27
  149.7 46.7 %collective-permute-start.11 = (bf16[2,128,4,128]{3,1,2,0:T(8,128)(2,1)}, bf16[2,128,4,128]{3,1,2,0:T(8,128)(2,1)}, u32[]{:S(2)}, u32[]{:S(2)}) collective-permute-start(bf16[2,128,4,128]{3,1,2,0:T(8,128)(2,1)} %get-tuple-element.44), channel_id=1, source_target_pairs={{24,0},{28,4},{32,8},{36,12},{40,16},{44,20},{48,24},{52,28},{56,3... | collective-permute-start | bytes 786440 | tf_op jit(solution)/shard_map/ppermute | solution.py:27
  151.0 45.4 %collective-permute-start.6 = (bf16[2,128,4,128]{3,1,2,0:T(8,128)(2,1)}, bf16[2,128,4,128]{3,1,2,0:T(8,128)(2,1)}, u32[]{:S(2)}, u32[]{:S(2)}) collective-permute-start(bf16[2,128,4,128]{3,1,2,0:T(8,128)(2,1)} %get-tuple-element.43), channel_id=1, source_target_pairs={{4,0},{8,4},{12,8},{16,12},{20,16},{24,20},{28,24},{32,28},{36,32}... | collective-permute-start | bytes 786440 | tf_op jit(solution)/shard_map/ppermute | solution.py:27
  162.9 33.4 %collective-permute-start.7 = (bf16[2,128,4,128]{3,1,2,0:T(8,128)(2,1)}, bf16[2,128,4,128]{3,1,2,0:T(8,128)(2,1)}, u32[]{:S(2)}, u32[]{:S(2)}) collective-permute-start(bf16[2,128,4,128]{3,1,2,0:T(8,128)(2,1)} %get-tuple-element.48), channel_id=1, source_target_pairs={{8,0},{12,4},{16,8},{20,12},{24,16},{28,20},{32,24},{36,28},{40,32... | collective-permute-start | bytes 786440 | tf_op jit(solution)/shard_map/ppermute | solution.py:27
  164.2 32.1 %collective-permute-start.8 = (bf16[2,128,4,128]{3,1,2,0:T(8,128)(2,1)}, bf16[2,128,4,128]{3,1,2,0:T(8,128)(2,1)}, u32[]{:S(2)}, u32[]{:S(2)}) collective-permute-start(bf16[2,128,4,128]{3,1,2,0:T(8,128)(2,1)} %get-tuple-element.47), channel_id=1, source_target_pairs={{12,0},{16,4},{20,8},{24,12},{28,16},{32,20},{36,24},{40,28},{44,3... | collective-permute-start | bytes 786440 | tf_op jit(solution)/shard_map/ppermute | solution.py:27
  175.9 35.2 %collective-permute-start.9 = (bf16[2,128,4,128]{3,1,2,0:T(8,128)(2,1)}, bf16[2,128,4,128]{3,1,2,0:T(8,128)(2,1)}, u32[]{:S(2)}, u32[]{:S(2)}) collective-permute-start(bf16[2,128,4,128]{3,1,2,0:T(8,128)(2,1)} %get-tuple-element.46), channel_id=1, source_target_pairs={{16,0},{20,4},{24,8},{28,12},{32,16},{36,20},{40,24},{44,28},{48,3... | collective-permute-start | bytes 786440 | tf_op jit(solution)/shard_map/ppermute | solution.py:27
  216.1 19.2 %copy-start.19 = (f32[128,16]{1,0:T(8,128)S(1)}, f32[128,16]{1,0:T(8,128)}, u32[]{:S(2)}) copy-start(f32[128,16]{1,0:T(8,128)} %copy-done.18) | copy-start | bytes 24580
  216.1 48.4 %all-to-all-start.2 = ((bf16[8,128,1024]{2,1,0:T(8,128)(2,1)}), bf16[8,128,1024]{2,1,0:T(8,128)(2,1)}, u32[]{:S(2)}, u32[]{:S(2)}) async-start(bf16[8,128,1024]{2,1,0:T(8,128)(2,1)} %broadcast_in_dim.56), calls=%async_computation.2 | async-start | bytes 4194304 | tf_op jit(solution)/shard_map/all_to_all | solution.py:79
  235.0 84.2 %reduce-scatter.2.cloned.1.call-start = ((), (), s32[]{:S(2)}) async-start(), calls=%async_computation.6 | async-start | bytes 2359296 | tf_op jit(solution)/shard_map/reduce_scatter | solution.py:213
  235.8 3.6 %copy-start.36 = (f32[1,128]{1,0:T(1,128)S(1)}, f32[1,128]{1,0:T(1,128)}, u32[]{:S(2)}) copy-start(f32[1,128]{1,0:T(1,128)} %param.14) | copy-start | bytes 1540
  235.8 3.6 %copy-start.14 = (bf16[128,4,64]{2,0,1:T(8,128)(2,1)S(1)}, bf16[128,4,64]{2,0,1:T(8,128)(2,1)}, u32[]{:S(2)}) copy-start(bf16[128,4,64]{2,0,1:T(8,128)(2,1)} %copy-done.13) | copy-start | bytes 196612
  235.8 3.6 %copy-start.16 = (bf16[128,4,64]{2,0,1:T(8,128)(2,1)S(1)}, bf16[128,4,64]{2,0,1:T(8,128)(2,1)}, u32[]{:S(2)}) copy-start(bf16[128,4,64]{2,0,1:T(8,128)(2,1)} %copy-done.15) | copy-start | bytes 196612
  273.9 4.0 %copy-start.37 = (bf16[512,1024]{1,0:T(8,128)(2,1)S(1)}, bf16[512,1024]{1,0:T(8,128)(2,1)}, u32[]{:S(2)}) copy-start(bf16[512,1024]{1,0:T(8,128)(2,1)} %all-gather.2.cloned.1.call-done) | copy-start | bytes 3145732
  281.7 19.0 %all-to-all-start.3 = ((bf16[8,128,512]{2,1,0:T(8,128)(2,1)}), bf16[8,128,512]{2,1,0:T(8,128)(2,1)}, u32[]{:S(2)}, u32[]{:S(2)}) async-start(bf16[8,128,512]{2,1,0:T(8,128)(2,1)} %bitcast.261), calls=%async_computation.4 | async-start | bytes 2097152 | tf_op jit(solution)/shard_map/all_to_all | solution.py:218
  286.0 2.4 copy-start.9
  286.0 2.5 copy-start.8
  286.0 2.6 copy-start.7
  300.7 15.4 %collective-permute-start.12 = (bf16[8,128,512]{2,1,0:T(8,128)(2,1)}, bf16[8,128,512]{2,1,0:T(8,128)(2,1)}, u32[]{:S(2)}, u32[]{:S(2)}) collective-permute-start(bf16[8,128,512]{2,1,0:T(8,128)(2,1)} %all-to-all-done.3), channel_id=1, source_target_pairs={{0,3},{1,0},{2,1},{3,2},{4,7},{5,4},{6,5},{7,6},{8,11},{9,8},{10,9... | collective-permute-start | bytes 3145736 | tf_op jit(solution)/shard_map/ppermute | solution.py:32
  306.0 3.7 %copy-start.3 = (f32[128,16,128]{2,1,0:T(8,128)S(1)}, f32[128,16,128]{2,1,0:T(8,128)}, u32[]{:S(2)}) copy-start(f32[128,16,128]{2,1,0:T(8,128)} %get-tuple-element.29) | copy-start | bytes 3145732
  (9 other events, 11.6 us)
Sparse Core Ops, SparseCore 0:
  20.8 36.1 all-gather.1
  269.2 32.9 reduce-scatter.1

commit v11 on v8

--- a/solution.py
+++ b/solution.py
@@ -2,6 +2,8 @@
 import jax.numpy as jnp
 from jax import lax
 import functools
+
+from jax.experimental.layout import Layout, with_layout_constraint
 
 from jax.sharding import Mesh, NamedSharding, PartitionSpec as P
 
@@ -205,6 +207,7 @@
     value_back = kv_total[1].reshape(tok_rows, kv_width).astype(jnp.bfloat16)
     both_back = jnp.concatenate([key_back, value_back], 1)
     group_back = gathered(both_back, "cb", row_parts)
+    group_back = with_layout_constraint(group_back, Layout(major_to_minor=(0, 1)))
     weight_part = lax.dot_general(
         inputs_slice, group_back, (((0,), (0,)), ((), ())), preferred_element_type=jnp.float32
     )

time: 323 us -> 320 us (level)
    all_to_all x1 -> x0, local copies, waits for them, and re-layouts: 3.93 us -> none  [gathered(): received = lax.all_to_all(copies, axis, 0, 0, tiled=True)]
    unnamed x104 -> x100, local copies, waits for them, and re-layouts: 13.8 us -> 15.6 us
where the time goes in v11:
time: 320 us; the launch traced here: 317 us
  waiting for transfers between devices  126 us (39%)
  starting transfers between devices  73.9 us (23%)
  local copies, waits for them, and re-layouts  43.7 us (14%)
  matrix products  39.7 us (12%)
  other arithmetic  19.1 us (6%)
  between operations  15.4 us (5%)
    ppermute x12, waiting for transfers between devices, passed_along(): return lax.ppermute(block, axis, route)  52 us
    ppermute x12, starting transfers between devices, passed_along(): return lax.ppermute(block, axis, route)  37.1 us
    all_to_all x1, waiting for transfers between devices, gathered(): received = lax.all_to_all(copies, axis, 0, 0, tiled=True)  24.3 us
    all_to_all x1, waiting for transfers between devices, summed_over(): received = lax.all_to_all(pieces, axis, 0, 0, tiled=True)  20.5 us
    all_to_all x1, starting transfers between devices, gathered(): received = lax.all_to_all(copies, axis, 0, 0, tiled=True)  17.9 us
    unnamed x100, local copies, waits for them, and re-layouts  15.6 us
    all_to_all x1, waiting for transfers between devices, local(): inputs_slice = lax.all_to_all(tokens_here, 'cb', 1, 0, tiled=True)  12.9 us
    all_gather x1, waiting for transfers between devices, local(): weight_slice = lax.all_gather(both_rows, 'cz', axis=0, tiled=True)  11.4 us
  transfers between devices with their start and end apart: 19, of which 10 were waited for; matrix products, arithmetic and copies ran while one was open for 20% of the time, Pallas kernels for 0%

profile of v11, /device:TPU:33, one launch (start us, length us, event | category | flops | bytes accessed | tf_op | source)
XLA Modules:
  0.0 317.3 jit_solution(3979022501244517066)
XLA Ops:
  7.2 1.5 pad_maximum_fusion.11
  8.8 2.3 copy.258
  11.1 6.7 %all-to-all-start = ((bf16[128,8,512]{0,2,1:T(8,128)(2,1)}), bf16[128,8,512]{0,2,1:T(8,128)(2,1)S(1)}, u32[]{:S(2)}, u32[]{:S(2)}) async-start(bf16[128,8,512]{0,2,1:T(8,128)(2,1)} %bitcast.2), calls=%async_computation | async-start | bytes 2097152 | tf_op jit(solution)/shard_map/all_to_all | solution.py:108
  20.4 12.9 %all-to-all-done = bf16[128,8,512]{0,2,1:T(8,128)(2,1)S(1)} async-done(((bf16[128,8,512]{0,2,1:T(8,128)(2,1)}), bf16[128,8,512]{0,2,1:T(8,128)(2,1)S(1)}, u32[]{:S(2)}, u32[]{:S(2)}) %all-to-all-start) | async-done | bytes 1048608 | tf_op jit(solution)/shard_map/all_to_all | solution.py:108
  33.4 1.3 copy.259
  34.7 11.4 %all-gather.2.cloned.1.call-done = bf16[512,1024]{1,0:T(8,128)(2,1)} async-done(((bf16[64,1024]{1,0:T(8,128)(2,1)}), bf16[512,1024]{1,0:T(8,128)(2,1)}) %all-gather.2.cloned.1.call-update) | async-done | bytes 1048592 | tf_op jit(solution)/shard_map/all_gather | solution.py:107
  46.1 4.2 %convolution_convert_fusion = bf16[1024,1024]{0,1:T(8,128)(2,1)} fusion(bf16[1024,512]{1,0:T(8,128)(2,1)} %bitcast.583, bf16[512,1024]{1,0:T(8,128)(2,1)} %all-gather.2.cloned.1.call-done), kind=kOutput, calls=%fused_computation | convolution fusion | flops 1074790400 | bytes 4194304 | tf_op jit(solution)/shard_map/dot_general | solution.py:110
  50.2 6.6 %all-to-all-start.1 = ((bf16[8,128,1024]{2,1,0:T(8,128)(2,1)}), bf16[8,128,1024]{2,1,0:T(8,128)(2,1)}, u32[]{:S(2)}, u32[]{:S(2)}) async-start(bf16[8,128,1024]{2,1,0:T(8,128)(2,1)} %bitcast.575), calls=%async_computation.1 | async-start | bytes 4194304 | tf_op jit(solution)/shard_map/all_to_all | solution.py:87
  57.6 1.3 copy.267
  62.1 20.5 %all-to-all-done.1 = bf16[8,128,1024]{2,1,0:T(8,128)(2,1)} async-done(((bf16[8,128,1024]{2,1,0:T(8,128)(2,1)}), bf16[8,128,1024]{2,1,0:T(8,128)(2,1)}, u32[]{:S(2)}, u32[]{:S(2)}) %all-to-all-start.1) | async-done | bytes 2097184 | tf_op jit(solution)/shard_map/all_to_all | solution.py:87
  82.6 2.0 reduce
  88.1 2.3 collective-permute-start
  90.4 4.2 %collective-permute-start.2 = (bf16[2,128,4,128]{3,1,2,0:T(8,128)(2,1)}, bf16[2,128,4,128]{3,1,2,0:T(8,128)(2,1)S(1)}, u32[]{:S(2)}, u32[]{:S(2)}) collective-permute-start(bf16[2,128,4,128]{3,1,2,0:T(8,128)(2,1)} %pad_maximum_fusion.2), channel_id=1, source_target_pairs={{0,12},{4,16},{8,20},{12,24},{16,28},{20,32},{24,36},{28,40},{32,4... | collective-permute-start | bytes 786440 | tf_op jit(solution)/shard_map/ppermute | solution.py:29
  94.6 3.2 collective-permute-start.3
  97.8 4.4 %collective-permute-start.4 = (bf16[2,128,4,128]{3,1,2,0:T(8,128)(2,1)}, bf16[2,128,4,128]{3,1,2,0:T(8,128)(2,1)}, u32[]{:S(2)}, u32[]{:S(2)}) collective-permute-start(bf16[2,128,4,128]{3,1,2,0:T(8,128)(2,1)} %pad_maximum_fusion.2), channel_id=1, source_target_pairs={{0,20},{4,24},{8,28},{12,32},{16,36},{20,40},{24,44},{28,48},{32,5... | collective-permute-start | bytes 786440 | tf_op jit(solution)/shard_map/ppermute | solution.py:29
  102.2 7.0 %collective-permute-start.5 = (bf16[2,128,4,128]{3,1,2,0:T(8,128)(2,1)}, bf16[2,128,4,128]{3,1,2,0:T(8,128)(2,1)}, u32[]{:S(2)}, u32[]{:S(2)}) collective-permute-start(bf16[2,128,4,128]{3,1,2,0:T(8,128)(2,1)} %pad_maximum_fusion.2), channel_id=1, source_target_pairs={{0,24},{4,28},{8,32},{12,36},{16,40},{20,44},{24,48},{28,52},{32,5... | collective-permute-start | bytes 786440 | tf_op jit(solution)/shard_map/ppermute | solution.py:29
  110.8 1.4 copy.322
  113.4 3.4 %collective-permute-start.1 = (bf16[2,128,4,128]{3,1,2,0:T(8,128)(2,1)}, bf16[2,128,4,128]{3,1,2,0:T(8,128)(2,1)S(1)}, u32[]{:S(2)}, u32[]{:S(2)}) collective-permute-start(bf16[2,128,4,128]{3,1,2,0:T(8,128)(2,1)} %pad_maximum_fusion.2), channel_id=1, source_target_pairs={{0,8},{4,12},{8,16},{12,20},{16,24},{20,28},{24,32},{28,36},{32,40... | collective-permute-start | bytes 786440 | tf_op jit(solution)/shard_map/ppermute | solution.py:29
  120.2 9.7 %collective-permute-done.5 = bf16[2,128,4,128]{3,1,2,0:T(8,128)(2,1)} collective-permute-done((bf16[2,128,4,128]{3,1,2,0:T(8,128)(2,1)}, bf16[2,128,4,128]{3,1,2,0:T(8,128)(2,1)}, u32[]{:S(2)}, u32[]{:S(2)}) %collective-permute-start.5) | collective-permute-done | bytes 262176 | tf_op jit(solution)/shard_map/ppermute | solution.py:29
  141.5 6.0 %collective-permute-start.6 = (bf16[2,128,4,128]{3,1,2,0:T(8,128)(2,1)S(1)}, bf16[2,128,4,128]{3,1,2,0:T(8,128)(2,1)S(1)}, u32[]{:S(2)}, u32[]{:S(2)}) collective-permute-start(bf16[2,128,4,128]{3,1,2,0:T(8,128)(2,1)S(1)} %pad_maximum_fusion.3), channel_id=1, source_target_pairs={{4,0},{8,4},{12,8},{16,12},{20,16},{24,20},{28,24},{32,28},{36,32}... | collective-permute-start | bytes 786440 | tf_op jit(solution)/shard_map/ppermute | solution.py:29
  154.9 1.4 collective-permute-start.10
  160.7 15.7 %collective-permute-done.8 = bf16[2,128,4,128]{3,1,2,0:T(8,128)(2,1)S(1)} collective-permute-done((bf16[2,128,4,128]{3,1,2,0:T(8,128)(2,1)S(1)}, bf16[2,128,4,128]{3,1,2,0:T(8,128)(2,1)S(1)}, u32[]{:S(2)}, u32[]{:S(2)}) %collective-permute-start.8) | collective-permute-done | bytes 262176 | tf_op jit(solution)/shard_map/ppermute | solution.py:29
  176.4 21.4 %collective-permute-done.9 = bf16[2,128,4,128]{3,1,2,0:T(8,128)(2,1)S(1)} collective-permute-done((bf16[2,128,4,128]{3,1,2,0:T(8,128)(2,1)S(1)}, bf16[2,128,4,128]{3,1,2,0:T(8,128)(2,1)S(1)}, u32[]{:S(2)}, u32[]{:S(2)}) %collective-permute-start.9) | collective-permute-done | bytes 262176 | tf_op jit(solution)/shard_map/ppermute | solution.py:29
  197.7 5.2 %collective-permute-done.11 = bf16[2,128,4,128]{3,1,2,0:T(8,128)(2,1)S(1)} collective-permute-done((bf16[2,128,4,128]{3,1,2,0:T(8,128)(2,1)S(1)}, bf16[2,128,4,128]{3,1,2,0:T(8,128)(2,1)S(1)}, u32[]{:S(2)}, u32[]{:S(2)}) %collective-permute-start.11) | collective-permute-done | bytes 262176 | tf_op jit(solution)/shard_map/ppermute | solution.py:29
  207.2 1.6 broadcast_in_dim.60
  208.9 17.9 %all-to-all-start.2 = ((bf16[8,128,1024]{2,1,0:T(8,128)(2,1)}), bf16[8,128,1024]{2,1,0:T(8,128)(2,1)}, u32[]{:S(2)}, u32[]{:S(2)}) async-start(bf16[8,128,1024]{2,1,0:T(8,128)(2,1)} %broadcast_in_dim.60), calls=%async_computation.2 | async-start | bytes 4194304 | tf_op jit(solution)/shard_map/all_to_all | solution.py:81
  226.8 1.3 mul.517
  228.1 1.4 mul.518
  229.5 1.3 mul.631
  230.8 2.4 mul.632
  233.3 24.3 %all-to-all-done.2 = bf16[8,128,1024]{2,1,0:T(8,128)(2,1)} async-done(((bf16[8,128,1024]{2,1,0:T(8,128)(2,1)}), bf16[8,128,1024]{2,1,0:T(8,128)(2,1)}, u32[]{:S(2)}, u32[]{:S(2)}) %all-to-all-start.2) | async-done | bytes 2097184 | tf_op jit(solution)/shard_map/all_to_all | solution.py:81
  257.6 4.5 %convolution_bitcast_fusion = f32[512,1024]{0,1:T(8,128)} fusion(bf16[1024,1024]{1,0:T(8,128)(2,1)} %bitcast.142, bf16[1024,512]{1,0:T(8,128)(2,1)} %bitcast.584), kind=kOutput, calls=%fused_computation.1 | convolution fusion | flops 1073741824 | bytes 5242880 | tf_op jit(solution)/shard_map/dot_general | solution.py:211
  262.1 2.9 copy.466
  265.7 4.1 %convolution_convert_fusion.1 = bf16[1024,512]{1,0:T(8,128)(2,1)} fusion(bf16[1024,1024]{1,0:T(8,128)(2,1)} %bitcast.142, bf16[512,1024]{1,0:T(8,128)(2,1)} %all-gather.2.cloned.1.call-done), kind=kOutput, calls=%fused_computation.2 | convolution fusion | flops 1074266112 | bytes 4194304 | tf_op jit(solution)/shard_map/dot_general | solution.py:216
  269.8 4.4 %all-to-all-start.3 = ((bf16[8,128,512]{2,1,0:T(8,128)(2,1)}), bf16[8,128,512]{2,1,0:T(8,128)(2,1)}, u32[]{:S(2)}, u32[]{:S(2)}) async-start(bf16[8,128,512]{2,1,0:T(8,128)(2,1)} %bitcast.585), calls=%async_computation.3 | async-start | bytes 2097152 | tf_op jit(solution)/shard_map/all_to_all | solution.py:220
  274.7 1.3 fusion.96
  276.4 1.3 fusion.98
  277.7 1.3 fusion.99
  282.0 1.6 copy.468
  283.6 2.4 copy.469
  286.0 2.8 multiply_add_fusion
  291.0 2.2 multiply_reduce_fusion
  293.2 1.3 mul.636
  294.5 2.5 mul.637
  298.1 3.0 fusion.88
  301.0 3.5 %collective-permute-done.12 = bf16[8,128,512]{2,1,0:T(8,128)(2,1)} collective-permute-done((bf16[8,128,512]{2,1,0:T(8,128)(2,1)}, bf16[8,128,512]{2,1,0:T(8,128)(2,1)}, u32[]{:S(2)}, u32[]{:S(2)}) %collective-permute-start.12) | collective-permute-done | bytes 1048608 | tf_op jit(solution)/shard_map/ppermute | solution.py:34
  304.5 1.8 copy.343
  306.3 1.3 broadcast_in_dim_reshape.3
  (216 shorter events, 53.6 us)
Async XLA Ops:
  7.2 38.9 %all-gather.2.cloned.1.call-start = ((), (), s32[]{:S(2)}) async-start(), calls=%async_computation.5 | async-start | bytes 1179648 | tf_op jit(solution)/shard_map/all_gather | solution.py:107
  8.8 9.0 %copy-start.13 = (bf16[1,128,2048]{2,1,0:T(8,128)(2,1)S(1)}, bf16[1,128,2048]{2,1,0:T(8,128)(2,1)}, u32[]{:S(2)}) copy-start(bf16[1,128,2048]{2,1,0:T(8,128)(2,1)} %param.9) | copy-start | bytes 1572868
  11.1 22.3 %all-to-all-start = ((bf16[128,8,512]{0,2,1:T(8,128)(2,1)}), bf16[128,8,512]{0,2,1:T(8,128)(2,1)S(1)}, u32[]{:S(2)}, u32[]{:S(2)}) async-start(bf16[128,8,512]{0,2,1:T(8,128)(2,1)} %bitcast.2), calls=%async_computation | async-start | bytes 2097152 | tf_op jit(solution)/shard_map/all_to_all | solution.py:108
  18.8 38.0 %copy-start.16 = (f32[128,64]{1,0:T(8,128)}, f32[128,64]{1,0:T(8,128)S(1)}, u32[]{:S(2)}) copy-start(f32[128,64]{1,0:T(8,128)S(1)} %get-tuple-element.83) | copy-start | bytes 98308
  18.8 38.0 %copy-start.20 = (f32[128,64]{1,0:T(8,128)}, f32[128,64]{1,0:T(8,128)S(1)}, u32[]{:S(2)}) copy-start(f32[128,64]{1,0:T(8,128)S(1)} %get-tuple-element.84) | copy-start | bytes 98308
  50.2 32.4 %all-to-all-start.1 = ((bf16[8,128,1024]{2,1,0:T(8,128)(2,1)}), bf16[8,128,1024]{2,1,0:T(8,128)(2,1)}, u32[]{:S(2)}, u32[]{:S(2)}) async-start(bf16[8,128,1024]{2,1,0:T(8,128)(2,1)} %bitcast.575), calls=%async_computation.1 | async-start | bytes 4194304 | tf_op jit(solution)/shard_map/all_to_all | solution.py:87
  57.4 2.8 copy-start.41
  62.1 24.7 %copy-start.17 = (f32[128,64]{1,0:T(8,128)S(1)}, f32[128,64]{1,0:T(8,128)}, u32[]{:S(2)}) copy-start(f32[128,64]{1,0:T(8,128)} %copy-done.16) | copy-start | bytes 98308
  62.1 24.7 %copy-start.21 = (f32[128,64]{1,0:T(8,128)S(1)}, f32[128,64]{1,0:T(8,128)}, u32[]{:S(2)}) copy-start(f32[128,64]{1,0:T(8,128)} %copy-done.20) | copy-start | bytes 98308
  87.0 31.1 %copy-start.11 = (bf16[128,4,64]{2,0,1:T(8,128)(2,1)}, bf16[128,4,64]{2,0,1:T(8,128)(2,1)S(1)}, u32[]{:S(2)}) copy-start(bf16[128,4,64]{2,0,1:T(8,128)(2,1)S(1)} %get-tuple-element.53) | copy-start | bytes 196612
  87.1 47.4 %copy-start.14 = (bf16[128,512]{0,1:T(8,128)(2,1)}, bf16[128,512]{0,1:T(8,128)(2,1)S(1)}, u32[]{:S(2)}) copy-start(bf16[128,512]{0,1:T(8,128)(2,1)S(1)} %copy.264) | copy-start | bytes 393220
  88.1 25.3 %collective-permute-start = (bf16[2,128,4,128]{3,1,2,0:T(8,128)(2,1)}, bf16[2,128,4,128]{3,1,2,0:T(8,128)(2,1)}, u32[]{:S(2)}, u32[]{:S(2)}) collective-permute-start(bf16[2,128,4,128]{3,1,2,0:T(8,128)(2,1)} %pad_maximum_fusion.2), channel_id=1, source_target_pairs={{0,4},{4,8},{8,12},{12,16},{16,20},{20,24},{24,28},{28,32},{32,36}... | collective-permute-start | bytes 786440 | tf_op jit(solution)/shard_map/ppermute | solution.py:29
  90.4 27.7 %collective-permute-start.2 = (bf16[2,128,4,128]{3,1,2,0:T(8,128)(2,1)}, bf16[2,128,4,128]{3,1,2,0:T(8,128)(2,1)S(1)}, u32[]{:S(2)}, u32[]{:S(2)}) collective-permute-start(bf16[2,128,4,128]{3,1,2,0:T(8,128)(2,1)} %pad_maximum_fusion.2), channel_id=1, source_target_pairs={{0,12},{4,16},{8,20},{12,24},{16,28},{20,32},{24,36},{28,40},{32,4... | collective-permute-start | bytes 786440 | tf_op jit(solution)/shard_map/ppermute | solution.py:29
  94.6 23.9 %collective-permute-start.3 = (bf16[2,128,4,128]{3,1,2,0:T(8,128)(2,1)}, bf16[2,128,4,128]{3,1,2,0:T(8,128)(2,1)S(1)}, u32[]{:S(2)}, u32[]{:S(2)}) collective-permute-start(bf16[2,128,4,128]{3,1,2,0:T(8,128)(2,1)} %pad_maximum_fusion.2), channel_id=1, source_target_pairs={{0,16},{4,20},{8,24},{12,28},{16,32},{20,36},{24,40},{28,44},{32,4... | collective-permute-start | bytes 786440 | tf_op jit(solution)/shard_map/ppermute | solution.py:29
  97.8 21.1 %collective-permute-start.4 = (bf16[2,128,4,128]{3,1,2,0:T(8,128)(2,1)}, bf16[2,128,4,128]{3,1,2,0:T(8,128)(2,1)}, u32[]{:S(2)}, u32[]{:S(2)}) collective-permute-start(bf16[2,128,4,128]{3,1,2,0:T(8,128)(2,1)} %pad_maximum_fusion.2), channel_id=1, source_target_pairs={{0,20},{4,24},{8,28},{12,32},{16,36},{20,40},{24,44},{28,48},{32,5... | collective-permute-start | bytes 786440 | tf_op jit(solution)/shard_map/ppermute | solution.py:29
  102.2 27.7 %collective-permute-start.5 = (bf16[2,128,4,128]{3,1,2,0:T(8,128)(2,1)}, bf16[2,128,4,128]{3,1,2,0:T(8,128)(2,1)}, u32[]{:S(2)}, u32[]{:S(2)}) collective-permute-start(bf16[2,128,4,128]{3,1,2,0:T(8,128)(2,1)} %pad_maximum_fusion.2), channel_id=1, source_target_pairs={{0,24},{4,28},{8,32},{12,36},{16,40},{20,44},{24,48},{28,52},{32,5... | collective-permute-start | bytes 786440 | tf_op jit(solution)/shard_map/ppermute | solution.py:29
  112.2 5.9 %copy-start.38 = (pred[128,128]{0,1:T(8,128)(4,1)S(1)}, pred[128,128]{0,1:T(8,128)(4,1)}, u32[]{:S(2)}) copy-start(pred[128,128]{0,1:T(8,128)(4,1)} %get-tuple-element.79) | copy-start | bytes 49156
  113.4 5.1 %copy-start.37 = (pred[128,128]{0,1:T(8,128)(4,1)S(1)}, pred[128,128]{0,1:T(8,128)(4,1)}, u32[]{:S(2)}) copy-start(pred[128,128]{0,1:T(8,128)(4,1)} %get-tuple-element.80) | copy-start | bytes 49156
  113.4 17.8 %collective-permute-start.1 = (bf16[2,128,4,128]{3,1,2,0:T(8,128)(2,1)}, bf16[2,128,4,128]{3,1,2,0:T(8,128)(2,1)S(1)}, u32[]{:S(2)}, u32[]{:S(2)}) collective-permute-start(bf16[2,128,4,128]{3,1,2,0:T(8,128)(2,1)} %pad_maximum_fusion.2), channel_id=1, source_target_pairs={{0,8},{4,12},{8,16},{12,20},{16,24},{20,28},{24,32},{28,36},{32,40... | collective-permute-start | bytes 786440 | tf_op jit(solution)/shard_map/ppermute | solution.py:29
  118.1 31.4 %copy-start.29 = (bf16[2,128,4,128]{3,1,2,0:T(8,128)(2,1)}, bf16[2,128,4,128]{3,1,2,0:T(8,128)(2,1)S(1)}, u32[]{:S(2)}) copy-start(bf16[2,128,4,128]{3,1,2,0:T(8,128)(2,1)S(1)} %collective-permute-done.2) | copy-start | bytes 786436
  118.5 32.9 %copy-start.30 = (bf16[2,128,4,128]{3,1,2,0:T(8,128)(2,1)}, bf16[2,128,4,128]{3,1,2,0:T(8,128)(2,1)S(1)}, u32[]{:S(2)}) copy-start(bf16[2,128,4,128]{3,1,2,0:T(8,128)(2,1)S(1)} %collective-permute-done.3) | copy-start | bytes 786436
  118.9 12.3 %copy-start.35 = (pred[128,128]{0,1:T(8,128)(4,1)S(1)}, pred[128,128]{0,1:T(8,128)(4,1)}, u32[]{:S(2)}) copy-start(pred[128,128]{0,1:T(8,128)(4,1)} %get-tuple-element.78) | copy-start | bytes 49156
  131.2 16.3 %copy-start.27 = (bf16[2,128,4,128]{3,1,2,0:T(8,128)(2,1)}, bf16[2,128,4,128]{3,1,2,0:T(8,128)(2,1)S(1)}, u32[]{:S(2)}) copy-start(bf16[2,128,4,128]{3,1,2,0:T(8,128)(2,1)S(1)} %collective-permute-done.1) | copy-start | bytes 786436
  141.1 7.0 %copy-start.6 = (bf16[4,4,128,128]{2,3,1,0:T(8,128)(2,1)}, bf16[4,4,128,128]{2,3,1,0:T(8,128)(2,1)S(1)}, u32[]{:S(2)}) copy-start(bf16[4,4,128,128]{2,3,1,0:T(8,128)(2,1)S(1)} %fusion.47) | copy-start | bytes 1572868
  141.5 17.3 %collective-permute-start.6 = (bf16[2,128,4,128]{3,1,2,0:T(8,128)(2,1)S(1)}, bf16[2,128,4,128]{3,1,2,0:T(8,128)(2,1)S(1)}, u32[]{:S(2)}, u32[]{:S(2)}) collective-permute-start(bf16[2,128,4,128]{3,1,2,0:T(8,128)(2,1)S(1)} %pad_maximum_fusion.3), channel_id=1, source_target_pairs={{4,0},{8,4},{12,8},{16,12},{20,16},{24,20},{28,24},{32,28},{36,32}... | collective-permute-start | bytes 786440 | tf_op jit(solution)/shard_map/ppermute | solution.py:29
  148.2 12.5 %collective-permute-start.7 = (bf16[2,128,4,128]{3,1,2,0:T(8,128)(2,1)S(1)}, bf16[2,128,4,128]{3,1,2,0:T(8,128)(2,1)S(1)}, u32[]{:S(2)}, u32[]{:S(2)}) collective-permute-start(bf16[2,128,4,128]{3,1,2,0:T(8,128)(2,1)S(1)} %pad_maximum_fusion.4), channel_id=1, source_target_pairs={{8,0},{12,4},{16,8},{20,12},{24,16},{28,20},{32,24},{36,28},{40,32... | collective-permute-start | bytes 786440 | tf_op jit(solution)/shard_map/ppermute | solution.py:29
  150.1 26.3 %collective-permute-start.8 = (bf16[2,128,4,128]{3,1,2,0:T(8,128)(2,1)S(1)}, bf16[2,128,4,128]{3,1,2,0:T(8,128)(2,1)S(1)}, u32[]{:S(2)}, u32[]{:S(2)}) collective-permute-start(bf16[2,128,4,128]{3,1,2,0:T(8,128)(2,1)S(1)} %pad_maximum_fusion.5), channel_id=1, source_target_pairs={{12,0},{16,4},{20,8},{24,12},{28,16},{32,20},{36,24},{40,28},{44,3... | collective-permute-start | bytes 786440 | tf_op jit(solution)/shard_map/ppermute | solution.py:29
  151.7 3.2 copy-start
  152.1 45.7 %collective-permute-start.9 = (bf16[2,128,4,128]{3,1,2,0:T(8,128)(2,1)S(1)}, bf16[2,128,4,128]{3,1,2,0:T(8,128)(2,1)S(1)}, u32[]{:S(2)}, u32[]{:S(2)}) collective-permute-start(bf16[2,128,4,128]{3,1,2,0:T(8,128)(2,1)S(1)} %pad_maximum_fusion.6), channel_id=1, source_target_pairs={{16,0},{20,4},{24,8},{28,12},{32,16},{36,20},{40,24},{44,28},{48,3... | collective-permute-start | bytes 786440 | tf_op jit(solution)/shard_map/ppermute | solution.py:29
  154.6 3.3 %copy-start.2 = (bf16[4,4,128,128]{2,3,1,0:T(8,128)(2,1)}, bf16[4,4,128,128]{2,3,1,0:T(8,128)(2,1)S(1)}, u32[]{:S(2)}) copy-start(bf16[4,4,128,128]{2,3,1,0:T(8,128)(2,1)S(1)} %fusion.51) | copy-start | bytes 1572868
  154.9 3.5 %copy-start.15 = (bf16[128,512]{0,1:T(8,128)(2,1)S(1)}, bf16[128,512]{0,1:T(8,128)(2,1)}, u32[]{:S(2)}) copy-start(bf16[128,512]{0,1:T(8,128)(2,1)} %copy-done.14) | copy-start | bytes 393220
  154.9 42.8 %collective-permute-start.10 = (bf16[2,128,4,128]{3,1,2,0:T(8,128)(2,1)S(1)}, bf16[2,128,4,128]{3,1,2,0:T(8,128)(2,1)S(1)}, u32[]{:S(2)}, u32[]{:S(2)}) collective-permute-start(bf16[2,128,4,128]{3,1,2,0:T(8,128)(2,1)S(1)} %pad_maximum_fusion.7), channel_id=1, source_target_pairs={{20,0},{24,4},{28,8},{32,12},{36,16},{40,20},{44,24},{48,28},{52,3... | collective-permute-start | bytes 786440 | tf_op jit(solution)/shard_map/ppermute | solution.py:29
  158.8 44.2 %collective-permute-start.11 = (bf16[2,128,4,128]{3,1,2,0:T(8,128)(2,1)S(1)}, bf16[2,128,4,128]{3,1,2,0:T(8,128)(2,1)S(1)}, u32[]{:S(2)}, u32[]{:S(2)}) collective-permute-start(bf16[2,128,4,128]{3,1,2,0:T(8,128)(2,1)S(1)} %pad_maximum_fusion.8), channel_id=1, source_target_pairs={{24,0},{28,4},{32,8},{36,12},{40,16},{44,20},{48,24},{52,28},{56,3... | collective-permute-start | bytes 786440 | tf_op jit(solution)/shard_map/ppermute | solution.py:29
  160.3 42.9 %copy-start.18 = (f32[128,64]{1,0:T(8,128)S(1)}, f32[128,64]{1,0:T(8,128)}, u32[]{:S(2)}) copy-start(f32[128,64]{1,0:T(8,128)} %copy-done.16) | copy-start | bytes 98308
  160.4 42.9 %copy-start.22 = (f32[128,64]{1,0:T(8,128)S(1)}, f32[128,64]{1,0:T(8,128)}, u32[]{:S(2)}) copy-start(f32[128,64]{1,0:T(8,128)} %copy-done.20) | copy-start | bytes 98308
  160.7 42.8 %copy-start.42 = (f32[1,128]{1,0:T(1,128)S(1)}, f32[1,128]{1,0:T(1,128)}, u32[]{:S(2)}) copy-start(f32[1,128]{1,0:T(1,128)} %param.15) | copy-start | bytes 1540
  203.2 3.8 %copy-start.25 = (bf16[128,1024]{1,0:T(8,128)(2,1)S(1)}, bf16[128,1024]{1,0:T(8,128)(2,1)}, u32[]{:S(2)}) copy-start(bf16[128,1024]{1,0:T(8,128)(2,1)} %copy-done.24) | copy-start | bytes 786436
  203.3 3.8 %copy-start.26 = (f32[128,512]{1,0:T(8,128)S(1)}, f32[128,512]{1,0:T(8,128)}, u32[]{:S(2)}) copy-start(f32[128,512]{1,0:T(8,128)} %copy.321) | copy-start | bytes 786436
  203.3 3.8 %copy-start.40 = (f32[512]{0:T(512)S(1)}, f32[512]{0:T(512)}, u32[]{:S(2)}) copy-start(f32[512]{0:T(512)} %broadcast_bitcast_fusion.1) | copy-start | bytes 6148
  208.9 17.9 %copy-start.33 = (f32[128,16]{1,0:T(8,128)S(1)}, f32[128,16]{1,0:T(8,128)}, u32[]{:S(2)}) copy-start(f32[128,16]{1,0:T(8,128)} %copy-done.32) | copy-start | bytes 24580
  208.9 48.7 %all-to-all-start.2 = ((bf16[8,128,1024]{2,1,0:T(8,128)(2,1)}), bf16[8,128,1024]{2,1,0:T(8,128)(2,1)}, u32[]{:S(2)}, u32[]{:S(2)}) async-start(bf16[8,128,1024]{2,1,0:T(8,128)(2,1)} %broadcast_in_dim.60), calls=%async_computation.2 | async-start | bytes 4194304 | tf_op jit(solution)/shard_map/all_to_all | solution.py:81
  226.7 80.9 %reduce-scatter.4.cloned.1.call-start = ((), (), s32[]{:S(2)}) async-start(), calls=%async_computation.6 | async-start | bytes 2359296
  269.8 4.4 %copy-start.12 = (bf16[128,4,64]{2,0,1:T(8,128)(2,1)S(1)}, bf16[128,4,64]{2,0,1:T(8,128)(2,1)}, u32[]{:S(2)}) copy-start(bf16[128,4,64]{2,0,1:T(8,128)(2,1)} %copy-done.11) | copy-start | bytes 196612
  269.8 19.9 %all-to-all-start.3 = ((bf16[8,128,512]{2,1,0:T(8,128)(2,1)}), bf16[8,128,512]{2,1,0:T(8,128)(2,1)}, u32[]{:S(2)}, u32[]{:S(2)}) async-start(bf16[8,128,512]{2,1,0:T(8,128)(2,1)} %bitcast.585), calls=%async_computation.3 | async-start | bytes 2097152 | tf_op jit(solution)/shard_map/all_to_all | solution.py:220
  282.0 4.0 %copy-start.19 = (f32[128,64]{1,0:T(8,128)S(1)}, f32[128,64]{1,0:T(8,128)}, u32[]{:S(2)}) copy-start(f32[128,64]{1,0:T(8,128)} %copy-done.16) | copy-start | bytes 98308
  282.0 4.0 %copy-start.23 = (f32[128,64]{1,0:T(8,128)S(1)}, f32[128,64]{1,0:T(8,128)}, u32[]{:S(2)}) copy-start(f32[128,64]{1,0:T(8,128)} %copy-done.20) | copy-start | bytes 98308
  289.7 14.8 %collective-permute-start.12 = (bf16[8,128,512]{2,1,0:T(8,128)(2,1)}, bf16[8,128,512]{2,1,0:T(8,128)(2,1)}, u32[]{:S(2)}, u32[]{:S(2)}) collective-permute-start(bf16[8,128,512]{2,1,0:T(8,128)(2,1)} %all-to-all-done.3), channel_id=1, source_target_pairs={{0,3},{1,0},{2,1},{3,2},{4,7},{5,4},{6,5},{7,6},{8,11},{9,8},{10,9... | collective-permute-start | bytes 3145736 | tf_op jit(solution)/shard_map/ppermute | solution.py:34
  294.5 3.6 %copy-start.10 = (f32[1,128,2048]{2,1,0:T(8,128)S(1)}, f32[1,128,2048]{2,1,0:T(8,128)}, u32[]{:S(2)}) copy-start(f32[1,128,2048]{2,1,0:T(8,128)} %mul.632) | copy-start | bytes 3145732
  (16 other events, 26.4 us)
Sparse Core Ops, SparseCore 0:
  10.3 35.6 all-gather.1
  265.1 35.8 reduce-scatter.3

commit v12 on v11

--- a/solution.py
+++ b/solution.py
@@ -211,6 +211,7 @@
     weight_part = lax.dot_general(
         inputs_slice, group_back, (((0,), (0,)), ((), ())), preferred_element_type=jnp.float32
     )
+    weight_part = with_layout_constraint(weight_part, Layout(major_to_minor=(0, 1)))
     weight_part, group_back = lax.optimization_barrier((weight_part, group_back))
     grad_rows = lax.psum_scatter(weight_part, "cz", scatter_dimension=0, tiled=True)
     slice_grad = lax.dot_general(

time: 320 us -> 315 us (0.984)
  local copies, waits for them, and re-layouts: 43.7 us -> 39.4 us
    unnamed x100 -> x95, local copies, waits for them, and re-layouts: 15.6 us -> 10.8 us
where the time goes in v12:
time: 315 us; the launch traced here: 313 us
  waiting for transfers between devices  126 us (40%)
  starting transfers between devices  73.9 us (23%)
  matrix products  39.7 us (13%)
  local copies, waits for them, and re-layouts  39.4 us (13%)
  other arithmetic  19 us (6%)
  between operations  15.4 us (5%)
    ppermute x12, waiting for transfers between devices, passed_along(): return lax.ppermute(block, axis, route)  52.1 us
    ppermute x12, starting transfers between devices, passed_along(): return lax.ppermute(block, axis, route)  37.1 us
    all_to_all x1, waiting for transfers between devices, gathered(): received = lax.all_to_all(copies, axis, 0, 0, tiled=True)  24.4 us
    all_to_all x1, waiting for transfers between devices, summed_over(): received = lax.all_to_all(pieces, axis, 0, 0, tiled=True)  20.5 us
    all_to_all x1, starting transfers between devices, gathered(): received = lax.all_to_all(copies, axis, 0, 0, tiled=True)  17.9 us
    all_to_all x1, waiting for transfers between devices, local(): inputs_slice = lax.all_to_all(tokens_here, 'cb', 1, 0, tiled=True)  13 us
    all_gather x1, waiting for transfers between devices, local(): weight_slice = lax.all_gather(both_rows, 'cz', axis=0, tiled=True)  11.4 us
    unnamed x95, local copies, waits for them, and re-layouts  10.8 us
  transfers between devices with their start and end apart: 19, of which 10 were waited for; matrix products, arithmetic and copies ran while one was open for 20% of the time, Pallas kernels for 0%

profile of v12, /device:TPU:33, one launch (start us, length us, event | category | flops | bytes accessed | tf_op | source)
XLA Modules:
  0.0 313.2 jit_solution(11205557846730289113)
XLA Ops:
  7.2 1.5 pad_maximum_fusion.11
  8.8 2.3 copy.252
  11.1 6.7 %all-to-all-start = ((bf16[128,8,512]{0,2,1:T(8,128)(2,1)}), bf16[128,8,512]{0,2,1:T(8,128)(2,1)S(1)}, u32[]{:S(2)}, u32[]{:S(2)}) async-start(bf16[128,8,512]{0,2,1:T(8,128)(2,1)} %bitcast.2), calls=%async_computation | async-start | bytes 2097152 | tf_op jit(solution)/shard_map/all_to_all | solution.py:108
  20.4 13.0 %all-to-all-done = bf16[128,8,512]{0,2,1:T(8,128)(2,1)S(1)} async-done(((bf16[128,8,512]{0,2,1:T(8,128)(2,1)}), bf16[128,8,512]{0,2,1:T(8,128)(2,1)S(1)}, u32[]{:S(2)}, u32[]{:S(2)}) %all-to-all-start) | async-done | bytes 1048608 | tf_op jit(solution)/shard_map/all_to_all | solution.py:108
  33.4 1.3 copy.253
  34.7 11.4 %all-gather.2.cloned.1.call-done = bf16[512,1024]{1,0:T(8,128)(2,1)} async-done(((bf16[64,1024]{1,0:T(8,128)(2,1)}), bf16[512,1024]{1,0:T(8,128)(2,1)}) %all-gather.2.cloned.1.call-update) | async-done | bytes 1048592 | tf_op jit(solution)/shard_map/all_gather | solution.py:107
  46.1 4.2 %convolution_convert_fusion = bf16[1024,1024]{0,1:T(8,128)(2,1)} fusion(bf16[1024,512]{1,0:T(8,128)(2,1)} %bitcast.582, bf16[512,1024]{1,0:T(8,128)(2,1)} %all-gather.2.cloned.1.call-done), kind=kOutput, calls=%fused_computation | convolution fusion | flops 1074790400 | bytes 4194304 | tf_op jit(solution)/shard_map/dot_general | solution.py:110
  50.2 6.6 %all-to-all-start.1 = ((bf16[8,128,1024]{2,1,0:T(8,128)(2,1)}), bf16[8,128,1024]{2,1,0:T(8,128)(2,1)}, u32[]{:S(2)}, u32[]{:S(2)}) async-start(bf16[8,128,1024]{2,1,0:T(8,128)(2,1)} %bitcast.576), calls=%async_computation.1 | async-start | bytes 4194304 | tf_op jit(solution)/shard_map/all_to_all | solution.py:87
  57.6 1.3 copy.261
  62.1 20.5 %all-to-all-done.1 = bf16[8,128,1024]{2,1,0:T(8,128)(2,1)} async-done(((bf16[8,128,1024]{2,1,0:T(8,128)(2,1)}), bf16[8,128,1024]{2,1,0:T(8,128)(2,1)}, u32[]{:S(2)}, u32[]{:S(2)}) %all-to-all-start.1) | async-done | bytes 2097184 | tf_op jit(solution)/shard_map/all_to_all | solution.py:87
  82.6 2.0 reduce
  88.0 2.3 collective-permute-start
  90.3 4.2 %collective-permute-start.2 = (bf16[2,128,4,128]{3,1,2,0:T(8,128)(2,1)}, bf16[2,128,4,128]{3,1,2,0:T(8,128)(2,1)S(1)}, u32[]{:S(2)}, u32[]{:S(2)}) collective-permute-start(bf16[2,128,4,128]{3,1,2,0:T(8,128)(2,1)} %pad_maximum_fusion.2), channel_id=1, source_target_pairs={{0,12},{4,16},{8,20},{12,24},{16,28},{20,32},{24,36},{28,40},{32,4... | collective-permute-start | bytes 786440 | tf_op jit(solution)/shard_map/ppermute | solution.py:29
  94.5 3.2 %collective-permute-start.3 = (bf16[2,128,4,128]{3,1,2,0:T(8,128)(2,1)}, bf16[2,128,4,128]{3,1,2,0:T(8,128)(2,1)S(1)}, u32[]{:S(2)}, u32[]{:S(2)}) collective-permute-start(bf16[2,128,4,128]{3,1,2,0:T(8,128)(2,1)} %pad_maximum_fusion.2), channel_id=1, source_target_pairs={{0,16},{4,20},{8,24},{12,28},{16,32},{20,36},{24,40},{28,44},{32,4... | collective-permute-start | bytes 786440 | tf_op jit(solution)/shard_map/ppermute | solution.py:29
  97.7 4.4 %collective-permute-start.4 = (bf16[2,128,4,128]{3,1,2,0:T(8,128)(2,1)}, bf16[2,128,4,128]{3,1,2,0:T(8,128)(2,1)}, u32[]{:S(2)}, u32[]{:S(2)}) collective-permute-start(bf16[2,128,4,128]{3,1,2,0:T(8,128)(2,1)} %pad_maximum_fusion.2), channel_id=1, source_target_pairs={{0,20},{4,24},{8,28},{12,32},{16,36},{20,40},{24,44},{28,48},{32,5... | collective-permute-start | bytes 786440 | tf_op jit(solution)/shard_map/ppermute | solution.py:29
  102.1 7.0 %collective-permute-start.5 = (bf16[2,128,4,128]{3,1,2,0:T(8,128)(2,1)}, bf16[2,128,4,128]{3,1,2,0:T(8,128)(2,1)}, u32[]{:S(2)}, u32[]{:S(2)}) collective-permute-start(bf16[2,128,4,128]{3,1,2,0:T(8,128)(2,1)} %pad_maximum_fusion.2), channel_id=1, source_target_pairs={{0,24},{4,28},{8,32},{12,36},{16,40},{20,44},{24,48},{28,52},{32,5... | collective-permute-start | bytes 786440 | tf_op jit(solution)/shard_map/ppermute | solution.py:29
  110.7 1.4 copy.316
  113.2 3.4 %collective-permute-start.1 = (bf16[2,128,4,128]{3,1,2,0:T(8,128)(2,1)}, bf16[2,128,4,128]{3,1,2,0:T(8,128)(2,1)S(1)}, u32[]{:S(2)}, u32[]{:S(2)}) collective-permute-start(bf16[2,128,4,128]{3,1,2,0:T(8,128)(2,1)} %pad_maximum_fusion.2), channel_id=1, source_target_pairs={{0,8},{4,12},{8,16},{12,20},{16,24},{20,28},{24,32},{28,36},{32,40... | collective-permute-start | bytes 786440 | tf_op jit(solution)/shard_map/ppermute | solution.py:29
  120.0 9.8 %collective-permute-done.5 = bf16[2,128,4,128]{3,1,2,0:T(8,128)(2,1)} collective-permute-done((bf16[2,128,4,128]{3,1,2,0:T(8,128)(2,1)}, bf16[2,128,4,128]{3,1,2,0:T(8,128)(2,1)}, u32[]{:S(2)}, u32[]{:S(2)}) %collective-permute-start.5) | collective-permute-done | bytes 262176 | tf_op jit(solution)/shard_map/ppermute | solution.py:29
  141.4 6.0 %collective-permute-start.6 = (bf16[2,128,4,128]{3,1,2,0:T(8,128)(2,1)S(1)}, bf16[2,128,4,128]{3,1,2,0:T(8,128)(2,1)S(1)}, u32[]{:S(2)}, u32[]{:S(2)}) collective-permute-start(bf16[2,128,4,128]{3,1,2,0:T(8,128)(2,1)S(1)} %pad_maximum_fusion.3), channel_id=1, source_target_pairs={{4,0},{8,4},{12,8},{16,12},{20,16},{24,20},{28,24},{32,28},{36,32}... | collective-permute-start | bytes 786440 | tf_op jit(solution)/shard_map/ppermute | solution.py:29
  154.8 1.4 collective-permute-start.10
  160.6 15.7 %collective-permute-done.8 = bf16[2,128,4,128]{3,1,2,0:T(8,128)(2,1)S(1)} collective-permute-done((bf16[2,128,4,128]{3,1,2,0:T(8,128)(2,1)S(1)}, bf16[2,128,4,128]{3,1,2,0:T(8,128)(2,1)S(1)}, u32[]{:S(2)}, u32[]{:S(2)}) %collective-permute-start.8) | collective-permute-done | bytes 262176 | tf_op jit(solution)/shard_map/ppermute | solution.py:29
  176.2 21.4 %collective-permute-done.9 = bf16[2,128,4,128]{3,1,2,0:T(8,128)(2,1)S(1)} collective-permute-done((bf16[2,128,4,128]{3,1,2,0:T(8,128)(2,1)S(1)}, bf16[2,128,4,128]{3,1,2,0:T(8,128)(2,1)S(1)}, u32[]{:S(2)}, u32[]{:S(2)}) %collective-permute-start.9) | collective-permute-done | bytes 262176 | tf_op jit(solution)/shard_map/ppermute | solution.py:29
  197.6 5.2 %collective-permute-done.11 = bf16[2,128,4,128]{3,1,2,0:T(8,128)(2,1)S(1)} collective-permute-done((bf16[2,128,4,128]{3,1,2,0:T(8,128)(2,1)S(1)}, bf16[2,128,4,128]{3,1,2,0:T(8,128)(2,1)S(1)}, u32[]{:S(2)}, u32[]{:S(2)}) %collective-permute-start.11) | collective-permute-done | bytes 262176 | tf_op jit(solution)/shard_map/ppermute | solution.py:29
  207.1 1.6 broadcast_in_dim.60
  208.8 17.9 %all-to-all-start.2 = ((bf16[8,128,1024]{2,1,0:T(8,128)(2,1)}), bf16[8,128,1024]{2,1,0:T(8,128)(2,1)}, u32[]{:S(2)}, u32[]{:S(2)}) async-start(bf16[8,128,1024]{2,1,0:T(8,128)(2,1)} %broadcast_in_dim.60), calls=%async_computation.2 | async-start | bytes 4194304 | tf_op jit(solution)/shard_map/all_to_all | solution.py:81
  226.7 1.3 mul.517
  228.0 1.4 mul.518
  229.4 1.3 mul.631
  230.7 2.4 mul.632
  233.1 24.4 %all-to-all-done.2 = bf16[8,128,1024]{2,1,0:T(8,128)(2,1)} async-done(((bf16[8,128,1024]{2,1,0:T(8,128)(2,1)}), bf16[8,128,1024]{2,1,0:T(8,128)(2,1)}, u32[]{:S(2)}, u32[]{:S(2)}) %all-to-all-start.2) | async-done | bytes 2097184 | tf_op jit(solution)/shard_map/all_to_all | solution.py:81
  257.5 4.5 %convolution_bitcast_fusion = f32[512,1024]{1,0:T(8,128)} fusion(bf16[1024,1024]{1,0:T(8,128)(2,1)} %bitcast.142, bf16[1024,512]{1,0:T(8,128)(2,1)} %bitcast.583), kind=kOutput, calls=%fused_computation.1 | convolution fusion | flops 1073741824 | bytes 5242880 | tf_op jit(solution)/shard_map/dot_general | solution.py:211
  262.6 4.1 %convolution_convert_fusion.1 = bf16[1024,512]{1,0:T(8,128)(2,1)} fusion(bf16[1024,1024]{1,0:T(8,128)(2,1)} %bitcast.142, bf16[512,1024]{1,0:T(8,128)(2,1)} %all-gather.2.cloned.1.call-done), kind=kOutput, calls=%fused_computation.2 | convolution fusion | flops 1074266112 | bytes 4194304 | tf_op jit(solution)/shard_map/dot_general | solution.py:217
  266.8 4.4 %all-to-all-start.3 = ((bf16[8,128,512]{2,1,0:T(8,128)(2,1)}), bf16[8,128,512]{2,1,0:T(8,128)(2,1)}, u32[]{:S(2)}, u32[]{:S(2)}) async-start(bf16[8,128,512]{2,1,0:T(8,128)(2,1)} %bitcast.584), calls=%async_computation.4 | async-start | bytes 2097152 | tf_op jit(solution)/shard_map/all_to_all | solution.py:221
  271.6 1.3 fusion.96
  273.4 1.3 fusion.98
  274.7 1.3 fusion.99
  278.9 1.6 copy.458
  280.5 2.4 copy.459
  282.9 2.8 multiply_add_fusion
  287.9 2.2 multiply_reduce_fusion
  290.1 1.3 mul.636
  291.4 2.5 mul.637
  295.0 3.0 fusion.88
  298.0 3.5 %collective-permute-done.12 = bf16[8,128,512]{2,1,0:T(8,128)(2,1)} collective-permute-done((bf16[8,128,512]{2,1,0:T(8,128)(2,1)}, bf16[8,128,512]{2,1,0:T(8,128)(2,1)}, u32[]{:S(2)}, u32[]{:S(2)}) %collective-permute-start.12) | collective-permute-done | bytes 1048608 | tf_op jit(solution)/shard_map/ppermute | solution.py:34
  301.5 1.8 copy.337
  303.3 1.3 broadcast_in_dim_reshape.3
  304.6 1.7 slice_bitcast_fusion.1
  (211 shorter events, 50.6 us)
Async XLA Ops:
  7.2 38.9 %all-gather.2.cloned.1.call-start = ((), (), s32[]{:S(2)}) async-start(), calls=%async_computation.5 | async-start | bytes 1179648 | tf_op jit(solution)/shard_map/all_gather | solution.py:107
  8.8 9.0 %copy-start.13 = (bf16[1,128,2048]{2,1,0:T(8,128)(2,1)S(1)}, bf16[1,128,2048]{2,1,0:T(8,128)(2,1)}, u32[]{:S(2)}) copy-start(bf16[1,128,2048]{2,1,0:T(8,128)(2,1)} %param.9) | copy-start | bytes 1572868
  11.1 22.3 %all-to-all-start = ((bf16[128,8,512]{0,2,1:T(8,128)(2,1)}), bf16[128,8,512]{0,2,1:T(8,128)(2,1)S(1)}, u32[]{:S(2)}, u32[]{:S(2)}) async-start(bf16[128,8,512]{0,2,1:T(8,128)(2,1)} %bitcast.2), calls=%async_computation | async-start | bytes 2097152 | tf_op jit(solution)/shard_map/all_to_all | solution.py:108
  18.8 38.0 %copy-start.16 = (f32[128,64]{1,0:T(8,128)}, f32[128,64]{1,0:T(8,128)S(1)}, u32[]{:S(2)}) copy-start(f32[128,64]{1,0:T(8,128)S(1)} %get-tuple-element.67) | copy-start | bytes 98308
  18.8 38.0 %copy-start.20 = (f32[128,64]{1,0:T(8,128)}, f32[128,64]{1,0:T(8,128)S(1)}, u32[]{:S(2)}) copy-start(f32[128,64]{1,0:T(8,128)S(1)} %get-tuple-element.68) | copy-start | bytes 98308
  50.2 32.4 %all-to-all-start.1 = ((bf16[8,128,1024]{2,1,0:T(8,128)(2,1)}), bf16[8,128,1024]{2,1,0:T(8,128)(2,1)}, u32[]{:S(2)}, u32[]{:S(2)}) async-start(bf16[8,128,1024]{2,1,0:T(8,128)(2,1)} %bitcast.576), calls=%async_computation.1 | async-start | bytes 4194304 | tf_op jit(solution)/shard_map/all_to_all | solution.py:87
  57.4 2.8 copy-start.41
  62.1 24.6 %copy-start.17 = (f32[128,64]{1,0:T(8,128)S(1)}, f32[128,64]{1,0:T(8,128)}, u32[]{:S(2)}) copy-start(f32[128,64]{1,0:T(8,128)} %copy-done.16) | copy-start | bytes 98308
  62.1 24.6 %copy-start.21 = (f32[128,64]{1,0:T(8,128)S(1)}, f32[128,64]{1,0:T(8,128)}, u32[]{:S(2)}) copy-start(f32[128,64]{1,0:T(8,128)} %copy-done.20) | copy-start | bytes 98308
  86.9 31.0 %copy-start.11 = (bf16[128,4,64]{2,0,1:T(8,128)(2,1)}, bf16[128,4,64]{2,0,1:T(8,128)(2,1)S(1)}, u32[]{:S(2)}) copy-start(bf16[128,4,64]{2,0,1:T(8,128)(2,1)S(1)} %get-tuple-element.37) | copy-start | bytes 196612
  87.0 47.4 %copy-start.14 = (bf16[128,512]{0,1:T(8,128)(2,1)}, bf16[128,512]{0,1:T(8,128)(2,1)S(1)}, u32[]{:S(2)}) copy-start(bf16[128,512]{0,1:T(8,128)(2,1)S(1)} %copy.258) | copy-start | bytes 393220
  88.0 25.2 %collective-permute-start = (bf16[2,128,4,128]{3,1,2,0:T(8,128)(2,1)}, bf16[2,128,4,128]{3,1,2,0:T(8,128)(2,1)}, u32[]{:S(2)}, u32[]{:S(2)}) collective-permute-start(bf16[2,128,4,128]{3,1,2,0:T(8,128)(2,1)} %pad_maximum_fusion.2), channel_id=1, source_target_pairs={{0,4},{4,8},{8,12},{12,16},{16,20},{20,24},{24,28},{28,32},{32,36}... | collective-permute-start | bytes 786440 | tf_op jit(solution)/shard_map/ppermute | solution.py:29
  90.3 27.6 %collective-permute-start.2 = (bf16[2,128,4,128]{3,1,2,0:T(8,128)(2,1)}, bf16[2,128,4,128]{3,1,2,0:T(8,128)(2,1)S(1)}, u32[]{:S(2)}, u32[]{:S(2)}) collective-permute-start(bf16[2,128,4,128]{3,1,2,0:T(8,128)(2,1)} %pad_maximum_fusion.2), channel_id=1, source_target_pairs={{0,12},{4,16},{8,20},{12,24},{16,28},{20,32},{24,36},{28,40},{32,4... | collective-permute-start | bytes 786440 | tf_op jit(solution)/shard_map/ppermute | solution.py:29
  94.5 23.8 %collective-permute-start.3 = (bf16[2,128,4,128]{3,1,2,0:T(8,128)(2,1)}, bf16[2,128,4,128]{3,1,2,0:T(8,128)(2,1)S(1)}, u32[]{:S(2)}, u32[]{:S(2)}) collective-permute-start(bf16[2,128,4,128]{3,1,2,0:T(8,128)(2,1)} %pad_maximum_fusion.2), channel_id=1, source_target_pairs={{0,16},{4,20},{8,24},{12,28},{16,32},{20,36},{24,40},{28,44},{32,4... | collective-permute-start | bytes 786440 | tf_op jit(solution)/shard_map/ppermute | solution.py:29
  97.7 21.0 %collective-permute-start.4 = (bf16[2,128,4,128]{3,1,2,0:T(8,128)(2,1)}, bf16[2,128,4,128]{3,1,2,0:T(8,128)(2,1)}, u32[]{:S(2)}, u32[]{:S(2)}) collective-permute-start(bf16[2,128,4,128]{3,1,2,0:T(8,128)(2,1)} %pad_maximum_fusion.2), channel_id=1, source_target_pairs={{0,20},{4,24},{8,28},{12,32},{16,36},{20,40},{24,44},{28,48},{32,5... | collective-permute-start | bytes 786440 | tf_op jit(solution)/shard_map/ppermute | solution.py:29
  102.1 27.7 %collective-permute-start.5 = (bf16[2,128,4,128]{3,1,2,0:T(8,128)(2,1)}, bf16[2,128,4,128]{3,1,2,0:T(8,128)(2,1)}, u32[]{:S(2)}, u32[]{:S(2)}) collective-permute-start(bf16[2,128,4,128]{3,1,2,0:T(8,128)(2,1)} %pad_maximum_fusion.2), channel_id=1, source_target_pairs={{0,24},{4,28},{8,32},{12,36},{16,40},{20,44},{24,48},{28,52},{32,5... | collective-permute-start | bytes 786440 | tf_op jit(solution)/shard_map/ppermute | solution.py:29
  112.0 5.9 %copy-start.38 = (pred[128,128]{0,1:T(8,128)(4,1)S(1)}, pred[128,128]{0,1:T(8,128)(4,1)}, u32[]{:S(2)}) copy-start(pred[128,128]{0,1:T(8,128)(4,1)} %get-tuple-element.63) | copy-start | bytes 49156
  113.2 5.1 %copy-start.37 = (pred[128,128]{0,1:T(8,128)(4,1)S(1)}, pred[128,128]{0,1:T(8,128)(4,1)}, u32[]{:S(2)}) copy-start(pred[128,128]{0,1:T(8,128)(4,1)} %get-tuple-element.64) | copy-start | bytes 49156
  113.2 17.9 %collective-permute-start.1 = (bf16[2,128,4,128]{3,1,2,0:T(8,128)(2,1)}, bf16[2,128,4,128]{3,1,2,0:T(8,128)(2,1)S(1)}, u32[]{:S(2)}, u32[]{:S(2)}) collective-permute-start(bf16[2,128,4,128]{3,1,2,0:T(8,128)(2,1)} %pad_maximum_fusion.2), channel_id=1, source_target_pairs={{0,8},{4,12},{8,16},{12,20},{16,24},{20,28},{24,32},{28,36},{32,40... | collective-permute-start | bytes 786440 | tf_op jit(solution)/shard_map/ppermute | solution.py:29
  117.9 31.5 %copy-start.29 = (bf16[2,128,4,128]{3,1,2,0:T(8,128)(2,1)}, bf16[2,128,4,128]{3,1,2,0:T(8,128)(2,1)S(1)}, u32[]{:S(2)}) copy-start(bf16[2,128,4,128]{3,1,2,0:T(8,128)(2,1)S(1)} %collective-permute-done.2) | copy-start | bytes 786436
  118.3 33.0 %copy-start.30 = (bf16[2,128,4,128]{3,1,2,0:T(8,128)(2,1)}, bf16[2,128,4,128]{3,1,2,0:T(8,128)(2,1)S(1)}, u32[]{:S(2)}) copy-start(bf16[2,128,4,128]{3,1,2,0:T(8,128)(2,1)S(1)} %collective-permute-done.3) | copy-start | bytes 786436
  118.7 12.4 %copy-start.35 = (pred[128,128]{0,1:T(8,128)(4,1)S(1)}, pred[128,128]{0,1:T(8,128)(4,1)}, u32[]{:S(2)}) copy-start(pred[128,128]{0,1:T(8,128)(4,1)} %get-tuple-element.62) | copy-start | bytes 49156
  131.1 16.2 %copy-start.27 = (bf16[2,128,4,128]{3,1,2,0:T(8,128)(2,1)}, bf16[2,128,4,128]{3,1,2,0:T(8,128)(2,1)S(1)}, u32[]{:S(2)}) copy-start(bf16[2,128,4,128]{3,1,2,0:T(8,128)(2,1)S(1)} %collective-permute-done.1) | copy-start | bytes 786436
  141.0 7.0 %copy-start.6 = (bf16[4,4,128,128]{2,3,1,0:T(8,128)(2,1)}, bf16[4,4,128,128]{2,3,1,0:T(8,128)(2,1)S(1)}, u32[]{:S(2)}) copy-start(bf16[4,4,128,128]{2,3,1,0:T(8,128)(2,1)S(1)} %fusion.47) | copy-start | bytes 1572868
  141.4 17.3 %collective-permute-start.6 = (bf16[2,128,4,128]{3,1,2,0:T(8,128)(2,1)S(1)}, bf16[2,128,4,128]{3,1,2,0:T(8,128)(2,1)S(1)}, u32[]{:S(2)}, u32[]{:S(2)}) collective-permute-start(bf16[2,128,4,128]{3,1,2,0:T(8,128)(2,1)S(1)} %pad_maximum_fusion.3), channel_id=1, source_target_pairs={{4,0},{8,4},{12,8},{16,12},{20,16},{24,20},{28,24},{32,28},{36,32}... | collective-permute-start | bytes 786440 | tf_op jit(solution)/shard_map/ppermute | solution.py:29
  148.0 12.5 %collective-permute-start.7 = (bf16[2,128,4,128]{3,1,2,0:T(8,128)(2,1)S(1)}, bf16[2,128,4,128]{3,1,2,0:T(8,128)(2,1)S(1)}, u32[]{:S(2)}, u32[]{:S(2)}) collective-permute-start(bf16[2,128,4,128]{3,1,2,0:T(8,128)(2,1)S(1)} %pad_maximum_fusion.4), channel_id=1, source_target_pairs={{8,0},{12,4},{16,8},{20,12},{24,16},{28,20},{32,24},{36,28},{40,32... | collective-permute-start | bytes 786440 | tf_op jit(solution)/shard_map/ppermute | solution.py:29
  150.0 26.3 %collective-permute-start.8 = (bf16[2,128,4,128]{3,1,2,0:T(8,128)(2,1)S(1)}, bf16[2,128,4,128]{3,1,2,0:T(8,128)(2,1)S(1)}, u32[]{:S(2)}, u32[]{:S(2)}) collective-permute-start(bf16[2,128,4,128]{3,1,2,0:T(8,128)(2,1)S(1)} %pad_maximum_fusion.5), channel_id=1, source_target_pairs={{12,0},{16,4},{20,8},{24,12},{28,16},{32,20},{36,24},{40,28},{44,3... | collective-permute-start | bytes 786440 | tf_op jit(solution)/shard_map/ppermute | solution.py:29
  151.6 3.2 %copy-start = (bf16[4,4,128,128]{2,3,1,0:T(8,128)(2,1)}, bf16[4,4,128,128]{2,3,1,0:T(8,128)(2,1)S(1)}, u32[]{:S(2)}) copy-start(bf16[4,4,128,128]{2,3,1,0:T(8,128)(2,1)S(1)} %fusion.50) | copy-start | bytes 1572868
  151.9 45.7 %collective-permute-start.9 = (bf16[2,128,4,128]{3,1,2,0:T(8,128)(2,1)S(1)}, bf16[2,128,4,128]{3,1,2,0:T(8,128)(2,1)S(1)}, u32[]{:S(2)}, u32[]{:S(2)}) collective-permute-start(bf16[2,128,4,128]{3,1,2,0:T(8,128)(2,1)S(1)} %pad_maximum_fusion.6), channel_id=1, source_target_pairs={{16,0},{20,4},{24,8},{28,12},{32,16},{36,20},{40,24},{44,28},{48,3... | collective-permute-start | bytes 786440 | tf_op jit(solution)/shard_map/ppermute | solution.py:29
  154.4 3.3 %copy-start.2 = (bf16[4,4,128,128]{2,3,1,0:T(8,128)(2,1)}, bf16[4,4,128,128]{2,3,1,0:T(8,128)(2,1)S(1)}, u32[]{:S(2)}) copy-start(bf16[4,4,128,128]{2,3,1,0:T(8,128)(2,1)S(1)} %fusion.51) | copy-start | bytes 1572868
  154.8 3.5 %copy-start.15 = (bf16[128,512]{0,1:T(8,128)(2,1)S(1)}, bf16[128,512]{0,1:T(8,128)(2,1)}, u32[]{:S(2)}) copy-start(bf16[128,512]{0,1:T(8,128)(2,1)} %copy-done.14) | copy-start | bytes 393220
  154.8 42.8 %collective-permute-start.10 = (bf16[2,128,4,128]{3,1,2,0:T(8,128)(2,1)S(1)}, bf16[2,128,4,128]{3,1,2,0:T(8,128)(2,1)S(1)}, u32[]{:S(2)}, u32[]{:S(2)}) collective-permute-start(bf16[2,128,4,128]{3,1,2,0:T(8,128)(2,1)S(1)} %pad_maximum_fusion.7), channel_id=1, source_target_pairs={{20,0},{24,4},{28,8},{32,12},{36,16},{40,20},{44,24},{48,28},{52,3... | collective-permute-start | bytes 786440 | tf_op jit(solution)/shard_map/ppermute | solution.py:29
  158.7 44.2 %collective-permute-start.11 = (bf16[2,128,4,128]{3,1,2,0:T(8,128)(2,1)S(1)}, bf16[2,128,4,128]{3,1,2,0:T(8,128)(2,1)S(1)}, u32[]{:S(2)}, u32[]{:S(2)}) collective-permute-start(bf16[2,128,4,128]{3,1,2,0:T(8,128)(2,1)S(1)} %pad_maximum_fusion.8), channel_id=1, source_target_pairs={{24,0},{28,4},{32,8},{36,12},{40,16},{44,20},{48,24},{52,28},{56,3... | collective-permute-start | bytes 786440 | tf_op jit(solution)/shard_map/ppermute | solution.py:29
  160.2 42.9 %copy-start.18 = (f32[128,64]{1,0:T(8,128)S(1)}, f32[128,64]{1,0:T(8,128)}, u32[]{:S(2)}) copy-start(f32[128,64]{1,0:T(8,128)} %copy-done.16) | copy-start | bytes 98308
  160.3 42.9 %copy-start.22 = (f32[128,64]{1,0:T(8,128)S(1)}, f32[128,64]{1,0:T(8,128)}, u32[]{:S(2)}) copy-start(f32[128,64]{1,0:T(8,128)} %copy-done.20) | copy-start | bytes 98308
  160.6 42.8 %copy-start.42 = (f32[1,128]{1,0:T(1,128)S(1)}, f32[1,128]{1,0:T(1,128)}, u32[]{:S(2)}) copy-start(f32[1,128]{1,0:T(1,128)} %param.15) | copy-start | bytes 1540
  203.1 3.8 %copy-start.25 = (bf16[128,1024]{1,0:T(8,128)(2,1)S(1)}, bf16[128,1024]{1,0:T(8,128)(2,1)}, u32[]{:S(2)}) copy-start(bf16[128,1024]{1,0:T(8,128)(2,1)} %copy-done.24) | copy-start | bytes 786436
  203.1 3.8 %copy-start.26 = (f32[128,512]{1,0:T(8,128)S(1)}, f32[128,512]{1,0:T(8,128)}, u32[]{:S(2)}) copy-start(f32[128,512]{1,0:T(8,128)} %copy.315) | copy-start | bytes 786436
  203.2 3.8 %copy-start.40 = (f32[512]{0:T(512)S(1)}, f32[512]{0:T(512)}, u32[]{:S(2)}) copy-start(f32[512]{0:T(512)} %broadcast_bitcast_fusion.1) | copy-start | bytes 6148
  208.8 17.9 %copy-start.33 = (f32[128,16]{1,0:T(8,128)S(1)}, f32[128,16]{1,0:T(8,128)}, u32[]{:S(2)}) copy-start(f32[128,16]{1,0:T(8,128)} %copy-done.32) | copy-start | bytes 24580
  208.8 48.7 %all-to-all-start.2 = ((bf16[8,128,1024]{2,1,0:T(8,128)(2,1)}), bf16[8,128,1024]{2,1,0:T(8,128)(2,1)}, u32[]{:S(2)}, u32[]{:S(2)}) async-start(bf16[8,128,1024]{2,1,0:T(8,128)(2,1)} %broadcast_in_dim.60), calls=%async_computation.2 | async-start | bytes 4194304 | tf_op jit(solution)/shard_map/all_to_all | solution.py:81
  226.6 78.0 %reduce-scatter.2.cloned.1.call-start = ((), (), s32[]{:S(2)}) async-start(), calls=%async_computation.6 | async-start | bytes 2359296 | tf_op jit(solution)/shard_map/reduce_scatter | solution.py:216
  266.8 4.4 %copy-start.12 = (bf16[128,4,64]{2,0,1:T(8,128)(2,1)S(1)}, bf16[128,4,64]{2,0,1:T(8,128)(2,1)}, u32[]{:S(2)}) copy-start(bf16[128,4,64]{2,0,1:T(8,128)(2,1)} %copy-done.11) | copy-start | bytes 196612
  266.8 19.9 %all-to-all-start.3 = ((bf16[8,128,512]{2,1,0:T(8,128)(2,1)}), bf16[8,128,512]{2,1,0:T(8,128)(2,1)}, u32[]{:S(2)}, u32[]{:S(2)}) async-start(bf16[8,128,512]{2,1,0:T(8,128)(2,1)} %bitcast.584), calls=%async_computation.4 | async-start | bytes 2097152 | tf_op jit(solution)/shard_map/all_to_all | solution.py:221
  278.9 4.0 %copy-start.19 = (f32[128,64]{1,0:T(8,128)S(1)}, f32[128,64]{1,0:T(8,128)}, u32[]{:S(2)}) copy-start(f32[128,64]{1,0:T(8,128)} %copy-done.16) | copy-start | bytes 98308
  278.9 4.0 %copy-start.23 = (f32[128,64]{1,0:T(8,128)S(1)}, f32[128,64]{1,0:T(8,128)}, u32[]{:S(2)}) copy-start(f32[128,64]{1,0:T(8,128)} %copy-done.20) | copy-start | bytes 98308
  286.7 14.8 %collective-permute-start.12 = (bf16[8,128,512]{2,1,0:T(8,128)(2,1)}, bf16[8,128,512]{2,1,0:T(8,128)(2,1)}, u32[]{:S(2)}, u32[]{:S(2)}) collective-permute-start(bf16[8,128,512]{2,1,0:T(8,128)(2,1)} %all-to-all-done.3), channel_id=1, source_target_pairs={{0,3},{1,0},{2,1},{3,2},{4,7},{5,4},{6,5},{7,6},{8,11},{9,8},{10,9... | collective-permute-start | bytes 3145736 | tf_op jit(solution)/shard_map/ppermute | solution.py:34
  291.4 3.6 %copy-start.10 = (f32[1,128,2048]{2,1,0:T(8,128)S(1)}, f32[1,128,2048]{2,1,0:T(8,128)}, u32[]{:S(2)}) copy-start(f32[1,128,2048]{2,1,0:T(8,128)} %mul.632) | copy-start | bytes 3145732
  (16 other events, 26.4 us)
Sparse Core Ops, SparseCore 0:
  10.3 35.6 all-gather.1
  262.1 35.8 reduce-scatter.1
